TPU v7x, 32 devices: a whole 2x2x4 slice. The times are simulated.
32 devices in a mesh: grp: 8 (over z, x), rep: 4 (over y, core).
Axes of the slice: x: 2, y: 2, z: 4, core: 2. Of those that a mesh axis runs over, the one named last changes fastest.
Arguments:
- three_center: bfloat16 [4, 64, 32, 6, 4096], P('rep', 'grp'), may hold values from -2 to 2
- metric: bfloat16 [4, 64, 64], P('rep'), may hold values from -0.75 to 0.75
- occupied: bfloat16 [2048, 48], replicated, may hold values from -0.3125 to 0.3125
- nu_list: int32 [32, 6], replicated, may hold values from 0 to 31, as said below
- nu_count: int32 [32], replicated, may hold values from 1 to 6
- block_size: int32 [32], replicated, may hold values from 32 to 64
Outputs:
- exchange_matrix: float32 [2048, 2048], P('rep', 'grp')
Inputs may be any that keep to these rules, and one draw needn't show every extreme that they name: `nu_list`: entry 0 of row m is m itself; the other entries of a row are distinct blocks other than m.
All inputs are finite; a program needn't handle non-finite values.
Results may differ from a plain program's by a relative error of at most 0.0024.
Values may be sent and summed in bfloat16 or wider, within the bound.
No kernel may reach another device: no remote copies, remote signals or barrier semaphores. Data moves between devices by JAX's collectives and lax.ppermute only.
A program may use at most 192 MiB of HBM per device.

v0:
```python
import jax
import jax.numpy as jnp
from jax import lax
from jax.sharding import PartitionSpec as P

NB = 64


def body(three_center, metric, occupied, nu_list, nu_count, block_size):
    n_mu, knu = nu_list.shape
    n_occ = occupied.shape[1]
    aux_dev = three_center.shape[1]
    lanes = jnp.arange(NB, dtype=jnp.int32)
    row_live = lanes[None, :] < block_size[:, None]
    col_live = lanes[None, None, :] < block_size[nu_list][:, :, None]
    slot_live = jnp.arange(knu, dtype=jnp.int32)[None, :] < nu_count[:, None]
    mask = row_live[:, None, :, None] & col_live[:, :, None, :] & slot_live[:, :, None, None]
    blocks = three_center[0].reshape(aux_dev, n_mu, knu, NB, NB)
    masked = jnp.where(mask[None], blocks, jnp.zeros((), jnp.bfloat16))
    picked = occupied.reshape(n_mu, NB, n_occ)[nu_list]
    half = jnp.einsum(
        "qmkab,mkbi->qmai", masked, picked, preferred_element_type=jnp.float32
    ).astype(jnp.bfloat16)
    half = half.reshape(aux_dev, n_mu, NB * n_occ)
    regrouped = lax.all_to_all(half, "grp", split_axis=1, concat_axis=0, tiled=True)
    n_aux = regrouped.shape[0]
    mu_dev = regrouped.shape[1]
    regrouped = regrouped.reshape(n_aux, mu_dev, NB, n_occ)
    orbital = jnp.einsum(
        "pq,qmai->mapi", metric[0], regrouped, preferred_element_type=jnp.float32
    ).astype(jnp.bfloat16)
    orbital = orbital.reshape(mu_dev * NB, n_aux * n_occ)
    term = jnp.dot(
        lax.all_gather(orbital, "grp", axis=0, tiled=True),
        orbital.T,
        preferred_element_type=jnp.float32,
    )
    return lax.psum_scatter(term, "rep", scatter_dimension=0, tiled=True)


def solution(mesh):
    return jax.shard_map(
        body,
        mesh=mesh,
        in_specs=(P("rep", "grp", None, None, None), P("rep", None, None), P(), P(), P(), P()),
        out_specs=P("rep", "grp"),
        check_vma=False,
    )
```

profile of v0, /device:TPU:0, one launch (start us, length us, event | category | flops | bytes accessed | tf_op | source)
XLA Modules:
  0.0 370.5 jit_solution(7674496762199158850)
XLA Ops:
  6.5 0.0 copy-start
  6.5 0.0 copy-start.1
  6.5 0.0 all-gather.2.cloned.1.call-start
  6.5 0.7 compare_select_fusion
  7.3 0.7 iota_compare_fusion.1
  8.0 0.7 iota_compare_fusion.2
  8.7 0.1 copy.22
  8.8 0.1 reshape.66
  8.9 0.0 copy-done.1
  8.9 0.0 copy-start.2
  8.9 1.6 gather_fusion.1
  10.5 0.1 reshape.73
  10.6 0.1 iota_compare_fusion
  10.7 0.0 copy-done.2
  10.7 0.4 reshape.60
  11.1 0.2 copy.23
  11.3 1.0 gather_fusion
  12.3 34.4 %reshape_squeeze.3 = bf16[8,32,6,64,64]{4,3,1,2,0:T(8,128)(2,1)} reshape(bf16[1,8,32,6,4096]{4,2,3,1,0:T(8,128)(2,1)} %param.6) | data formatting | bytes 25165824 | tf_op jit(solution)/shard_map/reshape;squeeze | solution.py:18
  46.7 2.3 and_and_fusion
  49.0 17.0 %fusion.3 = bf16[8,32,64,48]{2,3,0,1:T(8,128)(2,1)} fusion(bf16[32,6,64,48,1]{2,3,1,4,0:T(8,128)(2,1)S(1)} %bitcast.47, bf16[8,32,6,64,64]{4,3,1,2,0:T(8,128)(2,1)} %reshape_squeeze.3, pred[32,6,64,64]{3,2,1,0:T(8,128)(4,1)} %and_and_fusion), kind=kOutput, calls=%fused_computation.8 | convolution fusion | flops 611057664 | bytes 16121856 | tf_op jit(solution)/shard_map/qmkab,mkbi->qmai/dot_general | solution.py:21
  66.0 6.2 %copy.33 = bf16[8,32,64,48]{3,2,0,1:T(8,128)(2,1)} copy(bf16[8,32,64,48]{2,3,0,1:T(8,128)(2,1)} %fusion.3) | data formatting | bytes 3145728 | tf_op jit(solution)/shard_map/reshape | solution.py:24
  72.2 8.0 %reshape.87 = bf16[8,32,3072]{2,0,1:T(8,128)(2,1)S(1)} reshape(bf16[8,32,64,48]{3,2,0,1:T(8,128)(2,1)} %copy.33) | data formatting | bytes 3145728 | tf_op jit(solution)/shard_map/reshape | solution.py:24
  80.2 44.1 %all_to_all.15 = bf16[8,32,3072]{2,0,1:T(8,128)(2,1)S(1)} all-to-all(bf16[8,32,3072]{2,0,1:T(8,128)(2,1)S(1)} %reshape.87), channel_id=1, replica_groups=mesh['grp'=8,'rep'=4] {'grp'}, dimensions={1} | all-to-all | bytes 3145728 | tf_op jit(solution)/shard_map/all_to_all | solution.py:25
  124.2 0.1 copy.40
  124.3 5.3 %reshape.62 = bf16[64,4,64,48]{3,2,0,1:T(8,128)(2,1)} reshape(bf16[8,8,4,3072]{3,1,0,2:T(8,128)(2,1)S(1)} %bitcast.46) | data formatting | bytes 3145728 | tf_op jit(solution)/shard_map/reshape | solution.py:28
  129.7 6.4 %copy.28 = bf16[64,4,64,48]{0,2,3,1:T(8,128)(2,1)S(1)} copy(bf16[64,4,64,48]{3,2,0,1:T(8,128)(2,1)} %reshape.62) | data formatting | bytes 3145728 | tf_op jit(solution)/shard_map/reshape | solution.py:28
  136.1 0.0 copy-done
  136.1 2.6 convert_bitcast_fusion
  138.7 6.3 %copy.29 = bf16[4,64,64,48]{1,0,3,2:T(4,128)(2,1)S(1)} copy(bf16[4,64,64,48]{2,1,3,0:T(8,128)(2,1)} %convert_bitcast_fusion) | data formatting | bytes 3145728 | tf_op jit(solution)/shard_map/convert_element_type | solution.py:31
  145.1 3.0 reshape.63
  148.1 0.0 all-gather.2.cloned.1.call-update
  148.1 0.0 reduce-scatter.2.cloned.1.call-start
  148.2 175.7 %all-gather.2.cloned.1.call-done = bf16[2048,3072]{0,1:T(8,128)(2,1)} async-done(((bf16[256,3072]{0,1:T(8,128)(2,1)}), bf16[2048,3072]{0,1:T(8,128)(2,1)}) %all-gather.2.cloned.1.call-update) | async-done | bytes 12582928 | tf_op jit(solution)/shard_map/all_gather | solution.py:34
  323.9 10.0 %fusion.6 = f32[2048,256]{1,0:T(8,128)} fusion(bf16[2048,3072]{0,1:T(8,128)(2,1)} %all-gather.2.cloned.1.call-done, bf16[256,3072]{0,1:T(8,128)(2,1)} %reshape.63), kind=kOutput, calls=%fused_computation.18 | convolution fusion | flops 3221225472 | bytes 16252928 | tf_op jit(solution)/shard_map/dot_general | solution.py:33
  333.9 0.0 reduce-scatter.2.cloned.1.call-update
  333.9 29.8 %reduce-scatter.2.cloned.1.call-done = f32[512,256]{1,0:T(8,128)} async-done(((f32[2048,256]{1,0:T(8,128)}), f32[512,256]{1,0:T(8,128)}) %reduce-scatter.2.cloned.1.call-update) | async-done | bytes 524304 | tf_op jit(solution)/shard_map/reduce_scatter | solution.py:38
  (1 shorter events, 0.0 us)
Async XLA Ops:
  6.5 129.6 %copy-start = (bf16[1,64,64]{2,1,0:T(8,128)(2,1)S(1)}, bf16[1,64,64]{2,1,0:T(8,128)(2,1)}, u32[]{:S(2)}) copy-start(bf16[1,64,64]{2,1,0:T(8,128)(2,1)} %param.7) | copy-start | bytes 24580
  6.5 2.4 copy-start.1
  6.5 317.3 %all-gather.2.cloned.1.call-start = ((), (), s32[]{:S(2)}) async-start(), calls=%async_computation.2 | async-start | bytes 14155776 | tf_op jit(solution)/shard_map/all_gather | solution.py:34
  8.9 1.8 copy-start.2
  148.1 215.5 %reduce-scatter.2.cloned.1.call-start = ((), (), s32[]{:S(2)}) async-start(), calls=%async_computation.3 | async-start | bytes 2621440 | tf_op jit(solution)/shard_map/reduce_scatter | solution.py:38
Sparse Core Ops, SparseCore 0:
  148.2 175.5 all-gather.1
  334.0 29.5 reduce-scatter.1
where the time goes:
time: 372 us; the launch traced here: 370 us
  waiting for transfers between devices  205 us (55%)
  local copies, waits for them, and re-layouts  73.1 us (20%)
  blocking collectives  44.1 us (12%)
  matrix products  29.6 us (8%)
  between operations  13.5 us (4%)
  other arithmetic  4.59 us (1%)
    all_gather x1, waiting for transfers between devices, body(): lax.all_gather(orbital, 'grp', axis=0, tiled=True)  176 us
    all_to_all x1, blocking collectives, body(): lax.all_to_all(half, 'grp', split_axis=1, concat_axis=0, tiled=True)  44.1 us
    another operation x1, local copies, waits for them, and re-layouts, body(): blocks = three_center[0].reshape(aux_dev, n_mu, knu, NB, NB)  34.4 us
    reduce_scatter x1, waiting for transfers between devices, body(): return lax.psum_scatter(term, 'rep', scatter_dimension=0, tiled=True)  29.8 us
    dot_general x1, matrix products, body(): jnp.einsum('qmkab,mkbi->qmai', masked, picked, preferred_element_type=jnp...  17 us
    reshape x2, local copies, waits for them, and re-layouts, body(): half = half.reshape(aux_dev, n_mu, NB * n_occ)  14.1 us
    reshape x2, local copies, waits for them, and re-layouts, body(): regrouped = regrouped.reshape(n_aux, mu_dev, NB, n_occ)  11.8 us
    dot_general x1, matrix products, body(): jnp.dot(lax.all_gather(orbital, 'grp', axis=0, tiled=True), orbital.T, pr...  9.99 us
  transfers between devices with their start and end apart: 2, of which 2 were waited for; matrix products, arithmetic and copies ran while one was open for 0% of the time, Pallas kernels for 0%

commit v1 on v0

v1 whole, which is shorter than its diff:
```python
import jax
import jax.numpy as jnp
from jax import lax
from jax.sharding import PartitionSpec as P

NB = 64
N_CHUNKS = 4


def body(three_center, metric, occupied, nu_list, nu_count, block_size):
    n_mu, knu = nu_list.shape
    n_occ = occupied.shape[1]
    aux_dev = three_center.shape[1]
    occ_c = n_occ // N_CHUNKS
    lanes = jnp.arange(NB, dtype=jnp.int32)
    row_live = lanes[None, :] < block_size[:, None]
    col_live = lanes[None, None, :] < block_size[nu_list][:, :, None]
    slot_live = jnp.arange(knu, dtype=jnp.int32)[None, :] < nu_count[:, None]
    mask = row_live[:, None, :, None] & col_live[:, :, None, :] & slot_live[:, :, None, None]
    blocks = three_center[0].reshape(aux_dev, n_mu, knu, NB, NB)
    masked = jnp.where(mask[None], blocks, jnp.zeros((), jnp.bfloat16))
    picked = occupied.reshape(n_mu, NB, N_CHUNKS, occ_c)[nu_list]
    half = jnp.einsum(
        "qmkab,mkbci->cqmai", masked, picked, preferred_element_type=jnp.float32
    ).astype(jnp.bfloat16)
    half = half.reshape(N_CHUNKS, aux_dev, n_mu, NB * occ_c)
    n_grp = lax.axis_size("grp")
    rows = n_mu * NB // n_grp
    start = lax.axis_index("grp") * rows
    term = None
    for c in range(N_CHUNKS):
        gathered = lax.all_gather(half[c], "grp", axis=0, tiled=True)
        n_aux = gathered.shape[0]
        gathered = gathered.reshape(n_aux, n_mu, NB, occ_c)
        orbital = jnp.einsum(
            "pq,qmai->mapi", metric[0], gathered, preferred_element_type=jnp.float32
        ).astype(jnp.bfloat16)
        orbital = orbital.reshape(n_mu * NB, n_aux * occ_c)
        mine = lax.dynamic_slice_in_dim(orbital, start, rows, axis=0)
        part = jnp.dot(orbital, mine.T, preferred_element_type=jnp.float32)
        term = part if term is None else term + part
    return lax.psum_scatter(term, "rep", scatter_dimension=0, tiled=True)


def solution(mesh):
    return jax.shard_map(
        body,
        mesh=mesh,
        in_specs=(P("rep", "grp", None, None, None), P("rep", None, None), P(), P(), P(), P()),
        out_specs=P("rep", "grp"),
        check_vma=False,
    )
```

time: 372 us -> 885 us (2.38); the launches traced: 370 us -> 872 us
  waiting for transfers between devices: 205 us -> 601 us
  local copies, waits for them, and re-layouts: 73.1 us -> 201 us
  blocking collectives: 44.1 us -> 0 us
  matrix products: 29.6 us -> 53.9 us
    all_gather x1 -> x4, waiting for transfers between devices: 176 us -> 571 us  [body(): gathered = lax.all_gather(half[c], 'grp', axis=0, tiled=True)]
    reshape x7 -> x10, local copies, waits for them, and re-layouts: 29.4 us -> 101 us  [the longest x4 62.7 us: body(): gathered = gathered.reshape(n_aux, n_mu, NB, occ_c)]
    all_to_all x1 -> x0, blocking collectives: 44.1 us -> none  [body(): lax.all_to_all(half, 'grp', split_axis=1, concat_axis=0, tiled=True)]
    convert_element_type x1 -> x4, local copies, waits for them, and re-layouts: 6.35 us -> 37.6 us  [body(): orbital = jnp.einsum('pq,qmai->mapi', metric[0], gathered, preferred_elem...]
    dot_general x3 -> x9, matrix products: 29.6 us -> 53.9 us  [the longest x4 28.9 us: body(): jnp.einsum('pq,qmai->mapi', metric[0], gathered, preferred_element_type=j...]
    slice x0 -> x5, local copies, waits for them, and re-layouts: none -> 22 us  [body(): gathered = lax.all_gather(half[c], 'grp', axis=0, tiled=True)]
  transfers between devices with their start and end apart: 2 -> 5, of which waited for: 2 -> 5; matrix products, arithmetic and copies ran while one was open for 0% -> 16% of each run, Pallas kernels for 0% -> 0%
where the time goes in v1:
time: 885 us; the launch traced here: 872 us
  waiting for transfers between devices  601 us (68%)
  local copies, waits for them, and re-layouts  201 us (23%)
  matrix products  53.9 us (6%)
  between operations  13.5 us (2%)
    all_gather x4, waiting for transfers between devices, body(): gathered = lax.all_gather(half[c], 'grp', axis=0, tiled=True)  571 us
    reshape x4, local copies, waits for them, and re-layouts, body(): gathered = gathered.reshape(n_aux, n_mu, NB, occ_c)  62.7 us
    reshape x4, local copies, waits for them, and re-layouts, body(): orbital = orbital.reshape(n_mu * NB, n_aux * occ_c)  37.9 us
    convert_element_type x4, local copies, waits for them, and re-layouts, body(): orbital = jnp.einsum('pq,qmai->mapi', metric[0], gathered, preferred_elem...  37.6 us
    another operation x1, local copies, waits for them, and re-layouts, body(): blocks = three_center[0].reshape(aux_dev, n_mu, knu, NB, NB)  34.4 us
    reduce_scatter x1, waiting for transfers between devices, body(): return lax.psum_scatter(term, 'rep', scatter_dimension=0, tiled=True)  29.8 us
    dot_general x4, matrix products, body(): jnp.einsum('pq,qmai->mapi', metric[0], gathered, preferred_element_type=j...  28.9 us
    slice x5, local copies, waits for them, and re-layouts, body(): gathered = lax.all_gather(half[c], 'grp', axis=0, tiled=True)  22 us
  transfers between devices with their start and end apart: 5, of which 5 were waited for; matrix products, arithmetic and copies ran while one was open for 16% of the time, Pallas kernels for 0%

profile of v1, /device:TPU:0, one launch (start us, length us, event | category | flops | bytes accessed | tf_op | source)
XLA Modules:
  0.0 872.5 jit_solution(10821817166071291102)
XLA Ops:
  6.5 0.0 copy-start
  6.5 0.0 copy-start.6
  6.5 0.0 copy-start.1
  6.5 0.0 all-gather.5.cloned.1.call-start
  6.6 34.4 %reshape_squeeze.3 = bf16[8,32,6,64,64]{4,3,1,2,0:T(8,128)(2,1)} reshape(bf16[1,8,32,6,4096]{4,2,3,1,0:T(8,128)(2,1)} %param.6) | data formatting | bytes 25165824 | tf_op jit(solution)/shard_map/reshape;squeeze | solution.py:20
  41.0 0.0 copy-done.6
  41.0 0.1 iota_compare_fusion.1
  41.1 0.0 copy-done.5
  41.1 0.1 copy.27
  41.2 0.1 reshape.94
  41.3 0.0 copy-done.1
  41.3 0.1 iota_compare_fusion.2
  41.4 1.6 gather_fusion.1
  42.9 0.1 reshape.101
  43.0 0.1 iota_compare_fusion
  43.2 0.0 copy-done.4
  43.2 0.4 reshape.83
  43.5 0.3 copy.28
  43.9 2.6 gather_fusion
  46.5 1.6 and_and_fusion
  48.1 17.4 %fusion.4 = bf16[4,8,32,64,12]{3,4,1,0,2:T(8,128)(2,1)} fusion(bf16[8,32,6,64,64]{4,3,1,2,0:T(8,128)(2,1)} %reshape_squeeze.3, pred[32,6,64,64]{3,2,1,0:T(8,128)(4,1)S(1)} %and_and_fusion, bf16[32,6,64,4,12,1]{2,3,4,1,0,5:T(4,128)(2,1)S(1)} %bitcast.76), kind=kOutput, calls=%fused_computation.13 | convolution fusion | flops 611057664 | bytes 16121856 | tf_op jit(solution)/shard_map/qmkab,mkbci->cqmai/dot_general | solution.py:23
  65.4 4.3 fusion.22
  69.8 5.3 copy.31
  75.1 0.0 all-gather.5.cloned.1.call-update
  75.1 0.0 all-gather.7.cloned.1.call-start
  75.1 4.1 copy.35
  79.2 0.0 all-gather.7.cloned.1.call-update
  79.3 0.4 all-gather.9.cloned.1.call-start
  79.6 4.1 copy.39
  83.8 0.0 all-gather.9.cloned.1.call-update
  83.8 0.0 all-gather.11.cloned.1.call-start
  83.8 4.1 copy.43
  88.0 0.0 all-gather.11.cloned.1.call-update
  88.0 0.0 reduce-scatter.2.cloned.1.call-start
  88.1 166.5 %all-gather.5.cloned.1.call-done = bf16[64,32,768]{1,0,2:T(8,128)(2,1)} async-done(((bf16[8,32,768]{1,0,2:T(8,128)(2,1)}), bf16[64,32,768]{1,0,2:T(8,128)(2,1)}) %all-gather.5.cloned.1.call-update) | async-done | bytes 3145744 | tf_op jit(solution)/shard_map/all_gather | solution.py:32
  254.5 15.7 %copy.33 = bf16[64,32,64,12]{0,2,3,1:T(8,128)(2,1)} copy(bf16[64,32,64,12]{1,0,3,2:T(8,128)(2,1)} %bitcast.77) | data formatting | bytes 6291456 | tf_op jit(solution)/shard_map/reshape | solution.py:34
  270.3 0.0 copy-done
  270.3 7.2 convert_bitcast_fusion.3
  277.5 9.4 %copy.34 = bf16[32,64,64,12]{1,0,3,2:T(8,128)(2,1)} copy(bf16[32,64,64,12]{2,1,3,0:T(8,128)(2,1)} %convert_bitcast_fusion.3) | data formatting | bytes 6291456 | tf_op jit(solution)/shard_map/convert_element_type | solution.py:37
  286.9 9.7 %reshape.85 = bf16[2048,768]{0,1:T(8,128)(2,1)} reshape(bf16[32,64,64,12]{1,0,3,2:T(8,128)(2,1)} %copy.34) | data formatting | bytes 6291456 | tf_op jit(solution)/shard_map/reshape | solution.py:38
  296.6 134.7 %all-gather.7.cloned.1.call-done = bf16[64,32,768]{1,0,2:T(8,128)(2,1)} async-done(((bf16[8,32,768]{1,0,2:T(8,128)(2,1)}), bf16[64,32,768]{1,0,2:T(8,128)(2,1)}) %all-gather.7.cloned.1.call-update) | async-done | bytes 3145744 | tf_op jit(solution)/shard_map/all_gather | solution.py:32
  431.4 15.8 %copy.37 = bf16[64,32,64,12]{0,2,3,1:T(8,128)(2,1)} copy(bf16[64,32,64,12]{1,0,3,2:T(8,128)(2,1)} %bitcast.78) | data formatting | bytes 6291456 | tf_op jit(solution)/shard_map/reshape | solution.py:34
  447.1 7.3 convert_bitcast_fusion.2
  454.4 9.4 %copy.38 = bf16[32,64,64,12]{1,0,3,2:T(8,128)(2,1)} copy(bf16[32,64,64,12]{2,1,3,0:T(8,128)(2,1)} %convert_bitcast_fusion.2) | data formatting | bytes 6291456 | tf_op jit(solution)/shard_map/convert_element_type | solution.py:37
  463.8 8.5 reshape.87
  472.3 135.9 %all-gather.9.cloned.1.call-done = bf16[64,32,768]{1,0,2:T(8,128)(2,1)} async-done(((bf16[8,32,768]{1,0,2:T(8,128)(2,1)}), bf16[64,32,768]{1,0,2:T(8,128)(2,1)}) %all-gather.9.cloned.1.call-update) | async-done | bytes 3145744 | tf_op jit(solution)/shard_map/all_gather | solution.py:32
  608.2 15.8 %copy.41 = bf16[64,32,64,12]{0,2,3,1:T(8,128)(2,1)} copy(bf16[64,32,64,12]{1,0,3,2:T(8,128)(2,1)} %bitcast.79) | data formatting | bytes 6291456 | tf_op jit(solution)/shard_map/reshape | solution.py:34
  624.0 7.2 convert_bitcast_fusion.1
  631.1 9.5 %copy.42 = bf16[32,64,64,12]{1,0,3,2:T(8,128)(2,1)} copy(bf16[32,64,64,12]{2,1,3,0:T(8,128)(2,1)} %convert_bitcast_fusion.1) | data formatting | bytes 6291456 | tf_op jit(solution)/shard_map/convert_element_type | solution.py:37
  640.6 9.9 %reshape.89 = bf16[2048,768]{0,1:T(8,128)(2,1)} reshape(bf16[32,64,64,12]{1,0,3,2:T(8,128)(2,1)} %copy.42) | data formatting | bytes 6291456 | tf_op jit(solution)/shard_map/reshape | solution.py:38
  650.5 134.4 %all-gather.11.cloned.1.call-done = bf16[64,32,768]{1,0,2:T(8,128)(2,1)} async-done(((bf16[8,32,768]{1,0,2:T(8,128)(2,1)}), bf16[64,32,768]{1,0,2:T(8,128)(2,1)}) %all-gather.11.cloned.1.call-update) | async-done | bytes 3145744 | tf_op jit(solution)/shard_map/all_gather | solution.py:32
  784.9 15.5 %copy.45 = bf16[64,32,64,12]{0,2,3,1:T(8,128)(2,1)} copy(bf16[64,32,64,12]{1,0,3,2:T(8,128)(2,1)} %bitcast.80) | data formatting | bytes 6291456 | tf_op jit(solution)/shard_map/reshape | solution.py:34
  800.3 7.2 convert_bitcast_fusion
  807.6 9.4 %copy.46 = bf16[32,64,64,12]{1,0,3,2:T(8,128)(2,1)} copy(bf16[32,64,64,12]{2,1,3,0:T(8,128)(2,1)} %convert_bitcast_fusion) | data formatting | bytes 6291456 | tf_op jit(solution)/shard_map/convert_element_type | solution.py:37
  817.0 9.7 %reshape.91 = bf16[2048,768]{0,1:T(8,128)(2,1)} reshape(bf16[32,64,64,12]{1,0,3,2:T(8,128)(2,1)} %copy.46) | data formatting | bytes 6291456 | tf_op jit(solution)/shard_map/reshape | solution.py:38
  826.7 3.0 fusion.11
  829.7 0.0 copy-start.2
  829.7 1.1 convolution_add_fusion.2
  830.8 0.8 copy-done.2
  831.6 1.0 convolution_add_fusion.1
  832.6 0.8 copy-done.3
  833.5 2.5 convolution_add_fusion
  835.9 0.0 reduce-scatter.2.cloned.1.call-update
  836.0 29.8 %reduce-scatter.2.cloned.1.call-done = f32[512,256]{1,0:T(8,128)} async-done(((f32[2048,256]{1,0:T(8,128)}), f32[512,256]{1,0:T(8,128)}) %reduce-scatter.2.cloned.1.call-update) | async-done | bytes 524304 | tf_op jit(solution)/shard_map/reduce_scatter | solution.py:42
  (5 shorter events, 0.0 us)
Async XLA Ops:
  6.5 263.7 %copy-start = (bf16[1,64,64]{2,1,0:T(8,128)(2,1)S(1)}, bf16[1,64,64]{2,1,0:T(8,128)(2,1)}, u32[]{:S(2)}) copy-start(bf16[1,64,64]{2,1,0:T(8,128)(2,1)} %param.7) | copy-start | bytes 24580
  6.5 34.5 %copy-start.6 = (s32[32]{0:T(128)S(1)}, s32[32]{0:T(128)}, u32[]{:S(2)}) copy-start(s32[32]{0:T(128)} %param.10) | copy-start | bytes 388
  6.5 34.5 %copy-start.5 = (s32[32,6]{0,1:T(8,128)S(1)}, s32[32,6]{0,1:T(8,128)}, u32[]{:S(2)}) copy-start(s32[32,6]{0,1:T(8,128)} %param.9) | copy-start | bytes 2308
  6.5 34.8 %copy-start.1 = (s32[32]{0:T(128)S(1)}, s32[32]{0:T(128)}, u32[]{:S(2)}) copy-start(s32[32]{0:T(128)} %param.11) | copy-start | bytes 388
  6.5 248.0 %all-gather.5.cloned.1.call-start = ((), (), s32[]{:S(2)}) async-start(), calls=%async_computation.1 | async-start | bytes 14155776 | tf_op jit(solution)/shard_map/all_gather | solution.py:32
  41.4 1.8 copy-start.4
  75.1 356.3 %all-gather.7.cloned.1.call-start = ((), (), s32[]{:S(2)}) async-start(), calls=%async_computation.2 | async-start | bytes 14155776 | tf_op jit(solution)/shard_map/all_gather | solution.py:32
  79.3 528.9 %all-gather.9.cloned.1.call-start = ((), (), s32[]{:S(2)}) async-start(), calls=%async_computation.3 | async-start | bytes 14155776 | tf_op jit(solution)/shard_map/all_gather | solution.py:32
  83.8 701.1 %all-gather.11.cloned.1.call-start = ((), (), s32[]{:S(2)}) async-start(), calls=%async_computation.4 | async-start | bytes 14155776 | tf_op jit(solution)/shard_map/all_gather | solution.py:32
  88.0 777.7 %reduce-scatter.2.cloned.1.call-start = ((), (), s32[]{:S(2)}) async-start(), calls=%async_computation.5 | async-start | bytes 2621440 | tf_op jit(solution)/shard_map/reduce_scatter | solution.py:42
  829.7 1.9 copy-start.2
  831.6 1.9 copy-start.3
Sparse Core Ops, SparseCore 0:
  75.2 179.2 all-gather.4
  256.6 174.7 all-gather.6
  433.4 174.7 all-gather.8
  610.1 174.7 all-gather.10
  836.1 29.6 reduce-scatter.1

commit v2 on v1

v2 whole, which is shorter than its diff:
```python
import jax
import jax.numpy as jnp
import numpy as np
from jax import lax
from jax.sharding import PartitionSpec as P

NB = 64


def snake(a_size, b_size):
    if a_size % 2:
        return [(a, b) for b, a in snake(b_size, a_size)]
    if b_size == 1:
        return [(a, 0) for a in range(a_size)]
    path = []
    for a in range(a_size):
        cols = range(b_size) if a == 0 else (range(1, b_size) if a % 2 == 0 else range(b_size - 1, 0, -1))
        path += [(a, b) for b in cols]
    path += [(a, 0) for a in range(a_size - 1, 0, -1)]
    return path


def ring_order(mesh):
    n = mesh.shape["grp"]
    try:
        devs = np.asarray(mesh.devices).reshape(n, -1)[:, 0]
        coords = [tuple(d.coords) for d in devs]
    except (AttributeError, TypeError):
        return list(range(n))
    varying = [i for i in range(len(coords[0])) if len({c[i] for c in coords}) > 1]
    if len(varying) == 1:
        key = sorted(range(n), key=lambda g: coords[g][varying[0]])
        return key
    if len(varying) != 2:
        return list(range(n))
    i, j = varying
    avals = sorted({c[i] for c in coords})
    bvals = sorted({c[j] for c in coords})
    where = {(avals.index(c[i]), bvals.index(c[j])): g for g, c in enumerate(coords)}
    if len(where) != n:
        return list(range(n))
    return [where[p] for p in snake(len(avals), len(bvals))]


def make_body(ring):
    n = len(ring)
    pos_of = np.zeros(n, np.int32)
    for p, g in enumerate(ring):
        pos_of[g] = p
    ring_arr = np.asarray(ring, np.int32)
    fwd = [(ring[p], ring[(p + 1) % n]) for p in range(n)]
    bwd = [(ring[p], ring[(p - 1) % n]) for p in range(n)]

    def body(three_center, metric, occupied, nu_list, nu_count, block_size):
        n_mu, knu = nu_list.shape
        n_occ = occupied.shape[1]
        aux_dev = three_center.shape[1]
        lanes = jnp.arange(NB, dtype=jnp.int32)
        row_live = lanes[None, :] < block_size[:, None]
        col_live = lanes[None, None, :] < block_size[nu_list][:, :, None]
        slot_live = jnp.arange(knu, dtype=jnp.int32)[None, :] < nu_count[:, None]
        mask = row_live[:, None, :, None] & col_live[:, :, None, :] & slot_live[:, :, None, None]
        blocks = three_center[0].reshape(aux_dev, n_mu, knu, NB, NB)
        masked = jnp.where(mask[None], blocks, jnp.zeros((), jnp.bfloat16))
        picked = occupied.reshape(n_mu, NB, n_occ)[nu_list]
        half = jnp.einsum(
            "qmkab,mkbi->qmai", masked, picked, preferred_element_type=jnp.float32
        ).astype(jnp.bfloat16)
        half = half.reshape(aux_dev, n_mu, NB * n_occ)
        regrouped = lax.all_to_all(half, "grp", split_axis=1, concat_axis=0, tiled=True)
        n_aux = regrouped.shape[0]
        mu_dev = regrouped.shape[1]
        regrouped = regrouped.reshape(n_aux, mu_dev, NB, n_occ)
        orbital = jnp.einsum(
            "pq,qmai->mapi", metric[0], regrouped, preferred_element_type=jnp.float32
        ).astype(jnp.bfloat16)
        rows = mu_dev * NB
        orbital = orbital.reshape(rows, n_aux * n_occ)
        hr = rows // 2
        me = lax.axis_index("grp")
        pos = jnp.asarray(pos_of)[me]
        ring_c = jnp.asarray(ring_arr)
        term = jnp.zeros((n * rows, rows), jnp.float32)

        def place(term, piece, src, off):
            part = jnp.dot(piece, orbital.T, preferred_element_type=jnp.float32)
            return lax.dynamic_update_slice_in_dim(term, part, src * rows + off, axis=0)

        term = place(term, orbital, me, 0)
        a = orbital[:hr]
        b = orbital[hr:]
        for k in range(1, n):
            a = lax.ppermute(a, "grp", fwd)
            term = place(term, a, ring_c[(pos - k) % n], 0)
            b = lax.ppermute(b, "grp", bwd)
            term = place(term, b, ring_c[(pos + k) % n], hr)
        return lax.psum_scatter(term, "rep", scatter_dimension=0, tiled=True)

    return body


def solution(mesh):
    return jax.shard_map(
        make_body(ring_order(mesh)),
        mesh=mesh,
        in_specs=(P("rep", "grp", None, None, None), P("rep", None, None), P(), P(), P(), P()),
        out_specs=P("rep", "grp"),
        check_vma=False,
    )
```

time: 885 us -> 344 us (0.39); the launches traced: 872 us -> 342 us
  waiting for transfers between devices: 601 us -> 104 us
  local copies, waits for them, and re-layouts: 201 us -> 100 us
  blocking collectives: 0 us -> 44.1 us
  between operations: 13.5 us -> 31.8 us
  starting transfers between devices: 0.55 us -> 16.2 us
  matrix products: 53.9 us -> 42.1 us
    all_gather x4 -> x0, waiting for transfers between devices: 571 us -> none  [body(): gathered = lax.all_gather(half[c], 'grp', axis=0, tiled=True)]
    ppermute x0 -> x14, waiting for transfers between devices: none -> 70.9 us  [the longest x7 48.9 us: body(): a = lax.ppermute(a, 'grp', fwd)]
    reshape x10 -> x7, local copies, waits for them, and re-layouts: 101 us -> 32.9 us  [the longest x2 14.2 us: body(): half = half.reshape(aux_dev, n_mu, NB * n_occ)]
    all_to_all x0 -> x1, blocking collectives: none -> 44.1 us  [body(): lax.all_to_all(half, 'grp', split_axis=1, concat_axis=0, tiled=True)]
    convert_element_type x4 -> x1, local copies, waits for them, and re-layouts: 37.6 us -> 5.58 us  [body(): orbital = jnp.einsum('pq,qmai->mapi', metric[0], regrouped, preferred_ele...]
    ppermute x0 -> x14, starting transfers between devices: none -> 16.2 us  [the longest x7 10.5 us: body(): b = lax.ppermute(b, 'grp', bwd)]
    dot_general x9 -> x17, matrix products: 53.9 us -> 42.1 us  [the longest x15 22.2 us: place(): part = jnp.dot(piece, orbital.T, preferred_element_type=jnp.float32)]
  transfers between devices with their start and end apart: 5 -> 15, of which waited for: 5 -> 12; matrix products, arithmetic and copies ran while one was open for 16% -> 13% of each run, Pallas kernels for 0% -> 0%
where the time goes in v2:
time: 344 us; the launch traced here: 342 us
  waiting for transfers between devices  104 us (30%)
  local copies, waits for them, and re-layouts  100 us (29%)
  blocking collectives  44.1 us (13%)
  matrix products  42.1 us (12%)
  between operations  31.8 us (9%)
  starting transfers between devices  16.2 us (5%)
  other arithmetic  3.97 us (1%)
    ppermute x7, waiting for transfers between devices, body(): a = lax.ppermute(a, 'grp', fwd)  48.9 us
    all_to_all x1, blocking collectives, body(): lax.all_to_all(half, 'grp', split_axis=1, concat_axis=0, tiled=True)  44.1 us
    another operation x1, local copies, waits for them, and re-layouts, body(): blocks = three_center[0].reshape(aux_dev, n_mu, knu, NB, NB)  34.4 us
    reduce_scatter x1, waiting for transfers between devices, body(): return lax.psum_scatter(term, 'rep', scatter_dimension=0, tiled=True)  32.7 us
    dot_general x15, matrix products, place(): part = jnp.dot(piece, orbital.T, preferred_element_type=jnp.float32)  22.2 us
    ppermute x7, waiting for transfers between devices, body(): b = lax.ppermute(b, 'grp', bwd)  22 us
    dot_general x1, matrix products, body(): jnp.einsum('qmkab,mkbi->qmai', masked, picked, preferred_element_type=jnp...  17 us
    reshape x2, local copies, waits for them, and re-layouts, body(): half = half.reshape(aux_dev, n_mu, NB * n_occ)  14.2 us
  transfers between devices with their start and end apart: 15, of which 12 were waited for; matrix products, arithmetic and copies ran while one was open for 13% of the time, Pallas kernels for 0%

profile of v2, /device:TPU:0, one launch (start us, length us, event | category | flops | bytes accessed | tf_op | source)
XLA Modules:
  0.0 341.8 jit_solution(16332290625725403161)
XLA Ops:
  6.5 0.7 compare_select_fusion
  7.5 1.3 reshape.146
  9.0 0.7 iota_compare_fusion.2
  9.7 1.6 gather_fusion.1
  11.3 1.0 gather_fusion
  12.6 34.4 %reshape_squeeze.3 = bf16[8,32,6,64,64]{4,3,1,2,0:T(8,128)(2,1)} reshape(bf16[1,8,32,6,4096]{4,2,3,1,0:T(8,128)(2,1)} %param.8) | data formatting | bytes 25165824 | tf_op jit(solution)/shard_map/reshape;squeeze | solution.py:63
  47.0 2.3 and_and_fusion
  49.3 17.0 %fusion.3 = bf16[8,32,64,48]{2,3,0,1:T(8,128)(2,1)} fusion(bf16[32,6,64,48,1]{2,3,1,4,0:T(8,128)(2,1)S(1)} %bitcast.114, bf16[8,32,6,64,64]{4,3,1,2,0:T(8,128)(2,1)} %reshape_squeeze.3, pred[32,6,64,64]{3,2,1,0:T(8,128)(4,1)} %and_and_fusion), kind=kOutput, calls=%fused_computation.8 | convolution fusion | flops 611057664 | bytes 16121856 | tf_op jit(solution)/shard_map/qmkab,mkbi->qmai/dot_general | solution.py:66
  66.4 6.2 %copy.41 = bf16[8,32,64,48]{3,2,0,1:T(8,128)(2,1)} copy(bf16[8,32,64,48]{2,3,0,1:T(8,128)(2,1)} %fusion.3) | data formatting | bytes 3145728 | tf_op jit(solution)/shard_map/reshape | solution.py:69
  72.6 8.0 %reshape.173 = bf16[8,32,3072]{2,0,1:T(8,128)(2,1)S(1)} reshape(bf16[8,32,64,48]{3,2,0,1:T(8,128)(2,1)} %copy.41) | data formatting | bytes 3145728 | tf_op jit(solution)/shard_map/reshape | solution.py:69
  80.5 44.1 %all_to_all.15 = bf16[8,32,3072]{2,0,1:T(8,128)(2,1)S(1)} all-to-all(bf16[8,32,3072]{2,0,1:T(8,128)(2,1)S(1)} %reshape.173), channel_id=1, replica_groups=mesh['grp'=8,'rep'=4] {'grp'}, dimensions={1} | all-to-all | bytes 3145728 | tf_op jit(solution)/shard_map/all_to_all | solution.py:70
  124.7 5.3 %reshape.148 = bf16[64,4,64,48]{3,2,0,1:T(8,128)(2,1)} reshape(bf16[8,8,4,3072]{3,1,0,2:T(8,128)(2,1)S(1)} %bitcast.113) | data formatting | bytes 3145728 | tf_op jit(solution)/shard_map/reshape | solution.py:73
  130.0 7.1 %copy.34 = bf16[64,4,64,48]{0,2,3,1:T(8,128)(2,1)} copy(bf16[64,4,64,48]{3,2,0,1:T(8,128)(2,1)} %reshape.148) | data formatting | bytes 3145728 | tf_op jit(solution)/shard_map/reshape | solution.py:73
  137.2 2.9 convert_bitcast_fusion
  140.0 2.3 fusion.6
  142.3 5.2 %copy.36 = bf16[2,64,64,48]{1,0,3,2:T(2,128)(2,1)} copy(bf16[2,64,64,48]{2,1,3,0:T(8,128)(2,1)} %get-tuple-element.6) | data formatting | bytes 1572864 | tf_op jit(solution)/shard_map/slice | solution.py:90
  147.5 3.9 %slice.13 = bf16[128,3072]{0,1:T(8,128)(2,1)} reshape(bf16[2,64,64,48]{1,0,3,2:T(2,128)(2,1)} %copy.36) | data formatting | bytes 1572864 | tf_op jit(solution)/shard_map/slice | solution.py:90
  151.4 1.1 collective-permute-start
  152.5 5.2 %copy.37 = bf16[2,64,64,48]{1,0,3,2:T(2,128)(2,1)} copy(bf16[2,64,64,48]{2,1,3,0:T(8,128)(2,1)} %get-tuple-element.5) | data formatting | bytes 1572864 | tf_op jit(solution)/shard_map/slice | solution.py:91
  157.7 3.9 %slice.15 = bf16[128,3072]{0,1:T(8,128)(2,1)} reshape(bf16[2,64,64,48]{1,0,3,2:T(2,128)(2,1)} %copy.37) | data formatting | bytes 1572864 | tf_op jit(solution)/shard_map/slice | solution.py:91
  161.6 0.9 collective-permute-start.1
  162.5 7.4 %collective-permute-done = bf16[128,3072]{0,1:T(8,128)(2,1)} collective-permute-done((bf16[128,3072]{0,1:T(8,128)(2,1)}, bf16[128,3072]{0,1:T(8,128)(2,1)}, u32[]{:S(2)}, u32[]{:S(2)}) %collective-permute-start) | collective-permute-done | bytes 786464 | tf_op jit(solution)/shard_map/ppermute | solution.py:93
  169.9 0.8 collective-permute-start.2
  170.6 8.7 %collective-permute-done.1 = bf16[128,3072]{0,1:T(8,128)(2,1)S(1)} collective-permute-done((bf16[128,3072]{0,1:T(8,128)(2,1)}, bf16[128,3072]{0,1:T(8,128)(2,1)S(1)}, u32[]{:S(2)}, u32[]{:S(2)}) %collective-permute-start.1) | collective-permute-done | bytes 786464 | tf_op jit(solution)/shard_map/ppermute | solution.py:95
  179.3 0.9 copy-done.2
  180.2 1.3 collective-permute-start.3
  181.5 6.1 %collective-permute-done.2 = bf16[128,3072]{0,1:T(8,128)(2,1)} collective-permute-done((bf16[128,3072]{0,1:T(8,128)(2,1)}, bf16[128,3072]{0,1:T(8,128)(2,1)}, u32[]{:S(2)}, u32[]{:S(2)}) %collective-permute-start.2) | collective-permute-done | bytes 786464 | tf_op jit(solution)/shard_map/ppermute | solution.py:93
  187.6 0.5 collective-permute-start.4
  188.1 9.0 %collective-permute-done.3 = bf16[128,3072]{0,1:T(8,128)(2,1)} collective-permute-done((bf16[128,3072]{0,1:T(8,128)(2,1)S(1)}, bf16[128,3072]{0,1:T(8,128)(2,1)}, u32[]{:S(2)}, u32[]{:S(2)}) %collective-permute-start.3) | collective-permute-done | bytes 786464 | tf_op jit(solution)/shard_map/ppermute | solution.py:95
  197.1 1.8 collective-permute-start.5
  199.0 0.6 dynamic_slice.45
  208.9 0.7 fusion.7
  218.6 5.6 %copy.35 = bf16[4,64,64,48]{1,0,3,2:T(4,128)(2,1)} copy(bf16[4,64,64,48]{2,1,3,0:T(8,128)(2,1)S(1)} %convert_bitcast_fusion) | data formatting | bytes 3145728 | tf_op jit(solution)/shard_map/convert_element_type | solution.py:76
  224.2 4.8 %reshape.149 = bf16[256,3072]{0,1:T(8,128)(2,1)S(1)} reshape(bf16[4,64,64,48]{1,0,3,2:T(4,128)(2,1)} %copy.35) | data formatting | bytes 3145728 | tf_op jit(solution)/shard_map/reshape | solution.py:78
  229.0 1.5 broadcast_in_dim.12
  230.4 1.3 convolution_dynamic-update-slice_fusion
  231.9 2.2 convolution_dynamic-update-slice_fusion.14
  234.2 1.8 collective-permute-start.7
  236.0 1.1 convolution_dynamic-update-slice_fusion.13
  237.1 2.2 convolution_dynamic-update-slice_fusion.12
  239.3 10.4 %collective-permute-done.6 = bf16[128,3072]{0,1:T(8,128)(2,1)S(1)} collective-permute-done((bf16[128,3072]{0,1:T(8,128)(2,1)}, bf16[128,3072]{0,1:T(8,128)(2,1)S(1)}, u32[]{:S(2)}, u32[]{:S(2)}) %collective-permute-start.6) | collective-permute-done | bytes 786464 | tf_op jit(solution)/shard_map/ppermute | solution.py:93
  249.8 2.2 convolution_dynamic-update-slice_fusion.11
  252.1 1.8 collective-permute-start.9
  253.9 2.2 convolution_dynamic-update-slice_fusion.10
  256.1 2.2 convolution_dynamic-update-slice_fusion.9
  258.4 7.6 %collective-permute-done.8 = bf16[128,3072]{0,1:T(8,128)(2,1)S(1)} collective-permute-done((bf16[128,3072]{0,1:T(8,128)(2,1)S(1)}, bf16[128,3072]{0,1:T(8,128)(2,1)S(1)}, u32[]{:S(2)}, u32[]{:S(2)}) %collective-permute-start.8) | collective-permute-done | bytes 786464 | tf_op jit(solution)/shard_map/ppermute | solution.py:93
  265.9 1.6 collective-permute-start.10
  267.6 1.1 convolution_dynamic-update-slice_fusion.8
  268.6 1.1 collective-permute-done.9
  269.7 1.3 collective-permute-start.11
  271.0 1.1 convolution_dynamic-update-slice_fusion.7
  272.1 1.1 convolution_dynamic-update-slice_fusion.6
  273.2 10.4 %collective-permute-done.10 = bf16[128,3072]{0,1:T(8,128)(2,1)S(1)} collective-permute-done((bf16[128,3072]{0,1:T(8,128)(2,1)S(1)}, bf16[128,3072]{0,1:T(8,128)(2,1)S(1)}, u32[]{:S(2)}, u32[]{:S(2)}) %collective-permute-start.10) | collective-permute-done | bytes 786464 | tf_op jit(solution)/shard_map/ppermute | solution.py:93
  283.6 1.3 collective-permute-start.12
  285.0 1.1 convolution_dynamic-update-slice_fusion.5
  286.1 1.2 collective-permute-done.11
  287.3 1.5 collective-permute-start.13
  288.7 1.1 convolution_dynamic-update-slice_fusion.4
  289.8 1.1 convolution_dynamic-update-slice_fusion.3
  290.9 7.1 %collective-permute-done.12 = bf16[128,3072]{0,1:T(8,128)(2,1)S(1)} collective-permute-done((bf16[128,3072]{0,1:T(8,128)(2,1)S(1)}, bf16[128,3072]{0,1:T(8,128)(2,1)S(1)}, u32[]{:S(2)}, u32[]{:S(2)}) %collective-permute-start.12) | collective-permute-done | bytes 786464 | tf_op jit(solution)/shard_map/ppermute | solution.py:93
  298.0 1.1 convolution_dynamic-update-slice_fusion.2
  299.1 2.0 collective-permute-done.13
  301.1 1.1 convolution_dynamic-update-slice_fusion.1
  302.2 32.7 %reduce-scatter.2.cloned.1.call-done = f32[512,256]{1,0:T(8,128)} async-done(((f32[2048,256]{1,0:T(8,128)}), f32[512,256]{1,0:T(8,128)}) %reduce-scatter.2.cloned.1.call-update) | async-done | bytes 524304 | tf_op jit(solution)/shard_map/reduce_scatter | solution.py:97
  (28 shorter events, 1.2 us)
Async XLA Ops:
  6.5 130.6 %copy-start = (bf16[1,64,64]{2,1,0:T(8,128)(2,1)S(1)}, bf16[1,64,64]{2,1,0:T(8,128)(2,1)}, u32[]{:S(2)}) copy-start(bf16[1,64,64]{2,1,0:T(8,128)(2,1)} %param.9) | copy-start | bytes 24580
  6.5 3.2 copy-start.1
  6.5 328.4 %reduce-scatter.2.cloned.1.call-start = ((), (), s32[]{:S(2)}) async-start(), calls=%async_computation.2 | async-start | bytes 2621440 | tf_op jit(solution)/shard_map/reduce_scatter | solution.py:97
  11.2 1.3 copy-start.5
  151.4 18.5 %collective-permute-start = (bf16[128,3072]{0,1:T(8,128)(2,1)}, bf16[128,3072]{0,1:T(8,128)(2,1)}, u32[]{:S(2)}, u32[]{:S(2)}) collective-permute-start(bf16[128,3072]{0,1:T(8,128)(2,1)} %slice.13), channel_id=1, source_target_pairs={{0,8},{8,16},{16,24},{24,28},{28,20},{20,12},{12,4},{4,0},{1,9},{9... | collective-permute-start | bytes 2359304 | tf_op jit(solution)/shard_map/ppermute | solution.py:93
  152.5 46.5 %copy-start.6 = (s32[8]{0:T(128)S(1)}, s32[8]{0:T(128)}, u32[]{:S(2)}) copy-start(s32[8]{0:T(128)} %constant.168.clone) | copy-start | bytes 100
  157.7 51.2 %copy-start.4 = (s32[8]{0:T(128)S(1)}, s32[8]{0:T(128)}, u32[]{:S(2)}) copy-start(s32[8]{0:T(128)} %constant.169.clone) | copy-start | bytes 100
  161.6 17.7 %collective-permute-start.1 = (bf16[128,3072]{0,1:T(8,128)(2,1)}, bf16[128,3072]{0,1:T(8,128)(2,1)S(1)}, u32[]{:S(2)}, u32[]{:S(2)}) collective-permute-start(bf16[128,3072]{0,1:T(8,128)(2,1)} %slice.15), channel_id=1, source_target_pairs={{0,4},{8,0},{16,8},{24,16},{28,24},{20,28},{12,20},{4,12},{1,5},{9... | collective-permute-start | bytes 2359304 | tf_op jit(solution)/shard_map/ppermute | solution.py:95
  169.9 17.7 %collective-permute-start.2 = (bf16[128,3072]{0,1:T(8,128)(2,1)}, bf16[128,3072]{0,1:T(8,128)(2,1)}, u32[]{:S(2)}, u32[]{:S(2)}) collective-permute-start(bf16[128,3072]{0,1:T(8,128)(2,1)} %collective-permute-done), channel_id=1, source_target_pairs={{0,8},{8,16},{16,24},{24,28},{28,20},{20,12},{12,4},{4,0},{1,9},{9... | collective-permute-start | bytes 2359304 | tf_op jit(solution)/shard_map/ppermute | solution.py:93
  179.3 0.9 copy-start.2
  180.2 16.9 %collective-permute-start.3 = (bf16[128,3072]{0,1:T(8,128)(2,1)S(1)}, bf16[128,3072]{0,1:T(8,128)(2,1)}, u32[]{:S(2)}, u32[]{:S(2)}) collective-permute-start(bf16[128,3072]{0,1:T(8,128)(2,1)S(1)} %collective-permute-done.1), channel_id=1, source_target_pairs={{0,4},{8,0},{16,8},{24,16},{28,24},{20,28},{12,20},{4,12},{1,5},{9... | collective-permute-start | bytes 2359304 | tf_op jit(solution)/shard_map/ppermute | solution.py:95
  187.6 44.2 %collective-permute-start.4 = (bf16[128,3072]{0,1:T(8,128)(2,1)}, bf16[128,3072]{0,1:T(8,128)(2,1)}, u32[]{:S(2)}, u32[]{:S(2)}) collective-permute-start(bf16[128,3072]{0,1:T(8,128)(2,1)} %collective-permute-done.2), channel_id=1, source_target_pairs={{0,8},{8,16},{16,24},{24,28},{28,20},{20,12},{12,4},{4,0},{1,9},{9... | collective-permute-start | bytes 2359304 | tf_op jit(solution)/shard_map/ppermute | solution.py:93
  197.1 37.1 %collective-permute-start.5 = (bf16[128,3072]{0,1:T(8,128)(2,1)}, bf16[128,3072]{0,1:T(8,128)(2,1)}, u32[]{:S(2)}, u32[]{:S(2)}) collective-permute-start(bf16[128,3072]{0,1:T(8,128)(2,1)} %collective-permute-done.3), channel_id=1, source_target_pairs={{0,4},{8,0},{16,8},{24,16},{28,24},{20,28},{12,20},{4,12},{1,5},{9... | collective-permute-start | bytes 2359304 | tf_op jit(solution)/shard_map/ppermute | solution.py:95
  231.7 4.3 %copy-start.3 = (bf16[128,3072]{0,1:T(8,128)(2,1)S(1)}, bf16[128,3072]{0,1:T(8,128)(2,1)}, u32[]{:S(2)}) copy-start(bf16[128,3072]{0,1:T(8,128)(2,1)} %copy-done.2) | copy-start | bytes 2359300
  231.7 17.9 %collective-permute-start.6 = (bf16[128,3072]{0,1:T(8,128)(2,1)}, bf16[128,3072]{0,1:T(8,128)(2,1)S(1)}, u32[]{:S(2)}, u32[]{:S(2)}) collective-permute-start(bf16[128,3072]{0,1:T(8,128)(2,1)} %collective-permute-done.4), channel_id=1, source_target_pairs={{0,8},{8,16},{16,24},{24,28},{28,20},{20,12},{12,4},{4,0},{1,9},{9... | collective-permute-start | bytes 2359304 | tf_op jit(solution)/shard_map/ppermute | solution.py:93
  234.2 17.9 %collective-permute-start.7 = (bf16[128,3072]{0,1:T(8,128)(2,1)}, bf16[128,3072]{0,1:T(8,128)(2,1)S(1)}, u32[]{:S(2)}, u32[]{:S(2)}) collective-permute-start(bf16[128,3072]{0,1:T(8,128)(2,1)} %collective-permute-done.5), channel_id=1, source_target_pairs={{0,4},{8,0},{16,8},{24,16},{28,24},{20,28},{12,20},{4,12},{1,5},{9... | collective-permute-start | bytes 2359304 | tf_op jit(solution)/shard_map/ppermute | solution.py:95
  249.7 16.3 %collective-permute-start.8 = (bf16[128,3072]{0,1:T(8,128)(2,1)S(1)}, bf16[128,3072]{0,1:T(8,128)(2,1)S(1)}, u32[]{:S(2)}, u32[]{:S(2)}) collective-permute-start(bf16[128,3072]{0,1:T(8,128)(2,1)S(1)} %collective-permute-done.6), channel_id=1, source_target_pairs={{0,8},{8,16},{16,24},{24,28},{28,20},{20,12},{12,4},{4,0},{1,9},{9... | collective-permute-start | bytes 2359304 | tf_op jit(solution)/shard_map/ppermute | solution.py:93
  252.1 17.7 %collective-permute-start.9 = (bf16[128,3072]{0,1:T(8,128)(2,1)S(1)}, bf16[128,3072]{0,1:T(8,128)(2,1)S(1)}, u32[]{:S(2)}, u32[]{:S(2)}) collective-permute-start(bf16[128,3072]{0,1:T(8,128)(2,1)S(1)} %collective-permute-done.7), channel_id=1, source_target_pairs={{0,4},{8,0},{16,8},{24,16},{28,24},{20,28},{12,20},{4,12},{1,5},{9... | collective-permute-start | bytes 2359304 | tf_op jit(solution)/shard_map/ppermute | solution.py:95
  265.9 17.7 %collective-permute-start.10 = (bf16[128,3072]{0,1:T(8,128)(2,1)S(1)}, bf16[128,3072]{0,1:T(8,128)(2,1)S(1)}, u32[]{:S(2)}, u32[]{:S(2)}) collective-permute-start(bf16[128,3072]{0,1:T(8,128)(2,1)S(1)} %collective-permute-done.8), channel_id=1, source_target_pairs={{0,8},{8,16},{16,24},{24,28},{28,20},{20,12},{12,4},{4,0},{1,9},{9... | collective-permute-start | bytes 2359304 | tf_op jit(solution)/shard_map/ppermute | solution.py:93
  269.7 17.5 %collective-permute-start.11 = (bf16[128,3072]{0,1:T(8,128)(2,1)S(1)}, bf16[128,3072]{0,1:T(8,128)(2,1)S(1)}, u32[]{:S(2)}, u32[]{:S(2)}) collective-permute-start(bf16[128,3072]{0,1:T(8,128)(2,1)S(1)} %collective-permute-done.9), channel_id=1, source_target_pairs={{0,4},{8,0},{16,8},{24,16},{28,24},{20,28},{12,20},{4,12},{1,5},{9... | collective-permute-start | bytes 2359304 | tf_op jit(solution)/shard_map/ppermute | solution.py:95
  283.6 14.4 %collective-permute-start.12 = (bf16[128,3072]{0,1:T(8,128)(2,1)S(1)}, bf16[128,3072]{0,1:T(8,128)(2,1)S(1)}, u32[]{:S(2)}, u32[]{:S(2)}) collective-permute-start(bf16[128,3072]{0,1:T(8,128)(2,1)S(1)} %collective-permute-done.10), channel_id=1, source_target_pairs={{0,8},{8,16},{16,24},{24,28},{28,20},{20,12},{12,4},{4,0},{1,9},{9... | collective-permute-start | bytes 2359304 | tf_op jit(solution)/shard_map/ppermute | solution.py:93
  287.3 13.8 %collective-permute-start.13 = (bf16[128,3072]{0,1:T(8,128)(2,1)S(1)}, bf16[128,3072]{0,1:T(8,128)(2,1)S(1)}, u32[]{:S(2)}, u32[]{:S(2)}) collective-permute-start(bf16[128,3072]{0,1:T(8,128)(2,1)S(1)} %collective-permute-done.11), channel_id=1, source_target_pairs={{0,4},{8,0},{16,8},{24,16},{28,24},{20,28},{12,20},{4,12},{1,5},{9... | collective-permute-start | bytes 2359304 | tf_op jit(solution)/shard_map/ppermute | solution.py:95
Sparse Core Ops, SparseCore 0:
  302.3 32.5 reduce-scatter.1

commit v3 on v2

--- a/solution.py
+++ b/solution.py
@@ -48,8 +48,9 @@
     for p, g in enumerate(ring):
         pos_of[g] = p
     ring_arr = np.asarray(ring, np.int32)
-    fwd = [(ring[p], ring[(p + 1) % n]) for p in range(n)]
-    bwd = [(ring[p], ring[(p - 1) % n]) for p in range(n)]
+
+    def shifted(s):
+        return [(ring[p], ring[(p + s) % n]) for p in range(n)]
 
     def body(three_center, metric, occupied, nu_list, nu_count, block_size):
         n_mu, knu = nu_list.shape
@@ -76,24 +77,47 @@
         ).astype(jnp.bfloat16)
         rows = mu_dev * NB
         orbital = orbital.reshape(rows, n_aux * n_occ)
-        hr = rows // 2
         me = lax.axis_index("grp")
         pos = jnp.asarray(pos_of)[me]
         ring_c = jnp.asarray(ring_arr)
+
+        def start_of(off):
+            return ring_c[(pos + off) % n] * rows
+
+        radius = n // 4
+        held = {0: orbital}
+        fwd = orbital
+        bwd = orbital
+        for k in range(1, radius + 1):
+            fwd = lax.ppermute(fwd, "grp", shifted(1))
+            held[-k] = fwd
+            bwd = lax.ppermute(bwd, "grp", shifted(-1))
+            held[k] = bwd
+
+        def prod(xo, yo):
+            return jnp.dot(held[xo], held[yo].T, preferred_element_type=jnp.float32)
+
+        local = []
+        outgoing = {}
+        for d in range(n // 2 + 1):
+            xo = -((d + 1) // 2)
+            yo = xo + d
+            blk = prod(xo, yo)
+            s = d // 2
+            if s == 0:
+                local.append((-d, blk))
+            else:
+                outgoing.setdefault(s, []).append((-d, blk))
+            if 0 < d < n // 2:
+                outgoing.setdefault(xo, []).append((d, blk.T))
+        placed = list(local)
+        for s, items in sorted(outgoing.items()):
+            stack = jnp.stack([b for _, b in items])
+            got = lax.ppermute(stack, "grp", shifted(s))
+            placed += [(off, got[i]) for i, (off, _) in enumerate(items)]
         term = jnp.zeros((n * rows, rows), jnp.float32)
-
-        def place(term, piece, src, off):
-            part = jnp.dot(piece, orbital.T, preferred_element_type=jnp.float32)
-            return lax.dynamic_update_slice_in_dim(term, part, src * rows + off, axis=0)
-
-        term = place(term, orbital, me, 0)
-        a = orbital[:hr]
-        b = orbital[hr:]
-        for k in range(1, n):
-            a = lax.ppermute(a, "grp", fwd)
-            term = place(term, a, ring_c[(pos - k) % n], 0)
-            b = lax.ppermute(b, "grp", bwd)
-            term = place(term, b, ring_c[(pos + k) % n], hr)
+        for off, blk in placed:
+            term = lax.dynamic_update_slice_in_dim(term, blk, start_of(off), axis=0)
         return lax.psum_scatter(term, "rep", scatter_dimension=0, tiled=True)
 
     return body

time: 344 us -> 302 us (0.88)
  local copies, waits for them, and re-layouts: 100 us -> 81.1 us
  matrix products: 42.1 us -> 30.4 us
  between operations: 31.8 us -> 25.4 us
  starting transfers between devices: 16.2 us -> 10.3 us
    slice x5 -> x0, local copies, waits for them, and re-layouts: 20.4 us -> none  [the longest x3 11.4 us: body(): b = orbital[hr:]]
    dot_general x15 -> x5, matrix products: 22.2 us -> 10.8 us  [prod(): return jnp.dot(held[xo], held[yo].T, preferred_element_type=jnp.float32)]
    ppermute x14 -> x8, starting transfers between devices: 16.2 us -> 10.3 us  [the longest x4 6.22 us: body(): got = lax.ppermute(stack, 'grp', shifted(s))]
    ppermute x14 -> x8, waiting for transfers between devices: 70.9 us -> 72 us  [the longest x4 47.9 us: body(): got = lax.ppermute(stack, 'grp', shifted(s))]
  transfers between devices with their start and end apart: 15 -> 9, of which waited for: 12 -> 6; matrix products, arithmetic and copies ran while one was open for 13% -> 5% of each run, Pallas kernels for 0% -> 0%
where the time goes in v3:
time: 302 us; the launch traced here: 300 us
  waiting for transfers between devices  104 us (34%)
  local copies, waits for them, and re-layouts  81.1 us (27%)
  blocking collectives  44.1 us (15%)
  matrix products  30.4 us (10%)
  between operations  25.4 us (8%)
  starting transfers between devices  10.3 us (3%)
  other arithmetic  4.81 us (2%)
    ppermute x4, waiting for transfers between devices, body(): got = lax.ppermute(stack, 'grp', shifted(s))  47.9 us
    all_to_all x1, blocking collectives, body(): lax.all_to_all(half, 'grp', split_axis=1, concat_axis=0, tiled=True)  44.1 us
    another operation x1, local copies, waits for them, and re-layouts, body(): blocks = three_center[0].reshape(aux_dev, n_mu, knu, NB, NB)  34.4 us
    reduce_scatter x1, waiting for transfers between devices, body(): return lax.psum_scatter(term, 'rep', scatter_dimension=0, tiled=True)  32.1 us
    ppermute x2, waiting for transfers between devices, body(): fwd = lax.ppermute(fwd, 'grp', shifted(1))  24.1 us
    dot_general x1, matrix products, body(): jnp.einsum('qmkab,mkbi->qmai', masked, picked, preferred_element_type=jnp...  17 us
    reshape x2, local copies, waits for them, and re-layouts, body(): half = half.reshape(aux_dev, n_mu, NB * n_occ)  14.1 us
    reshape x2, local copies, waits for them, and re-layouts, body(): regrouped = regrouped.reshape(n_aux, mu_dev, NB, n_occ)  11.8 us
  transfers between devices with their start and end apart: 9, of which 6 were waited for; matrix products, arithmetic and copies ran while one was open for 5% of the time, Pallas kernels for 0%

profile of v3, /device:TPU:0, one launch (start us, length us, event | category | flops | bytes accessed | tf_op | source)
XLA Modules:
  0.0 300.3 jit_solution(18352104286980091404)
XLA Ops:
  6.5 0.0 copy-start
  6.5 0.0 reduce-scatter.2.cloned.1.call-start
  6.5 0.7 compare_select_fusion
  7.3 0.1 copy.33
  7.3 0.1 reshape.82
  7.5 1.3 reshape.76
  8.8 0.2 copy.34
  9.0 0.7 iota_compare_fusion.2
  9.7 1.6 gather_fusion.1
  11.2 0.0 copy-start.6
  11.3 1.0 gather_fusion
  12.3 0.1 reshape.89
  12.4 0.1 iota_compare_fusion
  12.5 0.0 copy-done.6
  12.5 0.1 iota_compare_fusion.1
  12.6 34.4 %reshape_squeeze.3 = bf16[8,32,6,64,64]{4,3,1,2,0:T(8,128)(2,1)} reshape(bf16[1,8,32,6,4096]{4,2,3,1,0:T(8,128)(2,1)} %param.8) | data formatting | bytes 25165824 | tf_op jit(solution)/shard_map/reshape;squeeze | solution.py:64
  47.0 2.3 and_and_fusion
  49.3 17.0 %fusion.3 = bf16[8,32,64,48]{2,3,0,1:T(8,128)(2,1)} fusion(bf16[32,6,64,48,1]{2,3,1,4,0:T(8,128)(2,1)S(1)} %bitcast.92, bf16[8,32,6,64,64]{4,3,1,2,0:T(8,128)(2,1)} %reshape_squeeze.3, pred[32,6,64,64]{3,2,1,0:T(8,128)(4,1)} %and_and_fusion), kind=kOutput, calls=%fused_computation.8 | convolution fusion | flops 611057664 | bytes 16121856 | tf_op jit(solution)/shard_map/qmkab,mkbi->qmai/dot_general | solution.py:67
  66.3 6.2 %copy.47 = bf16[8,32,64,48]{3,2,0,1:T(8,128)(2,1)} copy(bf16[8,32,64,48]{2,3,0,1:T(8,128)(2,1)} %fusion.3) | data formatting | bytes 3145728 | tf_op jit(solution)/shard_map/reshape | solution.py:70
  72.5 8.0 %reshape.103 = bf16[8,32,3072]{2,0,1:T(8,128)(2,1)S(1)} reshape(bf16[8,32,64,48]{3,2,0,1:T(8,128)(2,1)} %copy.47) | data formatting | bytes 3145728 | tf_op jit(solution)/shard_map/reshape | solution.py:70
  80.5 44.1 %all_to_all.15 = bf16[8,32,3072]{2,0,1:T(8,128)(2,1)S(1)} all-to-all(bf16[8,32,3072]{2,0,1:T(8,128)(2,1)S(1)} %reshape.103), channel_id=1, replica_groups=mesh['grp'=8,'rep'=4] {'grp'}, dimensions={1} | all-to-all | bytes 3145728 | tf_op jit(solution)/shard_map/all_to_all | solution.py:71
  124.5 0.1 copy.54
  124.7 5.3 %reshape.78 = bf16[64,4,64,48]{3,2,0,1:T(8,128)(2,1)} reshape(bf16[8,8,4,3072]{3,1,0,2:T(8,128)(2,1)S(1)} %bitcast.91) | data formatting | bytes 3145728 | tf_op jit(solution)/shard_map/reshape | solution.py:74
  130.0 6.4 %copy.39 = bf16[64,4,64,48]{0,2,3,1:T(8,128)(2,1)S(1)} copy(bf16[64,4,64,48]{3,2,0,1:T(8,128)(2,1)} %reshape.78) | data formatting | bytes 3145728 | tf_op jit(solution)/shard_map/reshape | solution.py:74
  136.4 2.6 convert_bitcast_fusion
  139.1 6.3 %copy.40 = bf16[4,64,64,48]{1,0,3,2:T(4,128)(2,1)S(1)} copy(bf16[4,64,64,48]{2,1,3,0:T(8,128)(2,1)} %convert_bitcast_fusion) | data formatting | bytes 3145728 | tf_op jit(solution)/shard_map/convert_element_type | solution.py:77
  145.4 0.0 copy-start.7
  145.4 0.0 copy-start.5
  145.4 3.0 %reshape.79 = bf16[256,3072]{0,1:T(8,128)(2,1)} reshape(bf16[4,64,64,48]{1,0,3,2:T(4,128)(2,1)S(1)} %copy.40) | data formatting | bytes 3145728 | tf_op jit(solution)/shard_map/reshape | solution.py:79
  148.4 1.1 collective-permute-start
  149.5 0.9 collective-permute-start.2
  150.5 0.0 copy-done.7
  150.5 0.6 dynamic_slice.27
  157.7 0.7 fusion.8
  159.7 24.1 %collective-permute-done = bf16[256,3072]{0,1:T(8,128)(2,1)} collective-permute-done((bf16[256,3072]{0,1:T(8,128)(2,1)}, bf16[256,3072]{0,1:T(8,128)(2,1)}, u32[]{:S(2)}, u32[]{:S(2)}) %collective-permute-start) | collective-permute-done | bytes 1572896 | tf_op jit(solution)/shard_map/ppermute | solution.py:92
  183.8 0.8 collective-permute-start.1
  184.5 0.1 broadcast_in_dim.12
  184.7 0.6 convolution_dynamic-update-slice_fusion
  185.3 0.0 collective-permute-done.2
  185.3 1.3 collective-permute-start.6
  186.6 2.0 constant_dynamic-update-slice_fusion.3
  188.7 2.5 fusion.10
  191.2 1.5 collective-permute-start.4
  196.6 33.9 %collective-permute-done.4 = f32[2,256,256]{1,2,0:T(8,128)} collective-permute-done((f32[2,256,256]{1,2,0:T(8,128)S(1)}, f32[2,256,256]{1,2,0:T(8,128)}, u32[]{:S(2)}, u32[]{:S(2)}) %collective-permute-start.4) | collective-permute-done | bytes 524320 | tf_op jit(solution)/shard_map/ppermute | solution.py:116
  230.5 1.1 slice_bitcast_fusion.2
  231.5 0.1 copy.42
  231.7 0.1 copy.43
  231.8 0.0 collective-permute-done.1
  231.8 2.5 fusion.9
  234.3 2.5 collective-permute-start.3
  236.8 0.8 pad_maximum_fusion.1
  237.6 0.6 collective-permute-start.5
  238.2 0.0 collective-permute-done.6
  238.2 3.2 %convolution_bitcast_fusion = f32[1,256,256]{2,1,0:T(8,128)} fusion(bf16[256,3072]{0,1:T(8,128)(2,1)} %collective-permute-done.1, bf16[256,3072]{0,1:T(8,128)(2,1)} %collective-permute-done.6), kind=kOutput, calls=%fused_computation.12 | convolution fusion | flops 402653184 | bytes 3407872 | tf_op jit(solution)/shard_map/dot_general | solution.py:98
  241.3 1.7 collective-permute-start.7
  243.0 3.7 %collective-permute-done.3 = f32[1,256,256]{1,2,0:T(8,128)S(1)} collective-permute-done((f32[1,256,256]{1,2,0:T(8,128)S(1)}, f32[1,256,256]{1,2,0:T(8,128)S(1)}, u32[]{:S(2)}, u32[]{:S(2)}) %collective-permute-start.3) | collective-permute-done | bytes 262176 | tf_op jit(solution)/shard_map/ppermute | solution.py:116
  246.7 0.7 copy-done.4
  247.4 1.1 copy.41
  248.6 4.6 %collective-permute-done.5 = f32[2,256,256]{2,1,0:T(8,128)S(1)} collective-permute-done((f32[2,256,256]{2,1,0:T(8,128)}, f32[2,256,256]{2,1,0:T(8,128)S(1)}, u32[]{:S(2)}, u32[]{:S(2)}) %collective-permute-start.5) | collective-permute-done | bytes 524320 | tf_op jit(solution)/shard_map/ppermute | solution.py:116
  253.3 5.8 %collective-permute-done.7 = f32[1,256,256]{2,1,0:T(8,128)} collective-permute-done((f32[1,256,256]{2,1,0:T(8,128)}, f32[1,256,256]{2,1,0:T(8,128)}, u32[]{:S(2)}, u32[]{:S(2)}) %collective-permute-start.7) | collective-permute-done | bytes 262176 | tf_op jit(solution)/shard_map/ppermute | solution.py:116
  259.0 1.0 bitcast_dynamic-update-slice_fusion
  260.0 1.3 copy-done.2
  261.3 0.0 reduce-scatter.2.cloned.1.call-update
  261.4 32.1 %reduce-scatter.2.cloned.1.call-done = f32[512,256]{1,0:T(8,128)} async-done(((f32[2048,256]{1,0:T(8,128)}), f32[512,256]{1,0:T(8,128)}) %reduce-scatter.2.cloned.1.call-update) | async-done | bytes 524304 | tf_op jit(solution)/shard_map/reduce_scatter | solution.py:121
  (15 shorter events, 0.2 us)
Async XLA Ops:
  6.5 129.9 %copy-start = (bf16[1,64,64]{2,1,0:T(8,128)(2,1)S(1)}, bf16[1,64,64]{2,1,0:T(8,128)(2,1)}, u32[]{:S(2)}) copy-start(bf16[1,64,64]{2,1,0:T(8,128)(2,1)} %param.9) | copy-start | bytes 24580
  6.5 3.2 %copy-start.1 = (s32[32]{0:T(128)S(1)}, s32[32]{0:T(128)}, u32[]{:S(2)}) copy-start(s32[32]{0:T(128)} %param.13) | copy-start | bytes 388
  6.5 286.9 %reduce-scatter.2.cloned.1.call-start = ((), (), s32[]{:S(2)}) async-start(), calls=%async_computation.2 | async-start | bytes 2621440 | tf_op jit(solution)/shard_map/reduce_scatter | solution.py:121
  11.2 1.3 copy-start.6
  145.4 5.1 %copy-start.7 = (s32[8]{0:T(128)S(1)}, s32[8]{0:T(128)}, u32[]{:S(2)}) copy-start(s32[8]{0:T(128)} %constant.85.clone) | copy-start | bytes 100
  145.4 12.2 %copy-start.5 = (s32[8]{0:T(128)S(1)}, s32[8]{0:T(128)}, u32[]{:S(2)}) copy-start(s32[8]{0:T(128)} %constant.86.clone) | copy-start | bytes 100
  148.4 35.3 %collective-permute-start = (bf16[256,3072]{0,1:T(8,128)(2,1)}, bf16[256,3072]{0,1:T(8,128)(2,1)}, u32[]{:S(2)}, u32[]{:S(2)}) collective-permute-start(bf16[256,3072]{0,1:T(8,128)(2,1)} %reshape.79), channel_id=1, source_target_pairs={{0,8},{8,16},{16,24},{24,28},{28,20},{20,12},{12,4},{4,0},{1,9},{9... | collective-permute-start | bytes 4718600 | tf_op jit(solution)/shard_map/ppermute | solution.py:92
  149.5 35.7 %collective-permute-start.2 = (bf16[256,3072]{0,1:T(8,128)(2,1)}, bf16[256,3072]{0,1:T(8,128)(2,1)}, u32[]{:S(2)}, u32[]{:S(2)}) collective-permute-start(bf16[256,3072]{0,1:T(8,128)(2,1)} %reshape.79), channel_id=1, source_target_pairs={{0,4},{8,0},{16,8},{24,16},{28,24},{20,28},{12,20},{4,12},{1,5},{9... | collective-permute-start | bytes 4718600 | tf_op jit(solution)/shard_map/ppermute | solution.py:94
  159.7 25.0 %copy-start.3 = (bf16[256,3072]{0,1:T(8,128)(2,1)S(1)}, bf16[256,3072]{0,1:T(8,128)(2,1)}, u32[]{:S(2)}) copy-start(bf16[256,3072]{0,1:T(8,128)(2,1)} %reshape.79) | copy-start | bytes 4718596
  183.8 48.0 %collective-permute-start.1 = (bf16[256,3072]{0,1:T(8,128)(2,1)}, bf16[256,3072]{0,1:T(8,128)(2,1)}, u32[]{:S(2)}, u32[]{:S(2)}) collective-permute-start(bf16[256,3072]{0,1:T(8,128)(2,1)} %collective-permute-done), channel_id=1, source_target_pairs={{0,8},{8,16},{16,24},{24,28},{28,20},{20,12},{12,4},{4,0},{1,9},{9... | collective-permute-start | bytes 4718600 | tf_op jit(solution)/shard_map/ppermute | solution.py:92
  185.3 52.9 %collective-permute-start.6 = (bf16[256,3072]{0,1:T(8,128)(2,1)}, bf16[256,3072]{0,1:T(8,128)(2,1)}, u32[]{:S(2)}, u32[]{:S(2)}) collective-permute-start(bf16[256,3072]{0,1:T(8,128)(2,1)} %collective-permute-done.2), channel_id=1, source_target_pairs={{0,4},{8,0},{16,8},{24,16},{28,24},{20,28},{12,20},{4,12},{1,5},{9... | collective-permute-start | bytes 4718600 | tf_op jit(solution)/shard_map/ppermute | solution.py:94
  191.2 39.3 %collective-permute-start.4 = (f32[2,256,256]{1,2,0:T(8,128)S(1)}, f32[2,256,256]{1,2,0:T(8,128)}, u32[]{:S(2)}, u32[]{:S(2)}) collective-permute-start(f32[2,256,256]{1,2,0:T(8,128)S(1)} %pad_maximum_fusion), channel_id=1, source_target_pairs={{0,4},{8,0},{16,8},{24,16},{28,24},{20,28},{12,20},{4,12},{1,5},{9... | collective-permute-start | bytes 1572872 | tf_op jit(solution)/shard_map/ppermute | solution.py:116
  234.3 12.4 %collective-permute-start.3 = (f32[1,256,256]{1,2,0:T(8,128)S(1)}, f32[1,256,256]{1,2,0:T(8,128)S(1)}, u32[]{:S(2)}, u32[]{:S(2)}) collective-permute-start(f32[1,256,256]{1,2,0:T(8,128)S(1)} %bitcast.96), channel_id=1, source_target_pairs={{0,12},{8,4},{16,0},{24,8},{28,16},{20,24},{12,28},{4,20},{1,13},{... | collective-permute-start | bytes 786440 | tf_op jit(solution)/shard_map/ppermute | solution.py:116
  237.6 15.6 %collective-permute-start.5 = (f32[2,256,256]{2,1,0:T(8,128)}, f32[2,256,256]{2,1,0:T(8,128)S(1)}, u32[]{:S(2)}, u32[]{:S(2)}) collective-permute-start(f32[2,256,256]{2,1,0:T(8,128)} %pad_maximum_fusion.1), channel_id=1, source_target_pairs={{0,8},{8,16},{16,24},{24,28},{28,20},{20,12},{12,4},{4,0},{1,9},{9... | collective-permute-start | bytes 1572872 | tf_op jit(solution)/shard_map/ppermute | solution.py:116
  241.3 17.7 %collective-permute-start.7 = (f32[1,256,256]{2,1,0:T(8,128)}, f32[1,256,256]{2,1,0:T(8,128)}, u32[]{:S(2)}, u32[]{:S(2)}) collective-permute-start(f32[1,256,256]{2,1,0:T(8,128)} %convolution_bitcast_fusion), channel_id=1, source_target_pairs={{0,16},{8,24},{16,28},{24,20},{28,12},{20,4},{12,0},{4,8},{1,17},{... | collective-permute-start | bytes 786440 | tf_op jit(solution)/shard_map/ppermute | solution.py:116
  246.7 0.7 copy-start.4
  260.0 1.3 copy-start.2
Sparse Core Ops, SparseCore 0:
  261.5 31.8 reduce-scatter.1

commit v4 on v3

--- a/solution.py
+++ b/solution.py
@@ -61,14 +61,31 @@
         col_live = lanes[None, None, :] < block_size[nu_list][:, :, None]
         slot_live = jnp.arange(knu, dtype=jnp.int32)[None, :] < nu_count[:, None]
         mask = row_live[:, None, :, None] & col_live[:, :, None, :] & slot_live[:, :, None, None]
-        blocks = three_center[0].reshape(aux_dev, n_mu, knu, NB, NB)
-        masked = jnp.where(mask[None], blocks, jnp.zeros((), jnp.bfloat16))
         picked = occupied.reshape(n_mu, NB, n_occ)[nu_list]
-        half = jnp.einsum(
-            "qmkab,mkbi->qmai", masked, picked, preferred_element_type=jnp.float32
-        ).astype(jnp.bfloat16)
-        half = half.reshape(aux_dev, n_mu, NB * n_occ)
-        regrouped = lax.all_to_all(half, "grp", split_axis=1, concat_axis=0, tiled=True)
+        me = lax.axis_index("grp")
+        pos = jnp.asarray(pos_of)[me]
+        ring_c = jnp.asarray(ring_arr)
+        mu_dev = n_mu // n
+        tc = three_center[0]
+        pieces = []
+        for s in range(n):
+            dest = ring_c[(pos + s) % n]
+            m0 = dest * mu_dev
+            chunk = lax.dynamic_slice_in_dim(tc, m0, mu_dev, axis=1)
+            chunk = chunk.reshape(aux_dev, mu_dev, knu, NB, NB)
+            live = lax.dynamic_slice_in_dim(mask, m0, mu_dev, axis=0)
+            masked = jnp.where(live[None], chunk, jnp.zeros((), jnp.bfloat16))
+            sel = lax.dynamic_slice_in_dim(picked, m0, mu_dev, axis=0)
+            half = jnp.einsum(
+                "qmkab,mkbi->qmai", masked, sel, preferred_element_type=jnp.float32
+            ).astype(jnp.bfloat16)
+            if s:
+                half = lax.ppermute(half, "grp", shifted(s))
+            pieces.append(half)
+        regrouped = jnp.zeros((n * aux_dev, mu_dev, NB, n_occ), jnp.bfloat16)
+        for s, half in enumerate(pieces):
+            src_g = ring_c[(pos - s) % n]
+            regrouped = lax.dynamic_update_slice_in_dim(regrouped, half, src_g * aux_dev, axis=0)
         n_aux = regrouped.shape[0]
         mu_dev = regrouped.shape[1]
         regrouped = regrouped.reshape(n_aux, mu_dev, NB, n_occ)
@@ -77,9 +94,6 @@
         ).astype(jnp.bfloat16)
         rows = mu_dev * NB
         orbital = orbital.reshape(rows, n_aux * n_occ)
-        me = lax.axis_index("grp")
-        pos = jnp.asarray(pos_of)[me]
-        ring_c = jnp.asarray(ring_arr)
 
         def start_of(off):
             return ring_c[(pos + off) % n] * rows

time: 302 us -> 694 us (2.30); the launches traced: 300 us -> 681 us
  local copies, waits for them, and re-layouts: 81.1 us -> 455 us
  blocking collectives: 44.1 us -> 0 us
  matrix products: 30.4 us -> 46.7 us
  between operations: 25.4 us -> 40.9 us
  starting transfers between devices: 10.3 us -> 23.7 us
    dynamic_update_slice x0 -> x8, local copies, waits for them, and re-layouts: none -> 342 us  [body(): lax.dynamic_update_slice_in_dim(regrouped, half, src_g * aux_dev, axis=0)]
    all_to_all x1 -> x0, blocking collectives: 44.1 us -> none  [body(): lax.all_to_all(half, 'grp', split_axis=1, concat_axis=0, tiled=True)]
    another operation x1 -> x0, local copies, waits for them, and re-layouts: 34.4 us -> none  [body(): blocks = three_center[0].reshape(aux_dev, n_mu, knu, NB, NB)]
    dynamic_slice x1 -> x11, local copies, waits for them, and re-layouts: 0.71 us -> 27.1 us  [the longest x9 24.1 us: body(): chunk = lax.dynamic_slice_in_dim(tc, m0, mu_dev, axis=1)]
    ppermute x0 -> x7, local copies, waits for them, and re-layouts: none -> 25.1 us  [body(): half = lax.ppermute(half, 'grp', shifted(s))]
    dot_general x1 -> x8, matrix products: 17 us -> 33.3 us  [body(): jnp.einsum('qmkab,mkbi->qmai', masked, sel, preferred_element_type=jnp.fl...]
    ppermute x0 -> x7, starting transfers between devices: none -> 14.6 us  [body(): half = lax.ppermute(half, 'grp', shifted(s))]
    reshape x4 -> x8, local copies, waits for them, and re-layouts: 25.9 us -> 34.8 us  [body(): chunk = chunk.reshape(aux_dev, mu_dev, knu, NB, NB)]
  transfers between devices with their start and end apart: 9 -> 16, of which waited for: 6 -> 6; matrix products, arithmetic and copies ran while one was open for 5% -> 60% of each run, Pallas kernels for 0% -> 0%
where the time goes in v4:
time: 694 us; the launch traced here: 681 us
  local copies, waits for them, and re-layouts  455 us (66%)
  waiting for transfers between devices  110 us (16%)
  matrix products  46.7 us (7%)
  between operations  40.9 us (6%)
  starting transfers between devices  23.7 us (3%)
    dynamic_update_slice x8, local copies, waits for them, and re-layouts, body(): lax.dynamic_update_slice_in_dim(regrouped, half, src_g * aux_dev, axis=0)  342 us
    ppermute x4, waiting for transfers between devices, body(): got = lax.ppermute(stack, 'grp', shifted(s))  46.3 us
    reshape x8, local copies, waits for them, and re-layouts, body(): chunk = chunk.reshape(aux_dev, mu_dev, knu, NB, NB)  34.8 us
    dot_general x8, matrix products, body(): jnp.einsum('qmkab,mkbi->qmai', masked, sel, preferred_element_type=jnp.fl...  33.3 us
    reduce_scatter x1, waiting for transfers between devices, body(): return lax.psum_scatter(term, 'rep', scatter_dimension=0, tiled=True)  32.5 us
    ppermute x2, waiting for transfers between devices, body(): fwd = lax.ppermute(fwd, 'grp', shifted(1))  31.1 us
    ppermute x7, local copies, waits for them, and re-layouts, body(): half = lax.ppermute(half, 'grp', shifted(s))  25.1 us
    dynamic_slice x9, local copies, waits for them, and re-layouts, body(): chunk = lax.dynamic_slice_in_dim(tc, m0, mu_dev, axis=1)  24.1 us
  transfers between devices with their start and end apart: 16, of which 6 were waited for; matrix products, arithmetic and copies ran while one was open for 60% of the time, Pallas kernels for 0%

profile of v4, /device:TPU:0, one launch (start us, length us, event | category | flops | bytes accessed | tf_op | source)
XLA Modules:
  0.0 681.2 jit_solution(13456826150961119870)
XLA Ops:
  6.5 1.3 dynamic_slice.129
  19.1 1.9 fusion.139
  28.5 1.6 gather_fusion.1
  30.9 2.3 gather_fusion
  33.2 1.5 and_and_fusion
  35.8 14.3 %constant_dynamic-slice_fusion = (bf16[1,8,4,6,4096]{4,2,3,1,0:T(4,128)(2,1)S(1)}, bf16[1,8,4,6,4096]{4,2,3,1,0:T(4,128)(2,1)}, bf16[1,8,4,6,4096]{4,2,3,1,0:T(4...) fusion(bf16[1,8,32,6,4096]{4,2,3,1,0:T(8,128)(2,1)} %param.8, ...), kind=kLoop, calls=%fused_computation.96 | loop fusion | bytes 25165856 | tf_op jit(solution)/shard_map/dynamic_slice | solution.py:74
  51.0 4.3 reshape.155
  55.4 4.5 fusion.101
  59.8 3.1 collective-permute-start.6
  63.8 4.3 reshape.153
  68.2 4.4 fusion.95
  72.6 3.6 collective-permute-start.4
  77.1 4.3 reshape.152
  81.4 4.4 fusion.92
  86.8 4.3 reshape.150
  91.1 4.4 fusion.86
  95.5 1.9 collective-permute-start.1
  98.3 4.3 reshape.149
  102.6 4.3 fusion.83
  106.9 2.9 collective-permute-start
  115.0 2.3 copy.36
  117.2 4.4 reshape.151
  121.6 2.3 copy.27
  123.9 4.3 reshape.148
  129.1 4.4 reshape.154
  133.5 4.5 fusion.89
  138.0 3.5 fusion.98
  142.4 2.2 collective-permute-start.5
  144.6 3.3 fusion.80
  147.9 2.8 copy.29
  150.7 2.5 broadcast_in_dim.82
  153.2 28.3 %dynamic_update_slice.48 = bf16[64,4,64,48]{0,2,3,1:T(8,128)(2,1)} dynamic-update-slice(bf16[64,4,64,48]{0,2,3,1:T(8,128)(2,1)} %broadcast_in_dim.82, bf16[8,4,64,48]{0,2,3,1:T(8,128)(2,1)S(1)} %copy.29, s32[]{:T(128)S(6)} %select_n.261, s32[]{:T(128)} %constant.154.clone.1, s32[]{:T(128)} %constant.154.clone.1, s32[]{:T(128)} %constant.154.clone.1) | dynamic-update-slice | bytes 393220 | tf_op jit(solution)/shard_map/dynamic_update_slice | solution.py:88
  181.5 3.8 copy.32
  185.3 44.8 %dynamic_update_slice.49 = bf16[64,4,64,48]{0,2,3,1:T(8,128)(2,1)S(1)} dynamic-update-slice(bf16[64,4,64,48]{0,2,3,1:T(8,128)(2,1)S(1)} %copy-done.2, bf16[8,4,64,48]{0,2,3,1:T(8,128)(2,1)} %copy.32, s32[]{:T(128)S(6)} %select_n.268, s32[]{:T(128)} %constant.154.clone.1, s32[]{:T(128)} %constant.154.clone.1, s32[]{:T(128)} %constant.154.clone.1) | dynamic-update-slice | bytes 393220 | tf_op jit(solution)/shard_map/dynamic_update_slice | solution.py:88
  230.2 3.7 copy.35
  233.9 44.8 %dynamic_update_slice.50 = bf16[64,4,64,48]{0,2,3,1:T(8,128)(2,1)S(1)} dynamic-update-slice(bf16[64,4,64,48]{0,2,3,1:T(8,128)(2,1)S(1)} %dynamic_update_slice.49, bf16[8,4,64,48]{0,2,3,1:T(8,128)(2,1)} %copy.35, s32[]{:T(128)S(6)} %select_n.275, s32[]{:T(128)} %constant.154.clone.1, s32[]{:T(128)} %constant.154.clone.1, s32[]{:T(128)} %constant.154.clone.1) | dynamic-update-slice | bytes 393220 | tf_op jit(solution)/shard_map/dynamic_update_slice | solution.py:88
  278.7 3.7 copy.38
  282.4 44.8 %dynamic_update_slice.51 = bf16[64,4,64,48]{0,2,3,1:T(8,128)(2,1)S(1)} dynamic-update-slice(bf16[64,4,64,48]{0,2,3,1:T(8,128)(2,1)S(1)} %dynamic_update_slice.50, bf16[8,4,64,48]{0,2,3,1:T(8,128)(2,1)} %copy.38, s32[]{:T(128)S(6)} %select_n.282, s32[]{:T(128)} %constant.154.clone.1, s32[]{:T(128)} %constant.154.clone.1, s32[]{:T(128)} %constant.154.clone.1) | dynamic-update-slice | bytes 393220 | tf_op jit(solution)/shard_map/dynamic_update_slice | solution.py:88
  327.3 3.7 copy.41
  331.0 44.8 %dynamic_update_slice.52 = bf16[64,4,64,48]{0,2,3,1:T(8,128)(2,1)S(1)} dynamic-update-slice(bf16[64,4,64,48]{0,2,3,1:T(8,128)(2,1)S(1)} %dynamic_update_slice.51, bf16[8,4,64,48]{0,2,3,1:T(8,128)(2,1)} %copy.41, s32[]{:T(128)S(6)} %select_n.289, s32[]{:T(128)} %constant.154.clone.1, s32[]{:T(128)} %constant.154.clone.1, s32[]{:T(128)} %constant.154.clone.1) | dynamic-update-slice | bytes 393220 | tf_op jit(solution)/shard_map/dynamic_update_slice | solution.py:88
  375.8 3.7 copy.44
  379.5 44.8 %dynamic_update_slice.53 = bf16[64,4,64,48]{0,2,3,1:T(8,128)(2,1)S(1)} dynamic-update-slice(bf16[64,4,64,48]{0,2,3,1:T(8,128)(2,1)S(1)} %dynamic_update_slice.52, bf16[8,4,64,48]{0,2,3,1:T(8,128)(2,1)} %copy.44, s32[]{:T(128)S(6)} %select_n.296, s32[]{:T(128)} %constant.154.clone.1, s32[]{:T(128)} %constant.154.clone.1, s32[]{:T(128)} %constant.154.clone.1) | dynamic-update-slice | bytes 393220 | tf_op jit(solution)/shard_map/dynamic_update_slice | solution.py:88
  424.4 3.7 copy.47
  428.1 44.8 %dynamic_update_slice.54 = bf16[64,4,64,48]{0,2,3,1:T(8,128)(2,1)S(1)} dynamic-update-slice(bf16[64,4,64,48]{0,2,3,1:T(8,128)(2,1)S(1)} %dynamic_update_slice.53, bf16[8,4,64,48]{0,2,3,1:T(8,128)(2,1)} %copy.47, s32[]{:T(128)S(6)} %select_n.303, s32[]{:T(128)} %constant.154.clone.1, s32[]{:T(128)} %constant.154.clone.1, s32[]{:T(128)} %constant.154.clone.1) | dynamic-update-slice | bytes 393220 | tf_op jit(solution)/shard_map/dynamic_update_slice | solution.py:88
  472.9 2.8 copy.50
  475.7 44.8 %dynamic_update_slice.55 = bf16[64,4,64,48]{0,2,3,1:T(8,128)(2,1)S(1)} dynamic-update-slice(bf16[64,4,64,48]{0,2,3,1:T(8,128)(2,1)S(1)} %dynamic_update_slice.54, bf16[8,4,64,48]{0,2,3,1:T(8,128)(2,1)} %copy.50, s32[]{:T(128)S(6)} %select_n.310, s32[]{:T(128)} %constant.154.clone.1, s32[]{:T(128)} %constant.154.clone.1, s32[]{:T(128)} %constant.154.clone.1) | dynamic-update-slice | bytes 393220 | tf_op jit(solution)/shard_map/dynamic_update_slice | solution.py:88
  520.5 2.6 convert_bitcast_fusion
  523.1 6.3 copy.51
  529.5 3.0 reshape.156
  533.2 1.3 collective-permute-start.9
  535.9 31.1 %collective-permute-done.7 = bf16[256,3072]{0,1:T(8,128)(2,1)} collective-permute-done((bf16[256,3072]{0,1:T(8,128)(2,1)}, bf16[256,3072]{0,1:T(8,128)(2,1)}, u32[]{:S(2)}, u32[]{:S(2)}) %collective-permute-start.7) | collective-permute-done | bytes 1572896 | tf_op jit(solution)/shard_map/ppermute | solution.py:106
  570.0 2.0 constant_dynamic-update-slice_fusion.3
  572.0 2.5 fusion.141
  574.6 1.3 collective-permute-start.11
  579.6 34.1 %collective-permute-done.11 = f32[2,256,256]{1,2,0:T(8,128)} collective-permute-done((f32[2,256,256]{1,2,0:T(8,128)S(1)}, f32[2,256,256]{1,2,0:T(8,128)}, u32[]{:S(2)}, u32[]{:S(2)}) %collective-permute-start.11) | collective-permute-done | bytes 524320 | tf_op jit(solution)/shard_map/ppermute | solution.py:130
  615.1 2.5 fusion.140
  617.6 1.5 collective-permute-start.10
  620.7 3.2 convolution_bitcast_fusion
  623.9 1.2 collective-permute-start.14
  625.1 3.2 collective-permute-done.10
  630.3 4.4 collective-permute-done.12
  634.8 4.5 collective-permute-done.14
  640.3 1.3 copy-done.3
  641.6 32.5 %reduce-scatter.2.cloned.1.call-done = f32[512,256]{1,0:T(8,128)} async-done(((f32[2048,256]{1,0:T(8,128)}), f32[512,256]{1,0:T(8,128)}) %reduce-scatter.2.cloned.1.call-update) | async-done | bytes 524304 | tf_op jit(solution)/shard_map/reduce_scatter | solution.py:135
  (80 shorter events, 20.0 us)
Async XLA Ops:
  6.5 514.0 %copy-start = (bf16[1,64,64]{2,1,0:T(8,128)(2,1)S(1)}, bf16[1,64,64]{2,1,0:T(8,128)(2,1)}, u32[]{:S(2)}) copy-start(bf16[1,64,64]{2,1,0:T(8,128)(2,1)} %param.9) | copy-start | bytes 24580
  6.5 22.0 %copy-start.1 = (s32[32]{0:T(128)S(1)}, s32[32]{0:T(128)}, u32[]{:S(2)}) copy-start(s32[32]{0:T(128)} %param.13) | copy-start | bytes 388
  6.5 667.6 %reduce-scatter.2.cloned.1.call-start = ((), (), s32[]{:S(2)}) async-start(), calls=%async_computation.1 | async-start | bytes 2621440 | tf_op jit(solution)/shard_map/reduce_scatter | solution.py:135
  28.5 1.8 copy-start.15
  55.4 7.6 %copy-start.7 = (bf16[1,8,4,6,4096]{4,2,3,1,0:T(4,128)(2,1)S(1)}, bf16[1,8,4,6,4096]{4,2,3,1,0:T(4,128)(2,1)}, u32[]{:S(2)}) copy-start(bf16[1,8,4,6,4096]{4,2,3,1,0:T(4,128)(2,1)} %get-tuple-element.6) | copy-start | bytes 4718596
  59.8 413.1 %collective-permute-start.6 = (bf16[8,4,64,48]{2,3,0,1:T(8,128)(2,1)}, bf16[8,4,64,48]{2,3,0,1:T(8,128)(2,1)S(1)}, u32[]{:S(2)}, u32[]{:S(2)}) collective-permute-start(bf16[8,4,64,48]{2,3,0,1:T(8,128)(2,1)} %fusion.101), channel_id=1, source_target_pairs={{0,4},{8,0},{16,8},{24,16},{28,24},{20,28},{12,20},{4,12},{1,5},{9... | collective-permute-start | bytes 589832 | tf_op jit(solution)/shard_map/ppermute | solution.py:83
  68.2 8.0 %copy-start.6 = (bf16[1,8,4,6,4096]{4,2,3,1,0:T(4,128)(2,1)S(1)}, bf16[1,8,4,6,4096]{4,2,3,1,0:T(4,128)(2,1)}, u32[]{:S(2)}) copy-start(bf16[1,8,4,6,4096]{4,2,3,1,0:T(4,128)(2,1)} %get-tuple-element.7) | copy-start | bytes 4718596
  72.6 303.2 %collective-permute-start.4 = (bf16[8,4,64,48]{2,3,0,1:T(8,128)(2,1)}, bf16[8,4,64,48]{2,3,0,1:T(8,128)(2,1)}, u32[]{:S(2)}, u32[]{:S(2)}) collective-permute-start(bf16[8,4,64,48]{2,3,0,1:T(8,128)(2,1)} %fusion.95), channel_id=1, source_target_pairs={{0,20},{8,12},{16,4},{24,0},{28,8},{20,16},{12,24},{4,28},{1,21},{... | collective-permute-start | bytes 589832 | tf_op jit(solution)/shard_map/ppermute | solution.py:83
  81.4 4.4 copy-start.5
  85.9 241.4 %collective-permute-start.3 = (bf16[8,4,64,48]{2,3,0,1:T(8,128)(2,1)}, bf16[8,4,64,48]{2,3,0,1:T(8,128)(2,1)}, u32[]{:S(2)}, u32[]{:S(2)}) collective-permute-start(bf16[8,4,64,48]{2,3,0,1:T(8,128)(2,1)} %fusion.92), channel_id=1, source_target_pairs={{0,28},{8,20},{16,12},{24,4},{28,0},{20,8},{12,16},{4,24},{1,29},{... | collective-permute-start | bytes 589832 | tf_op jit(solution)/shard_map/ppermute | solution.py:83
  91.1 6.3 copy-start.4
  95.5 46.0 %collective-permute-start.1 = (bf16[8,4,64,48]{2,3,0,1:T(8,128)(2,1)}, bf16[8,4,64,48]{2,3,0,1:T(8,128)(2,1)}, u32[]{:S(2)}, u32[]{:S(2)}) collective-permute-start(bf16[8,4,64,48]{2,3,0,1:T(8,128)(2,1)} %fusion.86), channel_id=1, source_target_pairs={{0,16},{8,24},{16,28},{24,20},{28,12},{20,4},{12,0},{4,8},{1,17},{... | collective-permute-start | bytes 589832 | tf_op jit(solution)/shard_map/ppermute | solution.py:83
  106.9 35.5 %collective-permute-start = (bf16[8,4,64,48]{2,3,0,1:T(8,128)(2,1)}, bf16[8,4,64,48]{2,3,0,1:T(8,128)(2,1)}, u32[]{:S(2)}, u32[]{:S(2)}) collective-permute-start(bf16[8,4,64,48]{2,3,0,1:T(8,128)(2,1)} %fusion.83), channel_id=1, source_target_pairs={{0,8},{8,16},{16,24},{24,28},{28,20},{20,12},{12,4},{4,0},{1,9},{9... | collective-permute-start | bytes 589832 | tf_op jit(solution)/shard_map/ppermute | solution.py:83
  129.1 4.4 copy-start.14
  133.5 4.5 copy-start.9
  133.5 4.5 copy-start.13
  138.0 6.6 copy-start.8
  138.0 6.6 copy-start.12
  141.5 137.2 %collective-permute-start.2 = (bf16[8,4,64,48]{2,3,0,1:T(8,128)(2,1)}, bf16[8,4,64,48]{2,3,0,1:T(8,128)(2,1)}, u32[]{:S(2)}, u32[]{:S(2)}) collective-permute-start(bf16[8,4,64,48]{2,3,0,1:T(8,128)(2,1)} %fusion.89), channel_id=1, source_target_pairs={{0,24},{8,28},{16,20},{24,12},{28,4},{20,0},{12,8},{4,16},{1,25},{... | collective-permute-start | bytes 589832 | tf_op jit(solution)/shard_map/ppermute | solution.py:83
  142.4 281.9 %collective-permute-start.5 = (bf16[8,4,64,48]{2,3,0,1:T(8,128)(2,1)}, bf16[8,4,64,48]{2,3,0,1:T(8,128)(2,1)}, u32[]{:S(2)}, u32[]{:S(2)}) collective-permute-start(bf16[8,4,64,48]{2,3,0,1:T(8,128)(2,1)} %fusion.98), channel_id=1, source_target_pairs={{0,12},{8,4},{16,0},{24,8},{28,16},{20,24},{12,28},{4,20},{1,13},{... | collective-permute-start | bytes 589832 | tf_op jit(solution)/shard_map/ppermute | solution.py:83
  181.5 3.9 copy-start.2
  532.5 34.5 %collective-permute-start.7 = (bf16[256,3072]{0,1:T(8,128)(2,1)}, bf16[256,3072]{0,1:T(8,128)(2,1)}, u32[]{:S(2)}, u32[]{:S(2)}) collective-permute-start(bf16[256,3072]{0,1:T(8,128)(2,1)} %reshape.156), channel_id=1, source_target_pairs={{0,8},{8,16},{16,24},{24,28},{28,20},{20,12},{12,4},{4,0},{1,9},{9... | collective-permute-start | bytes 4718600 | tf_op jit(solution)/shard_map/ppermute | solution.py:106
  533.2 35.7 %collective-permute-start.9 = (bf16[256,3072]{0,1:T(8,128)(2,1)}, bf16[256,3072]{0,1:T(8,128)(2,1)}, u32[]{:S(2)}, u32[]{:S(2)}) collective-permute-start(bf16[256,3072]{0,1:T(8,128)(2,1)} %reshape.156), channel_id=1, source_target_pairs={{0,4},{8,0},{16,8},{24,16},{28,24},{20,28},{12,20},{4,12},{1,5},{9... | collective-permute-start | bytes 4718600 | tf_op jit(solution)/shard_map/ppermute | solution.py:108
  535.9 32.4 %copy-start.10 = (bf16[256,3072]{0,1:T(8,128)(2,1)S(1)}, bf16[256,3072]{0,1:T(8,128)(2,1)}, u32[]{:S(2)}) copy-start(bf16[256,3072]{0,1:T(8,128)(2,1)} %reshape.156) | copy-start | bytes 4718596
  567.0 48.1 %collective-permute-start.8 = (bf16[256,3072]{0,1:T(8,128)(2,1)}, bf16[256,3072]{0,1:T(8,128)(2,1)}, u32[]{:S(2)}, u32[]{:S(2)}) collective-permute-start(bf16[256,3072]{0,1:T(8,128)(2,1)} %collective-permute-done.7), channel_id=1, source_target_pairs={{0,8},{8,16},{16,24},{24,28},{28,20},{20,12},{12,4},{4,0},{1,9},{9... | collective-permute-start | bytes 4718600 | tf_op jit(solution)/shard_map/ppermute | solution.py:106
  568.9 51.8 %collective-permute-start.13 = (bf16[256,3072]{0,1:T(8,128)(2,1)}, bf16[256,3072]{0,1:T(8,128)(2,1)}, u32[]{:S(2)}, u32[]{:S(2)}) collective-permute-start(bf16[256,3072]{0,1:T(8,128)(2,1)} %collective-permute-done.9), channel_id=1, source_target_pairs={{0,4},{8,0},{16,8},{24,16},{28,24},{20,28},{12,20},{4,12},{1,5},{9... | collective-permute-start | bytes 4718600 | tf_op jit(solution)/shard_map/ppermute | solution.py:108
  574.6 39.2 %collective-permute-start.11 = (f32[2,256,256]{1,2,0:T(8,128)S(1)}, f32[2,256,256]{1,2,0:T(8,128)}, u32[]{:S(2)}, u32[]{:S(2)}) collective-permute-start(f32[2,256,256]{1,2,0:T(8,128)S(1)} %pad_maximum_fusion), channel_id=1, source_target_pairs={{0,4},{8,0},{16,8},{24,16},{28,24},{20,28},{12,20},{4,12},{1,5},{9... | collective-permute-start | bytes 1572872 | tf_op jit(solution)/shard_map/ppermute | solution.py:130
  617.6 10.8 %collective-permute-start.10 = (f32[1,256,256]{1,2,0:T(8,128)S(1)}, f32[1,256,256]{1,2,0:T(8,128)S(1)}, u32[]{:S(2)}, u32[]{:S(2)}) collective-permute-start(f32[1,256,256]{1,2,0:T(8,128)S(1)} %bitcast.265), channel_id=1, source_target_pairs={{0,12},{8,4},{16,0},{24,8},{28,16},{20,24},{12,28},{4,20},{1,13},{... | collective-permute-start | bytes 786440 | tf_op jit(solution)/shard_map/ppermute | solution.py:130
  619.9 14.8 %collective-permute-start.12 = (f32[2,256,256]{2,1,0:T(8,128)}, f32[2,256,256]{2,1,0:T(8,128)S(1)}, u32[]{:S(2)}, u32[]{:S(2)}) collective-permute-start(f32[2,256,256]{2,1,0:T(8,128)} %pad_maximum_fusion.1), channel_id=1, source_target_pairs={{0,8},{8,16},{16,24},{24,28},{28,20},{20,12},{12,4},{4,0},{1,9},{9... | collective-permute-start | bytes 1572872 | tf_op jit(solution)/shard_map/ppermute | solution.py:130
  623.9 15.4 %collective-permute-start.14 = (f32[1,256,256]{2,1,0:T(8,128)}, f32[1,256,256]{2,1,0:T(8,128)}, u32[]{:S(2)}, u32[]{:S(2)}) collective-permute-start(f32[1,256,256]{2,1,0:T(8,128)} %convolution_bitcast_fusion), channel_id=1, source_target_pairs={{0,16},{8,24},{16,28},{24,20},{28,12},{20,4},{12,0},{4,8},{1,17},{... | collective-permute-start | bytes 786440 | tf_op jit(solution)/shard_map/ppermute | solution.py:130
  628.4 0.7 copy-start.11
  640.2 1.3 copy-start.3
Sparse Core Ops, SparseCore 0:
  641.7 32.3 reduce-scatter.1

commit v5 on v3

--- a/solution.py
+++ b/solution.py
@@ -60,13 +60,17 @@
         row_live = lanes[None, :] < block_size[:, None]
         col_live = lanes[None, None, :] < block_size[nu_list][:, :, None]
         slot_live = jnp.arange(knu, dtype=jnp.int32)[None, :] < nu_count[:, None]
-        mask = row_live[:, None, :, None] & col_live[:, :, None, :] & slot_live[:, :, None, None]
-        blocks = three_center[0].reshape(aux_dev, n_mu, knu, NB, NB)
-        masked = jnp.where(mask[None], blocks, jnp.zeros((), jnp.bfloat16))
+        keep = col_live & slot_live[:, :, None]
         picked = occupied.reshape(n_mu, NB, n_occ)[nu_list]
-        half = jnp.einsum(
-            "qmkab,mkbi->qmai", masked, picked, preferred_element_type=jnp.float32
-        ).astype(jnp.bfloat16)
+        picked = jnp.where(keep[..., None], picked, jnp.zeros((), jnp.bfloat16))
+        pair = 2
+        eye = jnp.eye(pair, dtype=jnp.bfloat16)
+        weight = jnp.einsum("xy,mkbi->mkxbyi", eye, picked).reshape(n_mu, knu, pair * NB, pair * n_occ)
+        tiles = NB // pair
+        tc = jnp.swapaxes(three_center[0], 1, 2).reshape(aux_dev, knu, n_mu, tiles, pair * NB)
+        half = jnp.einsum("qkmtl,mklc->qmtc", tc, weight, preferred_element_type=jnp.float32)
+        half = half.reshape(aux_dev, n_mu, NB, n_occ)
+        half = jnp.where(row_live[None, :, :, None], half, 0.0).astype(jnp.bfloat16)
         half = half.reshape(aux_dev, n_mu, NB * n_occ)
         regrouped = lax.all_to_all(half, "grp", split_axis=1, concat_axis=0, tiled=True)
         n_aux = regrouped.shape[0]

time: 302 us -> 288 us (0.954)
  local copies, waits for them, and re-layouts: 81.1 us -> 65.1 us
  other arithmetic: 4.81 us -> 13.4 us
  matrix products: 30.4 us -> 24.2 us
    another operation x1 -> x0, local copies, waits for them, and re-layouts: 34.4 us -> none  [body(): blocks = three_center[0].reshape(aux_dev, n_mu, knu, NB, NB)]
    unnamed x16 -> x17, local copies, waits for them, and re-layouts: 2.06 us -> 13.5 us
    transpose x0 -> x1, other arithmetic: none -> 10.2 us  [body(): jnp.einsum('xy,mkbi->mkxbyi', eye, picked)]
    dot_general x1, matrix products: 17 us -> 10.8 us  [body(): jnp.einsum('qkmtl,mklc->qmtc', tc, weight, preferred_element_type=jnp.flo...]
    reshape x2, local copies, waits for them, and re-layouts: 14.1 us -> 19.9 us  [the longest x1 15.7 us: body(): jnp.einsum('xy,mkbi->mkxbyi', eye, picked)]
where the time goes in v5:
time: 288 us; the launch traced here: 286 us
  waiting for transfers between devices  104 us (36%)
  local copies, waits for them, and re-layouts  65.1 us (23%)
  blocking collectives  44.1 us (15%)
  between operations  25.5 us (9%)
  matrix products  24.2 us (8%)
  other arithmetic  13.4 us (5%)
  starting transfers between devices  10.3 us (4%)
    ppermute x4, waiting for transfers between devices, body(): got = lax.ppermute(stack, 'grp', shifted(s))  47.9 us
    all_to_all x1, blocking collectives, body(): lax.all_to_all(half, 'grp', split_axis=1, concat_axis=0, tiled=True)  44.1 us
    reduce_scatter x1, waiting for transfers between devices, body(): return lax.psum_scatter(term, 'rep', scatter_dimension=0, tiled=True)  31.8 us
    ppermute x2, waiting for transfers between devices, body(): fwd = lax.ppermute(fwd, 'grp', shifted(1))  24.1 us
    reshape x1, local copies, waits for them, and re-layouts, body(): jnp.einsum('xy,mkbi->mkxbyi', eye, picked)  15.7 us
    unnamed x17, local copies, waits for them, and re-layouts  13.5 us
    reshape x2, local copies, waits for them, and re-layouts, body(): regrouped = regrouped.reshape(n_aux, mu_dev, NB, n_occ)  11.8 us
    dot_general x5, matrix products, prod(): return jnp.dot(held[xo], held[yo].T, preferred_element_type=jnp.float32)  10.8 us
  transfers between devices with their start and end apart: 9, of which 6 were waited for; matrix products, arithmetic and copies ran while one was open for 5% of the time, Pallas kernels for 0%

profile of v5, /device:TPU:0, one launch (start us, length us, event | category | flops | bytes accessed | tf_op | source)
XLA Modules:
  0.0 286.3 jit_solution(5779002835601970295)
XLA Ops:
  6.5 0.7 compare_select_fusion
  7.3 0.1 copy.21
  7.3 0.1 reshape.93
  7.5 1.3 reshape.85
  8.8 0.2 copy.22
  9.0 0.7 iota_compare_fusion.2
  9.7 1.6 gather_fusion
  11.2 0.0 copy-start.6
  11.3 1.0 gather_fusion.1
  12.3 0.1 reshape.92
  12.4 0.1 iota_compare_fusion.1
  12.5 0.1 fusion.10
  12.6 0.2 broadcast_select_fusion
  12.8 10.2 %multiply_bitcast_fusion = bf16[32,6,2,64,2,48]{3,2,5,4,1,0:T(2,128)(2,1)} fusion(bf16[2,2]{0,1:T(2,128)(2,1)S(1)} %compare_convert_fusion, bf16[32,6,64,48]{2,3,1,0:T(8,128)(2,1)S(1)} %broadcast_select_fusion), kind=kLoop, calls=%fused_computation.4 | loop fusion | flops 2359296 | bytes 5898248 | tf_op jit(solution)/shard_map/xy,mkbi->mkxbyi/transpose | solution.py:68
  23.0 15.7 %reshape.111 = bf16[32,6,128,96,1]{2,3,1,0,4:T(8,128)(2,1)} reshape(bf16[32,6,2,64,2,48]{3,2,5,4,1,0:T(2,128)(2,1)} %multiply_bitcast_fusion) | data formatting | bytes 9437184 | tf_op jit(solution)/shard_map/reshape | solution.py:68
  38.7 11.4 %copy.33 = bf16[192,8,32,128]{3,2,1,0:T(8,128)(2,1)} copy(bf16[192,8,32,128]{3,1,2,0:T(8,128)(2,1)} %bitcast.96) | data formatting | bytes 25165824
  50.2 10.8 %fusion.3 = bf16[8,32,32,96]{3,2,0,1:T(8,128)(2,1)} fusion(bf16[8,6,32,32,128]{4,3,2,1,0:T(8,128)(2,1)} %bitcast.97, bf16[32,6,128,96,1]{2,3,1,0,4:T(8,128)(2,1)} %reshape.111), kind=kOutput, calls=%fused_computation.9 | convolution fusion | flops 1207959552 | bytes 18874368 | tf_op jit(solution)/shard_map/qkmtl,mklc->qmtc/dot_general | solution.py:71
  60.9 4.2 %reshape.88 = bf16[8,32,3072]{2,0,1:T(8,128)(2,1)S(1)} reshape(bf16[8,32,32,96]{3,2,0,1:T(8,128)(2,1)} %fusion.3) | data formatting | bytes 3145728 | tf_op jit(solution)/shard_map/reshape | solution.py:72
  65.2 0.3 broadcast_in_dim.45
  65.5 0.8 broadcast_in_dim.46
  66.3 0.5 select_convert_fusion
  66.8 44.1 %all_to_all.15 = bf16[8,32,3072]{2,0,1:T(8,128)(2,1)S(1)} all-to-all(bf16[8,32,3072]{2,0,1:T(8,128)(2,1)S(1)} %select_convert_fusion), channel_id=1, replica_groups=mesh['grp'=8,'rep'=4] {'grp'}, dimensions={1} | all-to-all | bytes 3145728 | tf_op jit(solution)/shard_map/all_to_all | solution.py:75
  110.9 0.1 copy.24
  111.0 5.3 %reshape.89 = bf16[64,4,64,48]{3,2,0,1:T(8,128)(2,1)} reshape(bf16[8,8,4,3072]{3,1,0,2:T(8,128)(2,1)S(1)} %copy.24) | data formatting | bytes 3145728 | tf_op jit(solution)/shard_map/reshape | solution.py:78
  116.4 6.4 %copy.25 = bf16[64,4,64,48]{0,2,3,1:T(8,128)(2,1)S(1)} copy(bf16[64,4,64,48]{3,2,0,1:T(8,128)(2,1)} %reshape.89) | data formatting | bytes 3145728 | tf_op jit(solution)/shard_map/reshape | solution.py:78
  122.8 2.6 convert_bitcast_fusion
  125.4 6.3 %copy.26 = bf16[4,64,64,48]{1,0,3,2:T(4,128)(2,1)S(1)} copy(bf16[4,64,64,48]{2,1,3,0:T(8,128)(2,1)} %convert_bitcast_fusion) | data formatting | bytes 3145728 | tf_op jit(solution)/shard_map/convert_element_type | solution.py:81
  131.8 0.0 copy-start.7
  131.8 0.0 copy-start.5
  131.8 3.0 %reshape.90 = bf16[256,3072]{0,1:T(8,128)(2,1)} reshape(bf16[4,64,64,48]{1,0,3,2:T(4,128)(2,1)S(1)} %copy.26) | data formatting | bytes 3145728 | tf_op jit(solution)/shard_map/reshape | solution.py:83
  134.8 1.1 collective-permute-start
  135.9 0.9 collective-permute-start.2
  136.8 0.6 dynamic_slice.27
  144.0 0.7 fusion.12
  146.0 24.1 %collective-permute-done = bf16[256,3072]{0,1:T(8,128)(2,1)} collective-permute-done((bf16[256,3072]{0,1:T(8,128)(2,1)}, bf16[256,3072]{0,1:T(8,128)(2,1)}, u32[]{:S(2)}, u32[]{:S(2)}) %collective-permute-start) | collective-permute-done | bytes 1572896 | tf_op jit(solution)/shard_map/ppermute | solution.py:96
  170.1 0.8 collective-permute-start.1
  170.9 0.1 broadcast_in_dim.44
  171.0 0.6 convolution_dynamic-update-slice_fusion
  171.6 0.0 collective-permute-done.2
  171.7 1.3 collective-permute-start.6
  173.0 2.0 constant_dynamic-update-slice_fusion.3
  175.0 2.5 fusion.14
  177.5 1.5 collective-permute-start.4
  183.0 33.9 %collective-permute-done.4 = f32[2,256,256]{1,2,0:T(8,128)} collective-permute-done((f32[2,256,256]{1,2,0:T(8,128)S(1)}, f32[2,256,256]{1,2,0:T(8,128)}, u32[]{:S(2)}, u32[]{:S(2)}) %collective-permute-start.4) | collective-permute-done | bytes 524320 | tf_op jit(solution)/shard_map/ppermute | solution.py:120
  216.8 1.1 slice_bitcast_fusion.2
  217.9 0.1 copy.28
  218.0 0.1 copy.29
  218.2 0.0 collective-permute-done.1
  218.2 2.5 fusion.13
  220.7 2.5 collective-permute-start.3
  223.1 0.8 pad_maximum_fusion.1
  223.9 0.6 collective-permute-start.5
  224.5 0.0 collective-permute-done.6
  224.5 3.2 %convolution_bitcast_fusion = f32[1,256,256]{2,1,0:T(8,128)} fusion(bf16[256,3072]{0,1:T(8,128)(2,1)} %collective-permute-done.1, bf16[256,3072]{0,1:T(8,128)(2,1)} %collective-permute-done.6), kind=kOutput, calls=%fused_computation.11 | convolution fusion | flops 402653184 | bytes 3407872 | tf_op jit(solution)/shard_map/dot_general | solution.py:102
  227.7 1.7 collective-permute-start.7
  229.4 3.7 %collective-permute-done.3 = f32[1,256,256]{1,2,0:T(8,128)S(1)} collective-permute-done((f32[1,256,256]{1,2,0:T(8,128)S(1)}, f32[1,256,256]{1,2,0:T(8,128)S(1)}, u32[]{:S(2)}, u32[]{:S(2)}) %collective-permute-start.3) | collective-permute-done | bytes 262176 | tf_op jit(solution)/shard_map/ppermute | solution.py:120
  233.1 0.7 copy-done.4
  233.8 1.1 copy.27
  235.0 4.6 %collective-permute-done.5 = f32[2,256,256]{2,1,0:T(8,128)S(1)} collective-permute-done((f32[2,256,256]{2,1,0:T(8,128)}, f32[2,256,256]{2,1,0:T(8,128)S(1)}, u32[]{:S(2)}, u32[]{:S(2)}) %collective-permute-start.5) | collective-permute-done | bytes 524320 | tf_op jit(solution)/shard_map/ppermute | solution.py:120
  239.6 5.8 %collective-permute-done.7 = f32[1,256,256]{2,1,0:T(8,128)} collective-permute-done((f32[1,256,256]{2,1,0:T(8,128)}, f32[1,256,256]{2,1,0:T(8,128)}, u32[]{:S(2)}, u32[]{:S(2)}) %collective-permute-start.7) | collective-permute-done | bytes 262176 | tf_op jit(solution)/shard_map/ppermute | solution.py:120
  245.4 1.0 bitcast_dynamic-update-slice_fusion
  246.4 1.3 copy-done.2
  247.7 0.0 reduce-scatter.2.cloned.1.call-update
  247.7 31.8 %reduce-scatter.2.cloned.1.call-done = f32[512,256]{1,0:T(8,128)} async-done(((f32[2048,256]{1,0:T(8,128)}), f32[512,256]{1,0:T(8,128)}) %reduce-scatter.2.cloned.1.call-update) | async-done | bytes 524304 | tf_op jit(solution)/shard_map/reduce_scatter | solution.py:125
  (20 shorter events, 0.2 us)
Async XLA Ops:
  6.5 116.3 %copy-start = (bf16[1,64,64]{2,1,0:T(8,128)(2,1)S(1)}, bf16[1,64,64]{2,1,0:T(8,128)(2,1)}, u32[]{:S(2)}) copy-start(bf16[1,64,64]{2,1,0:T(8,128)(2,1)} %param.9) | copy-start | bytes 24580
  6.5 3.2 %copy-start.1 = (s32[32]{0:T(128)S(1)}, s32[32]{0:T(128)}, u32[]{:S(2)}) copy-start(s32[32]{0:T(128)} %param.13) | copy-start | bytes 388
  6.5 272.9 %reduce-scatter.2.cloned.1.call-start = ((), (), s32[]{:S(2)}) async-start(), calls=%async_computation.2 | async-start | bytes 2621440 | tf_op jit(solution)/shard_map/reduce_scatter | solution.py:125
  11.2 1.1 copy-start.6
  131.8 5.1 %copy-start.7 = (s32[8]{0:T(128)S(1)}, s32[8]{0:T(128)}, u32[]{:S(2)}) copy-start(s32[8]{0:T(128)} %constant.86.clone) | copy-start | bytes 100
  131.8 12.2 %copy-start.5 = (s32[8]{0:T(128)S(1)}, s32[8]{0:T(128)}, u32[]{:S(2)}) copy-start(s32[8]{0:T(128)} %constant.87.clone) | copy-start | bytes 100
  134.8 35.3 %collective-permute-start = (bf16[256,3072]{0,1:T(8,128)(2,1)}, bf16[256,3072]{0,1:T(8,128)(2,1)}, u32[]{:S(2)}, u32[]{:S(2)}) collective-permute-start(bf16[256,3072]{0,1:T(8,128)(2,1)} %reshape.90), channel_id=1, source_target_pairs={{0,8},{8,16},{16,24},{24,28},{28,20},{20,12},{12,4},{4,0},{1,9},{9... | collective-permute-start | bytes 4718600 | tf_op jit(solution)/shard_map/ppermute | solution.py:96
  135.9 35.7 %collective-permute-start.2 = (bf16[256,3072]{0,1:T(8,128)(2,1)}, bf16[256,3072]{0,1:T(8,128)(2,1)}, u32[]{:S(2)}, u32[]{:S(2)}) collective-permute-start(bf16[256,3072]{0,1:T(8,128)(2,1)} %reshape.90), channel_id=1, source_target_pairs={{0,4},{8,0},{16,8},{24,16},{28,24},{20,28},{12,20},{4,12},{1,5},{9... | collective-permute-start | bytes 4718600 | tf_op jit(solution)/shard_map/ppermute | solution.py:98
  146.0 25.0 %copy-start.3 = (bf16[256,3072]{0,1:T(8,128)(2,1)S(1)}, bf16[256,3072]{0,1:T(8,128)(2,1)}, u32[]{:S(2)}) copy-start(bf16[256,3072]{0,1:T(8,128)(2,1)} %reshape.90) | copy-start | bytes 4718596
  170.1 48.0 %collective-permute-start.1 = (bf16[256,3072]{0,1:T(8,128)(2,1)}, bf16[256,3072]{0,1:T(8,128)(2,1)}, u32[]{:S(2)}, u32[]{:S(2)}) collective-permute-start(bf16[256,3072]{0,1:T(8,128)(2,1)} %collective-permute-done), channel_id=1, source_target_pairs={{0,8},{8,16},{16,24},{24,28},{28,20},{20,12},{12,4},{4,0},{1,9},{9... | collective-permute-start | bytes 4718600 | tf_op jit(solution)/shard_map/ppermute | solution.py:96
  171.7 52.9 %collective-permute-start.6 = (bf16[256,3072]{0,1:T(8,128)(2,1)}, bf16[256,3072]{0,1:T(8,128)(2,1)}, u32[]{:S(2)}, u32[]{:S(2)}) collective-permute-start(bf16[256,3072]{0,1:T(8,128)(2,1)} %collective-permute-done.2), channel_id=1, source_target_pairs={{0,4},{8,0},{16,8},{24,16},{28,24},{20,28},{12,20},{4,12},{1,5},{9... | collective-permute-start | bytes 4718600 | tf_op jit(solution)/shard_map/ppermute | solution.py:98
  177.5 39.3 %collective-permute-start.4 = (f32[2,256,256]{1,2,0:T(8,128)S(1)}, f32[2,256,256]{1,2,0:T(8,128)}, u32[]{:S(2)}, u32[]{:S(2)}) collective-permute-start(f32[2,256,256]{1,2,0:T(8,128)S(1)} %pad_maximum_fusion), channel_id=1, source_target_pairs={{0,4},{8,0},{16,8},{24,16},{28,24},{20,28},{12,20},{4,12},{1,5},{9... | collective-permute-start | bytes 1572872 | tf_op jit(solution)/shard_map/ppermute | solution.py:120
  220.7 12.4 %collective-permute-start.3 = (f32[1,256,256]{1,2,0:T(8,128)S(1)}, f32[1,256,256]{1,2,0:T(8,128)S(1)}, u32[]{:S(2)}, u32[]{:S(2)}) collective-permute-start(f32[1,256,256]{1,2,0:T(8,128)S(1)} %bitcast.102), channel_id=1, source_target_pairs={{0,12},{8,4},{16,0},{24,8},{28,16},{20,24},{12,28},{4,20},{1,13},{... | collective-permute-start | bytes 786440 | tf_op jit(solution)/shard_map/ppermute | solution.py:120
  223.9 15.6 %collective-permute-start.5 = (f32[2,256,256]{2,1,0:T(8,128)}, f32[2,256,256]{2,1,0:T(8,128)S(1)}, u32[]{:S(2)}, u32[]{:S(2)}) collective-permute-start(f32[2,256,256]{2,1,0:T(8,128)} %pad_maximum_fusion.1), channel_id=1, source_target_pairs={{0,8},{8,16},{16,24},{24,28},{28,20},{20,12},{12,4},{4,0},{1,9},{9... | collective-permute-start | bytes 1572872 | tf_op jit(solution)/shard_map/ppermute | solution.py:120
  227.7 17.7 %collective-permute-start.7 = (f32[1,256,256]{2,1,0:T(8,128)}, f32[1,256,256]{2,1,0:T(8,128)}, u32[]{:S(2)}, u32[]{:S(2)}) collective-permute-start(f32[1,256,256]{2,1,0:T(8,128)} %convolution_bitcast_fusion), channel_id=1, source_target_pairs={{0,16},{8,24},{16,28},{24,20},{28,12},{20,4},{12,0},{4,8},{1,17},{... | collective-permute-start | bytes 786440 | tf_op jit(solution)/shard_map/ppermute | solution.py:120
  233.1 0.7 copy-start.4
  246.3 1.3 copy-start.2
Sparse Core Ops, SparseCore 0:
  247.8 31.6 reduce-scatter.1

commit v6 on v5

--- a/solution.py
+++ b/solution.py
@@ -64,8 +64,10 @@
         picked = occupied.reshape(n_mu, NB, n_occ)[nu_list]
         picked = jnp.where(keep[..., None], picked, jnp.zeros((), jnp.bfloat16))
         pair = 2
-        eye = jnp.eye(pair, dtype=jnp.bfloat16)
-        weight = jnp.einsum("xy,mkbi->mkxbyi", eye, picked).reshape(n_mu, knu, pair * NB, pair * n_occ)
+        blank = jnp.zeros_like(picked)
+        weight = jnp.concatenate(
+            [jnp.concatenate([picked, blank], axis=-1), jnp.concatenate([blank, picked], axis=-1)], axis=-2
+        )
         tiles = NB // pair
         tc = jnp.swapaxes(three_center[0], 1, 2).reshape(aux_dev, knu, n_mu, tiles, pair * NB)
         half = jnp.einsum("qkmtl,mklc->qmtc", tc, weight, preferred_element_type=jnp.float32)

time: 288 us -> 255 us (0.89)
  local copies, waits for them, and re-layouts: 65.1 us -> 45.3 us
  other arithmetic: 13.4 us -> 4.69 us
  matrix products: 24.2 us -> 20.5 us
    reshape x1 -> x0, local copies, waits for them, and re-layouts: 15.7 us -> none  [body(): jnp.einsum('xy,mkbi->mkxbyi', eye, picked)]
    transpose x1 -> x0, other arithmetic: 10.2 us -> none  [body(): jnp.einsum('xy,mkbi->mkxbyi', eye, picked)]
    unnamed x17, local copies, waits for them, and re-layouts: 13.5 us -> 9.42 us
    dot_general x1, matrix products: 10.8 us -> 7.1 us  [body(): jnp.einsum('qkmtl,mklc->qmtc', tc, weight, preferred_element_type=jnp.flo...]
  transfers between devices with their start and end apart: 9 -> 9, of which waited for: 6 -> 6; matrix products, arithmetic and copies ran while one was open for 5% -> 6% of each run, Pallas kernels for 0% -> 0%
where the time goes in v6:
time: 255 us; the launch traced here: 254 us
  waiting for transfers between devices  104 us (41%)
  local copies, waits for them, and re-layouts  45.3 us (18%)
  blocking collectives  44.1 us (17%)
  between operations  25.5 us (10%)
  matrix products  20.5 us (8%)
  starting transfers between devices  10.3 us (4%)
  other arithmetic  4.69 us (2%)
    ppermute x4, waiting for transfers between devices, body(): got = lax.ppermute(stack, 'grp', shifted(s))  47.9 us
    all_to_all x1, blocking collectives, body(): lax.all_to_all(half, 'grp', split_axis=1, concat_axis=0, tiled=True)  44.1 us
    reduce_scatter x1, waiting for transfers between devices, body(): return lax.psum_scatter(term, 'rep', scatter_dimension=0, tiled=True)  32.1 us
    ppermute x2, waiting for transfers between devices, body(): fwd = lax.ppermute(fwd, 'grp', shifted(1))  24.1 us
    reshape x2, local copies, waits for them, and re-layouts, body(): regrouped = regrouped.reshape(n_aux, mu_dev, NB, n_occ)  11.8 us
    dot_general x5, matrix products, prod(): return jnp.dot(held[xo], held[yo].T, preferred_element_type=jnp.float32)  10.8 us
    unnamed x17, local copies, waits for them, and re-layouts  9.42 us
    dot_general x1, matrix products, body(): jnp.einsum('qkmtl,mklc->qmtc', tc, weight, preferred_element_type=jnp.flo...  7.1 us
  transfers between devices with their start and end apart: 9, of which 6 were waited for; matrix products, arithmetic and copies ran while one was open for 6% of the time, Pallas kernels for 0%

profile of v6, /device:TPU:0, one launch (start us, length us, event | category | flops | bytes accessed | tf_op | source)
XLA Modules:
  0.0 254.4 jit_solution(10654440663715845184)
XLA Ops:
  6.5 0.0 reduce-scatter.2.cloned.1.call-start
  6.5 0.7 compare_select_fusion
  7.3 0.1 copy.20
  7.3 0.1 reshape.89
  7.5 1.3 reshape.82
  8.8 0.2 copy.21
  9.0 0.7 iota_compare_fusion.4
  9.7 1.6 gather_fusion
  11.2 0.0 copy-start.6
  11.3 1.0 gather_fusion.1
  12.3 0.1 reshape.88
  12.4 0.1 iota_compare_fusion.3
  12.5 7.4 %copy.32 = bf16[192,8,32,128]{3,2,1,0:T(8,128)(2,1)S(1)} copy(bf16[192,8,32,128]{3,1,2,0:T(8,128)(2,1)} %bitcast.94) | data formatting | bytes 25165824
  19.8 0.1 fusion.19
  20.0 1.7 broadcast_select_fusion
  21.6 7.1 %fusion.12 = bf16[8,32,32,96]{3,2,0,1:T(8,128)(2,1)} fusion(bf16[8,6,32,32,128]{4,3,2,1,0:T(8,128)(2,1)S(1)} %bitcast.95, bf16[32,6,64,48]{2,3,1,0:T(8,128)(2,1)} %broadcast_select_fusion), kind=kOutput, calls=%fused_computation.17 | convolution fusion | flops 1226833920 | bytes 15335424 | tf_op jit(solution)/shard_map/qkmtl,mklc->qmtc/dot_general | solution.py:73
  28.7 4.2 %reshape.84 = bf16[8,32,3072]{2,0,1:T(8,128)(2,1)S(1)} reshape(bf16[8,32,32,96]{3,2,0,1:T(8,128)(2,1)} %fusion.12) | data formatting | bytes 3145728 | tf_op jit(solution)/shard_map/reshape | solution.py:74
  33.0 0.3 broadcast_in_dim.46
  33.3 0.8 broadcast_in_dim.47
  34.1 0.5 select_convert_fusion
  34.6 44.1 %all_to_all.15 = bf16[8,32,3072]{2,0,1:T(8,128)(2,1)S(1)} all-to-all(bf16[8,32,3072]{2,0,1:T(8,128)(2,1)S(1)} %select_convert_fusion), channel_id=1, replica_groups=mesh['grp'=8,'rep'=4] {'grp'}, dimensions={1} | all-to-all | bytes 3145728 | tf_op jit(solution)/shard_map/all_to_all | solution.py:77
  78.7 0.1 copy.23
  78.8 5.3 %reshape.85 = bf16[64,4,64,48]{3,2,0,1:T(8,128)(2,1)} reshape(bf16[8,8,4,3072]{3,1,0,2:T(8,128)(2,1)S(1)} %copy.23) | data formatting | bytes 3145728 | tf_op jit(solution)/shard_map/reshape | solution.py:80
  84.1 6.4 %copy.24 = bf16[64,4,64,48]{0,2,3,1:T(8,128)(2,1)S(1)} copy(bf16[64,4,64,48]{3,2,0,1:T(8,128)(2,1)} %reshape.85) | data formatting | bytes 3145728 | tf_op jit(solution)/shard_map/reshape | solution.py:80
  90.6 2.6 %convert_bitcast_fusion = bf16[4,64,64,48]{2,1,3,0:T(8,128)(2,1)} fusion(bf16[64,4,64,48]{0,2,3,1:T(8,128)(2,1)S(1)} %copy.24, bf16[1,64,64]{2,1,0:T(8,128)(2,1)S(1)} %copy-done), kind=kOutput, calls=%fused_computation.13 | convolution fusion | flops 101449728 | bytes 3153920 | tf_op jit(solution)/shard_map/pq,qmai->mapi/dot_general | solution.py:81
  93.2 6.3 %copy.25 = bf16[4,64,64,48]{1,0,3,2:T(4,128)(2,1)S(1)} copy(bf16[4,64,64,48]{2,1,3,0:T(8,128)(2,1)} %convert_bitcast_fusion) | data formatting | bytes 3145728 | tf_op jit(solution)/shard_map/convert_element_type | solution.py:83
  99.6 0.0 copy-start.7
  99.6 0.0 copy-start.5
  99.6 3.0 %reshape.86 = bf16[256,3072]{0,1:T(8,128)(2,1)} reshape(bf16[4,64,64,48]{1,0,3,2:T(4,128)(2,1)S(1)} %copy.25) | data formatting | bytes 3145728 | tf_op jit(solution)/shard_map/reshape | solution.py:85
  102.6 1.1 collective-permute-start
  103.7 0.9 collective-permute-start.2
  104.6 0.6 dynamic_slice.27
  111.8 0.0 copy-done.5
  111.8 0.7 fusion.24
  113.8 24.1 %collective-permute-done = bf16[256,3072]{0,1:T(8,128)(2,1)} collective-permute-done((bf16[256,3072]{0,1:T(8,128)(2,1)}, bf16[256,3072]{0,1:T(8,128)(2,1)}, u32[]{:S(2)}, u32[]{:S(2)}) %collective-permute-start) | collective-permute-done | bytes 1572896 | tf_op jit(solution)/shard_map/ppermute | solution.py:98
  137.9 0.8 collective-permute-start.1
  138.7 0.1 broadcast_in_dim.45
  138.8 0.6 convolution_dynamic-update-slice_fusion
  139.4 0.0 collective-permute-done.2
  139.4 1.3 collective-permute-start.6
  140.8 2.0 constant_dynamic-update-slice_fusion.3
  142.8 2.5 fusion.26
  145.3 1.5 collective-permute-start.4
  150.7 33.9 %collective-permute-done.4 = f32[2,256,256]{1,2,0:T(8,128)} collective-permute-done((f32[2,256,256]{1,2,0:T(8,128)S(1)}, f32[2,256,256]{1,2,0:T(8,128)}, u32[]{:S(2)}, u32[]{:S(2)}) %collective-permute-start.4) | collective-permute-done | bytes 524320 | tf_op jit(solution)/shard_map/ppermute | solution.py:122
  184.6 1.1 slice_bitcast_fusion.2
  185.7 0.1 copy.27
  185.8 0.1 copy.28
  185.9 0.0 collective-permute-done.1
  186.0 2.5 fusion.25
  188.4 2.5 collective-permute-start.3
  190.9 0.8 pad_maximum_fusion.1
  191.7 0.6 collective-permute-start.5
  192.3 0.0 collective-permute-done.6
  192.3 3.2 %convolution_bitcast_fusion = f32[1,256,256]{2,1,0:T(8,128)} fusion(bf16[256,3072]{0,1:T(8,128)(2,1)} %collective-permute-done.1, bf16[256,3072]{0,1:T(8,128)(2,1)} %collective-permute-done.6), kind=kOutput, calls=%fused_computation.19 | convolution fusion | flops 402653184 | bytes 3407872 | tf_op jit(solution)/shard_map/dot_general | solution.py:104
  195.5 1.7 collective-permute-start.7
  197.2 3.7 %collective-permute-done.3 = f32[1,256,256]{1,2,0:T(8,128)S(1)} collective-permute-done((f32[1,256,256]{1,2,0:T(8,128)S(1)}, f32[1,256,256]{1,2,0:T(8,128)S(1)}, u32[]{:S(2)}, u32[]{:S(2)}) %collective-permute-start.3) | collective-permute-done | bytes 262176 | tf_op jit(solution)/shard_map/ppermute | solution.py:122
  200.9 0.7 copy-done.4
  201.6 1.1 copy.26
  202.8 4.6 %collective-permute-done.5 = f32[2,256,256]{2,1,0:T(8,128)S(1)} collective-permute-done((f32[2,256,256]{2,1,0:T(8,128)}, f32[2,256,256]{2,1,0:T(8,128)S(1)}, u32[]{:S(2)}, u32[]{:S(2)}) %collective-permute-start.5) | collective-permute-done | bytes 524320 | tf_op jit(solution)/shard_map/ppermute | solution.py:122
  207.4 5.8 %collective-permute-done.7 = f32[1,256,256]{2,1,0:T(8,128)} collective-permute-done((f32[1,256,256]{2,1,0:T(8,128)}, f32[1,256,256]{2,1,0:T(8,128)}, u32[]{:S(2)}, u32[]{:S(2)}) %collective-permute-start.7) | collective-permute-done | bytes 262176 | tf_op jit(solution)/shard_map/ppermute | solution.py:122
  213.2 1.0 bitcast_dynamic-update-slice_fusion
  214.1 1.3 copy-done.2
  215.5 0.0 reduce-scatter.2.cloned.1.call-update
  215.5 32.1 %reduce-scatter.2.cloned.1.call-done = f32[512,256]{1,0:T(8,128)} async-done(((f32[2048,256]{1,0:T(8,128)}), f32[512,256]{1,0:T(8,128)}) %reduce-scatter.2.cloned.1.call-update) | async-done | bytes 524304 | tf_op jit(solution)/shard_map/reduce_scatter | solution.py:127
  (17 shorter events, 0.2 us)
Async XLA Ops:
  6.5 84.0 %copy-start = (bf16[1,64,64]{2,1,0:T(8,128)(2,1)S(1)}, bf16[1,64,64]{2,1,0:T(8,128)(2,1)}, u32[]{:S(2)}) copy-start(bf16[1,64,64]{2,1,0:T(8,128)(2,1)} %param.9) | copy-start | bytes 24580
  6.5 3.2 %copy-start.1 = (s32[32]{0:T(128)S(1)}, s32[32]{0:T(128)}, u32[]{:S(2)}) copy-start(s32[32]{0:T(128)} %param.13) | copy-start | bytes 388
  6.5 241.0 %reduce-scatter.2.cloned.1.call-start = ((), (), s32[]{:S(2)}) async-start(), calls=%async_computation.2 | async-start | bytes 2621440 | tf_op jit(solution)/shard_map/reduce_scatter | solution.py:127
  11.2 1.1 copy-start.6
  99.6 5.1 %copy-start.7 = (s32[8]{0:T(128)S(1)}, s32[8]{0:T(128)}, u32[]{:S(2)}) copy-start(s32[8]{0:T(128)} %constant.87.clone) | copy-start | bytes 100
  99.6 12.2 %copy-start.5 = (s32[8]{0:T(128)S(1)}, s32[8]{0:T(128)}, u32[]{:S(2)}) copy-start(s32[8]{0:T(128)} %constant.88.clone) | copy-start | bytes 100
  102.6 35.3 %collective-permute-start = (bf16[256,3072]{0,1:T(8,128)(2,1)}, bf16[256,3072]{0,1:T(8,128)(2,1)}, u32[]{:S(2)}, u32[]{:S(2)}) collective-permute-start(bf16[256,3072]{0,1:T(8,128)(2,1)} %reshape.86), channel_id=1, source_target_pairs={{0,8},{8,16},{16,24},{24,28},{28,20},{20,12},{12,4},{4,0},{1,9},{9... | collective-permute-start | bytes 4718600 | tf_op jit(solution)/shard_map/ppermute | solution.py:98
  103.7 35.7 %collective-permute-start.2 = (bf16[256,3072]{0,1:T(8,128)(2,1)}, bf16[256,3072]{0,1:T(8,128)(2,1)}, u32[]{:S(2)}, u32[]{:S(2)}) collective-permute-start(bf16[256,3072]{0,1:T(8,128)(2,1)} %reshape.86), channel_id=1, source_target_pairs={{0,4},{8,0},{16,8},{24,16},{28,24},{20,28},{12,20},{4,12},{1,5},{9... | collective-permute-start | bytes 4718600 | tf_op jit(solution)/shard_map/ppermute | solution.py:100
  113.8 25.0 %copy-start.3 = (bf16[256,3072]{0,1:T(8,128)(2,1)S(1)}, bf16[256,3072]{0,1:T(8,128)(2,1)}, u32[]{:S(2)}) copy-start(bf16[256,3072]{0,1:T(8,128)(2,1)} %reshape.86) | copy-start | bytes 4718596
  137.9 48.0 %collective-permute-start.1 = (bf16[256,3072]{0,1:T(8,128)(2,1)}, bf16[256,3072]{0,1:T(8,128)(2,1)}, u32[]{:S(2)}, u32[]{:S(2)}) collective-permute-start(bf16[256,3072]{0,1:T(8,128)(2,1)} %collective-permute-done), channel_id=1, source_target_pairs={{0,8},{8,16},{16,24},{24,28},{28,20},{20,12},{12,4},{4,0},{1,9},{9... | collective-permute-start | bytes 4718600 | tf_op jit(solution)/shard_map/ppermute | solution.py:98
  139.4 52.9 %collective-permute-start.6 = (bf16[256,3072]{0,1:T(8,128)(2,1)}, bf16[256,3072]{0,1:T(8,128)(2,1)}, u32[]{:S(2)}, u32[]{:S(2)}) collective-permute-start(bf16[256,3072]{0,1:T(8,128)(2,1)} %collective-permute-done.2), channel_id=1, source_target_pairs={{0,4},{8,0},{16,8},{24,16},{28,24},{20,28},{12,20},{4,12},{1,5},{9... | collective-permute-start | bytes 4718600 | tf_op jit(solution)/shard_map/ppermute | solution.py:100
  145.3 39.3 %collective-permute-start.4 = (f32[2,256,256]{1,2,0:T(8,128)S(1)}, f32[2,256,256]{1,2,0:T(8,128)}, u32[]{:S(2)}, u32[]{:S(2)}) collective-permute-start(f32[2,256,256]{1,2,0:T(8,128)S(1)} %pad_maximum_fusion), channel_id=1, source_target_pairs={{0,4},{8,0},{16,8},{24,16},{28,24},{20,28},{12,20},{4,12},{1,5},{9... | collective-permute-start | bytes 1572872 | tf_op jit(solution)/shard_map/ppermute | solution.py:122
  188.4 12.4 %collective-permute-start.3 = (f32[1,256,256]{1,2,0:T(8,128)S(1)}, f32[1,256,256]{1,2,0:T(8,128)S(1)}, u32[]{:S(2)}, u32[]{:S(2)}) collective-permute-start(f32[1,256,256]{1,2,0:T(8,128)S(1)} %bitcast.100), channel_id=1, source_target_pairs={{0,12},{8,4},{16,0},{24,8},{28,16},{20,24},{12,28},{4,20},{1,13},{... | collective-permute-start | bytes 786440 | tf_op jit(solution)/shard_map/ppermute | solution.py:122
  191.7 15.6 %collective-permute-start.5 = (f32[2,256,256]{2,1,0:T(8,128)}, f32[2,256,256]{2,1,0:T(8,128)S(1)}, u32[]{:S(2)}, u32[]{:S(2)}) collective-permute-start(f32[2,256,256]{2,1,0:T(8,128)} %pad_maximum_fusion.1), channel_id=1, source_target_pairs={{0,8},{8,16},{16,24},{24,28},{28,20},{20,12},{12,4},{4,0},{1,9},{9... | collective-permute-start | bytes 1572872 | tf_op jit(solution)/shard_map/ppermute | solution.py:122
  195.5 17.7 %collective-permute-start.7 = (f32[1,256,256]{2,1,0:T(8,128)}, f32[1,256,256]{2,1,0:T(8,128)}, u32[]{:S(2)}, u32[]{:S(2)}) collective-permute-start(f32[1,256,256]{2,1,0:T(8,128)} %convolution_bitcast_fusion), channel_id=1, source_target_pairs={{0,16},{8,24},{16,28},{24,20},{28,12},{20,4},{12,0},{4,8},{1,17},{... | collective-permute-start | bytes 786440 | tf_op jit(solution)/shard_map/ppermute | solution.py:122
  200.9 0.7 copy-start.4
  214.1 1.3 copy-start.2
Sparse Core Ops, SparseCore 0:
  215.6 31.8 reduce-scatter.1

commit v7 on v6

--- a/solution.py
+++ b/solution.py
@@ -40,6 +40,24 @@
     if len(where) != n:
         return list(range(n))
     return [where[p] for p in snake(len(avals), len(bvals))]
+
+
+def scatter_sum(term):
+    n_rep = lax.axis_size("rep")
+    if n_rep & (n_rep - 1):
+        return lax.psum_scatter(term, "rep", scatter_dimension=0, tiled=True)
+    me = lax.axis_index("rep")
+    per = term.shape[0] // n_rep
+    buf = term
+    d = n_rep // 2
+    while d >= 1:
+        upper = (me // d) % 2
+        keep = lax.dynamic_slice_in_dim(buf, upper * d * per, d * per, axis=0)
+        send = lax.dynamic_slice_in_dim(buf, (1 - upper) * d * per, d * per, axis=0)
+        got = lax.ppermute(send, "rep", [(i, i ^ d) for i in range(n_rep)])
+        buf = keep + got
+        d //= 2
+    return buf
 
 
 def make_body(ring):
@@ -124,7 +142,7 @@
         term = jnp.zeros((n * rows, rows), jnp.float32)
         for off, blk in placed:
             term = lax.dynamic_update_slice_in_dim(term, blk, start_of(off), axis=0)
-        return lax.psum_scatter(term, "rep", scatter_dimension=0, tiled=True)
+        return scatter_sum(term)
 
     return body
 

time: 255 us -> 233 us (0.914)
  between operations: 25.5 us -> 12.1 us
  waiting for transfers between devices: 104 us -> 92.6 us
    reduce_scatter x1 -> x0, waiting for transfers between devices: 32.1 us -> none  [body(): return lax.psum_scatter(term, 'rep', scatter_dimension=0, tiled=True)]
    ppermute x0 -> x2, waiting for transfers between devices: none -> 20.6 us  [scatter_sum(): got = lax.ppermute(send, 'rep', [(i, i ^ d) for i in range(n_rep)])]
    unnamed x17 -> x15, local copies, waits for them, and re-layouts: 9.42 us -> 8.08 us
  transfers between devices with their start and end apart: 9 -> 10, of which waited for: 6 -> 7; matrix products, arithmetic and copies ran while one was open for 6% -> 7% of each run, Pallas kernels for 0% -> 0%
where the time goes in v7:
time: 233 us; the launch traced here: 232 us
  waiting for transfers between devices  92.6 us (40%)
  blocking collectives  44.1 us (19%)
  local copies, waits for them, and re-layouts  44 us (19%)
  matrix products  20.5 us (9%)
  between operations  12.1 us (5%)
  starting transfers between devices  12 us (5%)
  other arithmetic  6.91 us (3%)
    ppermute x4, waiting for transfers between devices, body(): got = lax.ppermute(stack, 'grp', shifted(s))  47.9 us
    all_to_all x1, blocking collectives, body(): lax.all_to_all(half, 'grp', split_axis=1, concat_axis=0, tiled=True)  44.1 us
    ppermute x2, waiting for transfers between devices, body(): fwd = lax.ppermute(fwd, 'grp', shifted(1))  24.1 us
    ppermute x2, waiting for transfers between devices, scatter_sum(): got = lax.ppermute(send, 'rep', [(i, i ^ d) for i in range(n_rep)])  20.6 us
    reshape x2, local copies, waits for them, and re-layouts, body(): regrouped = regrouped.reshape(n_aux, mu_dev, NB, n_occ)  11.8 us
    dot_general x5, matrix products, prod(): return jnp.dot(held[xo], held[yo].T, preferred_element_type=jnp.float32)  10.8 us
    unnamed x15, local copies, waits for them, and re-layouts  8.08 us
    dot_general x1, matrix products, body(): jnp.einsum('qkmtl,mklc->qmtc', tc, weight, preferred_element_type=jnp.flo...  7.1 us
  transfers between devices with their start and end apart: 10, of which 7 were waited for; matrix products, arithmetic and copies ran while one was open for 7% of the time, Pallas kernels for 0%

profile of v7, /device:TPU:0, one launch (start us, length us, event | category | flops | bytes accessed | tf_op | source)
XLA Modules:
  0.0 232.2 jit_solution(4725600632203180780)
XLA Ops:
  0.0 0.7 compare_select_fusion
  0.7 0.1 copy.20
  0.8 0.1 reshape.89
  0.9 1.3 reshape.82
  2.3 0.2 copy.21
  2.4 0.7 iota_compare_fusion.4
  3.2 1.6 gather_fusion
  4.7 0.0 copy-start.5
  4.7 1.0 gather_fusion.1
  5.8 0.1 reshape.88
  5.9 0.1 iota_compare_fusion.3
  5.9 7.4 %copy.32 = bf16[192,8,32,128]{3,2,1,0:T(8,128)(2,1)S(1)} copy(bf16[192,8,32,128]{3,1,2,0:T(8,128)(2,1)} %bitcast.94) | data formatting | bytes 25165824
  13.3 0.1 fusion.19
  13.4 1.7 broadcast_select_fusion
  15.1 7.1 %fusion.12 = bf16[8,32,32,96]{3,2,0,1:T(8,128)(2,1)} fusion(bf16[8,6,32,32,128]{4,3,2,1,0:T(8,128)(2,1)S(1)} %bitcast.95, bf16[32,6,64,48]{2,3,1,0:T(8,128)(2,1)} %broadcast_select_fusion), kind=kOutput, calls=%fused_computation.17 | convolution fusion | flops 1226833920 | bytes 15335424 | tf_op jit(solution)/shard_map/qkmtl,mklc->qmtc/dot_general | solution.py:91
  22.2 4.2 %reshape.84 = bf16[8,32,3072]{2,0,1:T(8,128)(2,1)S(1)} reshape(bf16[8,32,32,96]{3,2,0,1:T(8,128)(2,1)} %fusion.12) | data formatting | bytes 3145728 | tf_op jit(solution)/shard_map/reshape | solution.py:92
  26.4 0.3 broadcast_in_dim.46
  26.8 0.8 broadcast_in_dim.47
  27.6 0.5 select_convert_fusion
  28.1 44.1 %all_to_all.15 = bf16[8,32,3072]{2,0,1:T(8,128)(2,1)S(1)} all-to-all(bf16[8,32,3072]{2,0,1:T(8,128)(2,1)S(1)} %select_convert_fusion), channel_id=1, replica_groups=mesh['grp'=8,'rep'=4] {'grp'}, dimensions={1} | all-to-all | bytes 3145728 | tf_op jit(solution)/shard_map/all_to_all | solution.py:95
  72.2 0.1 copy.23
  72.3 5.3 %reshape.85 = bf16[64,4,64,48]{3,2,0,1:T(8,128)(2,1)} reshape(bf16[8,8,4,3072]{3,1,0,2:T(8,128)(2,1)S(1)} %copy.23) | data formatting | bytes 3145728 | tf_op jit(solution)/shard_map/reshape | solution.py:98
  77.6 6.4 %copy.24 = bf16[64,4,64,48]{0,2,3,1:T(8,128)(2,1)S(1)} copy(bf16[64,4,64,48]{3,2,0,1:T(8,128)(2,1)} %reshape.85) | data formatting | bytes 3145728 | tf_op jit(solution)/shard_map/reshape | solution.py:98
  84.1 2.6 %convert_bitcast_fusion = bf16[4,64,64,48]{2,1,3,0:T(8,128)(2,1)} fusion(bf16[64,4,64,48]{0,2,3,1:T(8,128)(2,1)S(1)} %copy.24, bf16[1,64,64]{2,1,0:T(8,128)(2,1)S(1)} %copy-done), kind=kOutput, calls=%fused_computation.13 | convolution fusion | flops 101449728 | bytes 3153920 | tf_op jit(solution)/shard_map/pq,qmai->mapi/dot_general | solution.py:99
  86.7 6.3 %copy.25 = bf16[4,64,64,48]{1,0,3,2:T(4,128)(2,1)S(1)} copy(bf16[4,64,64,48]{2,1,3,0:T(8,128)(2,1)} %convert_bitcast_fusion) | data formatting | bytes 3145728 | tf_op jit(solution)/shard_map/convert_element_type | solution.py:101
  93.0 0.0 copy-start.6
  93.0 0.0 copy-start.4
  93.0 3.0 %reshape.86 = bf16[256,3072]{0,1:T(8,128)(2,1)} reshape(bf16[4,64,64,48]{1,0,3,2:T(4,128)(2,1)S(1)} %copy.25) | data formatting | bytes 3145728 | tf_op jit(solution)/shard_map/reshape | solution.py:103
  96.0 1.1 collective-permute-start
  97.2 0.9 collective-permute-start.2
  98.1 0.6 dynamic_slice.39
  105.3 0.7 fusion.24
  107.3 24.1 %collective-permute-done = bf16[256,3072]{0,1:T(8,128)(2,1)} collective-permute-done((bf16[256,3072]{0,1:T(8,128)(2,1)}, bf16[256,3072]{0,1:T(8,128)(2,1)}, u32[]{:S(2)}, u32[]{:S(2)}) %collective-permute-start) | collective-permute-done | bytes 1572896 | tf_op jit(solution)/shard_map/ppermute | solution.py:116
  131.4 0.8 collective-permute-start.1
  132.1 0.1 broadcast_in_dim.45
  132.3 0.6 convolution_dynamic-update-slice_fusion
  132.9 1.3 collective-permute-start.6
  134.2 2.0 constant_dynamic-update-slice_fusion.3
  136.3 2.5 %fusion.26 = f32[256,256]{1,0:T(8,128)S(1)} fusion(bf16[256,3072]{0,1:T(8,128)(2,1)} %collective-permute-done, bf16[256,3072]{0,1:T(8,128)(2,1)} %collective-permute-done.2), kind=kOutput, calls=%fused_computation.49 | convolution fusion | flops 402653184 | bytes 3407872 | tf_op jit(solution)/shard_map/dot_general | solution.py:122
  138.8 1.5 collective-permute-start.4
  144.2 33.8 %collective-permute-done.4 = f32[2,256,256]{1,2,0:T(8,128)} collective-permute-done((f32[2,256,256]{1,2,0:T(8,128)S(1)}, f32[2,256,256]{1,2,0:T(8,128)}, u32[]{:S(2)}, u32[]{:S(2)}) %collective-permute-start.4) | collective-permute-done | bytes 524320 | tf_op jit(solution)/shard_map/ppermute | solution.py:140
  178.1 1.1 slice_bitcast_fusion.2
  179.1 0.1 copy.27
  179.3 0.1 copy.28
  179.4 0.0 collective-permute-done.1
  179.4 2.5 %fusion.25 = f32[256,256]{1,0:T(8,128)S(1)} fusion(bf16[256,3072]{0,1:T(8,128)(2,1)} %collective-permute-done.1, bf16[256,3072]{0,1:T(8,128)(2,1)} %collective-permute-done.2), kind=kOutput, calls=%fused_computation.48 | convolution fusion | flops 402653184 | bytes 3407872 | tf_op jit(solution)/shard_map/dot_general | solution.py:122
  181.9 2.5 %collective-permute-start.3 = (f32[1,256,256]{1,2,0:T(8,128)S(1)}, f32[1,256,256]{1,2,0:T(8,128)S(1)}, u32[]{:S(2)}, u32[]{:S(2)}) collective-permute-start(f32[1,256,256]{1,2,0:T(8,128)S(1)} %bitcast.100), channel_id=1, source_target_pairs={{0,12},{8,4},{16,0},{24,8},{28,16},{20,24},{12,28},{4,20},{1,13},{... | collective-permute-start | bytes 786440 | tf_op jit(solution)/shard_map/ppermute | solution.py:140
  184.4 0.8 pad_maximum_fusion.1
  185.2 0.6 collective-permute-start.5
  185.8 3.2 %convolution_bitcast_fusion = f32[1,256,256]{2,1,0:T(8,128)} fusion(bf16[256,3072]{0,1:T(8,128)(2,1)} %collective-permute-done.1, bf16[256,3072]{0,1:T(8,128)(2,1)} %collective-permute-done.6), kind=kOutput, calls=%fused_computation.19 | convolution fusion | flops 402653184 | bytes 3407872 | tf_op jit(solution)/shard_map/dot_general | solution.py:122
  189.0 1.7 collective-permute-start.7
  190.6 3.7 %collective-permute-done.3 = f32[1,256,256]{1,2,0:T(8,128)S(1)} collective-permute-done((f32[1,256,256]{1,2,0:T(8,128)S(1)}, f32[1,256,256]{1,2,0:T(8,128)S(1)}, u32[]{:S(2)}, u32[]{:S(2)}) %collective-permute-start.3) | collective-permute-done | bytes 262176 | tf_op jit(solution)/shard_map/ppermute | solution.py:140
  194.3 0.7 copy-done.3
  195.0 1.1 copy.26
  196.2 4.6 %collective-permute-done.5 = f32[2,256,256]{2,1,0:T(8,128)S(1)} collective-permute-done((f32[2,256,256]{2,1,0:T(8,128)}, f32[2,256,256]{2,1,0:T(8,128)S(1)}, u32[]{:S(2)}, u32[]{:S(2)}) %collective-permute-start.5) | collective-permute-done | bytes 524320 | tf_op jit(solution)/shard_map/ppermute | solution.py:140
  200.9 5.8 %collective-permute-done.7 = f32[1,256,256]{2,1,0:T(8,128)} collective-permute-done((f32[1,256,256]{2,1,0:T(8,128)}, f32[1,256,256]{2,1,0:T(8,128)}, u32[]{:S(2)}, u32[]{:S(2)}) %collective-permute-start.7) | collective-permute-done | bytes 262176 | tf_op jit(solution)/shard_map/ppermute | solution.py:140
  206.6 1.0 bitcast_dynamic-update-slice_fusion
  207.6 0.1 constant_dynamic-slice_fusion.1
  207.7 1.6 collective-permute-start.8
  209.3 18.7 %collective-permute-done.8 = f32[1024,256]{1,0:T(8,128)} collective-permute-done((f32[1024,256]{1,0:T(8,128)S(1)}, f32[1024,256]{1,0:T(8,128)}, u32[]{:S(2)}, u32[]{:S(2)}) %collective-permute-start.8) | collective-permute-done | bytes 1048608 | tf_op jit(solution)/shard_map/ppermute | solution.py:57
  228.0 1.4 dynamic-slice_add_fusion
  229.4 0.1 collective-permute-start.9
  229.5 1.9 collective-permute-done.9
  231.4 0.9 dynamic-slice_add_fusion.1
  (20 shorter events, 0.2 us)
Async XLA Ops:
  0.0 84.0 %copy-start = (bf16[1,64,64]{2,1,0:T(8,128)(2,1)S(1)}, bf16[1,64,64]{2,1,0:T(8,128)(2,1)}, u32[]{:S(2)}) copy-start(bf16[1,64,64]{2,1,0:T(8,128)(2,1)} %param.9) | copy-start | bytes 24580
  0.0 3.2 %copy-start.1 = (s32[32]{0:T(128)S(1)}, s32[32]{0:T(128)}, u32[]{:S(2)}) copy-start(s32[32]{0:T(128)} %param.13) | copy-start | bytes 388
  4.7 1.1 copy-start.5
  93.0 5.1 %copy-start.6 = (s32[8]{0:T(128)S(1)}, s32[8]{0:T(128)}, u32[]{:S(2)}) copy-start(s32[8]{0:T(128)} %constant.125.clone) | copy-start | bytes 100
  93.0 12.2 %copy-start.4 = (s32[8]{0:T(128)S(1)}, s32[8]{0:T(128)}, u32[]{:S(2)}) copy-start(s32[8]{0:T(128)} %constant.126.clone) | copy-start | bytes 100
  96.0 35.3 %collective-permute-start = (bf16[256,3072]{0,1:T(8,128)(2,1)}, bf16[256,3072]{0,1:T(8,128)(2,1)}, u32[]{:S(2)}, u32[]{:S(2)}) collective-permute-start(bf16[256,3072]{0,1:T(8,128)(2,1)} %reshape.86), channel_id=1, source_target_pairs={{0,8},{8,16},{16,24},{24,28},{28,20},{20,12},{12,4},{4,0},{1,9},{9... | collective-permute-start | bytes 4718600 | tf_op jit(solution)/shard_map/ppermute | solution.py:116
  97.2 35.7 %collective-permute-start.2 = (bf16[256,3072]{0,1:T(8,128)(2,1)}, bf16[256,3072]{0,1:T(8,128)(2,1)}, u32[]{:S(2)}, u32[]{:S(2)}) collective-permute-start(bf16[256,3072]{0,1:T(8,128)(2,1)} %reshape.86), channel_id=1, source_target_pairs={{0,4},{8,0},{16,8},{24,16},{28,24},{20,28},{12,20},{4,12},{1,5},{9... | collective-permute-start | bytes 4718600 | tf_op jit(solution)/shard_map/ppermute | solution.py:118
  107.3 25.0 %copy-start.2 = (bf16[256,3072]{0,1:T(8,128)(2,1)S(1)}, bf16[256,3072]{0,1:T(8,128)(2,1)}, u32[]{:S(2)}) copy-start(bf16[256,3072]{0,1:T(8,128)(2,1)} %reshape.86) | copy-start | bytes 4718596
  131.4 48.0 %collective-permute-start.1 = (bf16[256,3072]{0,1:T(8,128)(2,1)}, bf16[256,3072]{0,1:T(8,128)(2,1)}, u32[]{:S(2)}, u32[]{:S(2)}) collective-permute-start(bf16[256,3072]{0,1:T(8,128)(2,1)} %collective-permute-done), channel_id=1, source_target_pairs={{0,8},{8,16},{16,24},{24,28},{28,20},{20,12},{12,4},{4,0},{1,9},{9... | collective-permute-start | bytes 4718600 | tf_op jit(solution)/shard_map/ppermute | solution.py:116
  132.9 52.9 %collective-permute-start.6 = (bf16[256,3072]{0,1:T(8,128)(2,1)}, bf16[256,3072]{0,1:T(8,128)(2,1)}, u32[]{:S(2)}, u32[]{:S(2)}) collective-permute-start(bf16[256,3072]{0,1:T(8,128)(2,1)} %collective-permute-done.2), channel_id=1, source_target_pairs={{0,4},{8,0},{16,8},{24,16},{28,24},{20,28},{12,20},{4,12},{1,5},{9... | collective-permute-start | bytes 4718600 | tf_op jit(solution)/shard_map/ppermute | solution.py:118
  138.8 39.3 %collective-permute-start.4 = (f32[2,256,256]{1,2,0:T(8,128)S(1)}, f32[2,256,256]{1,2,0:T(8,128)}, u32[]{:S(2)}, u32[]{:S(2)}) collective-permute-start(f32[2,256,256]{1,2,0:T(8,128)S(1)} %pad_maximum_fusion), channel_id=1, source_target_pairs={{0,4},{8,0},{16,8},{24,16},{28,24},{20,28},{12,20},{4,12},{1,5},{9... | collective-permute-start | bytes 1572872 | tf_op jit(solution)/shard_map/ppermute | solution.py:140
  181.9 12.4 %collective-permute-start.3 = (f32[1,256,256]{1,2,0:T(8,128)S(1)}, f32[1,256,256]{1,2,0:T(8,128)S(1)}, u32[]{:S(2)}, u32[]{:S(2)}) collective-permute-start(f32[1,256,256]{1,2,0:T(8,128)S(1)} %bitcast.100), channel_id=1, source_target_pairs={{0,12},{8,4},{16,0},{24,8},{28,16},{20,24},{12,28},{4,20},{1,13},{... | collective-permute-start | bytes 786440 | tf_op jit(solution)/shard_map/ppermute | solution.py:140
  185.2 15.6 %collective-permute-start.5 = (f32[2,256,256]{2,1,0:T(8,128)}, f32[2,256,256]{2,1,0:T(8,128)S(1)}, u32[]{:S(2)}, u32[]{:S(2)}) collective-permute-start(f32[2,256,256]{2,1,0:T(8,128)} %pad_maximum_fusion.1), channel_id=1, source_target_pairs={{0,8},{8,16},{16,24},{24,28},{28,20},{20,12},{12,4},{4,0},{1,9},{9... | collective-permute-start | bytes 1572872 | tf_op jit(solution)/shard_map/ppermute | solution.py:140
  189.0 17.7 %collective-permute-start.7 = (f32[1,256,256]{2,1,0:T(8,128)}, f32[1,256,256]{2,1,0:T(8,128)}, u32[]{:S(2)}, u32[]{:S(2)}) collective-permute-start(f32[1,256,256]{2,1,0:T(8,128)} %convolution_bitcast_fusion), channel_id=1, source_target_pairs={{0,16},{8,24},{16,28},{24,20},{28,12},{20,4},{12,0},{4,8},{1,17},{... | collective-permute-start | bytes 786440 | tf_op jit(solution)/shard_map/ppermute | solution.py:140
  194.3 0.7 copy-start.3
  207.7 20.3 %collective-permute-start.8 = (f32[1024,256]{1,0:T(8,128)S(1)}, f32[1024,256]{1,0:T(8,128)}, u32[]{:S(2)}, u32[]{:S(2)}) collective-permute-start(f32[1024,256]{1,0:T(8,128)S(1)} %constant_dynamic-slice_fusion.1), channel_id=1, source_target_pairs={{0,2},{1,3},{2,0},{3,1},{4,6},{5,7},{6,4},{7,5},{8,10},{9,11},{10,... | collective-permute-start | bytes 3145736 | tf_op jit(solution)/shard_map/ppermute | solution.py:57
  229.4 2.0 collective-permute-start.9

commit v8 on v7

--- a/solution.py
+++ b/solution.py
@@ -88,19 +88,18 @@
         )
         tiles = NB // pair
         tc = jnp.swapaxes(three_center[0], 1, 2).reshape(aux_dev, knu, n_mu, tiles, pair * NB)
-        half = jnp.einsum("qkmtl,mklc->qmtc", tc, weight, preferred_element_type=jnp.float32)
-        half = half.reshape(aux_dev, n_mu, NB, n_occ)
-        half = jnp.where(row_live[None, :, :, None], half, 0.0).astype(jnp.bfloat16)
-        half = half.reshape(aux_dev, n_mu, NB * n_occ)
-        regrouped = lax.all_to_all(half, "grp", split_axis=1, concat_axis=0, tiled=True)
-        n_aux = regrouped.shape[0]
-        mu_dev = regrouped.shape[1]
-        regrouped = regrouped.reshape(n_aux, mu_dev, NB, n_occ)
-        orbital = jnp.einsum(
-            "pq,qmai->mapi", metric[0], regrouped, preferred_element_type=jnp.float32
-        ).astype(jnp.bfloat16)
+        weight = weight.reshape(n_mu, knu, pair * NB, pair, n_occ)
+        half = jnp.einsum("qkmtl,mklai->qimta", tc, weight, preferred_element_type=jnp.float32)
+        half = half.reshape(aux_dev, n_occ, n_mu, NB)
+        half = jnp.where(row_live[None, None], half, 0.0).astype(jnp.bfloat16)
+        mu_dev = n_mu // n
         rows = mu_dev * NB
-        orbital = orbital.reshape(rows, n_aux * n_occ)
+        half = half.reshape(aux_dev, n_occ, n, rows).transpose(2, 0, 1, 3)
+        regrouped = lax.all_to_all(half, "grp", split_axis=0, concat_axis=0, tiled=True)
+        n_aux = n * aux_dev
+        regrouped = regrouped.reshape(n_aux, n_occ * rows)
+        orbital = jnp.dot(metric[0], regrouped, preferred_element_type=jnp.float32).astype(jnp.bfloat16)
+        orbital = orbital.reshape(n_aux * n_occ, rows)
         me = lax.axis_index("grp")
         pos = jnp.asarray(pos_of)[me]
         ring_c = jnp.asarray(ring_arr)
@@ -119,7 +118,9 @@
             held[k] = bwd
 
         def prod(xo, yo):
-            return jnp.dot(held[xo], held[yo].T, preferred_element_type=jnp.float32)
+            return lax.dot_general(
+                held[xo], held[yo], (((0,), (0,)), ((), ())), preferred_element_type=jnp.float32
+            )
 
         local = []
         outgoing = {}

time: 233 us -> 236 us (1.013)
  local copies, waits for them, and re-layouts: 44 us -> 34.1 us
  other arithmetic: 6.91 us -> 15.6 us
  matrix products: 20.5 us -> 24.9 us
    reshape x4 -> x1, local copies, waits for them, and re-layouts: 19 us -> 1.64 us  [body(): orbital = orbital.reshape(n_aux * n_occ, rows)]
    transpose x0 -> x2, local copies, waits for them, and re-layouts: none -> 10.1 us  [the longest x1 6.11 us: body(): jnp.einsum('qkmtl,mklai->qimta', tc, weight, preferred_element_type=jnp.f...]
    transpose x0 -> x1, other arithmetic: none -> 7.69 us  [body(): half = half.reshape(aux_dev, n_occ, n, rows).transpose(2, 0, 1, 3)]
    convert_element_type x1 -> x0, local copies, waits for them, and re-layouts: 6.35 us -> none  [body(): orbital = jnp.einsum('pq,qmai->mapi', metric[0], regrouped, preferred_ele...]
    unnamed x15 -> x14, local copies, waits for them, and re-layouts: 8.08 us -> 12.8 us
    dot_general x7, matrix products: 20.5 us -> 24.9 us  [the longest x5 13.2 us: prod(): lax.dot_general(held[xo], held[yo], (((0,), (0,)), ((), ())), preferred_e...]
    concatenate x0 -> x1, other arithmetic: none -> 3.68 us  [body(): jnp.concatenate([jnp.concatenate([picked, blank], axis=-1), jnp.concatena...]
  transfers between devices with their start and end apart: 10 -> 10, of which waited for: 7 -> 7; matrix products, arithmetic and copies ran while one was open for 7% -> 8% of each run, Pallas kernels for 0% -> 0%
where the time goes in v8:
time: 236 us; the launch traced here: 235 us
  waiting for transfers between devices  92.6 us (39%)
  blocking collectives  44.1 us (19%)
  local copies, waits for them, and re-layouts  34.1 us (14%)
  matrix products  24.9 us (11%)
  other arithmetic  15.6 us (7%)
  starting transfers between devices  12.2 us (5%)
  between operations  11.7 us (5%)
    ppermute x4, waiting for transfers between devices, body(): got = lax.ppermute(stack, 'grp', shifted(s))  47.8 us
    all_to_all x1, blocking collectives, body(): lax.all_to_all(half, 'grp', split_axis=0, concat_axis=0, tiled=True)  44.1 us
    ppermute x2, waiting for transfers between devices, body(): fwd = lax.ppermute(fwd, 'grp', shifted(1))  24.2 us
    ppermute x2, waiting for transfers between devices, scatter_sum(): got = lax.ppermute(send, 'rep', [(i, i ^ d) for i in range(n_rep)])  20.6 us
    dot_general x5, matrix products, prod(): lax.dot_general(held[xo], held[yo], (((0,), (0,)), ((), ())), preferred_e...  13.2 us
    unnamed x14, local copies, waits for them, and re-layouts  12.8 us
    dot_general x1, matrix products, body(): jnp.einsum('qkmtl,mklai->qimta', tc, weight, preferred_element_type=jnp.f...  11.1 us
    transpose x1, other arithmetic, body(): half = half.reshape(aux_dev, n_occ, n, rows).transpose(2, 0, 1, 3)  7.69 us
  transfers between devices with their start and end apart: 10, of which 7 were waited for; matrix products, arithmetic and copies ran while one was open for 8% of the time, Pallas kernels for 0%

profile of v8, /device:TPU:0, one launch (start us, length us, event | category | flops | bytes accessed | tf_op | source)
XLA Modules:
  0.0 235.1 jit_solution(2590318393410437515)
XLA Ops:
  0.0 0.7 compare_select_fusion
  0.7 0.1 copy.30
  0.8 0.1 reshape.90
  0.9 1.3 reshape.82
  2.2 0.2 copy.31
  2.4 0.0 copy-start.1
  2.4 1.0 gather_fusion.1
  3.5 0.0 copy-start.4
  3.5 1.6 gather_fusion
  5.0 0.1 reshape.89
  5.1 0.1 iota_compare_fusion.3
  5.2 0.1 fusion.15
  5.4 0.2 broadcast_select_fusion
  5.6 3.7 %fusion.5 = bf16[32,6,128,96]{2,3,1,0:T(8,128)(2,1)} fusion(bf16[32,6,64,48]{2,3,1,0:T(8,128)(2,1)S(1)} %broadcast_select_fusion), kind=kLoop, calls=%fused_computation.11 | loop fusion | flops 18874368 | bytes 5898240 | tf_op jit(solution)/shard_map/concatenate | solution.py:86
  9.3 11.4 %copy.46 = bf16[192,8,32,128]{3,2,1,0:T(8,128)(2,1)} copy(bf16[192,8,32,128]{3,1,2,0:T(8,128)(2,1)} %bitcast.84) | data formatting | bytes 25165824
  20.7 11.1 %fusion.8 = bf16[8,48,32,32,2]{1,3,0,4,2:T(8,128)(2,1)} fusion(bf16[8,6,32,32,128,1]{4,3,2,1,0,5:T(8,128)(2,1)} %bitcast.85, bf16[32,6,128,2,48,1]{2,4,3,1,0,5:T(8,128)(2,1)} %bitcast.87), kind=kOutput, calls=%fused_computation.14 | convolution fusion | flops 1207959552 | bytes 18874368 | tf_op jit(solution)/shard_map/qkmtl,mklai->qimta/dot_general | solution.py:92
  31.8 6.1 %copy.34 = bf16[8,48,32,32,2]{1,0,4,3,2:T(8,128)(2,1)} copy(bf16[8,48,32,32,2]{1,3,0,4,2:T(8,128)(2,1)} %fusion.8) | data formatting | bytes 3145728 | tf_op jit(solution)/shard_map/qkmtl,mklai->qimta/transpose | solution.py:92
  37.9 0.1 lt.169
  38.0 0.1 lt.170
  38.1 0.1 lt.167
  38.2 7.7 %fusion.7 = bf16[8,8,48,256]{2,1,3,0:T(8,128)(2,1)} fusion(bf16[8,48,8,256]{1,0,3,2:T(8,128)(2,1)} %bitcast.82, pred[8,256]{1,0:T(8,128)(4,1)S(1)} %broadcast_compare_fusion), kind=kLoop, calls=%fused_computation.13 | loop fusion | flops 786432 | bytes 3147776 | tf_op jit(solution)/shard_map/transpose | solution.py:97
  45.8 4.0 %copy.35 = bf16[8,8,48,256]{3,2,1,0:T(8,128)(2,1)S(1)} copy(bf16[8,8,48,256]{2,1,3,0:T(8,128)(2,1)} %fusion.7) | data formatting | bytes 3145728 | tf_op jit(solution)/shard_map/transpose | solution.py:97
  49.8 44.1 %all_to_all.5 = bf16[8,8,48,256]{3,2,1,0:T(8,128)(2,1)S(1)} all-to-all(bf16[8,8,48,256]{3,2,1,0:T(8,128)(2,1)S(1)} %copy.35), channel_id=1, replica_groups=mesh['grp'=8,'rep'=4] {'grp'}, dimensions={0} | all-to-all | bytes 3145728 | tf_op jit(solution)/shard_map/all_to_all | solution.py:98
  93.9 0.6 copy.47
  94.6 0.6 fusion
  95.1 0.0 copy-start.5
  95.1 0.0 copy-start.3
  95.1 1.6 reshape.87
  96.8 1.1 collective-permute-start
  97.9 0.9 collective-permute-start.2
  98.8 0.6 dynamic_slice.39
  106.0 0.7 fusion.17
  107.9 24.2 %collective-permute-done = bf16[3072,256]{1,0:T(8,128)(2,1)} collective-permute-done((bf16[3072,256]{1,0:T(8,128)(2,1)}, bf16[3072,256]{1,0:T(8,128)(2,1)}, u32[]{:S(2)}, u32[]{:S(2)}) %collective-permute-start) | collective-permute-done | bytes 1572896 | tf_op jit(solution)/shard_map/ppermute | solution.py:115
  132.1 0.8 collective-permute-start.1
  132.8 0.1 broadcast_in_dim.24
  133.0 2.6 %convolution_dynamic-update-slice_fusion = f32[2048,256]{1,0:T(8,128)S(1)} fusion(f32[2048,256]{1,0:T(8,128)S(1)} %broadcast_in_dim.24, s32[]{:T(128)S(6)} %select_n.130, bf16[3072,256]{1,0:T(8,128)(2,1)} %reshape.87), kind=kOutput, calls=%fused_computation.16 | convolution fusion | flops 402653184 | bytes 3407876 | tf_op jit(solution)/shard_map/dot_general | solution.py:121
  135.6 0.0 collective-permute-done.2
  135.6 1.5 collective-permute-start.6
  137.1 2.5 %constant_dynamic-update-slice_fusion.3 = (f32[2048,256]{1,0:T(8,128)S(1)}, f32[256,256]{1,0:T(8,128)S(1)}) fusion(f32[2048,256]{1,0:T(8,128)S(1)} %convolution_dynamic-update-slice_fusion, s32[]{:T(128)S(6)} %select_n.133, bf16[3072,256]{1,0:T(8,128)(2,1)} %collective-permute-done, bf16[3072,256]{1,0:T(8,128)(2,1)} %reshape.87), kind=kOutput, calls=%fused_computation.41 | convolution fusion | flops 402653184 | bytes 3670020 | tf_op jit(solution)/shard_map/dot_general | solution.py:121
  139.6 2.5 %fusion.19 = f32[256,256]{1,0:T(8,128)S(1)} fusion(bf16[3072,256]{1,0:T(8,128)(2,1)} %collective-permute-done, bf16[3072,256]{1,0:T(8,128)(2,1)} %collective-permute-done.2), kind=kOutput, calls=%fused_computation.44 | convolution fusion | flops 402653184 | bytes 3407872 | tf_op jit(solution)/shard_map/dot_general | solution.py:121
  142.1 1.5 collective-permute-start.4
  147.2 33.7 %collective-permute-done.4 = f32[2,256,256]{1,2,0:T(8,128)} collective-permute-done((f32[2,256,256]{1,2,0:T(8,128)S(1)}, f32[2,256,256]{1,2,0:T(8,128)}, u32[]{:S(2)}, u32[]{:S(2)}) %collective-permute-start.4) | collective-permute-done | bytes 524320 | tf_op jit(solution)/shard_map/ppermute | solution.py:141
  180.9 1.1 slice_bitcast_fusion.2
  182.0 0.1 copy.37
  182.1 0.1 copy.38
  182.3 2.5 %fusion.18 = f32[256,256]{1,0:T(8,128)S(1)} fusion(bf16[3072,256]{1,0:T(8,128)(2,1)} %collective-permute-done.1, bf16[3072,256]{1,0:T(8,128)(2,1)} %collective-permute-done.2), kind=kOutput, calls=%fused_computation.43 | convolution fusion | flops 402653184 | bytes 3407872 | tf_op jit(solution)/shard_map/dot_general | solution.py:121
  184.7 2.5 %collective-permute-start.3 = (f32[1,256,256]{1,2,0:T(8,128)S(1)}, f32[1,256,256]{1,2,0:T(8,128)S(1)}, u32[]{:S(2)}, u32[]{:S(2)}) collective-permute-start(f32[1,256,256]{1,2,0:T(8,128)S(1)} %bitcast.91), channel_id=1, source_target_pairs={{0,12},{8,4},{16,0},{24,8},{28,16},{20,24},{12,28},{4,20},{1,13},{... | collective-permute-start | bytes 786440 | tf_op jit(solution)/shard_map/ppermute | solution.py:141
  187.2 0.8 pad_maximum_fusion.1
  188.0 0.6 collective-permute-start.5
  188.6 3.2 %convolution_bitcast_fusion = f32[1,256,256]{2,1,0:T(8,128)} fusion(bf16[3072,256]{1,0:T(8,128)(2,1)} %collective-permute-done.1, bf16[3072,256]{1,0:T(8,128)(2,1)} %collective-permute-done.6), kind=kOutput, calls=%fused_computation.17 | convolution fusion | flops 402653184 | bytes 3407872 | tf_op jit(solution)/shard_map/dot_general | solution.py:121
  191.8 1.7 collective-permute-start.7
  193.5 3.7 %collective-permute-done.3 = f32[1,256,256]{1,2,0:T(8,128)S(1)} collective-permute-done((f32[1,256,256]{1,2,0:T(8,128)S(1)}, f32[1,256,256]{1,2,0:T(8,128)S(1)}, u32[]{:S(2)}, u32[]{:S(2)}) %collective-permute-start.3) | collective-permute-done | bytes 262176 | tf_op jit(solution)/shard_map/ppermute | solution.py:141
  197.2 0.7 copy-done.2
  197.9 1.1 copy.36
  199.1 4.6 %collective-permute-done.5 = f32[2,256,256]{2,1,0:T(8,128)S(1)} collective-permute-done((f32[2,256,256]{2,1,0:T(8,128)}, f32[2,256,256]{2,1,0:T(8,128)S(1)}, u32[]{:S(2)}, u32[]{:S(2)}) %collective-permute-start.5) | collective-permute-done | bytes 524320 | tf_op jit(solution)/shard_map/ppermute | solution.py:141
  203.7 5.7 %collective-permute-done.7 = f32[1,256,256]{2,1,0:T(8,128)} collective-permute-done((f32[1,256,256]{2,1,0:T(8,128)}, f32[1,256,256]{2,1,0:T(8,128)}, u32[]{:S(2)}, u32[]{:S(2)}) %collective-permute-start.7) | collective-permute-done | bytes 262176 | tf_op jit(solution)/shard_map/ppermute | solution.py:141
  209.5 1.0 bitcast_dynamic-update-slice_fusion
  210.4 0.1 constant_dynamic-slice_fusion.1
  210.5 1.6 collective-permute-start.8
  212.1 18.7 %collective-permute-done.8 = f32[1024,256]{1,0:T(8,128)} collective-permute-done((f32[1024,256]{1,0:T(8,128)S(1)}, f32[1024,256]{1,0:T(8,128)}, u32[]{:S(2)}, u32[]{:S(2)}) %collective-permute-start.8) | collective-permute-done | bytes 1048608 | tf_op jit(solution)/shard_map/ppermute | solution.py:57
  230.8 1.4 dynamic-slice_add_fusion
  232.2 0.1 collective-permute-start.9
  232.3 1.9 collective-permute-done.9
  234.2 0.9 dynamic-slice_add_fusion.1
  (19 shorter events, 0.2 us)
Async XLA Ops:
  0.0 94.5 %copy-start = (bf16[1,64,64]{2,1,0:T(8,128)(2,1)S(1)}, bf16[1,64,64]{2,1,0:T(8,128)(2,1)}, u32[]{:S(2)}) copy-start(bf16[1,64,64]{2,1,0:T(8,128)(2,1)} %param.9) | copy-start | bytes 24580
  2.4 1.0 copy-start.1
  3.5 1.7 copy-start.4
  95.1 3.7 %copy-start.5 = (s32[8]{0:T(128)S(1)}, s32[8]{0:T(128)}, u32[]{:S(2)}) copy-start(s32[8]{0:T(128)} %constant.125.clone) | copy-start | bytes 100
  95.1 10.9 %copy-start.3 = (s32[8]{0:T(128)S(1)}, s32[8]{0:T(128)}, u32[]{:S(2)}) copy-start(s32[8]{0:T(128)} %constant.126.clone) | copy-start | bytes 100
  96.8 35.3 %collective-permute-start = (bf16[3072,256]{1,0:T(8,128)(2,1)}, bf16[3072,256]{1,0:T(8,128)(2,1)}, u32[]{:S(2)}, u32[]{:S(2)}) collective-permute-start(bf16[3072,256]{1,0:T(8,128)(2,1)} %reshape.87), channel_id=1, source_target_pairs={{0,8},{8,16},{16,24},{24,28},{28,20},{20,12},{12,4},{4,0},{1,9},{9... | collective-permute-start | bytes 4718600 | tf_op jit(solution)/shard_map/ppermute | solution.py:115
  97.9 37.7 %collective-permute-start.2 = (bf16[3072,256]{1,0:T(8,128)(2,1)}, bf16[3072,256]{1,0:T(8,128)(2,1)}, u32[]{:S(2)}, u32[]{:S(2)}) collective-permute-start(bf16[3072,256]{1,0:T(8,128)(2,1)} %reshape.87), channel_id=1, source_target_pairs={{0,4},{8,0},{16,8},{24,16},{28,24},{20,28},{12,20},{4,12},{1,5},{9... | collective-permute-start | bytes 4718600 | tf_op jit(solution)/shard_map/ppermute | solution.py:117
  132.1 50.1 %collective-permute-start.1 = (bf16[3072,256]{1,0:T(8,128)(2,1)}, bf16[3072,256]{1,0:T(8,128)(2,1)}, u32[]{:S(2)}, u32[]{:S(2)}) collective-permute-start(bf16[3072,256]{1,0:T(8,128)(2,1)} %collective-permute-done), channel_id=1, source_target_pairs={{0,8},{8,16},{16,24},{24,28},{28,20},{20,12},{12,4},{4,0},{1,9},{9... | collective-permute-start | bytes 4718600 | tf_op jit(solution)/shard_map/ppermute | solution.py:115
  135.6 53.0 %collective-permute-start.6 = (bf16[3072,256]{1,0:T(8,128)(2,1)}, bf16[3072,256]{1,0:T(8,128)(2,1)}, u32[]{:S(2)}, u32[]{:S(2)}) collective-permute-start(bf16[3072,256]{1,0:T(8,128)(2,1)} %collective-permute-done.2), channel_id=1, source_target_pairs={{0,4},{8,0},{16,8},{24,16},{28,24},{20,28},{12,20},{4,12},{1,5},{9... | collective-permute-start | bytes 4718600 | tf_op jit(solution)/shard_map/ppermute | solution.py:117
  142.1 38.8 %collective-permute-start.4 = (f32[2,256,256]{1,2,0:T(8,128)S(1)}, f32[2,256,256]{1,2,0:T(8,128)}, u32[]{:S(2)}, u32[]{:S(2)}) collective-permute-start(f32[2,256,256]{1,2,0:T(8,128)S(1)} %pad_maximum_fusion), channel_id=1, source_target_pairs={{0,4},{8,0},{16,8},{24,16},{28,24},{20,28},{12,20},{4,12},{1,5},{9... | collective-permute-start | bytes 1572872 | tf_op jit(solution)/shard_map/ppermute | solution.py:141
  184.7 12.4 %collective-permute-start.3 = (f32[1,256,256]{1,2,0:T(8,128)S(1)}, f32[1,256,256]{1,2,0:T(8,128)S(1)}, u32[]{:S(2)}, u32[]{:S(2)}) collective-permute-start(f32[1,256,256]{1,2,0:T(8,128)S(1)} %bitcast.91), channel_id=1, source_target_pairs={{0,12},{8,4},{16,0},{24,8},{28,16},{20,24},{12,28},{4,20},{1,13},{... | collective-permute-start | bytes 786440 | tf_op jit(solution)/shard_map/ppermute | solution.py:141
  188.0 15.6 %collective-permute-start.5 = (f32[2,256,256]{2,1,0:T(8,128)}, f32[2,256,256]{2,1,0:T(8,128)S(1)}, u32[]{:S(2)}, u32[]{:S(2)}) collective-permute-start(f32[2,256,256]{2,1,0:T(8,128)} %pad_maximum_fusion.1), channel_id=1, source_target_pairs={{0,8},{8,16},{16,24},{24,28},{28,20},{20,12},{12,4},{4,0},{1,9},{9... | collective-permute-start | bytes 1572872 | tf_op jit(solution)/shard_map/ppermute | solution.py:141
  191.8 17.7 %collective-permute-start.7 = (f32[1,256,256]{2,1,0:T(8,128)}, f32[1,256,256]{2,1,0:T(8,128)}, u32[]{:S(2)}, u32[]{:S(2)}) collective-permute-start(f32[1,256,256]{2,1,0:T(8,128)} %convolution_bitcast_fusion), channel_id=1, source_target_pairs={{0,16},{8,24},{16,28},{24,20},{28,12},{20,4},{12,0},{4,8},{1,17},{... | collective-permute-start | bytes 786440 | tf_op jit(solution)/shard_map/ppermute | solution.py:141
  197.2 0.7 copy-start.2
  210.5 20.3 %collective-permute-start.8 = (f32[1024,256]{1,0:T(8,128)S(1)}, f32[1024,256]{1,0:T(8,128)}, u32[]{:S(2)}, u32[]{:S(2)}) collective-permute-start(f32[1024,256]{1,0:T(8,128)S(1)} %constant_dynamic-slice_fusion.1), channel_id=1, source_target_pairs={{0,2},{1,3},{2,0},{3,1},{4,6},{5,7},{6,4},{7,5},{8,10},{9,11},{10,... | collective-permute-start | bytes 3145736 | tf_op jit(solution)/shard_map/ppermute | solution.py:57
  232.2 2.0 collective-permute-start.9

commit v9 on v7

--- a/solution.py
+++ b/solution.py
@@ -47,17 +47,18 @@
     if n_rep & (n_rep - 1):
         return lax.psum_scatter(term, "rep", scatter_dimension=0, tiled=True)
     me = lax.axis_index("rep")
+    bits = n_rep.bit_length() - 1
     per = term.shape[0] // n_rep
-    buf = term
-    d = n_rep // 2
-    while d >= 1:
-        upper = (me // d) % 2
-        keep = lax.dynamic_slice_in_dim(buf, upper * d * per, d * per, axis=0)
-        send = lax.dynamic_slice_in_dim(buf, (1 - upper) * d * per, d * per, axis=0)
+    buf = term.reshape((2,) * bits + (per,) + term.shape[1:])
+    for b in range(bits):
+        d = 1 << b
+        axis = buf.ndim - 3
+        mine = (me // d) % 2
+        keep = lax.dynamic_index_in_dim(buf, mine, axis=axis, keepdims=False)
+        send = lax.dynamic_index_in_dim(buf, 1 - mine, axis=axis, keepdims=False)
         got = lax.ppermute(send, "rep", [(i, i ^ d) for i in range(n_rep)])
         buf = keep + got
-        d //= 2
-    return buf
+    return buf.reshape(per, term.shape[1])
 
 
 def make_body(ring):

time: 233 us -> 228 us (0.979)
  waiting for transfers between devices: 92.6 us -> 87.2 us
    ppermute x2, waiting for transfers between devices: 20.6 us -> 15.2 us  [scatter_sum(): got = lax.ppermute(send, 'rep', [(i, i ^ d) for i in range(n_rep)])]
where the time goes in v9:
time: 228 us; the launch traced here: 227 us
  waiting for transfers between devices  87.2 us (38%)
  blocking collectives  44.1 us (19%)
  local copies, waits for them, and re-layouts  44 us (19%)
  matrix products  20.5 us (9%)
  between operations  12.2 us (5%)
  starting transfers between devices  12 us (5%)
  other arithmetic  6.91 us (3%)
    ppermute x4, waiting for transfers between devices, body(): got = lax.ppermute(stack, 'grp', shifted(s))  47.9 us
    all_to_all x1, blocking collectives, body(): lax.all_to_all(half, 'grp', split_axis=1, concat_axis=0, tiled=True)  44.1 us
    ppermute x2, waiting for transfers between devices, body(): fwd = lax.ppermute(fwd, 'grp', shifted(1))  24.1 us
    ppermute x2, waiting for transfers between devices, scatter_sum(): got = lax.ppermute(send, 'rep', [(i, i ^ d) for i in range(n_rep)])  15.2 us
    reshape x2, local copies, waits for them, and re-layouts, body(): regrouped = regrouped.reshape(n_aux, mu_dev, NB, n_occ)  11.8 us
    dot_general x5, matrix products, prod(): return jnp.dot(held[xo], held[yo].T, preferred_element_type=jnp.float32)  10.8 us
    unnamed x15, local copies, waits for them, and re-layouts  8.08 us
    dot_general x1, matrix products, body(): jnp.einsum('qkmtl,mklc->qmtc', tc, weight, preferred_element_type=jnp.flo...  7.1 us
  transfers between devices with their start and end apart: 10, of which 7 were waited for; matrix products, arithmetic and copies ran while one was open for 7% of the time, Pallas kernels for 0%

profile of v9, /device:TPU:0, one launch (start us, length us, event | category | flops | bytes accessed | tf_op | source)
XLA Modules:
  0.0 226.9 jit_solution(14402941831414586398)
XLA Ops:
  0.0 0.7 compare_select_fusion
  0.7 0.1 copy.20
  0.8 0.1 reshape.93
  0.9 1.3 reshape.85
  2.3 0.2 copy.21
  2.4 0.7 iota_compare_fusion.4
  3.2 1.6 gather_fusion
  4.7 0.0 copy-start.5
  4.7 1.0 gather_fusion.1
  5.8 0.1 reshape.92
  5.9 0.1 iota_compare_fusion.3
  5.9 7.4 %copy.32 = bf16[192,8,32,128]{3,2,1,0:T(8,128)(2,1)S(1)} copy(bf16[192,8,32,128]{3,1,2,0:T(8,128)(2,1)} %bitcast.103) | data formatting | bytes 25165824
  13.3 0.1 fusion.19
  13.4 1.7 broadcast_select_fusion
  15.1 7.1 %fusion.12 = bf16[8,32,32,96]{3,2,0,1:T(8,128)(2,1)} fusion(bf16[8,6,32,32,128]{4,3,2,1,0:T(8,128)(2,1)S(1)} %bitcast.104, bf16[32,6,64,48]{2,3,1,0:T(8,128)(2,1)} %broadcast_select_fusion), kind=kOutput, calls=%fused_computation.17 | convolution fusion | flops 1226833920 | bytes 15335424 | tf_op jit(solution)/shard_map/qkmtl,mklc->qmtc/dot_general | solution.py:92
  22.2 4.2 %reshape.87 = bf16[8,32,3072]{2,0,1:T(8,128)(2,1)S(1)} reshape(bf16[8,32,32,96]{3,2,0,1:T(8,128)(2,1)} %fusion.12) | data formatting | bytes 3145728 | tf_op jit(solution)/shard_map/reshape | solution.py:93
  26.4 0.3 broadcast_in_dim.46
  26.8 0.8 broadcast_in_dim.47
  27.6 0.5 select_convert_fusion
  28.1 44.1 %all_to_all.15 = bf16[8,32,3072]{2,0,1:T(8,128)(2,1)S(1)} all-to-all(bf16[8,32,3072]{2,0,1:T(8,128)(2,1)S(1)} %select_convert_fusion), channel_id=1, replica_groups=mesh['grp'=8,'rep'=4] {'grp'}, dimensions={1} | all-to-all | bytes 3145728 | tf_op jit(solution)/shard_map/all_to_all | solution.py:96
  72.2 0.1 copy.23
  72.3 5.3 %reshape.88 = bf16[64,4,64,48]{3,2,0,1:T(8,128)(2,1)} reshape(bf16[8,8,4,3072]{3,1,0,2:T(8,128)(2,1)S(1)} %copy.23) | data formatting | bytes 3145728 | tf_op jit(solution)/shard_map/reshape | solution.py:99
  77.6 6.4 %copy.24 = bf16[64,4,64,48]{0,2,3,1:T(8,128)(2,1)S(1)} copy(bf16[64,4,64,48]{3,2,0,1:T(8,128)(2,1)} %reshape.88) | data formatting | bytes 3145728 | tf_op jit(solution)/shard_map/reshape | solution.py:99
  84.1 2.6 %convert_bitcast_fusion = bf16[4,64,64,48]{2,1,3,0:T(8,128)(2,1)} fusion(bf16[64,4,64,48]{0,2,3,1:T(8,128)(2,1)S(1)} %copy.24, bf16[1,64,64]{2,1,0:T(8,128)(2,1)S(1)} %copy-done), kind=kOutput, calls=%fused_computation.13 | convolution fusion | flops 101449728 | bytes 3153920 | tf_op jit(solution)/shard_map/pq,qmai->mapi/dot_general | solution.py:100
  86.7 6.3 %copy.25 = bf16[4,64,64,48]{1,0,3,2:T(4,128)(2,1)S(1)} copy(bf16[4,64,64,48]{2,1,3,0:T(8,128)(2,1)} %convert_bitcast_fusion) | data formatting | bytes 3145728 | tf_op jit(solution)/shard_map/convert_element_type | solution.py:102
  93.0 0.0 copy-start.6
  93.0 0.0 copy-start.4
  93.0 3.0 %reshape.89 = bf16[256,3072]{0,1:T(8,128)(2,1)} reshape(bf16[4,64,64,48]{1,0,3,2:T(4,128)(2,1)S(1)} %copy.25) | data formatting | bytes 3145728 | tf_op jit(solution)/shard_map/reshape | solution.py:104
  96.0 1.1 collective-permute-start
  97.2 0.9 collective-permute-start.2
  98.1 0.6 dynamic_slice.41
  105.3 0.7 fusion.24
  107.3 24.1 %collective-permute-done = bf16[256,3072]{0,1:T(8,128)(2,1)} collective-permute-done((bf16[256,3072]{0,1:T(8,128)(2,1)}, bf16[256,3072]{0,1:T(8,128)(2,1)}, u32[]{:S(2)}, u32[]{:S(2)}) %collective-permute-start) | collective-permute-done | bytes 1572896 | tf_op jit(solution)/shard_map/ppermute | solution.py:117
  131.4 0.8 collective-permute-start.1
  132.1 0.1 broadcast_in_dim.45
  132.3 0.6 convolution_dynamic-update-slice_fusion
  132.9 1.3 collective-permute-start.6
  134.2 2.0 constant_dynamic-update-slice_fusion.3
  136.3 2.5 %fusion.26 = f32[256,256]{1,0:T(8,128)S(1)} fusion(bf16[256,3072]{0,1:T(8,128)(2,1)} %collective-permute-done, bf16[256,3072]{0,1:T(8,128)(2,1)} %collective-permute-done.2), kind=kOutput, calls=%fused_computation.49 | convolution fusion | flops 402653184 | bytes 3407872 | tf_op jit(solution)/shard_map/dot_general | solution.py:123
  138.8 1.5 collective-permute-start.4
  144.2 33.8 %collective-permute-done.4 = f32[2,256,256]{1,2,0:T(8,128)} collective-permute-done((f32[2,256,256]{1,2,0:T(8,128)S(1)}, f32[2,256,256]{1,2,0:T(8,128)}, u32[]{:S(2)}, u32[]{:S(2)}) %collective-permute-start.4) | collective-permute-done | bytes 524320 | tf_op jit(solution)/shard_map/ppermute | solution.py:141
  178.1 1.1 slice_bitcast_fusion.2
  179.1 0.1 copy.27
  179.3 0.1 copy.28
  179.4 0.0 collective-permute-done.1
  179.4 2.5 %fusion.25 = f32[256,256]{1,0:T(8,128)S(1)} fusion(bf16[256,3072]{0,1:T(8,128)(2,1)} %collective-permute-done.1, bf16[256,3072]{0,1:T(8,128)(2,1)} %collective-permute-done.2), kind=kOutput, calls=%fused_computation.48 | convolution fusion | flops 402653184 | bytes 3407872 | tf_op jit(solution)/shard_map/dot_general | solution.py:123
  181.9 2.5 %collective-permute-start.3 = (f32[1,256,256]{1,2,0:T(8,128)S(1)}, f32[1,256,256]{1,2,0:T(8,128)S(1)}, u32[]{:S(2)}, u32[]{:S(2)}) collective-permute-start(f32[1,256,256]{1,2,0:T(8,128)S(1)} %bitcast.111), channel_id=1, source_target_pairs={{0,12},{8,4},{16,0},{24,8},{28,16},{20,24},{12,28},{4,20},{1,13},{... | collective-permute-start | bytes 786440 | tf_op jit(solution)/shard_map/ppermute | solution.py:141
  184.4 0.8 pad_maximum_fusion.1
  185.2 0.6 collective-permute-start.5
  185.8 3.2 %convolution_bitcast_fusion = f32[1,256,256]{2,1,0:T(8,128)} fusion(bf16[256,3072]{0,1:T(8,128)(2,1)} %collective-permute-done.1, bf16[256,3072]{0,1:T(8,128)(2,1)} %collective-permute-done.6), kind=kOutput, calls=%fused_computation.19 | convolution fusion | flops 402653184 | bytes 3407872 | tf_op jit(solution)/shard_map/dot_general | solution.py:123
  189.0 1.7 collective-permute-start.7
  190.6 3.7 %collective-permute-done.3 = f32[1,256,256]{1,2,0:T(8,128)S(1)} collective-permute-done((f32[1,256,256]{1,2,0:T(8,128)S(1)}, f32[1,256,256]{1,2,0:T(8,128)S(1)}, u32[]{:S(2)}, u32[]{:S(2)}) %collective-permute-start.3) | collective-permute-done | bytes 262176 | tf_op jit(solution)/shard_map/ppermute | solution.py:141
  194.3 0.7 copy-done.3
  195.0 1.1 copy.26
  196.2 4.6 %collective-permute-done.5 = f32[2,256,256]{2,1,0:T(8,128)S(1)} collective-permute-done((f32[2,256,256]{2,1,0:T(8,128)}, f32[2,256,256]{2,1,0:T(8,128)S(1)}, u32[]{:S(2)}, u32[]{:S(2)}) %collective-permute-start.5) | collective-permute-done | bytes 524320 | tf_op jit(solution)/shard_map/ppermute | solution.py:141
  200.9 5.8 %collective-permute-done.7 = f32[1,256,256]{2,1,0:T(8,128)} collective-permute-done((f32[1,256,256]{2,1,0:T(8,128)}, f32[1,256,256]{2,1,0:T(8,128)}, u32[]{:S(2)}, u32[]{:S(2)}) %collective-permute-start.7) | collective-permute-done | bytes 262176 | tf_op jit(solution)/shard_map/ppermute | solution.py:141
  206.6 1.0 bitcast_dynamic-update-slice_fusion
  207.6 0.1 dynamic-slice_bitcast_fusion
  207.7 0.1 collective-permute-start.8
  207.8 2.7 %collective-permute-done.8 = f32[2,512,256]{2,1,0:T(8,128)} collective-permute-done((f32[2,512,256]{2,1,0:T(8,128)S(1)}, f32[2,512,256]{2,1,0:T(8,128)}, u32[]{:S(2)}, u32[]{:S(2)}) %collective-permute-start.8) | collective-permute-done | bytes 1048608 | tf_op jit(solution)/shard_map/ppermute | solution.py:59
  210.5 1.4 bitcast_add_fusion
  212.0 1.6 collective-permute-start.9
  213.5 12.4 %collective-permute-done.9 = f32[512,256]{1,0:T(8,128)S(1)} collective-permute-done((f32[512,256]{1,0:T(8,128)S(1)}, f32[512,256]{1,0:T(8,128)S(1)}, u32[]{:S(2)}, u32[]{:S(2)}) %collective-permute-start.9) | collective-permute-done | bytes 524320 | tf_op jit(solution)/shard_map/ppermute | solution.py:59
  226.0 0.9 bitcast_add_fusion.1
  (20 shorter events, 0.2 us)
Async XLA Ops:
  0.0 84.0 %copy-start = (bf16[1,64,64]{2,1,0:T(8,128)(2,1)S(1)}, bf16[1,64,64]{2,1,0:T(8,128)(2,1)}, u32[]{:S(2)}) copy-start(bf16[1,64,64]{2,1,0:T(8,128)(2,1)} %param.9) | copy-start | bytes 24580
  0.0 3.2 %copy-start.1 = (s32[32]{0:T(128)S(1)}, s32[32]{0:T(128)}, u32[]{:S(2)}) copy-start(s32[32]{0:T(128)} %param.13) | copy-start | bytes 388
  4.7 1.1 copy-start.5
  93.0 5.1 %copy-start.6 = (s32[8]{0:T(128)S(1)}, s32[8]{0:T(128)}, u32[]{:S(2)}) copy-start(s32[8]{0:T(128)} %constant.133.clone) | copy-start | bytes 100
  93.0 12.2 %copy-start.4 = (s32[8]{0:T(128)S(1)}, s32[8]{0:T(128)}, u32[]{:S(2)}) copy-start(s32[8]{0:T(128)} %constant.134.clone) | copy-start | bytes 100
  96.0 35.3 %collective-permute-start = (bf16[256,3072]{0,1:T(8,128)(2,1)}, bf16[256,3072]{0,1:T(8,128)(2,1)}, u32[]{:S(2)}, u32[]{:S(2)}) collective-permute-start(bf16[256,3072]{0,1:T(8,128)(2,1)} %reshape.89), channel_id=1, source_target_pairs={{0,8},{8,16},{16,24},{24,28},{28,20},{20,12},{12,4},{4,0},{1,9},{9... | collective-permute-start | bytes 4718600 | tf_op jit(solution)/shard_map/ppermute | solution.py:117
  97.2 35.7 %collective-permute-start.2 = (bf16[256,3072]{0,1:T(8,128)(2,1)}, bf16[256,3072]{0,1:T(8,128)(2,1)}, u32[]{:S(2)}, u32[]{:S(2)}) collective-permute-start(bf16[256,3072]{0,1:T(8,128)(2,1)} %reshape.89), channel_id=1, source_target_pairs={{0,4},{8,0},{16,8},{24,16},{28,24},{20,28},{12,20},{4,12},{1,5},{9... | collective-permute-start | bytes 4718600 | tf_op jit(solution)/shard_map/ppermute | solution.py:119
  107.3 25.0 %copy-start.2 = (bf16[256,3072]{0,1:T(8,128)(2,1)S(1)}, bf16[256,3072]{0,1:T(8,128)(2,1)}, u32[]{:S(2)}) copy-start(bf16[256,3072]{0,1:T(8,128)(2,1)} %reshape.89) | copy-start | bytes 4718596
  131.4 48.0 %collective-permute-start.1 = (bf16[256,3072]{0,1:T(8,128)(2,1)}, bf16[256,3072]{0,1:T(8,128)(2,1)}, u32[]{:S(2)}, u32[]{:S(2)}) collective-permute-start(bf16[256,3072]{0,1:T(8,128)(2,1)} %collective-permute-done), channel_id=1, source_target_pairs={{0,8},{8,16},{16,24},{24,28},{28,20},{20,12},{12,4},{4,0},{1,9},{9... | collective-permute-start | bytes 4718600 | tf_op jit(solution)/shard_map/ppermute | solution.py:117
  132.9 52.9 %collective-permute-start.6 = (bf16[256,3072]{0,1:T(8,128)(2,1)}, bf16[256,3072]{0,1:T(8,128)(2,1)}, u32[]{:S(2)}, u32[]{:S(2)}) collective-permute-start(bf16[256,3072]{0,1:T(8,128)(2,1)} %collective-permute-done.2), channel_id=1, source_target_pairs={{0,4},{8,0},{16,8},{24,16},{28,24},{20,28},{12,20},{4,12},{1,5},{9... | collective-permute-start | bytes 4718600 | tf_op jit(solution)/shard_map/ppermute | solution.py:119
  138.8 39.3 %collective-permute-start.4 = (f32[2,256,256]{1,2,0:T(8,128)S(1)}, f32[2,256,256]{1,2,0:T(8,128)}, u32[]{:S(2)}, u32[]{:S(2)}) collective-permute-start(f32[2,256,256]{1,2,0:T(8,128)S(1)} %pad_maximum_fusion), channel_id=1, source_target_pairs={{0,4},{8,0},{16,8},{24,16},{28,24},{20,28},{12,20},{4,12},{1,5},{9... | collective-permute-start | bytes 1572872 | tf_op jit(solution)/shard_map/ppermute | solution.py:141
  181.9 12.4 %collective-permute-start.3 = (f32[1,256,256]{1,2,0:T(8,128)S(1)}, f32[1,256,256]{1,2,0:T(8,128)S(1)}, u32[]{:S(2)}, u32[]{:S(2)}) collective-permute-start(f32[1,256,256]{1,2,0:T(8,128)S(1)} %bitcast.111), channel_id=1, source_target_pairs={{0,12},{8,4},{16,0},{24,8},{28,16},{20,24},{12,28},{4,20},{1,13},{... | collective-permute-start | bytes 786440 | tf_op jit(solution)/shard_map/ppermute | solution.py:141
  185.2 15.6 %collective-permute-start.5 = (f32[2,256,256]{2,1,0:T(8,128)}, f32[2,256,256]{2,1,0:T(8,128)S(1)}, u32[]{:S(2)}, u32[]{:S(2)}) collective-permute-start(f32[2,256,256]{2,1,0:T(8,128)} %pad_maximum_fusion.1), channel_id=1, source_target_pairs={{0,8},{8,16},{16,24},{24,28},{28,20},{20,12},{12,4},{4,0},{1,9},{9... | collective-permute-start | bytes 1572872 | tf_op jit(solution)/shard_map/ppermute | solution.py:141
  189.0 17.7 %collective-permute-start.7 = (f32[1,256,256]{2,1,0:T(8,128)}, f32[1,256,256]{2,1,0:T(8,128)}, u32[]{:S(2)}, u32[]{:S(2)}) collective-permute-start(f32[1,256,256]{2,1,0:T(8,128)} %convolution_bitcast_fusion), channel_id=1, source_target_pairs={{0,16},{8,24},{16,28},{24,20},{28,12},{20,4},{12,0},{4,8},{1,17},{... | collective-permute-start | bytes 786440 | tf_op jit(solution)/shard_map/ppermute | solution.py:141
  194.3 0.7 copy-start.3
  207.7 2.9 %collective-permute-start.8 = (f32[2,512,256]{2,1,0:T(8,128)S(1)}, f32[2,512,256]{2,1,0:T(8,128)}, u32[]{:S(2)}, u32[]{:S(2)}) collective-permute-start(f32[2,512,256]{2,1,0:T(8,128)S(1)} %dynamic-slice_bitcast_fusion), channel_id=1, source_target_pairs={{0,1},{1,0},{2,3},{3,2},{4,5},{5,4},{6,7},{7,6},{8,9},{9,8},{10,11... | collective-permute-start | bytes 3145736 | tf_op jit(solution)/shard_map/ppermute | solution.py:59
  212.0 14.0 %collective-permute-start.9 = (f32[512,256]{1,0:T(8,128)S(1)}, f32[512,256]{1,0:T(8,128)S(1)}, u32[]{:S(2)}, u32[]{:S(2)}) collective-permute-start(f32[512,256]{1,0:T(8,128)S(1)} %dynamic-slice_bitcast_fusion.1), channel_id=1, source_target_pairs={{0,2},{1,3},{2,0},{3,1},{4,6},{5,7},{6,4},{7,5},{8,10},{9,11},{10,... | collective-permute-start | bytes 1572872 | tf_op jit(solution)/shard_map/ppermute | solution.py:59

commit v10 on v9

--- a/solution.py
+++ b/solution.py
@@ -93,19 +93,27 @@
         half = half.reshape(aux_dev, n_mu, NB, n_occ)
         half = jnp.where(row_live[None, :, :, None], half, 0.0).astype(jnp.bfloat16)
         half = half.reshape(aux_dev, n_mu, NB * n_occ)
-        regrouped = lax.all_to_all(half, "grp", split_axis=1, concat_axis=0, tiled=True)
-        n_aux = regrouped.shape[0]
-        mu_dev = regrouped.shape[1]
-        regrouped = regrouped.reshape(n_aux, mu_dev, NB, n_occ)
-        orbital = jnp.einsum(
-            "pq,qmai->mapi", metric[0], regrouped, preferred_element_type=jnp.float32
-        ).astype(jnp.bfloat16)
-        rows = mu_dev * NB
-        orbital = orbital.reshape(rows, n_aux * n_occ)
         me = lax.axis_index("grp")
         pos = jnp.asarray(pos_of)[me]
         ring_c = jnp.asarray(ring_arr)
-
+        mu_dev = n_mu // n
+        pieces = []
+        for s in range(n):
+            dest = ring_c[(pos + s) % n]
+            piece = lax.dynamic_slice_in_dim(half, dest * mu_dev, mu_dev, axis=1)
+            if s:
+                piece = lax.ppermute(piece, "grp", shifted(s))
+            pieces.append(piece)
+        stacked = jnp.stack(pieces).reshape(n, aux_dev, mu_dev, NB, n_occ)
+        srcs = ring_c[(pos - jnp.arange(n, dtype=jnp.int32)) % n]
+        cols = (srcs[:, None] * aux_dev + jnp.arange(aux_dev, dtype=jnp.int32)[None, :]).reshape(-1)
+        factor = jnp.take(metric[0], cols, axis=1).reshape(-1, n, aux_dev)
+        orbital = jnp.einsum(
+            "psq,sqmai->mapi", factor, stacked, preferred_element_type=jnp.float32
+        ).astype(jnp.bfloat16)
+        n_aux = n * aux_dev
+        rows = mu_dev * NB
+        orbital = orbital.reshape(rows, n_aux * n_occ)
         def start_of(off):
             return ring_c[(pos + off) % n] * rows
 

time: 228 us -> 271 us (1.19)
  blocking collectives: 44.1 us -> 0 us
  local copies, waits for them, and re-layouts: 44 us -> 84 us
  starting transfers between devices: 12 us -> 40.5 us
  between operations: 12.2 us -> 19.8 us
  waiting for transfers between devices: 87.2 us -> 93.6 us
    another operation x0 -> x17, local copies, waits for them, and re-layouts: none -> 47 us  [body(): stacked = jnp.stack(pieces).reshape(n, aux_dev, mu_dev, NB, n_occ)]
    all_to_all x1 -> x0, blocking collectives: 44.1 us -> none  [body(): lax.all_to_all(half, 'grp', split_axis=1, concat_axis=0, tiled=True)]
    ppermute x0 -> x7, starting transfers between devices: none -> 31.2 us  [body(): piece = lax.ppermute(piece, 'grp', shifted(s))]
    reshape x2 -> x0, local copies, waits for them, and re-layouts: 11.8 us -> none  [body(): regrouped = regrouped.reshape(n_aux, mu_dev, NB, n_occ)]
    ppermute x2, waiting for transfers between devices: 24.1 us -> 31.2 us  [body(): fwd = lax.ppermute(fwd, 'grp', shifted(1))]
    ppermute x4, starting transfers between devices: 6.22 us -> 3.28 us  [body(): got = lax.ppermute(stack, 'grp', shifted(s))]
    unnamed x15 -> x16, local copies, waits for them, and re-layouts: 8.08 us -> 8.18 us
  transfers between devices with their start and end apart: 10 -> 17, of which waited for: 7 -> 6; matrix products, arithmetic and copies ran while one was open for 7% -> 16% of each run, Pallas kernels for 0% -> 0%
where the time goes in v10:
time: 271 us; the launch traced here: 268 us
  waiting for transfers between devices  93.6 us (35%)
  local copies, waits for them, and re-layouts  84 us (31%)
  starting transfers between devices  40.5 us (15%)
  matrix products  22.9 us (8%)
  between operations  19.8 us (7%)
  other arithmetic  7.73 us (3%)
    ppermute x4, waiting for transfers between devices, body(): got = lax.ppermute(stack, 'grp', shifted(s))  47.1 us
    another operation x17, local copies, waits for them, and re-layouts, body(): stacked = jnp.stack(pieces).reshape(n, aux_dev, mu_dev, NB, n_occ)  47 us
    ppermute x7, starting transfers between devices, body(): piece = lax.ppermute(piece, 'grp', shifted(s))  31.2 us
    ppermute x2, waiting for transfers between devices, body(): fwd = lax.ppermute(fwd, 'grp', shifted(1))  31.2 us
    ppermute x2, waiting for transfers between devices, scatter_sum(): got = lax.ppermute(send, 'rep', [(i, i ^ d) for i in range(n_rep)])  15.2 us
    dot_general x5, matrix products, prod(): return jnp.dot(held[xo], held[yo].T, preferred_element_type=jnp.float32)  10.8 us
    unnamed x16, local copies, waits for them, and re-layouts  8.18 us
    dot_general x1, matrix products, body(): jnp.einsum('qkmtl,mklc->qmtc', tc, weight, preferred_element_type=jnp.flo...  7.16 us
  transfers between devices with their start and end apart: 17, of which 6 were waited for; matrix products, arithmetic and copies ran while one was open for 16% of the time, Pallas kernels for 0%

profile of v10, /device:TPU:0, one launch (start us, length us, event | category | flops | bytes accessed | tf_op | source)
XLA Modules:
  0.0 268.5 jit_solution(4401222044119097543)
XLA Ops:
  0.0 1.2 dynamic_slice.81
  10.5 1.8 fusion.31
  17.3 0.7 compare_select_fusion.1
  18.2 1.3 reshape.211
  19.7 0.7 iota_compare_fusion.4
  20.4 1.6 gather_fusion
  22.0 1.0 gather_fusion.1
  23.2 7.4 %copy.55 = bf16[192,8,32,128]{3,2,1,0:T(8,128)(2,1)S(1)} copy(bf16[192,8,32,128]{3,1,2,0:T(8,128)(2,1)} %bitcast.131) | data formatting | bytes 25165824
  30.7 1.7 broadcast_select_fusion
  32.4 7.2 %fusion.13 = bf16[8,32,32,96]{3,2,0,1:T(8,128)(2,1)} fusion(bf16[8,6,32,32,128]{4,3,2,1,0:T(8,128)(2,1)S(1)} %bitcast.132, bf16[32,6,64,48]{2,3,1,0:T(8,128)(2,1)} %broadcast_select_fusion), kind=kOutput, calls=%fused_computation.20 | convolution fusion | flops 1226833920 | bytes 15335424 | tf_op jit(solution)/shard_map/qkmtl,mklc->qmtc/dot_general | solution.py:92
  39.5 4.2 %reshape.213 = bf16[8,32,3072]{2,0,1:T(8,128)(2,1)S(1)} reshape(bf16[8,32,32,96]{3,2,0,1:T(8,128)(2,1)} %fusion.13) | data formatting | bytes 3145728 | tf_op jit(solution)/shard_map/reshape | solution.py:93
  44.1 0.8 broadcast_in_dim.60
  45.5 0.9 constant_dynamic-slice_fusion
  46.4 3.0 %collective-permute-start = (bf16[8,4,3072]{2,0,1:T(8,128)(2,1)S(1)}, bf16[8,4,3072]{2,0,1:T(8,128)(2,1)S(1)}, u32[]{:S(2)}, u32[]{:S(2)}) collective-permute-start(bf16[8,4,3072]{2,0,1:T(8,128)(2,1)S(1)} %get-tuple-element.11), channel_id=1, source_target_pairs={{0,8},{8,16},{16,24},{24,28},{28,20},{20,12},{12,4},{4,0},{1,9},{9... | collective-permute-start | bytes 589832 | tf_op jit(solution)/shard_map/ppermute | solution.py:105
  49.5 2.6 collective-permute-start.1
  52.1 1.3 collective-permute-start.2
  53.3 2.4 collective-permute-start.3
  56.1 0.7 fusion.25
  56.8 0.6 gather_fusion.2
  57.7 16.3 %collective-permute-start.5 = (bf16[8,4,3072]{2,0,1:T(8,128)(2,1)S(1)}, bf16[8,4,3072]{2,0,1:T(8,128)(2,1)}, u32[]{:S(2)}, u32[]{:S(2)}) collective-permute-start(bf16[8,4,3072]{2,0,1:T(8,128)(2,1)S(1)} %get-tuple-element.6), channel_id=1, source_target_pairs={{0,12},{8,4},{16,0},{24,8},{28,16},{20,24},{12,28},{4,20},{1,13},{... | collective-permute-start | bytes 589832 | tf_op jit(solution)/shard_map/ppermute | solution.py:105
  74.0 5.3 %collective-permute-start.6 = (bf16[8,4,3072]{2,0,1:T(8,128)(2,1)S(1)}, bf16[8,4,3072]{2,0,1:T(8,128)(2,1)}, u32[]{:S(2)}, u32[]{:S(2)}) collective-permute-start(bf16[8,4,3072]{2,0,1:T(8,128)(2,1)S(1)} %get-tuple-element.5), channel_id=1, source_target_pairs={{0,4},{8,0},{16,8},{24,16},{28,24},{20,28},{12,20},{4,12},{1,5},{9... | collective-permute-start | bytes 589832 | tf_op jit(solution)/shard_map/ppermute | solution.py:105
  79.3 0.5 stack.51
  79.8 1.1 copy.36
  81.0 0.7 copy.44
  81.7 0.6 gather_fusion.3
  82.9 1.1 copy.37
  84.0 0.5 stack.53
  84.6 1.1 copy.38
  85.7 2.2 stack.54
  88.0 2.4 copy.39
  90.5 2.2 stack.55
  92.7 3.0 %copy.40 = bf16[1,8,4,64,48]{3,0,1,4,2:T(2,128)(2,1)} copy(bf16[1,8,4,64,48]{4,3,1,2,0:T(8,128)(2,1)} %stack.55) | data formatting | bytes 393216 | tf_op jit(solution)/shard_map/stack | solution.py:107
  95.7 2.2 stack.56
  98.0 3.0 %copy.41 = bf16[1,8,4,64,48]{3,0,1,4,2:T(2,128)(2,1)} copy(bf16[1,8,4,64,48]{4,3,1,2,0:T(8,128)(2,1)} %stack.56) | data formatting | bytes 393216 | tf_op jit(solution)/shard_map/stack | solution.py:107
  101.0 2.2 stack.57
  103.2 3.1 %copy.42 = bf16[1,8,4,64,48]{3,0,1,4,2:T(2,128)(2,1)} copy(bf16[1,8,4,64,48]{4,3,1,2,0:T(8,128)(2,1)} %stack.57) | data formatting | bytes 393216 | tf_op jit(solution)/shard_map/stack | solution.py:107
  106.3 2.2 stack.58
  108.6 3.0 %copy.43 = bf16[1,8,4,64,48]{3,0,1,4,2:T(2,128)(2,1)} copy(bf16[1,8,4,64,48]{4,3,1,2,0:T(8,128)(2,1)} %stack.58) | data formatting | bytes 393216 | tf_op jit(solution)/shard_map/stack | solution.py:107
  111.6 16.2 %stack.59 = bf16[8,8,4,64,48]{3,0,1,4,2:T(8,128)(2,1)} concatenate(bf16[1,8,4,64,48]{3,0,1,4,2:T(2,128)(2,1)S(1)} %copy.36, bf16[1,8,4,64,48]{3,0,1,4,2:T(2,128)(2,1)S(1)} %copy.37, bf16[1,8,4,64,48]{3,0,1,4,2:T(2,128)(2,1)S(1)} %copy.38, bf16[1,8,4,64,48]{3,0,1,4,2:T(2,128)(2,1)S(1)} %copy.39, bf16[1,8,4,64,48]{3,0,1,4,2:T(2,128)(2,1)} %copy.40, ...), dimensions={0} | concatenate | bytes 3145728 | tf_op jit(solution)/shard_map/stack | solution.py:107
  127.8 4.9 %fusion.11 = bf16[4,64,64,48]{2,1,3,0:T(8,128)(2,1)} fusion(bf16[8,8,4,64,48]{3,0,1,4,2:T(8,128)(2,1)} %stack.59, bf16[64,8,8]{0,2,1:T(8,128)(2,1)S(1)} %bitcast.142, pred[8,8]{0,1:T(8,128)(4,1)S(1)} %copy-done.5), kind=kOutput, calls=%fused_computation.16 | convolution fusion | flops 101453824 | bytes 3153984 | tf_op jit(solution)/shard_map/psq,sqmai->mapi/dot_general | solution.py:111
  132.7 6.3 %copy.47 = bf16[4,64,64,48]{1,0,3,2:T(4,128)(2,1)S(1)} copy(bf16[4,64,64,48]{2,1,3,0:T(8,128)(2,1)} %fusion.11) | data formatting | bytes 3145728 | tf_op jit(solution)/shard_map/convert_element_type | solution.py:113
  139.0 3.0 %reshape.214 = bf16[256,3072]{0,1:T(8,128)(2,1)} reshape(bf16[4,64,64,48]{1,0,3,2:T(4,128)(2,1)S(1)} %copy.47) | data formatting | bytes 3145728 | tf_op jit(solution)/shard_map/reshape | solution.py:116
  142.0 2.0 collective-permute-start.9
  145.4 31.2 %collective-permute-done.7 = bf16[256,3072]{0,1:T(8,128)(2,1)} collective-permute-done((bf16[256,3072]{0,1:T(8,128)(2,1)}, bf16[256,3072]{0,1:T(8,128)(2,1)}, u32[]{:S(2)}, u32[]{:S(2)}) %collective-permute-start.7) | collective-permute-done | bytes 1572896 | tf_op jit(solution)/shard_map/ppermute | solution.py:125
  176.7 0.6 convolution_dynamic-update-slice_fusion
  177.4 2.3 collective-permute-start.13
  179.7 2.0 constant_dynamic-update-slice_fusion.3
  181.7 2.5 fusion.33
  188.1 34.1 %collective-permute-done.11 = f32[2,256,256]{1,2,0:T(8,128)} collective-permute-done((f32[2,256,256]{1,2,0:T(8,128)S(1)}, f32[2,256,256]{1,2,0:T(8,128)}, u32[]{:S(2)}, u32[]{:S(2)}) %collective-permute-start.11) | collective-permute-done | bytes 524320 | tf_op jit(solution)/shard_map/ppermute | solution.py:149
  222.2 1.1 slice_bitcast_fusion.2
  223.5 2.5 fusion.32
  226.0 0.8 pad_maximum_fusion.1
  227.1 2.6 collective-permute-start.10
  229.8 3.2 %convolution_bitcast_fusion = f32[1,256,256]{2,1,0:T(8,128)} fusion(bf16[256,3072]{0,1:T(8,128)(2,1)} %collective-permute-done.8, bf16[256,3072]{0,1:T(8,128)(2,1)} %collective-permute-done.13), kind=kOutput, calls=%fused_computation.22 | convolution fusion | flops 402653184 | bytes 3407872 | tf_op jit(solution)/shard_map/dot_general | solution.py:131
  233.2 9.8 %collective-permute-done.10 = f32[1,256,256]{1,2,0:T(8,128)S(1)} collective-permute-done((f32[1,256,256]{1,2,0:T(8,128)S(1)}, f32[1,256,256]{1,2,0:T(8,128)S(1)}, u32[]{:S(2)}, u32[]{:S(2)}) %collective-permute-start.10) | collective-permute-done | bytes 262176 | tf_op jit(solution)/shard_map/ppermute | solution.py:149
  243.0 0.7 copy-done.3
  243.7 1.1 copy.48
  245.0 3.3 %collective-permute-done.14 = f32[1,256,256]{2,1,0:T(8,128)} collective-permute-done((f32[1,256,256]{2,1,0:T(8,128)}, f32[1,256,256]{2,1,0:T(8,128)}, u32[]{:S(2)}, u32[]{:S(2)}) %collective-permute-start.14) | collective-permute-done | bytes 262176 | tf_op jit(solution)/shard_map/ppermute | solution.py:149
  248.2 1.0 bitcast_dynamic-update-slice_fusion
  249.4 2.7 %collective-permute-done.15 = f32[2,512,256]{2,1,0:T(8,128)} collective-permute-done((f32[2,512,256]{2,1,0:T(8,128)S(1)}, f32[2,512,256]{2,1,0:T(8,128)}, u32[]{:S(2)}, u32[]{:S(2)}) %collective-permute-start.15) | collective-permute-done | bytes 1048608 | tf_op jit(solution)/shard_map/ppermute | solution.py:59
  252.1 1.4 bitcast_add_fusion
  253.6 1.6 collective-permute-start.16
  255.1 12.5 %collective-permute-done.16 = f32[512,256]{1,0:T(8,128)S(1)} collective-permute-done((f32[512,256]{1,0:T(8,128)S(1)}, f32[512,256]{1,0:T(8,128)S(1)}, u32[]{:S(2)}, u32[]{:S(2)}) %collective-permute-start.16) | collective-permute-done | bytes 524320 | tf_op jit(solution)/shard_map/ppermute | solution.py:59
  267.6 0.9 bitcast_add_fusion.1
  (60 shorter events, 4.2 us)
Async XLA Ops:
  0.0 20.4 %copy-start = (s32[32]{0:T(128)S(1)}, s32[32]{0:T(128)}, u32[]{:S(2)}) copy-start(s32[32]{0:T(128)} %param.13) | copy-start | bytes 388
  22.0 1.1 copy-start.6
  45.5 11.3 %copy-start.1 = (s32[8]{0:T(128)S(1)}, s32[8]{0:T(128)}, u32[]{:S(2)}) copy-start(s32[8]{0:T(128)} %constant.201.clone) | copy-start | bytes 100
  45.5 35.5 %copy-start.4 = (bf16[1,64,64]{2,1,0:T(8,128)(2,1)S(1)}, bf16[1,64,64]{2,1,0:T(8,128)(2,1)}, u32[]{:S(2)}) copy-start(bf16[1,64,64]{2,1,0:T(8,128)(2,1)} %param.9) | copy-start | bytes 24580
  46.4 11.3 %collective-permute-start = (bf16[8,4,3072]{2,0,1:T(8,128)(2,1)S(1)}, bf16[8,4,3072]{2,0,1:T(8,128)(2,1)S(1)}, u32[]{:S(2)}, u32[]{:S(2)}) collective-permute-start(bf16[8,4,3072]{2,0,1:T(8,128)(2,1)S(1)} %get-tuple-element.11), channel_id=1, source_target_pairs={{0,8},{8,16},{16,24},{24,28},{28,20},{20,12},{12,4},{4,0},{1,9},{9... | collective-permute-start | bytes 589832 | tf_op jit(solution)/shard_map/ppermute | solution.py:105
  49.5 24.5 %collective-permute-start.1 = (bf16[8,4,3072]{2,0,1:T(8,128)(2,1)S(1)}, bf16[8,4,3072]{2,0,1:T(8,128)(2,1)S(1)}, u32[]{:S(2)}, u32[]{:S(2)}) collective-permute-start(bf16[8,4,3072]{2,0,1:T(8,128)(2,1)S(1)} %get-tuple-element.10), channel_id=1, source_target_pairs={{0,16},{8,24},{16,28},{24,20},{28,12},{20,4},{12,0},{4,8},{1,17},{... | collective-permute-start | bytes 589832 | tf_op jit(solution)/shard_map/ppermute | solution.py:105
  52.1 33.7 %collective-permute-start.2 = (bf16[8,4,3072]{2,0,1:T(8,128)(2,1)S(1)}, bf16[8,4,3072]{2,0,1:T(8,128)(2,1)}, u32[]{:S(2)}, u32[]{:S(2)}) collective-permute-start(bf16[8,4,3072]{2,0,1:T(8,128)(2,1)S(1)} %get-tuple-element.9), channel_id=1, source_target_pairs={{0,24},{8,28},{16,20},{24,12},{28,4},{20,0},{12,8},{4,16},{1,25},{... | collective-permute-start | bytes 589832 | tf_op jit(solution)/shard_map/ppermute | solution.py:105
  53.3 37.1 %collective-permute-start.3 = (bf16[8,4,3072]{2,0,1:T(8,128)(2,1)}, bf16[8,4,3072]{2,0,1:T(8,128)(2,1)}, u32[]{:S(2)}, u32[]{:S(2)}) collective-permute-start(bf16[8,4,3072]{2,0,1:T(8,128)(2,1)} %get-tuple-element.8), channel_id=1, source_target_pairs={{0,28},{8,20},{16,12},{24,4},{28,0},{20,8},{12,16},{4,24},{1,29},{... | collective-permute-start | bytes 589832 | tf_op jit(solution)/shard_map/ppermute | solution.py:105
  55.8 40.0 %collective-permute-start.4 = (bf16[8,4,3072]{2,0,1:T(8,128)(2,1)}, bf16[8,4,3072]{2,0,1:T(8,128)(2,1)}, u32[]{:S(2)}, u32[]{:S(2)}) collective-permute-start(bf16[8,4,3072]{2,0,1:T(8,128)(2,1)} %get-tuple-element.7), channel_id=1, source_target_pairs={{0,20},{8,12},{16,4},{24,0},{28,8},{20,16},{12,24},{4,28},{1,21},{... | collective-permute-start | bytes 589832 | tf_op jit(solution)/shard_map/ppermute | solution.py:105
  57.7 43.3 %collective-permute-start.5 = (bf16[8,4,3072]{2,0,1:T(8,128)(2,1)S(1)}, bf16[8,4,3072]{2,0,1:T(8,128)(2,1)}, u32[]{:S(2)}, u32[]{:S(2)}) collective-permute-start(bf16[8,4,3072]{2,0,1:T(8,128)(2,1)S(1)} %get-tuple-element.6), channel_id=1, source_target_pairs={{0,12},{8,4},{16,0},{24,8},{28,16},{20,24},{12,28},{4,20},{1,13},{... | collective-permute-start | bytes 589832 | tf_op jit(solution)/shard_map/ppermute | solution.py:105
  74.0 32.3 %collective-permute-start.6 = (bf16[8,4,3072]{2,0,1:T(8,128)(2,1)S(1)}, bf16[8,4,3072]{2,0,1:T(8,128)(2,1)}, u32[]{:S(2)}, u32[]{:S(2)}) collective-permute-start(bf16[8,4,3072]{2,0,1:T(8,128)(2,1)S(1)} %get-tuple-element.5), channel_id=1, source_target_pairs={{0,4},{8,0},{16,8},{24,16},{28,24},{20,28},{12,20},{4,12},{1,5},{9... | collective-permute-start | bytes 589832 | tf_op jit(solution)/shard_map/ppermute | solution.py:105
  111.6 16.2 %copy-start.5 = (pred[8,8]{0,1:T(8,128)(4,1)S(1)}, pred[8,8]{0,1:T(8,128)(4,1)}, u32[]{:S(2)}) copy-start(pred[8,8]{0,1:T(8,128)(4,1)} %copy.44) | copy-start | bytes 196
  142.0 34.6 %collective-permute-start.7 = (bf16[256,3072]{0,1:T(8,128)(2,1)}, bf16[256,3072]{0,1:T(8,128)(2,1)}, u32[]{:S(2)}, u32[]{:S(2)}) collective-permute-start(bf16[256,3072]{0,1:T(8,128)(2,1)} %reshape.214), channel_id=1, source_target_pairs={{0,8},{8,16},{16,24},{24,28},{28,20},{20,12},{12,4},{4,0},{1,9},{9... | collective-permute-start | bytes 4718600 | tf_op jit(solution)/shard_map/ppermute | solution.py:125
  142.0 35.3 %collective-permute-start.9 = (bf16[256,3072]{0,1:T(8,128)(2,1)}, bf16[256,3072]{0,1:T(8,128)(2,1)}, u32[]{:S(2)}, u32[]{:S(2)}) collective-permute-start(bf16[256,3072]{0,1:T(8,128)(2,1)} %reshape.214), channel_id=1, source_target_pairs={{0,4},{8,0},{16,8},{24,16},{28,24},{20,28},{12,20},{4,12},{1,5},{9... | collective-permute-start | bytes 4718600 | tf_op jit(solution)/shard_map/ppermute | solution.py:127
  145.4 31.4 %copy-start.2 = (bf16[256,3072]{0,1:T(8,128)(2,1)S(1)}, bf16[256,3072]{0,1:T(8,128)(2,1)}, u32[]{:S(2)}) copy-start(bf16[256,3072]{0,1:T(8,128)(2,1)} %reshape.214) | copy-start | bytes 4718596
  176.6 46.9 %collective-permute-start.8 = (bf16[256,3072]{0,1:T(8,128)(2,1)}, bf16[256,3072]{0,1:T(8,128)(2,1)}, u32[]{:S(2)}, u32[]{:S(2)}) collective-permute-start(bf16[256,3072]{0,1:T(8,128)(2,1)} %collective-permute-done.7), channel_id=1, source_target_pairs={{0,8},{8,16},{16,24},{24,28},{28,20},{20,12},{12,4},{4,0},{1,9},{9... | collective-permute-start | bytes 4718600 | tf_op jit(solution)/shard_map/ppermute | solution.py:125
  177.4 52.4 %collective-permute-start.13 = (bf16[256,3072]{0,1:T(8,128)(2,1)}, bf16[256,3072]{0,1:T(8,128)(2,1)}, u32[]{:S(2)}, u32[]{:S(2)}) collective-permute-start(bf16[256,3072]{0,1:T(8,128)(2,1)} %collective-permute-done.9), channel_id=1, source_target_pairs={{0,4},{8,0},{16,8},{24,16},{28,24},{20,28},{12,20},{4,12},{1,5},{9... | collective-permute-start | bytes 4718600 | tf_op jit(solution)/shard_map/ppermute | solution.py:127
  184.2 37.9 %collective-permute-start.11 = (f32[2,256,256]{1,2,0:T(8,128)S(1)}, f32[2,256,256]{1,2,0:T(8,128)}, u32[]{:S(2)}, u32[]{:S(2)}) collective-permute-start(f32[2,256,256]{1,2,0:T(8,128)S(1)} %pad_maximum_fusion), channel_id=1, source_target_pairs={{0,4},{8,0},{16,8},{24,16},{28,24},{20,28},{12,20},{4,12},{1,5},{9... | collective-permute-start | bytes 1572872 | tf_op jit(solution)/shard_map/ppermute | solution.py:149
  226.8 18.1 %collective-permute-start.12 = (f32[2,256,256]{2,1,0:T(8,128)}, f32[2,256,256]{2,1,0:T(8,128)S(1)}, u32[]{:S(2)}, u32[]{:S(2)}) collective-permute-start(f32[2,256,256]{2,1,0:T(8,128)} %pad_maximum_fusion.1), channel_id=1, source_target_pairs={{0,8},{8,16},{16,24},{24,28},{28,20},{20,12},{12,4},{4,0},{1,9},{9... | collective-permute-start | bytes 1572872 | tf_op jit(solution)/shard_map/ppermute | solution.py:149
  227.1 15.9 %collective-permute-start.10 = (f32[1,256,256]{1,2,0:T(8,128)S(1)}, f32[1,256,256]{1,2,0:T(8,128)S(1)}, u32[]{:S(2)}, u32[]{:S(2)}) collective-permute-start(f32[1,256,256]{1,2,0:T(8,128)S(1)} %bitcast.140), channel_id=1, source_target_pairs={{0,12},{8,4},{16,0},{24,8},{28,16},{20,24},{12,28},{4,20},{1,13},{... | collective-permute-start | bytes 786440 | tf_op jit(solution)/shard_map/ppermute | solution.py:149
  232.9 15.3 %collective-permute-start.14 = (f32[1,256,256]{2,1,0:T(8,128)}, f32[1,256,256]{2,1,0:T(8,128)}, u32[]{:S(2)}, u32[]{:S(2)}) collective-permute-start(f32[1,256,256]{2,1,0:T(8,128)} %convolution_bitcast_fusion), channel_id=1, source_target_pairs={{0,16},{8,24},{16,28},{24,20},{28,12},{20,4},{12,0},{4,8},{1,17},{... | collective-permute-start | bytes 786440 | tf_op jit(solution)/shard_map/ppermute | solution.py:149
  243.0 0.7 copy-start.3
  249.3 2.9 %collective-permute-start.15 = (f32[2,512,256]{2,1,0:T(8,128)S(1)}, f32[2,512,256]{2,1,0:T(8,128)}, u32[]{:S(2)}, u32[]{:S(2)}) collective-permute-start(f32[2,512,256]{2,1,0:T(8,128)S(1)} %dynamic-slice_bitcast_fusion), channel_id=1, source_target_pairs={{0,1},{1,0},{2,3},{3,2},{4,5},{5,4},{6,7},{7,6},{8,9},{9,8},{10,11... | collective-permute-start | bytes 3145736 | tf_op jit(solution)/shard_map/ppermute | solution.py:59
  253.6 14.0 %collective-permute-start.16 = (f32[512,256]{1,0:T(8,128)S(1)}, f32[512,256]{1,0:T(8,128)S(1)}, u32[]{:S(2)}, u32[]{:S(2)}) collective-permute-start(f32[512,256]{1,0:T(8,128)S(1)} %dynamic-slice_bitcast_fusion.1), channel_id=1, source_target_pairs={{0,2},{1,3},{2,0},{3,1},{4,6},{5,7},{6,4},{7,5},{8,10},{9,11},{10,... | collective-permute-start | bytes 1572872 | tf_op jit(solution)/shard_map/ppermute | solution.py:59

commit v11 on v9

--- a/solution.py
+++ b/solution.py
@@ -96,10 +96,9 @@
         regrouped = lax.all_to_all(half, "grp", split_axis=1, concat_axis=0, tiled=True)
         n_aux = regrouped.shape[0]
         mu_dev = regrouped.shape[1]
-        regrouped = regrouped.reshape(n_aux, mu_dev, NB, n_occ)
-        orbital = jnp.einsum(
-            "pq,qmai->mapi", metric[0], regrouped, preferred_element_type=jnp.float32
-        ).astype(jnp.bfloat16)
+        mixed = jnp.dot(metric[0], regrouped.reshape(n_aux, -1), preferred_element_type=jnp.float32)
+        mixed = mixed.astype(jnp.bfloat16).reshape(n_aux, mu_dev, NB, n_occ)
+        orbital = jnp.transpose(mixed, (1, 2, 0, 3))
         rows = mu_dev * NB
         orbital = orbital.reshape(rows, n_aux * n_occ)
         me = lax.axis_index("grp")

time: 228 us -> 219 us (0.961)
  local copies, waits for them, and re-layouts: 44 us -> 36.8 us
    reshape x2 -> x1, local copies, waits for them, and re-layouts: 11.8 us -> 5.33 us  [body(): mixed = mixed.astype(jnp.bfloat16).reshape(n_aux, mu_dev, NB, n_occ)]
    convert_element_type x1 -> x0, local copies, waits for them, and re-layouts: 6.35 us -> none  [body(): orbital = jnp.einsum('pq,qmai->mapi', metric[0], regrouped, preferred_ele...]
    transpose x0 -> x1, local copies, waits for them, and re-layouts: none -> 5.65 us  [body(): orbital = jnp.transpose(mixed, (1, 2, 0, 3))]
where the time goes in v11:
time: 219 us; the launch traced here: 218 us
  waiting for transfers between devices  87 us (40%)
  blocking collectives  44.1 us (20%)
  local copies, waits for them, and re-layouts  36.8 us (17%)
  matrix products  18.4 us (8%)
  starting transfers between devices  12.2 us (6%)
  between operations  12.1 us (6%)
  other arithmetic  6.91 us (3%)
    ppermute x4, waiting for transfers between devices, body(): got = lax.ppermute(stack, 'grp', shifted(s))  47.7 us
    all_to_all x1, blocking collectives, body(): lax.all_to_all(half, 'grp', split_axis=1, concat_axis=0, tiled=True)  44.1 us
    ppermute x2, waiting for transfers between devices, body(): fwd = lax.ppermute(fwd, 'grp', shifted(1))  24.1 us
    ppermute x2, waiting for transfers between devices, scatter_sum(): got = lax.ppermute(send, 'rep', [(i, i ^ d) for i in range(n_rep)])  15.2 us
    dot_general x5, matrix products, prod(): return jnp.dot(held[xo], held[yo].T, preferred_element_type=jnp.float32)  10.8 us
    unnamed x15, local copies, waits for them, and re-layouts  8.08 us
    dot_general x1, matrix products, body(): jnp.einsum('qkmtl,mklc->qmtc', tc, weight, preferred_element_type=jnp.flo...  7.1 us
    ppermute x4, starting transfers between devices, body(): got = lax.ppermute(stack, 'grp', shifted(s))  6.4 us
  transfers between devices with their start and end apart: 10, of which 7 were waited for; matrix products, arithmetic and copies ran while one was open for 7% of the time, Pallas kernels for 0%

profile of v11, /device:TPU:0, one launch (start us, length us, event | category | flops | bytes accessed | tf_op | source)
XLA Modules:
  0.0 217.5 jit_solution(16432820316852675105)
XLA Ops:
  0.0 0.7 compare_select_fusion
  0.7 0.1 copy.19
  0.8 0.1 reshape.97
  0.9 1.3 reshape.88
  2.3 0.2 copy.20
  2.4 0.7 iota_compare_fusion.4
  3.2 1.6 gather_fusion
  4.7 0.0 copy-start.5
  4.7 1.0 gather_fusion.1
  5.8 0.1 reshape.96
  5.9 0.1 iota_compare_fusion.3
  5.9 7.4 %copy.28 = bf16[192,8,32,128]{3,2,1,0:T(8,128)(2,1)S(1)} copy(bf16[192,8,32,128]{3,1,2,0:T(8,128)(2,1)} %bitcast.99) | data formatting | bytes 25165824
  13.3 0.1 fusion.20
  13.5 1.7 broadcast_select_fusion
  15.1 7.1 %fusion.13 = bf16[8,32,32,96]{3,2,0,1:T(8,128)(2,1)} fusion(bf16[8,6,32,32,128]{4,3,2,1,0:T(8,128)(2,1)S(1)} %bitcast.100, bf16[32,6,64,48]{2,3,1,0:T(8,128)(2,1)} %broadcast_select_fusion), kind=kOutput, calls=%fused_computation.18 | convolution fusion | flops 1226833920 | bytes 15335424 | tf_op jit(solution)/shard_map/qkmtl,mklc->qmtc/dot_general | solution.py:92
  22.2 4.2 %reshape.90 = bf16[8,32,3072]{2,0,1:T(8,128)(2,1)S(1)} reshape(bf16[8,32,32,96]{3,2,0,1:T(8,128)(2,1)} %fusion.13) | data formatting | bytes 3145728 | tf_op jit(solution)/shard_map/reshape | solution.py:93
  26.4 0.3 broadcast_in_dim.46
  26.8 0.8 broadcast_in_dim.47
  27.6 0.5 select_convert_fusion
  28.1 44.1 %all_to_all.15 = bf16[8,32,3072]{2,0,1:T(8,128)(2,1)S(1)} all-to-all(bf16[8,32,3072]{2,0,1:T(8,128)(2,1)S(1)} %select_convert_fusion), channel_id=1, replica_groups=mesh['grp'=8,'rep'=4] {'grp'}, dimensions={1} | all-to-all | bytes 3145728 | tf_op jit(solution)/shard_map/all_to_all | solution.py:96
  72.2 0.6 fusion
  72.7 5.3 %reshape.92 = bf16[64,4,64,48]{3,2,1,0:T(8,128)(2,1)} reshape(bf16[64,12288]{1,0:T(8,128)(2,1)S(1)} %fusion) | data formatting | bytes 3145728 | tf_op jit(solution)/shard_map/reshape | solution.py:100
  78.0 5.6 %copy.22 = bf16[4,64,64,48]{1,0,3,2:T(4,128)(2,1)S(1)} copy(bf16[4,64,64,48]{3,1,0,2:T(8,128)(2,1)} %bitcast.97) | data formatting | bytes 3145728 | tf_op jit(solution)/shard_map/transpose | solution.py:101
  83.7 0.0 copy-start.6
  83.7 0.0 copy-start.4
  83.7 3.0 %reshape.93 = bf16[256,3072]{0,1:T(8,128)(2,1)} reshape(bf16[4,64,64,48]{1,0,3,2:T(4,128)(2,1)S(1)} %copy.22) | data formatting | bytes 3145728 | tf_op jit(solution)/shard_map/reshape | solution.py:103
  86.7 1.1 collective-permute-start
  87.8 0.9 collective-permute-start.2
  88.8 0.6 dynamic_slice.41
  96.0 0.7 fusion.25
  97.9 24.1 %collective-permute-done = bf16[256,3072]{0,1:T(8,128)(2,1)} collective-permute-done((bf16[256,3072]{0,1:T(8,128)(2,1)}, bf16[256,3072]{0,1:T(8,128)(2,1)}, u32[]{:S(2)}, u32[]{:S(2)}) %collective-permute-start) | collective-permute-done | bytes 1572896 | tf_op jit(solution)/shard_map/ppermute | solution.py:116
  122.0 0.7 collective-permute-start.1
  122.8 0.1 broadcast_in_dim.45
  122.9 0.6 convolution_dynamic-update-slice_fusion
  123.6 0.0 collective-permute-done.2
  123.6 1.3 collective-permute-start.6
  124.9 2.0 constant_dynamic-update-slice_fusion.3
  126.9 2.5 %fusion.27 = f32[256,256]{1,0:T(8,128)S(1)} fusion(bf16[256,3072]{0,1:T(8,128)(2,1)} %collective-permute-done, bf16[256,3072]{0,1:T(8,128)(2,1)} %collective-permute-done.2), kind=kOutput, calls=%fused_computation.50 | convolution fusion | flops 402653184 | bytes 3407872 | tf_op jit(solution)/shard_map/dot_general | solution.py:122
  129.5 1.7 collective-permute-start.4
  135.1 33.7 %collective-permute-done.4 = f32[2,256,256]{1,2,0:T(8,128)} collective-permute-done((f32[2,256,256]{1,2,0:T(8,128)S(1)}, f32[2,256,256]{1,2,0:T(8,128)}, u32[]{:S(2)}, u32[]{:S(2)}) %collective-permute-start.4) | collective-permute-done | bytes 524320 | tf_op jit(solution)/shard_map/ppermute | solution.py:140
  168.7 1.1 slice_bitcast_fusion.2
  169.8 0.1 copy.24
  169.9 0.1 copy.25
  170.1 0.0 collective-permute-done.1
  170.1 2.5 %fusion.26 = f32[256,256]{1,0:T(8,128)S(1)} fusion(bf16[256,3072]{0,1:T(8,128)(2,1)} %collective-permute-done.1, bf16[256,3072]{0,1:T(8,128)(2,1)} %collective-permute-done.2), kind=kOutput, calls=%fused_computation.49 | convolution fusion | flops 402653184 | bytes 3407872 | tf_op jit(solution)/shard_map/dot_general | solution.py:122
  172.6 2.4 %collective-permute-start.3 = (f32[1,256,256]{1,2,0:T(8,128)S(1)}, f32[1,256,256]{1,2,0:T(8,128)S(1)}, u32[]{:S(2)}, u32[]{:S(2)}) collective-permute-start(f32[1,256,256]{1,2,0:T(8,128)S(1)} %bitcast.107), channel_id=1, source_target_pairs={{0,12},{8,4},{16,0},{24,8},{28,16},{20,24},{12,28},{4,20},{1,13},{... | collective-permute-start | bytes 786440 | tf_op jit(solution)/shard_map/ppermute | solution.py:140
  175.0 0.8 pad_maximum_fusion.1
  175.9 0.6 collective-permute-start.5
  176.5 0.0 collective-permute-done.6
  176.5 3.2 %convolution_bitcast_fusion = f32[1,256,256]{2,1,0:T(8,128)} fusion(bf16[256,3072]{0,1:T(8,128)(2,1)} %collective-permute-done.1, bf16[256,3072]{0,1:T(8,128)(2,1)} %collective-permute-done.6), kind=kOutput, calls=%fused_computation.20 | convolution fusion | flops 402653184 | bytes 3407872 | tf_op jit(solution)/shard_map/dot_general | solution.py:122
  179.6 1.7 collective-permute-start.7
  181.3 3.7 %collective-permute-done.3 = f32[1,256,256]{1,2,0:T(8,128)S(1)} collective-permute-done((f32[1,256,256]{1,2,0:T(8,128)S(1)}, f32[1,256,256]{1,2,0:T(8,128)S(1)}, u32[]{:S(2)}, u32[]{:S(2)}) %collective-permute-start.3) | collective-permute-done | bytes 262176 | tf_op jit(solution)/shard_map/ppermute | solution.py:140
  185.0 0.7 copy-done.3
  185.7 1.1 copy.23
  186.9 4.6 %collective-permute-done.5 = f32[2,256,256]{2,1,0:T(8,128)S(1)} collective-permute-done((f32[2,256,256]{2,1,0:T(8,128)}, f32[2,256,256]{2,1,0:T(8,128)S(1)}, u32[]{:S(2)}, u32[]{:S(2)}) %collective-permute-start.5) | collective-permute-done | bytes 524320 | tf_op jit(solution)/shard_map/ppermute | solution.py:140
  191.5 5.8 %collective-permute-done.7 = f32[1,256,256]{2,1,0:T(8,128)} collective-permute-done((f32[1,256,256]{2,1,0:T(8,128)}, f32[1,256,256]{2,1,0:T(8,128)}, u32[]{:S(2)}, u32[]{:S(2)}) %collective-permute-start.7) | collective-permute-done | bytes 262176 | tf_op jit(solution)/shard_map/ppermute | solution.py:140
  197.3 1.0 bitcast_dynamic-update-slice_fusion
  198.3 0.1 dynamic-slice_bitcast_fusion
  198.4 0.1 collective-permute-start.8
  198.5 2.7 %collective-permute-done.8 = f32[2,512,256]{2,1,0:T(8,128)} collective-permute-done((f32[2,512,256]{2,1,0:T(8,128)S(1)}, f32[2,512,256]{2,1,0:T(8,128)}, u32[]{:S(2)}, u32[]{:S(2)}) %collective-permute-start.8) | collective-permute-done | bytes 1048608 | tf_op jit(solution)/shard_map/ppermute | solution.py:59
  201.2 1.4 bitcast_add_fusion
  202.6 1.6 collective-permute-start.9
  204.2 12.4 %collective-permute-done.9 = f32[512,256]{1,0:T(8,128)S(1)} collective-permute-done((f32[512,256]{1,0:T(8,128)S(1)}, f32[512,256]{1,0:T(8,128)S(1)}, u32[]{:S(2)}, u32[]{:S(2)}) %collective-permute-start.9) | collective-permute-done | bytes 524320 | tf_op jit(solution)/shard_map/ppermute | solution.py:59
  216.7 0.9 bitcast_add_fusion.1
  (18 shorter events, 0.2 us)
Async XLA Ops:
  0.0 72.2 %copy-start = (bf16[1,64,64]{2,1,0:T(8,128)(2,1)S(1)}, bf16[1,64,64]{2,1,0:T(8,128)(2,1)}, u32[]{:S(2)}) copy-start(bf16[1,64,64]{2,1,0:T(8,128)(2,1)} %param.9) | copy-start | bytes 24580
  0.0 3.2 %copy-start.1 = (s32[32]{0:T(128)S(1)}, s32[32]{0:T(128)}, u32[]{:S(2)}) copy-start(s32[32]{0:T(128)} %param.13) | copy-start | bytes 388
  4.7 1.1 copy-start.5
  83.7 5.1 %copy-start.6 = (s32[8]{0:T(128)S(1)}, s32[8]{0:T(128)}, u32[]{:S(2)}) copy-start(s32[8]{0:T(128)} %constant.133.clone) | copy-start | bytes 100
  83.7 12.2 %copy-start.4 = (s32[8]{0:T(128)S(1)}, s32[8]{0:T(128)}, u32[]{:S(2)}) copy-start(s32[8]{0:T(128)} %constant.134.clone) | copy-start | bytes 100
  86.7 35.3 %collective-permute-start = (bf16[256,3072]{0,1:T(8,128)(2,1)}, bf16[256,3072]{0,1:T(8,128)(2,1)}, u32[]{:S(2)}, u32[]{:S(2)}) collective-permute-start(bf16[256,3072]{0,1:T(8,128)(2,1)} %reshape.93), channel_id=1, source_target_pairs={{0,8},{8,16},{16,24},{24,28},{28,20},{20,12},{12,4},{4,0},{1,9},{9... | collective-permute-start | bytes 4718600 | tf_op jit(solution)/shard_map/ppermute | solution.py:116
  87.8 35.7 %collective-permute-start.2 = (bf16[256,3072]{0,1:T(8,128)(2,1)}, bf16[256,3072]{0,1:T(8,128)(2,1)}, u32[]{:S(2)}, u32[]{:S(2)}) collective-permute-start(bf16[256,3072]{0,1:T(8,128)(2,1)} %reshape.93), channel_id=1, source_target_pairs={{0,4},{8,0},{16,8},{24,16},{28,24},{20,28},{12,20},{4,12},{1,5},{9... | collective-permute-start | bytes 4718600 | tf_op jit(solution)/shard_map/ppermute | solution.py:118
  97.9 25.0 %copy-start.2 = (bf16[256,3072]{0,1:T(8,128)(2,1)S(1)}, bf16[256,3072]{0,1:T(8,128)(2,1)}, u32[]{:S(2)}) copy-start(bf16[256,3072]{0,1:T(8,128)(2,1)} %reshape.93) | copy-start | bytes 4718596
  122.0 48.0 %collective-permute-start.1 = (bf16[256,3072]{0,1:T(8,128)(2,1)}, bf16[256,3072]{0,1:T(8,128)(2,1)}, u32[]{:S(2)}, u32[]{:S(2)}) collective-permute-start(bf16[256,3072]{0,1:T(8,128)(2,1)} %collective-permute-done), channel_id=1, source_target_pairs={{0,8},{8,16},{16,24},{24,28},{28,20},{20,12},{12,4},{4,0},{1,9},{9... | collective-permute-start | bytes 4718600 | tf_op jit(solution)/shard_map/ppermute | solution.py:116
  123.6 52.9 %collective-permute-start.6 = (bf16[256,3072]{0,1:T(8,128)(2,1)}, bf16[256,3072]{0,1:T(8,128)(2,1)}, u32[]{:S(2)}, u32[]{:S(2)}) collective-permute-start(bf16[256,3072]{0,1:T(8,128)(2,1)} %collective-permute-done.2), channel_id=1, source_target_pairs={{0,4},{8,0},{16,8},{24,16},{28,24},{20,28},{12,20},{4,12},{1,5},{9... | collective-permute-start | bytes 4718600 | tf_op jit(solution)/shard_map/ppermute | solution.py:118
  129.5 39.3 %collective-permute-start.4 = (f32[2,256,256]{1,2,0:T(8,128)S(1)}, f32[2,256,256]{1,2,0:T(8,128)}, u32[]{:S(2)}, u32[]{:S(2)}) collective-permute-start(f32[2,256,256]{1,2,0:T(8,128)S(1)} %pad_maximum_fusion), channel_id=1, source_target_pairs={{0,4},{8,0},{16,8},{24,16},{28,24},{20,28},{12,20},{4,12},{1,5},{9... | collective-permute-start | bytes 1572872 | tf_op jit(solution)/shard_map/ppermute | solution.py:140
  172.6 12.4 %collective-permute-start.3 = (f32[1,256,256]{1,2,0:T(8,128)S(1)}, f32[1,256,256]{1,2,0:T(8,128)S(1)}, u32[]{:S(2)}, u32[]{:S(2)}) collective-permute-start(f32[1,256,256]{1,2,0:T(8,128)S(1)} %bitcast.107), channel_id=1, source_target_pairs={{0,12},{8,4},{16,0},{24,8},{28,16},{20,24},{12,28},{4,20},{1,13},{... | collective-permute-start | bytes 786440 | tf_op jit(solution)/shard_map/ppermute | solution.py:140
  175.9 15.6 %collective-permute-start.5 = (f32[2,256,256]{2,1,0:T(8,128)}, f32[2,256,256]{2,1,0:T(8,128)S(1)}, u32[]{:S(2)}, u32[]{:S(2)}) collective-permute-start(f32[2,256,256]{2,1,0:T(8,128)} %pad_maximum_fusion.1), channel_id=1, source_target_pairs={{0,8},{8,16},{16,24},{24,28},{28,20},{20,12},{12,4},{4,0},{1,9},{9... | collective-permute-start | bytes 1572872 | tf_op jit(solution)/shard_map/ppermute | solution.py:140
  179.6 17.7 %collective-permute-start.7 = (f32[1,256,256]{2,1,0:T(8,128)}, f32[1,256,256]{2,1,0:T(8,128)}, u32[]{:S(2)}, u32[]{:S(2)}) collective-permute-start(f32[1,256,256]{2,1,0:T(8,128)} %convolution_bitcast_fusion), channel_id=1, source_target_pairs={{0,16},{8,24},{16,28},{24,20},{28,12},{20,4},{12,0},{4,8},{1,17},{... | collective-permute-start | bytes 786440 | tf_op jit(solution)/shard_map/ppermute | solution.py:140
  185.0 0.7 copy-start.3
  198.4 2.9 %collective-permute-start.8 = (f32[2,512,256]{2,1,0:T(8,128)S(1)}, f32[2,512,256]{2,1,0:T(8,128)}, u32[]{:S(2)}, u32[]{:S(2)}) collective-permute-start(f32[2,512,256]{2,1,0:T(8,128)S(1)} %dynamic-slice_bitcast_fusion), channel_id=1, source_target_pairs={{0,1},{1,0},{2,3},{3,2},{4,5},{5,4},{6,7},{7,6},{8,9},{9,8},{10,11... | collective-permute-start | bytes 3145736 | tf_op jit(solution)/shard_map/ppermute | solution.py:59
  202.6 14.0 %collective-permute-start.9 = (f32[512,256]{1,0:T(8,128)S(1)}, f32[512,256]{1,0:T(8,128)S(1)}, u32[]{:S(2)}, u32[]{:S(2)}) collective-permute-start(f32[512,256]{1,0:T(8,128)S(1)} %dynamic-slice_bitcast_fusion.1), channel_id=1, source_target_pairs={{0,2},{1,3},{2,0},{3,1},{4,6},{5,7},{6,4},{7,5},{8,10},{9,11},{10,... | collective-permute-start | bytes 1572872 | tf_op jit(solution)/shard_map/ppermute | solution.py:59

commit v12 on v9

--- a/solution.py
+++ b/solution.py
@@ -96,9 +96,9 @@
         regrouped = lax.all_to_all(half, "grp", split_axis=1, concat_axis=0, tiled=True)
         n_aux = regrouped.shape[0]
         mu_dev = regrouped.shape[1]
-        regrouped = regrouped.reshape(n_aux, mu_dev, NB, n_occ)
-        orbital = jnp.einsum(
-            "pq,qmai->mapi", metric[0], regrouped, preferred_element_type=jnp.float32
+        orbital = lax.dot_general(
+            regrouped.reshape(n_aux, mu_dev * NB, n_occ), metric[0], (((0,), (1,)), ((), ())),
+            preferred_element_type=jnp.float32,
         ).astype(jnp.bfloat16)
         rows = mu_dev * NB
         orbital = orbital.reshape(rows, n_aux * n_occ)

time: 228 us -> 219 us (0.961)
  local copies, waits for them, and re-layouts: 44 us -> 33.5 us
    convert_element_type x1 -> x0, local copies, waits for them, and re-layouts: 6.35 us -> none  [body(): orbital = jnp.einsum('pq,qmai->mapi', metric[0], regrouped, preferred_ele...]
    reshape x3 -> x2, local copies, waits for them, and re-layouts: 14.8 us -> 9.46 us  [body(): regrouped.reshape(n_aux, mu_dev * NB, n_occ)]
    dot_general x5, matrix products: 10.8 us -> 13.2 us  [prod(): return jnp.dot(held[xo], held[yo].T, preferred_element_type=jnp.float32)]
    unnamed x15 -> x13, local copies, waits for them, and re-layouts: 8.08 us -> 8.09 us
  transfers between devices with their start and end apart: 10 -> 10, of which waited for: 7 -> 7; matrix products, arithmetic and copies ran while one was open for 7% -> 8% of each run, Pallas kernels for 0% -> 0%
where the time goes in v12:
time: 219 us; the launch traced here: 218 us
  waiting for transfers between devices  87.2 us (40%)
  blocking collectives  44.1 us (20%)
  local copies, waits for them, and re-layouts  33.5 us (15%)
  matrix products  22 us (10%)
  starting transfers between devices  12.2 us (6%)
  between operations  11.7 us (5%)
  other arithmetic  6.92 us (3%)
    ppermute x4, waiting for transfers between devices, body(): got = lax.ppermute(stack, 'grp', shifted(s))  47.8 us
    all_to_all x1, blocking collectives, body(): lax.all_to_all(half, 'grp', split_axis=1, concat_axis=0, tiled=True)  44.1 us
    ppermute x2, waiting for transfers between devices, body(): fwd = lax.ppermute(fwd, 'grp', shifted(1))  24.2 us
    ppermute x2, waiting for transfers between devices, scatter_sum(): got = lax.ppermute(send, 'rep', [(i, i ^ d) for i in range(n_rep)])  15.2 us
    dot_general x5, matrix products, prod(): return jnp.dot(held[xo], held[yo].T, preferred_element_type=jnp.float32)  13.2 us
    reshape x2, local copies, waits for them, and re-layouts, body(): regrouped.reshape(n_aux, mu_dev * NB, n_occ)  9.46 us
    unnamed x13, local copies, waits for them, and re-layouts  8.09 us
    dot_general x1, matrix products, body(): jnp.einsum('qkmtl,mklc->qmtc', tc, weight, preferred_element_type=jnp.flo...  7.1 us
  transfers between devices with their start and end apart: 10, of which 7 were waited for; matrix products, arithmetic and copies ran while one was open for 8% of the time, Pallas kernels for 0%

profile of v12, /device:TPU:0, one launch (start us, length us, event | category | flops | bytes accessed | tf_op | source)
XLA Modules:
  0.0 217.5 jit_solution(16980053513620754093)
XLA Ops:
  0.0 0.7 compare_select_fusion
  0.7 0.1 copy.19
  0.8 0.1 reshape.93
  0.9 1.3 reshape.85
  2.3 0.2 copy.20
  2.4 0.7 iota_compare_fusion.4
  3.2 1.6 gather_fusion
  4.7 0.0 copy-start.4
  4.7 1.0 gather_fusion.1
  5.8 0.1 reshape.92
  5.9 0.1 iota_compare_fusion.3
  5.9 7.4 %copy.29 = bf16[192,8,32,128]{3,2,1,0:T(8,128)(2,1)S(1)} copy(bf16[192,8,32,128]{3,1,2,0:T(8,128)(2,1)} %bitcast.97) | data formatting | bytes 25165824
  13.3 0.1 fusion.20
  13.4 1.7 broadcast_select_fusion
  15.1 7.1 %fusion.12 = bf16[8,32,32,96]{3,2,0,1:T(8,128)(2,1)} fusion(bf16[8,6,32,32,128]{4,3,2,1,0:T(8,128)(2,1)S(1)} %bitcast.98, bf16[32,6,64,48]{2,3,1,0:T(8,128)(2,1)} %broadcast_select_fusion), kind=kOutput, calls=%fused_computation.16 | convolution fusion | flops 1226833920 | bytes 15335424 | tf_op jit(solution)/shard_map/qkmtl,mklc->qmtc/dot_general | solution.py:92
  22.2 4.2 %reshape.87 = bf16[8,32,3072]{2,0,1:T(8,128)(2,1)S(1)} reshape(bf16[8,32,32,96]{3,2,0,1:T(8,128)(2,1)} %fusion.12) | data formatting | bytes 3145728 | tf_op jit(solution)/shard_map/reshape | solution.py:93
  26.4 0.3 broadcast_in_dim.46
  26.8 0.8 broadcast_in_dim.47
  27.6 0.5 select_convert_fusion
  28.1 44.1 %all_to_all.15 = bf16[8,32,3072]{2,0,1:T(8,128)(2,1)S(1)} all-to-all(bf16[8,32,3072]{2,0,1:T(8,128)(2,1)S(1)} %select_convert_fusion), channel_id=1, replica_groups=mesh['grp'=8,'rep'=4] {'grp'}, dimensions={1} | all-to-all | bytes 3145728 | tf_op jit(solution)/shard_map/all_to_all | solution.py:96
  72.2 1.2 copy.22
  73.4 5.2 %reshape.88 = bf16[64,256,48]{2,1,0:T(8,128)(2,1)} reshape(bf16[8,8,4,3072]{3,2,1,0:T(4,128)(2,1)S(1)} %copy.22) | data formatting | bytes 3145728 | tf_op jit(solution)/shard_map/reshape | solution.py:100
  78.6 4.3 %copy.23 = bf16[64,256,48]{1,0,2:T(8,128)(2,1)S(1)} copy(bf16[64,256,48]{2,1,0:T(8,128)(2,1)} %reshape.88) | data formatting | bytes 3145728 | tf_op jit(solution)/shard_map/reshape | solution.py:100
  82.9 0.0 copy-start.5
  82.9 0.0 copy-start.3
  82.9 1.7 convolution_convert_fusion
  84.6 1.1 collective-permute-start
  85.7 0.9 collective-permute-start.2
  86.6 0.6 dynamic_slice.41
  93.8 0.7 fusion.25
  95.7 24.2 %collective-permute-done = bf16[256,3072]{0,1:T(8,128)(2,1)} collective-permute-done((bf16[256,3072]{0,1:T(8,128)(2,1)}, bf16[256,3072]{0,1:T(8,128)(2,1)}, u32[]{:S(2)}, u32[]{:S(2)}) %collective-permute-start) | collective-permute-done | bytes 1572896 | tf_op jit(solution)/shard_map/ppermute | solution.py:117
  119.9 0.8 collective-permute-start.1
  120.7 0.1 broadcast_in_dim.45
  120.8 2.6 %fusion.17 = f32[2048,256]{1,0:T(8,128)S(1)} fusion(f32[2048,256]{1,0:T(8,128)S(1)} %broadcast_in_dim.45, s32[]{:T(128)S(6)} %select_n.132, bf16[256,48,64]{0,2,1:T(8,128)(2,1)} %convolution_convert_fusion), kind=kOutput, calls=%fused_computation.20 | convolution fusion | flops 402653184 | bytes 3407876 | tf_op jit(solution)/shard_map/dot_general | solution.py:123
  123.4 0.0 collective-permute-done.2
  123.4 1.5 collective-permute-start.6
  124.9 2.5 %constant_dynamic-update-slice_fusion.3 = (f32[2048,256]{1,0:T(8,128)S(1)}, f32[256,256]{1,0:T(8,128)S(1)}) fusion(f32[2048,256]{1,0:T(8,128)S(1)} %fusion.17, s32[]{:T(128)S(6)} %select_n.135, bf16[256,3072]{0,1:T(8,128)(2,1)} %collective-permute-done, bf16[256,3072]{0,1:T(8,128)(2,1)} %bitcast.15), kind=kOutput, calls=%fused_computation.44 | convolution fusion | flops 402653184 | bytes 3670020 | tf_op jit(solution)/shard_map/dot_general | solution.py:123
  127.4 2.5 %fusion.27 = f32[256,256]{1,0:T(8,128)S(1)} fusion(bf16[256,3072]{0,1:T(8,128)(2,1)} %collective-permute-done, bf16[256,3072]{0,1:T(8,128)(2,1)} %collective-permute-done.2), kind=kOutput, calls=%fused_computation.50 | convolution fusion | flops 402653184 | bytes 3407872 | tf_op jit(solution)/shard_map/dot_general | solution.py:123
  129.9 1.5 collective-permute-start.4
  135.0 33.7 %collective-permute-done.4 = f32[2,256,256]{1,2,0:T(8,128)} collective-permute-done((f32[2,256,256]{1,2,0:T(8,128)S(1)}, f32[2,256,256]{1,2,0:T(8,128)}, u32[]{:S(2)}, u32[]{:S(2)}) %collective-permute-start.4) | collective-permute-done | bytes 524320 | tf_op jit(solution)/shard_map/ppermute | solution.py:141
  168.7 1.1 slice_bitcast_fusion.2
  169.8 0.1 copy.25
  169.9 0.1 copy.26
  170.1 0.0 collective-permute-done.1
  170.1 2.5 %fusion.26 = f32[256,256]{1,0:T(8,128)S(1)} fusion(bf16[256,3072]{0,1:T(8,128)(2,1)} %collective-permute-done.1, bf16[256,3072]{0,1:T(8,128)(2,1)} %collective-permute-done.2), kind=kOutput, calls=%fused_computation.49 | convolution fusion | flops 402653184 | bytes 3407872 | tf_op jit(solution)/shard_map/dot_general | solution.py:123
  172.6 2.5 %collective-permute-start.3 = (f32[1,256,256]{1,2,0:T(8,128)S(1)}, f32[1,256,256]{1,2,0:T(8,128)S(1)}, u32[]{:S(2)}, u32[]{:S(2)}) collective-permute-start(f32[1,256,256]{1,2,0:T(8,128)S(1)} %bitcast.105), channel_id=1, source_target_pairs={{0,12},{8,4},{16,0},{24,8},{28,16},{20,24},{12,28},{4,20},{1,13},{... | collective-permute-start | bytes 786440 | tf_op jit(solution)/shard_map/ppermute | solution.py:141
  175.0 0.8 pad_maximum_fusion.1
  175.9 0.6 collective-permute-start.5
  176.4 0.0 collective-permute-done.6
  176.4 3.2 %convolution_bitcast_fusion = f32[1,256,256]{2,1,0:T(8,128)} fusion(bf16[256,3072]{0,1:T(8,128)(2,1)} %collective-permute-done.1, bf16[256,3072]{0,1:T(8,128)(2,1)} %collective-permute-done.6), kind=kOutput, calls=%fused_computation.18 | convolution fusion | flops 402653184 | bytes 3407872 | tf_op jit(solution)/shard_map/dot_general | solution.py:123
  179.6 1.7 collective-permute-start.7
  181.3 3.7 %collective-permute-done.3 = f32[1,256,256]{1,2,0:T(8,128)S(1)} collective-permute-done((f32[1,256,256]{1,2,0:T(8,128)S(1)}, f32[1,256,256]{1,2,0:T(8,128)S(1)}, u32[]{:S(2)}, u32[]{:S(2)}) %collective-permute-start.3) | collective-permute-done | bytes 262176 | tf_op jit(solution)/shard_map/ppermute | solution.py:141
  185.0 0.7 copy-done.2
  185.7 1.1 copy.24
  186.9 4.6 %collective-permute-done.5 = f32[2,256,256]{2,1,0:T(8,128)S(1)} collective-permute-done((f32[2,256,256]{2,1,0:T(8,128)}, f32[2,256,256]{2,1,0:T(8,128)S(1)}, u32[]{:S(2)}, u32[]{:S(2)}) %collective-permute-start.5) | collective-permute-done | bytes 524320 | tf_op jit(solution)/shard_map/ppermute | solution.py:141
  191.5 5.8 %collective-permute-done.7 = f32[1,256,256]{2,1,0:T(8,128)} collective-permute-done((f32[1,256,256]{2,1,0:T(8,128)}, f32[1,256,256]{2,1,0:T(8,128)}, u32[]{:S(2)}, u32[]{:S(2)}) %collective-permute-start.7) | collective-permute-done | bytes 262176 | tf_op jit(solution)/shard_map/ppermute | solution.py:141
  197.3 1.0 bitcast_dynamic-update-slice_fusion
  198.3 0.1 dynamic-slice_bitcast_fusion
  198.4 0.1 collective-permute-start.8
  198.5 2.7 %collective-permute-done.8 = f32[2,512,256]{2,1,0:T(8,128)} collective-permute-done((f32[2,512,256]{2,1,0:T(8,128)S(1)}, f32[2,512,256]{2,1,0:T(8,128)}, u32[]{:S(2)}, u32[]{:S(2)}) %collective-permute-start.8) | collective-permute-done | bytes 1048608 | tf_op jit(solution)/shard_map/ppermute | solution.py:59
  201.2 1.4 bitcast_add_fusion
  202.6 1.6 collective-permute-start.9
  204.2 12.4 %collective-permute-done.9 = f32[512,256]{1,0:T(8,128)S(1)} collective-permute-done((f32[512,256]{1,0:T(8,128)S(1)}, f32[512,256]{1,0:T(8,128)S(1)}, u32[]{:S(2)}, u32[]{:S(2)}) %collective-permute-start.9) | collective-permute-done | bytes 524320 | tf_op jit(solution)/shard_map/ppermute | solution.py:59
  216.7 0.9 bitcast_add_fusion.1
  (16 shorter events, 0.2 us)
Async XLA Ops:
  0.0 82.9 %copy-start = (bf16[1,64,64]{2,1,0:T(8,128)(2,1)S(1)}, bf16[1,64,64]{2,1,0:T(8,128)(2,1)}, u32[]{:S(2)}) copy-start(bf16[1,64,64]{2,1,0:T(8,128)(2,1)} %param.9) | copy-start | bytes 24580
  0.0 3.2 %copy-start.1 = (s32[32]{0:T(128)S(1)}, s32[32]{0:T(128)}, u32[]{:S(2)}) copy-start(s32[32]{0:T(128)} %param.13) | copy-start | bytes 388
  4.7 1.1 copy-start.4
  82.9 3.8 %copy-start.5 = (s32[8]{0:T(128)S(1)}, s32[8]{0:T(128)}, u32[]{:S(2)}) copy-start(s32[8]{0:T(128)} %constant.133.clone) | copy-start | bytes 100
  82.9 11.0 %copy-start.3 = (s32[8]{0:T(128)S(1)}, s32[8]{0:T(128)}, u32[]{:S(2)}) copy-start(s32[8]{0:T(128)} %constant.134.clone) | copy-start | bytes 100
  84.6 35.3 %collective-permute-start = (bf16[256,3072]{0,1:T(8,128)(2,1)}, bf16[256,3072]{0,1:T(8,128)(2,1)}, u32[]{:S(2)}, u32[]{:S(2)}) collective-permute-start(bf16[256,3072]{0,1:T(8,128)(2,1)} %bitcast.15), channel_id=1, source_target_pairs={{0,8},{8,16},{16,24},{24,28},{28,20},{20,12},{12,4},{4,0},{1,9},{9... | collective-permute-start | bytes 4718600 | tf_op jit(solution)/shard_map/ppermute | solution.py:117
  85.7 37.7 %collective-permute-start.2 = (bf16[256,3072]{0,1:T(8,128)(2,1)}, bf16[256,3072]{0,1:T(8,128)(2,1)}, u32[]{:S(2)}, u32[]{:S(2)}) collective-permute-start(bf16[256,3072]{0,1:T(8,128)(2,1)} %bitcast.15), channel_id=1, source_target_pairs={{0,4},{8,0},{16,8},{24,16},{28,24},{20,28},{12,20},{4,12},{1,5},{9... | collective-permute-start | bytes 4718600 | tf_op jit(solution)/shard_map/ppermute | solution.py:119
  119.9 50.1 %collective-permute-start.1 = (bf16[256,3072]{0,1:T(8,128)(2,1)}, bf16[256,3072]{0,1:T(8,128)(2,1)}, u32[]{:S(2)}, u32[]{:S(2)}) collective-permute-start(bf16[256,3072]{0,1:T(8,128)(2,1)} %collective-permute-done), channel_id=1, source_target_pairs={{0,8},{8,16},{16,24},{24,28},{28,20},{20,12},{12,4},{4,0},{1,9},{9... | collective-permute-start | bytes 4718600 | tf_op jit(solution)/shard_map/ppermute | solution.py:117
  123.4 53.0 %collective-permute-start.6 = (bf16[256,3072]{0,1:T(8,128)(2,1)}, bf16[256,3072]{0,1:T(8,128)(2,1)}, u32[]{:S(2)}, u32[]{:S(2)}) collective-permute-start(bf16[256,3072]{0,1:T(8,128)(2,1)} %collective-permute-done.2), channel_id=1, source_target_pairs={{0,4},{8,0},{16,8},{24,16},{28,24},{20,28},{12,20},{4,12},{1,5},{9... | collective-permute-start | bytes 4718600 | tf_op jit(solution)/shard_map/ppermute | solution.py:119
  129.9 38.8 %collective-permute-start.4 = (f32[2,256,256]{1,2,0:T(8,128)S(1)}, f32[2,256,256]{1,2,0:T(8,128)}, u32[]{:S(2)}, u32[]{:S(2)}) collective-permute-start(f32[2,256,256]{1,2,0:T(8,128)S(1)} %pad_maximum_fusion), channel_id=1, source_target_pairs={{0,4},{8,0},{16,8},{24,16},{28,24},{20,28},{12,20},{4,12},{1,5},{9... | collective-permute-start | bytes 1572872 | tf_op jit(solution)/shard_map/ppermute | solution.py:141
  172.6 12.4 %collective-permute-start.3 = (f32[1,256,256]{1,2,0:T(8,128)S(1)}, f32[1,256,256]{1,2,0:T(8,128)S(1)}, u32[]{:S(2)}, u32[]{:S(2)}) collective-permute-start(f32[1,256,256]{1,2,0:T(8,128)S(1)} %bitcast.105), channel_id=1, source_target_pairs={{0,12},{8,4},{16,0},{24,8},{28,16},{20,24},{12,28},{4,20},{1,13},{... | collective-permute-start | bytes 786440 | tf_op jit(solution)/shard_map/ppermute | solution.py:141
  175.9 15.6 %collective-permute-start.5 = (f32[2,256,256]{2,1,0:T(8,128)}, f32[2,256,256]{2,1,0:T(8,128)S(1)}, u32[]{:S(2)}, u32[]{:S(2)}) collective-permute-start(f32[2,256,256]{2,1,0:T(8,128)} %pad_maximum_fusion.1), channel_id=1, source_target_pairs={{0,8},{8,16},{16,24},{24,28},{28,20},{20,12},{12,4},{4,0},{1,9},{9... | collective-permute-start | bytes 1572872 | tf_op jit(solution)/shard_map/ppermute | solution.py:141
  179.6 17.7 %collective-permute-start.7 = (f32[1,256,256]{2,1,0:T(8,128)}, f32[1,256,256]{2,1,0:T(8,128)}, u32[]{:S(2)}, u32[]{:S(2)}) collective-permute-start(f32[1,256,256]{2,1,0:T(8,128)} %convolution_bitcast_fusion), channel_id=1, source_target_pairs={{0,16},{8,24},{16,28},{24,20},{28,12},{20,4},{12,0},{4,8},{1,17},{... | collective-permute-start | bytes 786440 | tf_op jit(solution)/shard_map/ppermute | solution.py:141
  185.0 0.7 copy-start.2
  198.4 2.9 %collective-permute-start.8 = (f32[2,512,256]{2,1,0:T(8,128)S(1)}, f32[2,512,256]{2,1,0:T(8,128)}, u32[]{:S(2)}, u32[]{:S(2)}) collective-permute-start(f32[2,512,256]{2,1,0:T(8,128)S(1)} %dynamic-slice_bitcast_fusion), channel_id=1, source_target_pairs={{0,1},{1,0},{2,3},{3,2},{4,5},{5,4},{6,7},{7,6},{8,9},{9,8},{10,11... | collective-permute-start | bytes 3145736 | tf_op jit(solution)/shard_map/ppermute | solution.py:59
  202.6 14.0 %collective-permute-start.9 = (f32[512,256]{1,0:T(8,128)S(1)}, f32[512,256]{1,0:T(8,128)S(1)}, u32[]{:S(2)}, u32[]{:S(2)}) collective-permute-start(f32[512,256]{1,0:T(8,128)S(1)} %dynamic-slice_bitcast_fusion.1), channel_id=1, source_target_pairs={{0,2},{1,3},{2,0},{3,1},{4,6},{5,7},{6,4},{7,5},{8,10},{9,11},{10,... | collective-permute-start | bytes 1572872 | tf_op jit(solution)/shard_map/ppermute | solution.py:59

commit v13 on v11

--- a/solution.py
+++ b/solution.py
@@ -82,10 +82,11 @@
         keep = col_live & slot_live[:, :, None]
         picked = occupied.reshape(n_mu, NB, n_occ)[nu_list]
         picked = jnp.where(keep[..., None], picked, jnp.zeros((), jnp.bfloat16))
-        pair = 2
+        pair = 4
         blank = jnp.zeros_like(picked)
         weight = jnp.concatenate(
-            [jnp.concatenate([picked, blank], axis=-1), jnp.concatenate([blank, picked], axis=-1)], axis=-2
+            [jnp.concatenate([picked if j == r else blank for j in range(pair)], axis=-1) for r in range(pair)],
+            axis=-2,
         )
         tiles = NB // pair
         tc = jnp.swapaxes(three_center[0], 1, 2).reshape(aux_dev, knu, n_mu, tiles, pair * NB)

time: 219 us -> 235 us (1.073)
  matrix products: 18.4 us -> 28.8 us
  local copies, waits for them, and re-layouts: 36.8 us -> 42.2 us
    dot_general x1, matrix products: 7.1 us -> 17.4 us  [body(): jnp.einsum('qkmtl,mklc->qmtc', tc, weight, preferred_element_type=jnp.flo...]
    unnamed x15, local copies, waits for them, and re-layouts: 8.08 us -> 12.7 us
where the time goes in v13:
time: 235 us; the launch traced here: 233 us
  waiting for transfers between devices  87.2 us (37%)
  blocking collectives  44.1 us (19%)
  local copies, waits for them, and re-layouts  42.2 us (18%)
  matrix products  28.8 us (12%)
  starting transfers between devices  12.2 us (5%)
  between operations  12.2 us (5%)
  other arithmetic  6.88 us (3%)
    ppermute x4, waiting for transfers between devices, body(): got = lax.ppermute(stack, 'grp', shifted(s))  47.9 us
    all_to_all x1, blocking collectives, body(): lax.all_to_all(half, 'grp', split_axis=1, concat_axis=0, tiled=True)  44.1 us
    ppermute x2, waiting for transfers between devices, body(): fwd = lax.ppermute(fwd, 'grp', shifted(1))  24.1 us
    dot_general x1, matrix products, body(): jnp.einsum('qkmtl,mklc->qmtc', tc, weight, preferred_element_type=jnp.flo...  17.4 us
    ppermute x2, waiting for transfers between devices, scatter_sum(): got = lax.ppermute(send, 'rep', [(i, i ^ d) for i in range(n_rep)])  15.2 us
    unnamed x15, local copies, waits for them, and re-layouts  12.7 us
    dot_general x5, matrix products, prod(): return jnp.dot(held[xo], held[yo].T, preferred_element_type=jnp.float32)  10.8 us
    ppermute x4, starting transfers between devices, body(): got = lax.ppermute(stack, 'grp', shifted(s))  6.22 us
  transfers between devices with their start and end apart: 10, of which 7 were waited for; matrix products, arithmetic and copies ran while one was open for 7% of the time, Pallas kernels for 0%

profile of v13, /device:TPU:0, one launch (start us, length us, event | category | flops | bytes accessed | tf_op | source)
XLA Modules:
  0.0 233.4 jit_solution(16779369286095043461)
XLA Ops:
  0.0 0.7 compare_select_fusion
  0.7 0.1 copy.19
  0.8 0.1 reshape.97
  0.9 1.3 reshape.88
  2.3 0.2 copy.20
  2.4 0.7 iota_compare_fusion.4
  3.2 1.6 gather_fusion
  4.7 0.0 copy-start.5
  4.7 1.0 gather_fusion.1
  5.8 0.1 reshape.96
  5.9 0.1 iota_compare_fusion.3
  5.9 11.9 %copy.28 = bf16[192,8,16,256]{3,2,1,0:T(8,128)(2,1)} copy(bf16[192,8,16,256]{3,1,2,0:T(8,128)(2,1)} %bitcast.99) | data formatting | bytes 25165824
  17.9 0.1 fusion.18
  18.0 1.6 broadcast_select_fusion
  19.6 1.1 broadcast.69
  20.7 0.3 broadcast_in_dim.51
  21.0 17.4 %fusion.11 = bf16[8,32,16,192]{3,2,0,1:T(8,128)(2,1)} fusion(bf16[8,6,32,16,256]{4,3,2,1,0:T(8,128)(2,1)} %bitcast.100, bf16[32,6,64,48]{2,3,1,0:T(8,128)(2,1)} %broadcast_select_fusion, bf16[32,6,64,48]{2,3,1,0:T(8,128)(2,1)S(1)} %broadcast_in_dim.51, bf16[32,6,64,96]{2,3,1,0:T(8,128)(2,1)S(1)} %broadcast.69), kind=kOutput, calls=%fused_computation.17 | convolution fusion | flops 2604662784 | bytes 18874368 | tf_op jit(solution)/shard_map/qkmtl,mklc->qmtc/dot_general | solution.py:93
  38.4 3.7 %reshape.90 = bf16[8,32,3072]{2,0,1:T(8,128)(2,1)S(1)} reshape(bf16[8,32,16,192]{3,2,0,1:T(8,128)(2,1)} %fusion.11) | data formatting | bytes 3145728 | tf_op jit(solution)/shard_map/reshape | solution.py:94
  42.1 0.3 broadcast_in_dim.46
  42.4 0.8 broadcast_in_dim.47
  43.2 0.5 select_convert_fusion
  43.8 44.1 %all_to_all.15 = bf16[8,32,3072]{2,0,1:T(8,128)(2,1)S(1)} all-to-all(bf16[8,32,3072]{2,0,1:T(8,128)(2,1)S(1)} %select_convert_fusion), channel_id=1, replica_groups=mesh['grp'=8,'rep'=4] {'grp'}, dimensions={1} | all-to-all | bytes 3145728 | tf_op jit(solution)/shard_map/all_to_all | solution.py:97
  87.8 0.6 fusion.8
  88.4 5.3 %reshape.92 = bf16[64,4,64,48]{3,2,1,0:T(8,128)(2,1)} reshape(bf16[64,12288]{1,0:T(8,128)(2,1)S(1)} %fusion.8) | data formatting | bytes 3145728 | tf_op jit(solution)/shard_map/reshape | solution.py:101
  93.7 5.6 %copy.22 = bf16[4,64,64,48]{1,0,3,2:T(4,128)(2,1)S(1)} copy(bf16[4,64,64,48]{3,1,0,2:T(8,128)(2,1)} %bitcast.97) | data formatting | bytes 3145728 | tf_op jit(solution)/shard_map/transpose | solution.py:102
  99.3 0.0 copy-start.6
  99.4 0.0 copy-start.4
  99.4 3.0 %reshape.93 = bf16[256,3072]{0,1:T(8,128)(2,1)} reshape(bf16[4,64,64,48]{1,0,3,2:T(4,128)(2,1)S(1)} %copy.22) | data formatting | bytes 3145728 | tf_op jit(solution)/shard_map/reshape | solution.py:104
  102.4 1.1 collective-permute-start
  103.5 0.9 collective-permute-start.2
  104.4 0.6 dynamic_slice.41
  111.6 0.7 fusion.24
  113.6 24.1 %collective-permute-done = bf16[256,3072]{0,1:T(8,128)(2,1)} collective-permute-done((bf16[256,3072]{0,1:T(8,128)(2,1)}, bf16[256,3072]{0,1:T(8,128)(2,1)}, u32[]{:S(2)}, u32[]{:S(2)}) %collective-permute-start) | collective-permute-done | bytes 1572896 | tf_op jit(solution)/shard_map/ppermute | solution.py:117
  137.7 0.8 collective-permute-start.1
  138.5 0.1 broadcast_in_dim.45
  138.6 0.6 convolution_dynamic-update-slice_fusion
  139.2 0.0 collective-permute-done.2
  139.2 1.5 collective-permute-start.6
  140.7 2.0 constant_dynamic-update-slice_fusion.3
  142.8 2.5 %fusion.26 = f32[256,256]{1,0:T(8,128)S(1)} fusion(bf16[256,3072]{0,1:T(8,128)(2,1)} %collective-permute-done, bf16[256,3072]{0,1:T(8,128)(2,1)} %collective-permute-done.2), kind=kOutput, calls=%fused_computation.50 | convolution fusion | flops 402653184 | bytes 3407872 | tf_op jit(solution)/shard_map/dot_general | solution.py:123
  145.3 1.5 collective-permute-start.4
  150.7 33.8 %collective-permute-done.4 = f32[2,256,256]{1,2,0:T(8,128)} collective-permute-done((f32[2,256,256]{1,2,0:T(8,128)S(1)}, f32[2,256,256]{1,2,0:T(8,128)}, u32[]{:S(2)}, u32[]{:S(2)}) %collective-permute-start.4) | collective-permute-done | bytes 524320 | tf_op jit(solution)/shard_map/ppermute | solution.py:141
  184.6 1.1 slice_bitcast_fusion.2
  185.6 0.1 copy.24
  185.8 0.1 copy.25
  185.9 2.5 %fusion.25 = f32[256,256]{1,0:T(8,128)S(1)} fusion(bf16[256,3072]{0,1:T(8,128)(2,1)} %collective-permute-done.1, bf16[256,3072]{0,1:T(8,128)(2,1)} %collective-permute-done.2), kind=kOutput, calls=%fused_computation.49 | convolution fusion | flops 402653184 | bytes 3407872 | tf_op jit(solution)/shard_map/dot_general | solution.py:123
  188.4 2.5 %collective-permute-start.3 = (f32[1,256,256]{1,2,0:T(8,128)S(1)}, f32[1,256,256]{1,2,0:T(8,128)S(1)}, u32[]{:S(2)}, u32[]{:S(2)}) collective-permute-start(f32[1,256,256]{1,2,0:T(8,128)S(1)} %bitcast.107), channel_id=1, source_target_pairs={{0,12},{8,4},{16,0},{24,8},{28,16},{20,24},{12,28},{4,20},{1,13},{... | collective-permute-start | bytes 786440 | tf_op jit(solution)/shard_map/ppermute | solution.py:141
  190.9 0.8 pad_maximum_fusion.1
  191.7 0.6 collective-permute-start.5
  192.3 3.2 %convolution_bitcast_fusion = f32[1,256,256]{2,1,0:T(8,128)} fusion(bf16[256,3072]{0,1:T(8,128)(2,1)} %collective-permute-done.1, bf16[256,3072]{0,1:T(8,128)(2,1)} %collective-permute-done.6), kind=kOutput, calls=%fused_computation.19 | convolution fusion | flops 402653184 | bytes 3407872 | tf_op jit(solution)/shard_map/dot_general | solution.py:123
  195.5 1.7 collective-permute-start.7
  197.1 3.7 %collective-permute-done.3 = f32[1,256,256]{1,2,0:T(8,128)S(1)} collective-permute-done((f32[1,256,256]{1,2,0:T(8,128)S(1)}, f32[1,256,256]{1,2,0:T(8,128)S(1)}, u32[]{:S(2)}, u32[]{:S(2)}) %collective-permute-start.3) | collective-permute-done | bytes 262176 | tf_op jit(solution)/shard_map/ppermute | solution.py:141
  200.9 0.7 copy-done.3
  201.5 1.1 copy.23
  202.7 4.6 %collective-permute-done.5 = f32[2,256,256]{2,1,0:T(8,128)S(1)} collective-permute-done((f32[2,256,256]{2,1,0:T(8,128)}, f32[2,256,256]{2,1,0:T(8,128)S(1)}, u32[]{:S(2)}, u32[]{:S(2)}) %collective-permute-start.5) | collective-permute-done | bytes 524320 | tf_op jit(solution)/shard_map/ppermute | solution.py:141
  207.4 5.7 %collective-permute-done.7 = f32[1,256,256]{2,1,0:T(8,128)} collective-permute-done((f32[1,256,256]{2,1,0:T(8,128)}, f32[1,256,256]{2,1,0:T(8,128)}, u32[]{:S(2)}, u32[]{:S(2)}) %collective-permute-start.7) | collective-permute-done | bytes 262176 | tf_op jit(solution)/shard_map/ppermute | solution.py:141
  213.1 1.0 bitcast_dynamic-update-slice_fusion
  214.1 0.1 dynamic-slice_bitcast_fusion
  214.2 0.1 collective-permute-start.8
  214.3 2.7 %collective-permute-done.8 = f32[2,512,256]{2,1,0:T(8,128)} collective-permute-done((f32[2,512,256]{2,1,0:T(8,128)S(1)}, f32[2,512,256]{2,1,0:T(8,128)}, u32[]{:S(2)}, u32[]{:S(2)}) %collective-permute-start.8) | collective-permute-done | bytes 1048608 | tf_op jit(solution)/shard_map/ppermute | solution.py:59
  217.1 1.4 bitcast_add_fusion
  218.5 1.6 collective-permute-start.9
  220.1 12.4 %collective-permute-done.9 = f32[512,256]{1,0:T(8,128)S(1)} collective-permute-done((f32[512,256]{1,0:T(8,128)S(1)}, f32[512,256]{1,0:T(8,128)S(1)}, u32[]{:S(2)}, u32[]{:S(2)}) %collective-permute-start.9) | collective-permute-done | bytes 524320 | tf_op jit(solution)/shard_map/ppermute | solution.py:59
  232.5 0.9 bitcast_add_fusion.1
  (20 shorter events, 0.2 us)
Async XLA Ops:
  0.0 87.8 %copy-start = (bf16[1,64,64]{2,1,0:T(8,128)(2,1)S(1)}, bf16[1,64,64]{2,1,0:T(8,128)(2,1)}, u32[]{:S(2)}) copy-start(bf16[1,64,64]{2,1,0:T(8,128)(2,1)} %param.9) | copy-start | bytes 24580
  0.0 3.2 %copy-start.1 = (s32[32]{0:T(128)S(1)}, s32[32]{0:T(128)}, u32[]{:S(2)}) copy-start(s32[32]{0:T(128)} %param.13) | copy-start | bytes 388
  4.7 1.1 copy-start.5
  99.3 5.1 %copy-start.6 = (s32[8]{0:T(128)S(1)}, s32[8]{0:T(128)}, u32[]{:S(2)}) copy-start(s32[8]{0:T(128)} %constant.135.clone) | copy-start | bytes 100
  99.4 12.2 %copy-start.4 = (s32[8]{0:T(128)S(1)}, s32[8]{0:T(128)}, u32[]{:S(2)}) copy-start(s32[8]{0:T(128)} %constant.136.clone) | copy-start | bytes 100
  102.4 35.3 %collective-permute-start = (bf16[256,3072]{0,1:T(8,128)(2,1)}, bf16[256,3072]{0,1:T(8,128)(2,1)}, u32[]{:S(2)}, u32[]{:S(2)}) collective-permute-start(bf16[256,3072]{0,1:T(8,128)(2,1)} %reshape.93), channel_id=1, source_target_pairs={{0,8},{8,16},{16,24},{24,28},{28,20},{20,12},{12,4},{4,0},{1,9},{9... | collective-permute-start | bytes 4718600 | tf_op jit(solution)/shard_map/ppermute | solution.py:117
  103.5 35.7 %collective-permute-start.2 = (bf16[256,3072]{0,1:T(8,128)(2,1)}, bf16[256,3072]{0,1:T(8,128)(2,1)}, u32[]{:S(2)}, u32[]{:S(2)}) collective-permute-start(bf16[256,3072]{0,1:T(8,128)(2,1)} %reshape.93), channel_id=1, source_target_pairs={{0,4},{8,0},{16,8},{24,16},{28,24},{20,28},{12,20},{4,12},{1,5},{9... | collective-permute-start | bytes 4718600 | tf_op jit(solution)/shard_map/ppermute | solution.py:119
  113.6 25.0 %copy-start.2 = (bf16[256,3072]{0,1:T(8,128)(2,1)S(1)}, bf16[256,3072]{0,1:T(8,128)(2,1)}, u32[]{:S(2)}) copy-start(bf16[256,3072]{0,1:T(8,128)(2,1)} %reshape.93) | copy-start | bytes 4718596
  137.7 48.2 %collective-permute-start.1 = (bf16[256,3072]{0,1:T(8,128)(2,1)}, bf16[256,3072]{0,1:T(8,128)(2,1)}, u32[]{:S(2)}, u32[]{:S(2)}) collective-permute-start(bf16[256,3072]{0,1:T(8,128)(2,1)} %collective-permute-done), channel_id=1, source_target_pairs={{0,8},{8,16},{16,24},{24,28},{28,20},{20,12},{12,4},{4,0},{1,9},{9... | collective-permute-start | bytes 4718600 | tf_op jit(solution)/shard_map/ppermute | solution.py:117
  139.2 53.0 %collective-permute-start.6 = (bf16[256,3072]{0,1:T(8,128)(2,1)}, bf16[256,3072]{0,1:T(8,128)(2,1)}, u32[]{:S(2)}, u32[]{:S(2)}) collective-permute-start(bf16[256,3072]{0,1:T(8,128)(2,1)} %collective-permute-done.2), channel_id=1, source_target_pairs={{0,4},{8,0},{16,8},{24,16},{28,24},{20,28},{12,20},{4,12},{1,5},{9... | collective-permute-start | bytes 4718600 | tf_op jit(solution)/shard_map/ppermute | solution.py:119
  145.3 39.3 %collective-permute-start.4 = (f32[2,256,256]{1,2,0:T(8,128)S(1)}, f32[2,256,256]{1,2,0:T(8,128)}, u32[]{:S(2)}, u32[]{:S(2)}) collective-permute-start(f32[2,256,256]{1,2,0:T(8,128)S(1)} %pad_maximum_fusion), channel_id=1, source_target_pairs={{0,4},{8,0},{16,8},{24,16},{28,24},{20,28},{12,20},{4,12},{1,5},{9... | collective-permute-start | bytes 1572872 | tf_op jit(solution)/shard_map/ppermute | solution.py:141
  188.4 12.4 %collective-permute-start.3 = (f32[1,256,256]{1,2,0:T(8,128)S(1)}, f32[1,256,256]{1,2,0:T(8,128)S(1)}, u32[]{:S(2)}, u32[]{:S(2)}) collective-permute-start(f32[1,256,256]{1,2,0:T(8,128)S(1)} %bitcast.107), channel_id=1, source_target_pairs={{0,12},{8,4},{16,0},{24,8},{28,16},{20,24},{12,28},{4,20},{1,13},{... | collective-permute-start | bytes 786440 | tf_op jit(solution)/shard_map/ppermute | solution.py:141
  191.7 15.6 %collective-permute-start.5 = (f32[2,256,256]{2,1,0:T(8,128)}, f32[2,256,256]{2,1,0:T(8,128)S(1)}, u32[]{:S(2)}, u32[]{:S(2)}) collective-permute-start(f32[2,256,256]{2,1,0:T(8,128)} %pad_maximum_fusion.1), channel_id=1, source_target_pairs={{0,8},{8,16},{16,24},{24,28},{28,20},{20,12},{12,4},{4,0},{1,9},{9... | collective-permute-start | bytes 1572872 | tf_op jit(solution)/shard_map/ppermute | solution.py:141
  195.5 17.7 %collective-permute-start.7 = (f32[1,256,256]{2,1,0:T(8,128)}, f32[1,256,256]{2,1,0:T(8,128)}, u32[]{:S(2)}, u32[]{:S(2)}) collective-permute-start(f32[1,256,256]{2,1,0:T(8,128)} %convolution_bitcast_fusion), channel_id=1, source_target_pairs={{0,16},{8,24},{16,28},{24,20},{28,12},{20,4},{12,0},{4,8},{1,17},{... | collective-permute-start | bytes 786440 | tf_op jit(solution)/shard_map/ppermute | solution.py:141
  200.9 0.7 copy-start.3
  214.2 2.9 %collective-permute-start.8 = (f32[2,512,256]{2,1,0:T(8,128)S(1)}, f32[2,512,256]{2,1,0:T(8,128)}, u32[]{:S(2)}, u32[]{:S(2)}) collective-permute-start(f32[2,512,256]{2,1,0:T(8,128)S(1)} %dynamic-slice_bitcast_fusion), channel_id=1, source_target_pairs={{0,1},{1,0},{2,3},{3,2},{4,5},{5,4},{6,7},{7,6},{8,9},{9,8},{10,11... | collective-permute-start | bytes 3145736 | tf_op jit(solution)/shard_map/ppermute | solution.py:59
  218.5 14.0 %collective-permute-start.9 = (f32[512,256]{1,0:T(8,128)S(1)}, f32[512,256]{1,0:T(8,128)S(1)}, u32[]{:S(2)}, u32[]{:S(2)}) collective-permute-start(f32[512,256]{1,0:T(8,128)S(1)} %dynamic-slice_bitcast_fusion.1), channel_id=1, source_target_pairs={{0,2},{1,3},{2,0},{3,1},{4,6},{5,7},{6,4},{7,5},{8,10},{9,11},{10,... | collective-permute-start | bytes 1572872 | tf_op jit(solution)/shard_map/ppermute | solution.py:59

commit v14 on v11

--- a/solution.py
+++ b/solution.py
@@ -82,44 +82,53 @@
         keep = col_live & slot_live[:, :, None]
         picked = occupied.reshape(n_mu, NB, n_occ)[nu_list]
         picked = jnp.where(keep[..., None], picked, jnp.zeros((), jnp.bfloat16))
-        pair = 2
-        blank = jnp.zeros_like(picked)
-        weight = jnp.concatenate(
-            [jnp.concatenate([picked, blank], axis=-1), jnp.concatenate([blank, picked], axis=-1)], axis=-2
-        )
-        tiles = NB // pair
-        tc = jnp.swapaxes(three_center[0], 1, 2).reshape(aux_dev, knu, n_mu, tiles, pair * NB)
-        half = jnp.einsum("qkmtl,mklc->qmtc", tc, weight, preferred_element_type=jnp.float32)
-        half = half.reshape(aux_dev, n_mu, NB, n_occ)
-        half = jnp.where(row_live[None, :, :, None], half, 0.0).astype(jnp.bfloat16)
-        half = half.reshape(aux_dev, n_mu, NB * n_occ)
-        regrouped = lax.all_to_all(half, "grp", split_axis=1, concat_axis=0, tiled=True)
-        n_aux = regrouped.shape[0]
-        mu_dev = regrouped.shape[1]
-        mixed = jnp.dot(metric[0], regrouped.reshape(n_aux, -1), preferred_element_type=jnp.float32)
-        mixed = mixed.astype(jnp.bfloat16).reshape(n_aux, mu_dev, NB, n_occ)
-        orbital = jnp.transpose(mixed, (1, 2, 0, 3))
-        rows = mu_dev * NB
-        orbital = orbital.reshape(rows, n_aux * n_occ)
         me = lax.axis_index("grp")
         pos = jnp.asarray(pos_of)[me]
         ring_c = jnp.asarray(ring_arr)
+        pair = 2
+        tiles = NB // pair
+        tc = jnp.swapaxes(three_center[0], 1, 2).reshape(aux_dev, knu, n_mu, tiles, pair * NB)
+        n_split = 2 if n_occ % 2 == 0 else 1
+        occ_c = n_occ // n_split
+        radius = n // 4
+        helds = []
+        for h in range(n_split):
+            part = picked[..., h * occ_c:(h + 1) * occ_c]
+            blank = jnp.zeros_like(part)
+            weight = jnp.concatenate(
+                [jnp.concatenate([part, blank], axis=-1), jnp.concatenate([blank, part], axis=-1)], axis=-2
+            )
+            half = jnp.einsum("qkmtl,mklc->qmtc", tc, weight, preferred_element_type=jnp.float32)
+            half = half.reshape(aux_dev, n_mu, NB, occ_c)
+            half = jnp.where(row_live[None, :, :, None], half, 0.0).astype(jnp.bfloat16)
+            half = half.reshape(aux_dev, n_mu, NB * occ_c)
+            regrouped = lax.all_to_all(half, "grp", split_axis=1, concat_axis=0, tiled=True)
+            n_aux = regrouped.shape[0]
+            mu_dev = regrouped.shape[1]
+            mixed = jnp.dot(metric[0], regrouped.reshape(n_aux, -1), preferred_element_type=jnp.float32)
+            mixed = mixed.astype(jnp.bfloat16).reshape(n_aux, mu_dev, NB, occ_c)
+            orbital = jnp.transpose(mixed, (1, 2, 0, 3))
+            rows = mu_dev * NB
+            orbital = orbital.reshape(rows, n_aux * occ_c)
+            held = {0: orbital}
+            fwd = orbital
+            bwd = orbital
+            for k in range(1, radius + 1):
+                fwd = lax.ppermute(fwd, "grp", shifted(1))
+                held[-k] = fwd
+                bwd = lax.ppermute(bwd, "grp", shifted(-1))
+                held[k] = bwd
+            helds.append(held)
 
         def start_of(off):
             return ring_c[(pos + off) % n] * rows
 
-        radius = n // 4
-        held = {0: orbital}
-        fwd = orbital
-        bwd = orbital
-        for k in range(1, radius + 1):
-            fwd = lax.ppermute(fwd, "grp", shifted(1))
-            held[-k] = fwd
-            bwd = lax.ppermute(bwd, "grp", shifted(-1))
-            held[k] = bwd
-
         def prod(xo, yo):
-            return jnp.dot(held[xo], held[yo].T, preferred_element_type=jnp.float32)
+            out = None
+            for held in helds:
+                one = jnp.dot(held[xo], held[yo].T, preferred_element_type=jnp.float32)
+                out = one if out is None else out + one
+            return out
 
         local = []
         outgoing = {}

time: 219 us -> 223 us (1.018)
  waiting for transfers between devices: 87 us -> 65.9 us
  matrix products: 18.4 us -> 37.8 us
  blocking collectives: 44.1 us -> 27.3 us
  local copies, waits for them, and re-layouts: 36.8 us -> 47.5 us
  starting transfers between devices: 12.2 us -> 22.2 us
  other arithmetic: 6.91 us -> 9.15 us
    ppermute x4, waiting for transfers between devices: 47.7 us -> 11.9 us  [body(): got = lax.ppermute(stack, 'grp', shifted(s))]
    all_to_all x1, blocking collectives: 44.1 us -> 27.3 us  [body(): lax.all_to_all(half, 'grp', split_axis=1, concat_axis=0, tiled=True)]
    ppermute x2 -> x4, waiting for transfers between devices: 0.01 us -> 14.3 us  [body(): bwd = lax.ppermute(bwd, 'grp', shifted(-1))]
    dot_general x1 -> x2, matrix products: 7.1 us -> 19.1 us  [body(): jnp.einsum('qkmtl,mklc->qmtc', tc, weight, preferred_element_type=jnp.flo...]
    dot_general x5 -> x10, matrix products: 10.8 us -> 16.9 us  [prod(): one = jnp.dot(held[xo], held[yo].T, preferred_element_type=jnp.float32)]
    unnamed x15 -> x23, local copies, waits for them, and re-layouts: 8.08 us -> 12.4 us
    all_to_all x0 -> x1, starting transfers between devices: none -> 4.23 us  [body(): lax.all_to_all(half, 'grp', split_axis=1, concat_axis=0, tiled=True)]
    ppermute x2 -> x4, starting transfers between devices: 2.25 us -> 5.42 us  [body(): bwd = lax.ppermute(bwd, 'grp', shifted(-1))]
  transfers between devices with their start and end apart: 10 -> 15, of which waited for: 7 -> 11; matrix products, arithmetic and copies ran while one was open for 7% -> 17% of each run, Pallas kernels for 0% -> 0%
where the time goes in v14:
time: 223 us; the launch traced here: 222 us
  waiting for transfers between devices  65.9 us (30%)
  local copies, waits for them, and re-layouts  47.5 us (21%)
  matrix products  37.8 us (17%)
  blocking collectives  27.3 us (12%)
  starting transfers between devices  22.2 us (10%)
  between operations  12.1 us (5%)
  other arithmetic  9.15 us (4%)
    all_to_all x1, blocking collectives, body(): lax.all_to_all(half, 'grp', split_axis=1, concat_axis=0, tiled=True)  27.3 us
    ppermute x4, waiting for transfers between devices, body(): fwd = lax.ppermute(fwd, 'grp', shifted(1))  22.4 us
    dot_general x2, matrix products, body(): jnp.einsum('qkmtl,mklc->qmtc', tc, weight, preferred_element_type=jnp.flo...  19.1 us
    dot_general x10, matrix products, prod(): one = jnp.dot(held[xo], held[yo].T, preferred_element_type=jnp.float32)  16.9 us
    ppermute x2, waiting for transfers between devices, scatter_sum(): got = lax.ppermute(send, 'rep', [(i, i ^ d) for i in range(n_rep)])  15.2 us
    ppermute x4, waiting for transfers between devices, body(): bwd = lax.ppermute(bwd, 'grp', shifted(-1))  14.3 us
    unnamed x23, local copies, waits for them, and re-layouts  12.4 us
    ppermute x4, waiting for transfers between devices, body(): got = lax.ppermute(stack, 'grp', shifted(s))  11.9 us
  transfers between devices with their start and end apart: 15, of which 11 were waited for; matrix products, arithmetic and copies ran while one was open for 17% of the time, Pallas kernels for 0%

profile of v14, /device:TPU:0, one launch (start us, length us, event | category | flops | bytes accessed | tf_op | source)
XLA Modules:
  0.0 221.8 jit_solution(2052945128078964596)
XLA Ops:
  0.0 0.7 compare_select_fusion
  0.9 1.3 reshape.104
  2.4 1.3 iota_compare_fusion.4
  3.8 1.5 gather_fusion
  5.3 1.0 gather_fusion.1
  6.7 1.8 broadcast_select_fusion
  8.5 1.4 fusion.47
  9.9 11.6 %copy.39 = bf16[192,8,32,128]{3,2,1,0:T(8,128)(2,1)} copy(bf16[192,8,32,128]{3,1,2,0:T(8,128)(2,1)} %bitcast.141) | data formatting | bytes 25165824
  21.5 9.7 %fusion.22 = bf16[8,32,32,48]{3,2,0,1:T(8,128)(2,1)} fusion(bf16[8,6,32,32,128]{4,3,2,1,0:T(8,128)(2,1)} %bitcast.142, bf16[32,6,64,24]{2,3,1,0:T(8,128)(2,1)} %get-tuple-element.8, bf16[32,6,64,48]{2,3,1,0:T(8,128)(2,1)S(1)} %copy-done.3), kind=kOutput, calls=%fused_computation.27 | convolution fusion | flops 611057664 | bytes 15138816 | tf_op jit(solution)/shard_map/qkmtl,mklc->qmtc/dot_general | solution.py:101
  31.3 4.5 %reshape.106 = bf16[8,32,1536]{2,0,1:T(8,128)(2,1)S(1)} reshape(bf16[8,32,32,48]{3,2,0,1:T(8,128)(2,1)} %fusion.22) | data formatting | bytes 1572864 | tf_op jit(solution)/shard_map/reshape | solution.py:102
  35.8 9.4 %fusion.27 = bf16[8,32,32,48]{3,2,0,1:T(8,128)(2,1)} fusion(bf16[8,6,32,32,128]{4,3,2,1,0:T(8,128)(2,1)} %bitcast.143, bf16[32,6,64,24]{2,3,1,0:T(8,128)(2,1)S(1)} %get-tuple-element.7), kind=kOutput, calls=%fused_computation.28 | convolution fusion | flops 613416960 | bytes 13959168 | tf_op jit(solution)/shard_map/qkmtl,mklc->qmtc/dot_general | solution.py:101
  45.1 4.7 %reshape.110 = bf16[8,32,1536]{2,0,1:T(8,128)(2,1)S(1)} reshape(bf16[8,32,32,48]{3,2,0,1:T(8,128)(2,1)} %fusion.27) | data formatting | bytes 1572864 | tf_op jit(solution)/shard_map/reshape | solution.py:102
  50.2 0.7 broadcast_in_dim.51
  50.9 1.3 select_convert_fusion
  52.2 27.3 %all_to_all.30 = bf16[8,32,1536]{2,0,1:T(8,128)(2,1)S(1)} all-to-all(bf16[8,32,1536]{2,0,1:T(8,128)(2,1)S(1)} %get-tuple-element.11), channel_id=1, replica_groups=mesh['grp'=8,'rep'=4] {'grp'}, dimensions={1} | all-to-all | bytes 1572864 | tf_op jit(solution)/shard_map/all_to_all | solution.py:105
  79.5 4.2 %all-to-all-start = ((bf16[8,32,1536]{2,0,1:T(8,128)(2,1)}), bf16[8,32,1536]{2,0,1:T(8,128)(2,1)}, u32[]{:S(2)}, u32[]{:S(2)}) async-start(bf16[8,32,1536]{2,0,1:T(8,128)(2,1)} %get-tuple-element.12), calls=%async_computation | async-start | bytes 1572864 | tf_op jit(solution)/shard_map/all_to_all | solution.py:105
  83.7 0.6 dynamic_slice.41
  91.0 0.7 fusion.48
  93.3 0.9 copy.30
  94.1 3.2 %copy.31 = bf16[4,64,64,24]{1,0,3,2:T(4,128)(2,1)S(1)} copy(bf16[4,64,64,24]{2,3,1,0:T(8,128)(2,1)S(1)} %bitcast.146) | data formatting | bytes 1572864 | tf_op jit(solution)/shard_map/transpose | solution.py:110
  97.3 1.7 reshape.113
  99.1 1.9 collective-permute-start.1
  101.1 2.2 all-to-all-done
  103.3 1.5 fusion.4
  104.7 0.9 copy.27
  105.6 3.2 %copy.28 = bf16[4,64,64,24]{1,0,3,2:T(4,128)(2,1)S(1)} copy(bf16[4,64,64,24]{2,3,1,0:T(8,128)(2,1)S(1)} %bitcast.147) | data formatting | bytes 1572864 | tf_op jit(solution)/shard_map/transpose | solution.py:110
  108.8 1.8 reshape.109
  110.8 2.1 collective-permute-start.3
  113.0 1.8 fusion.49
  114.9 1.8 fusion.34
  116.7 3.2 %collective-permute-done.1 = bf16[256,1536]{0,1:T(8,128)(2,1)} collective-permute-done((bf16[256,1536]{0,1:T(8,128)(2,1)}, bf16[256,1536]{0,1:T(8,128)(2,1)}, u32[]{:S(2)}, u32[]{:S(2)}) %collective-permute-start.1) | collective-permute-done | bytes 786464 | tf_op jit(solution)/shard_map/ppermute | solution.py:117
  119.9 1.9 collective-permute-start.4
  121.8 1.8 fusion.50
  123.6 1.8 fusion.52
  125.3 11.3 %collective-permute-done = bf16[256,1536]{0,1:T(8,128)(2,1)S(1)} collective-permute-done((bf16[256,1536]{0,1:T(8,128)(2,1)}, bf16[256,1536]{0,1:T(8,128)(2,1)S(1)}, u32[]{:S(2)}, u32[]{:S(2)}) %collective-permute-start) | collective-permute-done | bytes 786464 | tf_op jit(solution)/shard_map/ppermute | solution.py:117
  136.8 0.4 convolution_add_fusion.1
  137.2 1.6 constant_dynamic-update-slice_fusion.3
  138.7 0.8 pad_maximum_fusion
  139.6 2.1 collective-permute-start.7
  145.4 2.1 collective-permute-start.10
  147.5 1.1 collective-permute-start.9
  148.6 6.1 %collective-permute-done.7 = f32[2,256,256]{1,2,0:T(8,128)} collective-permute-done((f32[2,256,256]{1,2,0:T(8,128)}, f32[2,256,256]{1,2,0:T(8,128)}, u32[]{:S(2)}, u32[]{:S(2)}) %collective-permute-start.7) | collective-permute-done | bytes 524320 | tf_op jit(solution)/shard_map/ppermute | solution.py:149
  154.7 1.8 slice_bitcast_fusion.2
  156.5 0.9 copy.33
  157.4 1.1 copy.34
  158.5 1.8 fusion.51
  160.2 7.9 %collective-permute-done.2 = bf16[256,1536]{0,1:T(8,128)(2,1)} collective-permute-done((bf16[256,1536]{0,1:T(8,128)(2,1)S(1)}, bf16[256,1536]{0,1:T(8,128)(2,1)}, u32[]{:S(2)}, u32[]{:S(2)}) %collective-permute-start.2) | collective-permute-done | bytes 786464 | tf_op jit(solution)/shard_map/ppermute | solution.py:117
  168.1 1.8 convolution_add_fusion.2
  169.9 3.8 %collective-permute-start.6 = (f32[1,256,256]{1,2,0:T(8,128)S(1)}, f32[1,256,256]{1,2,0:T(8,128)S(1)}, u32[]{:S(2)}, u32[]{:S(2)}) collective-permute-start(f32[1,256,256]{1,2,0:T(8,128)S(1)} %bitcast.152), channel_id=1, source_target_pairs={{0,12},{8,4},{16,0},{24,8},{28,16},{20,24},{12,28},{4,20},{1,13},{... | collective-permute-start | bytes 786440 | tf_op jit(solution)/shard_map/ppermute | solution.py:149
  173.7 0.8 pad_maximum_fusion.1
  174.5 0.8 collective-permute-start.8
  175.3 1.8 fusion.53
  177.1 14.2 %collective-permute-done.9 = bf16[256,1536]{0,1:T(8,128)(2,1)} collective-permute-done((bf16[256,1536]{0,1:T(8,128)(2,1)}, bf16[256,1536]{0,1:T(8,128)(2,1)}, u32[]{:S(2)}, u32[]{:S(2)}) %collective-permute-start.9) | collective-permute-done | bytes 786464 | tf_op jit(solution)/shard_map/ppermute | solution.py:119
  191.3 2.5 %fusion.35 = f32[1,256,256]{2,1,0:T(8,128)} fusion(f32[256,256]{1,0:T(8,128)S(1)} %fusion.53, bf16[256,1536]{0,1:T(8,128)(2,1)} %collective-permute-done.2, bf16[256,1536]{0,1:T(8,128)(2,1)} %collective-permute-done.9), kind=kOutput, calls=%fused_computation.39 | convolution fusion | flops 201392128 | bytes 2097152 | tf_op jit(solution)/shard_map/dot_general | solution.py:129
  193.9 2.2 collective-permute-done.6
  196.1 0.7 copy-done.5
  196.8 1.1 copy.32
  198.1 3.5 %collective-permute-done.11 = f32[1,256,256]{2,1,0:T(8,128)} collective-permute-done((f32[1,256,256]{2,1,0:T(8,128)}, f32[1,256,256]{2,1,0:T(8,128)}, u32[]{:S(2)}, u32[]{:S(2)}) %collective-permute-start.11) | collective-permute-done | bytes 262176 | tf_op jit(solution)/shard_map/ppermute | solution.py:149
  201.6 1.0 bitcast_dynamic-update-slice_fusion
  202.8 2.7 %collective-permute-done.12 = f32[2,512,256]{2,1,0:T(8,128)} collective-permute-done((f32[2,512,256]{2,1,0:T(8,128)S(1)}, f32[2,512,256]{2,1,0:T(8,128)}, u32[]{:S(2)}, u32[]{:S(2)}) %collective-permute-start.12) | collective-permute-done | bytes 1048608 | tf_op jit(solution)/shard_map/ppermute | solution.py:59
  205.5 1.4 bitcast_add_fusion
  206.9 1.6 collective-permute-start.13
  208.5 12.4 %collective-permute-done.13 = f32[512,256]{1,0:T(8,128)S(1)} collective-permute-done((f32[512,256]{1,0:T(8,128)S(1)}, f32[512,256]{1,0:T(8,128)S(1)}, u32[]{:S(2)}, u32[]{:S(2)}) %collective-permute-start.13) | collective-permute-done | bytes 524320 | tf_op jit(solution)/shard_map/ppermute | solution.py:59
  221.0 0.9 bitcast_add_fusion.1
  (48 shorter events, 2.5 us)
Async XLA Ops:
  0.0 92.9 %copy-start = (bf16[1,64,64]{2,1,0:T(8,128)(2,1)S(1)}, bf16[1,64,64]{2,1,0:T(8,128)(2,1)}, u32[]{:S(2)}) copy-start(bf16[1,64,64]{2,1,0:T(8,128)(2,1)} %param.9) | copy-start | bytes 24580
  0.0 3.7 %copy-start.1 = (s32[32]{0:T(128)S(1)}, s32[32]{0:T(128)}, u32[]{:S(2)}) copy-start(s32[32]{0:T(128)} %param.13) | copy-start | bytes 388
  5.3 1.2 copy-start.9
  5.3 1.4 copy-start.8
  9.9 11.6 %copy-start.3 = (bf16[32,6,64,48]{2,3,1,0:T(8,128)(2,1)S(1)}, bf16[32,6,64,48]{2,3,1,0:T(8,128)(2,1)}, u32[]{:S(2)}) copy-start(bf16[32,6,64,48]{2,3,1,0:T(8,128)(2,1)} %get-tuple-element.5) | copy-start | bytes 3538948
  45.1 4.7 %copy-start.7 = (pred[32,64]{1,0:T(8,128)(4,1)S(1)}, pred[32,64]{1,0:T(8,128)(4,1)}, u32[]{:S(2)}) copy-start(pred[32,64]{1,0:T(8,128)(4,1)} %iota_compare_fusion.4) | copy-start | bytes 6148
  52.2 31.6 %copy-start.10 = (s32[8]{0:T(128)S(1)}, s32[8]{0:T(128)}, u32[]{:S(2)}) copy-start(s32[8]{0:T(128)} %constant.135.clone) | copy-start | bytes 100
  52.2 38.8 %copy-start.6 = (s32[8]{0:T(128)S(1)}, s32[8]{0:T(128)}, u32[]{:S(2)}) copy-start(s32[8]{0:T(128)} %constant.136.clone) | copy-start | bytes 100
  79.5 23.8 %all-to-all-start = ((bf16[8,32,1536]{2,0,1:T(8,128)(2,1)}), bf16[8,32,1536]{2,0,1:T(8,128)(2,1)}, u32[]{:S(2)}, u32[]{:S(2)}) async-start(bf16[8,32,1536]{2,0,1:T(8,128)(2,1)} %get-tuple-element.12), calls=%async_computation | async-start | bytes 1572864 | tf_op jit(solution)/shard_map/all_to_all | solution.py:105
  99.1 20.8 %collective-permute-start.1 = (bf16[256,1536]{0,1:T(8,128)(2,1)}, bf16[256,1536]{0,1:T(8,128)(2,1)}, u32[]{:S(2)}, u32[]{:S(2)}) collective-permute-start(bf16[256,1536]{0,1:T(8,128)(2,1)} %reshape.113), channel_id=1, source_target_pairs={{0,8},{8,16},{16,24},{24,28},{28,20},{20,12},{12,4},{4,0},{1,9},{9... | collective-permute-start | bytes 2359304 | tf_op jit(solution)/shard_map/ppermute | solution.py:117
  101.0 22.6 %collective-permute-start.5 = (bf16[256,1536]{0,1:T(8,128)(2,1)}, bf16[256,1536]{0,1:T(8,128)(2,1)}, u32[]{:S(2)}, u32[]{:S(2)}) collective-permute-start(bf16[256,1536]{0,1:T(8,128)(2,1)} %reshape.113), channel_id=1, source_target_pairs={{0,4},{8,0},{16,8},{24,16},{28,24},{20,28},{12,20},{4,12},{1,5},{9... | collective-permute-start | bytes 2359304 | tf_op jit(solution)/shard_map/ppermute | solution.py:119
  110.6 26.0 %collective-permute-start = (bf16[256,1536]{0,1:T(8,128)(2,1)}, bf16[256,1536]{0,1:T(8,128)(2,1)S(1)}, u32[]{:S(2)}, u32[]{:S(2)}) collective-permute-start(bf16[256,1536]{0,1:T(8,128)(2,1)} %reshape.109), channel_id=1, source_target_pairs={{0,8},{8,16},{16,24},{24,28},{28,20},{20,12},{12,4},{4,0},{1,9},{9... | collective-permute-start | bytes 2359304 | tf_op jit(solution)/shard_map/ppermute | solution.py:117
  110.8 25.9 %collective-permute-start.3 = (bf16[256,1536]{0,1:T(8,128)(2,1)}, bf16[256,1536]{0,1:T(8,128)(2,1)S(1)}, u32[]{:S(2)}, u32[]{:S(2)}) collective-permute-start(bf16[256,1536]{0,1:T(8,128)(2,1)} %reshape.109), channel_id=1, source_target_pairs={{0,4},{8,0},{16,8},{24,16},{28,24},{20,28},{12,20},{4,12},{1,5},{9... | collective-permute-start | bytes 2359304 | tf_op jit(solution)/shard_map/ppermute | solution.py:119
  119.9 38.6 %collective-permute-start.4 = (bf16[256,1536]{0,1:T(8,128)(2,1)}, bf16[256,1536]{0,1:T(8,128)(2,1)}, u32[]{:S(2)}, u32[]{:S(2)}) collective-permute-start(bf16[256,1536]{0,1:T(8,128)(2,1)} %collective-permute-done.1), channel_id=1, source_target_pairs={{0,8},{8,16},{16,24},{24,28},{28,20},{20,12},{12,4},{4,0},{1,9},{9... | collective-permute-start | bytes 2359304 | tf_op jit(solution)/shard_map/ppermute | solution.py:117
  136.8 2.0 copy-start.2
  139.6 15.2 %collective-permute-start.7 = (f32[2,256,256]{1,2,0:T(8,128)}, f32[2,256,256]{1,2,0:T(8,128)}, u32[]{:S(2)}, u32[]{:S(2)}) collective-permute-start(f32[2,256,256]{1,2,0:T(8,128)} %pad_maximum_fusion), channel_id=1, source_target_pairs={{0,4},{8,0},{16,8},{24,16},{28,24},{20,28},{12,20},{4,12},{1,5},{9... | collective-permute-start | bytes 1572872 | tf_op jit(solution)/shard_map/ppermute | solution.py:149
  141.7 26.4 %collective-permute-start.2 = (bf16[256,1536]{0,1:T(8,128)(2,1)S(1)}, bf16[256,1536]{0,1:T(8,128)(2,1)}, u32[]{:S(2)}, u32[]{:S(2)}) collective-permute-start(bf16[256,1536]{0,1:T(8,128)(2,1)S(1)} %collective-permute-done), channel_id=1, source_target_pairs={{0,8},{8,16},{16,24},{24,28},{28,20},{20,12},{12,4},{4,0},{1,9},{9... | collective-permute-start | bytes 2359304 | tf_op jit(solution)/shard_map/ppermute | solution.py:117
  145.4 29.9 %collective-permute-start.10 = (bf16[256,1536]{0,1:T(8,128)(2,1)}, bf16[256,1536]{0,1:T(8,128)(2,1)}, u32[]{:S(2)}, u32[]{:S(2)}) collective-permute-start(bf16[256,1536]{0,1:T(8,128)(2,1)} %collective-permute-done.5), channel_id=1, source_target_pairs={{0,4},{8,0},{16,8},{24,16},{28,24},{20,28},{12,20},{4,12},{1,5},{9... | collective-permute-start | bytes 2359304 | tf_op jit(solution)/shard_map/ppermute | solution.py:119
  147.5 43.7 %collective-permute-start.9 = (bf16[256,1536]{0,1:T(8,128)(2,1)}, bf16[256,1536]{0,1:T(8,128)(2,1)}, u32[]{:S(2)}, u32[]{:S(2)}) collective-permute-start(bf16[256,1536]{0,1:T(8,128)(2,1)} %copy-done.2), channel_id=1, source_target_pairs={{0,4},{8,0},{16,8},{24,16},{28,24},{20,28},{12,20},{4,12},{1,5},{9... | collective-permute-start | bytes 2359304 | tf_op jit(solution)/shard_map/ppermute | solution.py:119
  169.9 26.2 %collective-permute-start.6 = (f32[1,256,256]{1,2,0:T(8,128)S(1)}, f32[1,256,256]{1,2,0:T(8,128)S(1)}, u32[]{:S(2)}, u32[]{:S(2)}) collective-permute-start(f32[1,256,256]{1,2,0:T(8,128)S(1)} %bitcast.152), channel_id=1, source_target_pairs={{0,12},{8,4},{16,0},{24,8},{28,16},{20,24},{12,28},{4,20},{1,13},{... | collective-permute-start | bytes 786440 | tf_op jit(solution)/shard_map/ppermute | solution.py:149
  174.5 23.4 %copy-start.4 = (f32[256,256]{1,0:T(8,128)S(1)}, f32[256,256]{1,0:T(8,128)}, u32[]{:S(2)}) copy-start(f32[256,256]{1,0:T(8,128)} %copy.33) | copy-start | bytes 786436
  174.5 23.5 %collective-permute-start.8 = (f32[2,256,256]{2,1,0:T(8,128)}, f32[2,256,256]{2,1,0:T(8,128)S(1)}, u32[]{:S(2)}, u32[]{:S(2)}) collective-permute-start(f32[2,256,256]{2,1,0:T(8,128)} %pad_maximum_fusion.1), channel_id=1, source_target_pairs={{0,8},{8,16},{16,24},{24,28},{28,20},{20,12},{12,4},{4,0},{1,9},{9... | collective-permute-start | bytes 1572872 | tf_op jit(solution)/shard_map/ppermute | solution.py:149
  193.8 7.9 %collective-permute-start.11 = (f32[1,256,256]{2,1,0:T(8,128)}, f32[1,256,256]{2,1,0:T(8,128)}, u32[]{:S(2)}, u32[]{:S(2)}) collective-permute-start(f32[1,256,256]{2,1,0:T(8,128)} %fusion.35), channel_id=1, source_target_pairs={{0,16},{8,24},{16,28},{24,20},{28,12},{20,4},{12,0},{4,8},{1,17},{... | collective-permute-start | bytes 786440 | tf_op jit(solution)/shard_map/ppermute | solution.py:149
  196.1 0.7 copy-start.5
  202.7 2.9 %collective-permute-start.12 = (f32[2,512,256]{2,1,0:T(8,128)S(1)}, f32[2,512,256]{2,1,0:T(8,128)}, u32[]{:S(2)}, u32[]{:S(2)}) collective-permute-start(f32[2,512,256]{2,1,0:T(8,128)S(1)} %dynamic-slice_bitcast_fusion), channel_id=1, source_target_pairs={{0,1},{1,0},{2,3},{3,2},{4,5},{5,4},{6,7},{7,6},{8,9},{9,8},{10,11... | collective-permute-start | bytes 3145736 | tf_op jit(solution)/shard_map/ppermute | solution.py:59
  206.9 14.0 %collective-permute-start.13 = (f32[512,256]{1,0:T(8,128)S(1)}, f32[512,256]{1,0:T(8,128)S(1)}, u32[]{:S(2)}, u32[]{:S(2)}) collective-permute-start(f32[512,256]{1,0:T(8,128)S(1)} %dynamic-slice_bitcast_fusion.1), channel_id=1, source_target_pairs={{0,2},{1,3},{2,0},{3,1},{4,6},{5,7},{6,4},{7,5},{8,10},{9,11},{10,... | collective-permute-start | bytes 1572872 | tf_op jit(solution)/shard_map/ppermute | solution.py:59

commit v15 on v14

--- a/solution.py
+++ b/solution.py
@@ -92,16 +92,16 @@
         occ_c = n_occ // n_split
         radius = n // 4
         helds = []
+        pieces = picked.reshape(n_mu, knu, NB, n_split, occ_c)
+        blank = jnp.zeros_like(pieces)
+        weight = jnp.concatenate(
+            [jnp.concatenate([pieces, blank], axis=-1), jnp.concatenate([blank, pieces], axis=-1)], axis=-3
+        )
+        whole = jnp.einsum("qkmtl,mklhc->qmthc", tc, weight, preferred_element_type=jnp.float32)
+        whole = whole.reshape(aux_dev, n_mu, tiles, n_split, pair, occ_c)
+        whole = jnp.where(row_live.reshape(1, n_mu, tiles, 1, pair, 1), whole, 0.0).astype(jnp.bfloat16)
         for h in range(n_split):
-            part = picked[..., h * occ_c:(h + 1) * occ_c]
-            blank = jnp.zeros_like(part)
-            weight = jnp.concatenate(
-                [jnp.concatenate([part, blank], axis=-1), jnp.concatenate([blank, part], axis=-1)], axis=-2
-            )
-            half = jnp.einsum("qkmtl,mklc->qmtc", tc, weight, preferred_element_type=jnp.float32)
-            half = half.reshape(aux_dev, n_mu, NB, occ_c)
-            half = jnp.where(row_live[None, :, :, None], half, 0.0).astype(jnp.bfloat16)
-            half = half.reshape(aux_dev, n_mu, NB * occ_c)
+            half = whole[:, :, :, h].reshape(aux_dev, n_mu, NB * occ_c)
             regrouped = lax.all_to_all(half, "grp", split_axis=1, concat_axis=0, tiled=True)
             n_aux = regrouped.shape[0]
             mu_dev = regrouped.shape[1]

time: 223 us -> 246 us (1.10)
  local copies, waits for them, and re-layouts: 47.5 us -> 93.5 us
  blocking collectives: 27.3 us -> 0 us
  starting transfers between devices: 22.2 us -> 31.3 us
  matrix products: 37.8 us -> 31.2 us
    another operation x0 -> x4, local copies, waits for them, and re-layouts: none -> 43.3 us  [body(): half = whole[:, :, :, h].reshape(aux_dev, n_mu, NB * occ_c)]
    all_to_all x1 -> x0, blocking collectives: 27.3 us -> none  [body(): lax.all_to_all(half, 'grp', split_axis=1, concat_axis=0, tiled=True)]
    reshape x2 -> x0, local copies, waits for them, and re-layouts: 9.22 us -> none  [body(): half = half.reshape(aux_dev, n_mu, NB, occ_c)]
    all_to_all x1 -> x2, starting transfers between devices: 4.23 us -> 13.2 us  [body(): lax.all_to_all(half, 'grp', split_axis=1, concat_axis=0, tiled=True)]
    transpose x0 -> x1, local copies, waits for them, and re-layouts: none -> 7.93 us  [body(): jnp.einsum('qkmtl,mklhc->qmthc', tc, weight, preferred_element_type=jnp.f...]
    dot_general x2 -> x1, matrix products: 19.1 us -> 13.6 us  [body(): jnp.einsum('qkmtl,mklhc->qmthc', tc, weight, preferred_element_type=jnp.f...]
    all_to_all x0 -> x2, local copies, waits for them, and re-layouts: none -> 3.08 us  [body(): lax.all_to_all(half, 'grp', split_axis=1, concat_axis=0, tiled=True)]
    convert_element_type x1, other arithmetic: 1.27 us -> 4.34 us  [body(): jnp.where(row_live.reshape(1, n_mu, tiles, 1, pair, 1), whole, 0.0)]
  transfers between devices with their start and end apart: 15 -> 16, of which waited for: 11 -> 10; matrix products, arithmetic and copies ran while one was open for 17% -> 25% of each run, Pallas kernels for 0% -> 0%
where the time goes in v15:
time: 246 us; the launch traced here: 243 us
  local copies, waits for them, and re-layouts  93.5 us (38%)
  waiting for transfers between devices  63.9 us (26%)
  starting transfers between devices  31.3 us (13%)
  matrix products  31.2 us (13%)
  between operations  12.2 us (5%)
  other arithmetic  10.9 us (4%)
    another operation x4, local copies, waits for them, and re-layouts, body(): half = whole[:, :, :, h].reshape(aux_dev, n_mu, NB * occ_c)  43.3 us
    ppermute x4, waiting for transfers between devices, body(): fwd = lax.ppermute(fwd, 'grp', shifted(1))  24 us
    dot_general x10, matrix products, prod(): one = jnp.dot(held[xo], held[yo].T, preferred_element_type=jnp.float32)  16.8 us
    ppermute x2, waiting for transfers between devices, scatter_sum(): got = lax.ppermute(send, 'rep', [(i, i ^ d) for i in range(n_rep)])  15.2 us
    dot_general x1, matrix products, body(): jnp.einsum('qkmtl,mklhc->qmthc', tc, weight, preferred_element_type=jnp.f...  13.6 us
    ppermute x4, waiting for transfers between devices, body(): bwd = lax.ppermute(bwd, 'grp', shifted(-1))  13.4 us
    all_to_all x2, starting transfers between devices, body(): lax.all_to_all(half, 'grp', split_axis=1, concat_axis=0, tiled=True)  13.2 us
    unnamed x19, local copies, waits for them, and re-layouts  12.5 us
  transfers between devices with their start and end apart: 16, of which 10 were waited for; matrix products, arithmetic and copies ran while one was open for 25% of the time, Pallas kernels for 0%

profile of v15, /device:TPU:0, one launch (start us, length us, event | category | flops | bytes accessed | tf_op | source)
XLA Modules:
  0.0 242.9 jit_solution(300465846935971111)
XLA Ops:
  0.0 0.7 compare_select_fusion
  0.9 1.3 reshape.96
  2.4 1.0 gather_fusion.1
  3.5 1.6 gather_fusion
  5.2 11.5 %copy.69 = bf16[192,8,32,128]{3,2,1,0:T(8,128)(2,1)} copy(bf16[192,8,32,128]{3,1,2,0:T(8,128)(2,1)} %bitcast.133) | data formatting | bytes 25165824
  16.8 1.7 copy_select_fusion
  18.5 13.6 %fusion.13 = bf16[8,32,32,2,48]{4,2,0,3,1:T(8,128)(2,1)} fusion(bf16[8,6,32,32,128,1]{4,3,2,1,0,5:T(8,128)(2,1)} %bitcast.134, bf16[32,6,64,2,24]{2,4,1,3,0:T(8,128)(2,1)} %copy_select_fusion), kind=kOutput, calls=%fused_computation.18 | convolution fusion | flops 1226833920 | bytes 15335424 | tf_op jit(solution)/shard_map/qkmtl,mklhc->qmthc/dot_general | solution.py:100
  32.1 7.9 %copy.46 = bf16[8,32,32,2,48]{2,4,3,1,0:T(8,128)(2,1)} copy(bf16[8,32,32,2,48]{4,2,0,3,1:T(8,128)(2,1)} %fusion.13) | data formatting | bytes 3145728 | tf_op jit(solution)/shard_map/qkmtl,mklhc->qmthc/transpose | solution.py:100
  40.1 4.3 %select_convert_fusion = bf16[8,32,32,2,2,24]{2,5,4,3,1,0:T(8,128)(2,1)S(1)} fusion(bf16[8,32,32,2,2,24]{2,5,4,3,1,0:T(8,128)(2,1)} %bitcast.131, pred[32,32,2]{1,2,0:T(4,128)(4,1)S(1)} %broadcast_compare_fusion), kind=kLoop, calls=%fused_computation.4 | loop fusion | flops 786432 | bytes 3147776 | tf_op jit(solution)/shard_map/convert_element_type | solution.py:102
  44.5 3.3 %fusion.29 = (bf16[8,32,32,1,2,24]{2,5,4,3,1,0:T(8,128)(2,1)}, bf16[8,32,32,1,2,24]{2,5,4,3,1,0:T(8,128)(2,1)S(1)}) fusion(bf16[8,32,32,2,2,24]{2,5,4,3,1,0:T(8,128)(2,1)S(1)} %select_convert_fusion), kind=kLoop, calls=%fused_computation.59 | loop fusion | bytes 3145728 | tf_op jit(solution)/shard_map/slice | solution.py:104
  47.8 10.2 %copy.66 = bf16[8,32,32,1,2,24]{5,4,2,0,1,3:T(2,128)(2,1)} copy(bf16[8,32,32,1,2,24]{2,5,4,3,1,0:T(8,128)(2,1)} %get-tuple-element.5) | data formatting | bytes 1572864 | tf_op jit(solution)/shard_map/reshape;squeeze | solution.py:104
  58.0 12.8 %reshape.131 = bf16[8,32,1536]{2,0,1:T(8,128)(2,1)} reshape(bf16[8,32,32,1,2,24]{5,4,2,0,1,3:T(2,128)(2,1)} %copy.66) | data formatting | bytes 1572864 | tf_op jit(solution)/shard_map/reshape;squeeze | solution.py:104
  70.8 7.3 %all-to-all-start.1 = ((bf16[8,32,1536]{2,0,1:T(8,128)(2,1)}), bf16[8,32,1536]{2,0,1:T(8,128)(2,1)}, u32[]{:S(2)}, u32[]{:S(2)}) async-start(bf16[8,32,1536]{2,0,1:T(8,128)(2,1)} %reshape.131), calls=%async_computation.1 | async-start | bytes 1572864 | tf_op jit(solution)/shard_map/all_to_all | solution.py:105
  78.1 7.5 %copy.65 = bf16[8,32,32,1,2,24]{5,4,2,0,1,3:T(2,128)(2,1)} copy(bf16[8,32,32,1,2,24]{2,5,4,3,1,0:T(8,128)(2,1)S(1)} %get-tuple-element.6) | data formatting | bytes 1572864 | tf_op jit(solution)/shard_map/reshape;squeeze | solution.py:104
  85.5 12.8 %reshape.130 = bf16[8,32,1536]{2,0,1:T(8,128)(2,1)} reshape(bf16[8,32,32,1,2,24]{5,4,2,0,1,3:T(2,128)(2,1)} %copy.65) | data formatting | bytes 1572864 | tf_op jit(solution)/shard_map/reshape;squeeze | solution.py:104
  98.4 6.0 %all-to-all-start = ((bf16[8,32,1536]{2,0,1:T(8,128)(2,1)}), bf16[8,32,1536]{2,0,1:T(8,128)(2,1)}, u32[]{:S(2)}, u32[]{:S(2)}) async-start(bf16[8,32,1536]{2,0,1:T(8,128)(2,1)} %reshape.130), calls=%async_computation | async-start | bytes 1572864 | tf_op jit(solution)/shard_map/all_to_all | solution.py:105
  111.6 0.7 fusion.30
  113.6 1.5 copy.79
  115.6 0.9 copy.55
  116.5 3.2 %copy.56 = bf16[4,64,64,24]{1,0,3,2:T(4,128)(2,1)S(1)} copy(bf16[4,64,64,24]{2,3,1,0:T(8,128)(2,1)S(1)} %bitcast.137) | data formatting | bytes 1572864 | tf_op jit(solution)/shard_map/transpose | solution.py:110
  119.7 1.7 reshape.104
  121.5 2.0 collective-permute-start.1
  124.2 1.5 copy.80
  126.2 0.9 copy.50
  127.1 3.2 %copy.51 = bf16[4,64,64,24]{1,0,3,2:T(4,128)(2,1)S(1)} copy(bf16[4,64,64,24]{2,3,1,0:T(8,128)(2,1)S(1)} %bitcast.138) | data formatting | bytes 1572864 | tf_op jit(solution)/shard_map/transpose | solution.py:110
  130.3 1.7 reshape.101
  132.0 1.4 collective-permute-start
  133.4 0.7 collective-permute-start.3
  134.1 1.8 fusion.31
  136.0 1.8 fusion.19
  137.8 4.5 %collective-permute-done.1 = bf16[256,1536]{0,1:T(8,128)(2,1)} collective-permute-done((bf16[256,1536]{0,1:T(8,128)(2,1)}, bf16[256,1536]{0,1:T(8,128)(2,1)}, u32[]{:S(2)}, u32[]{:S(2)}) %collective-permute-start.1) | collective-permute-done | bytes 786464 | tf_op jit(solution)/shard_map/ppermute | solution.py:117
  142.3 2.0 collective-permute-start.4
  144.3 1.8 fusion.32
  146.1 1.8 fusion.34
  147.8 11.2 %collective-permute-done = bf16[256,1536]{0,1:T(8,128)(2,1)S(1)} collective-permute-done((bf16[256,1536]{0,1:T(8,128)(2,1)}, bf16[256,1536]{0,1:T(8,128)(2,1)S(1)}, u32[]{:S(2)}, u32[]{:S(2)}) %collective-permute-start) | collective-permute-done | bytes 786464 | tf_op jit(solution)/shard_map/ppermute | solution.py:117
  159.4 1.6 constant_dynamic-update-slice_fusion.3
  161.0 0.8 pad_maximum_fusion
  161.8 2.0 collective-permute-start.7
  167.6 2.1 collective-permute-start.10
  169.7 1.5 collective-permute-start.9
  171.2 5.8 %collective-permute-done.7 = f32[2,256,256]{1,2,0:T(8,128)} collective-permute-done((f32[2,256,256]{1,2,0:T(8,128)}, f32[2,256,256]{1,2,0:T(8,128)}, u32[]{:S(2)}, u32[]{:S(2)}) %collective-permute-start.7) | collective-permute-done | bytes 524320 | tf_op jit(solution)/shard_map/ppermute | solution.py:149
  177.0 1.8 slice_bitcast_fusion.2
  178.8 0.9 copy.58
  179.6 1.1 copy.59
  180.7 1.8 fusion.33
  182.5 8.3 %collective-permute-done.2 = bf16[256,1536]{0,1:T(8,128)(2,1)} collective-permute-done((bf16[256,1536]{0,1:T(8,128)(2,1)S(1)}, bf16[256,1536]{0,1:T(8,128)(2,1)}, u32[]{:S(2)}, u32[]{:S(2)}) %collective-permute-start.2) | collective-permute-done | bytes 786464 | tf_op jit(solution)/shard_map/ppermute | solution.py:117
  190.8 1.8 convolution_add_fusion.2
  192.6 2.7 %collective-permute-start.6 = (f32[1,256,256]{1,2,0:T(8,128)S(1)}, f32[1,256,256]{1,2,0:T(8,128)S(1)}, u32[]{:S(2)}, u32[]{:S(2)}) collective-permute-start(f32[1,256,256]{1,2,0:T(8,128)S(1)} %bitcast.146), channel_id=1, source_target_pairs={{0,12},{8,4},{16,0},{24,8},{28,16},{20,24},{12,28},{4,20},{1,13},{... | collective-permute-start | bytes 786440 | tf_op jit(solution)/shard_map/ppermute | solution.py:149
  195.3 0.8 pad_maximum_fusion.1
  196.1 0.9 collective-permute-start.8
  197.0 1.8 fusion.35
  198.8 13.4 %collective-permute-done.9 = bf16[256,1536]{0,1:T(8,128)(2,1)} collective-permute-done((bf16[256,1536]{0,1:T(8,128)(2,1)}, bf16[256,1536]{0,1:T(8,128)(2,1)}, u32[]{:S(2)}, u32[]{:S(2)}) %collective-permute-start.9) | collective-permute-done | bytes 786464 | tf_op jit(solution)/shard_map/ppermute | solution.py:119
  212.2 2.5 %fusion.20 = f32[1,256,256]{2,1,0:T(8,128)} fusion(f32[256,256]{1,0:T(8,128)S(1)} %fusion.35, bf16[256,1536]{0,1:T(8,128)(2,1)} %collective-permute-done.2, bf16[256,1536]{0,1:T(8,128)(2,1)} %collective-permute-done.9), kind=kOutput, calls=%fused_computation.27 | convolution fusion | flops 201392128 | bytes 2097152 | tf_op jit(solution)/shard_map/dot_general | solution.py:129
  214.7 1.2 collective-permute-start.11
  215.9 2.7 %collective-permute-done.6 = f32[1,256,256]{1,2,0:T(8,128)S(1)} collective-permute-done((f32[1,256,256]{1,2,0:T(8,128)S(1)}, f32[1,256,256]{1,2,0:T(8,128)S(1)}, u32[]{:S(2)}, u32[]{:S(2)}) %collective-permute-start.6) | collective-permute-done | bytes 262176 | tf_op jit(solution)/shard_map/ppermute | solution.py:149
  218.6 0.7 copy-done.4
  219.3 1.1 copy.57
  220.6 2.1 collective-permute-done.11
  222.7 1.0 bitcast_dynamic-update-slice_fusion
  223.9 2.7 %collective-permute-done.12 = f32[2,512,256]{2,1,0:T(8,128)} collective-permute-done((f32[2,512,256]{2,1,0:T(8,128)S(1)}, f32[2,512,256]{2,1,0:T(8,128)}, u32[]{:S(2)}, u32[]{:S(2)}) %collective-permute-start.12) | collective-permute-done | bytes 1048608 | tf_op jit(solution)/shard_map/ppermute | solution.py:59
  226.6 1.4 bitcast_add_fusion
  228.0 1.6 collective-permute-start.13
  229.6 12.4 %collective-permute-done.13 = f32[512,256]{1,0:T(8,128)S(1)} collective-permute-done((f32[512,256]{1,0:T(8,128)S(1)}, f32[512,256]{1,0:T(8,128)S(1)}, u32[]{:S(2)}, u32[]{:S(2)}) %collective-permute-start.13) | collective-permute-done | bytes 524320 | tf_op jit(solution)/shard_map/ppermute | solution.py:59
  242.0 0.9 bitcast_add_fusion.1
  (48 shorter events, 3.9 us)
Async XLA Ops:
  0.0 115.3 %copy-start = (bf16[1,64,64]{2,1,0:T(8,128)(2,1)S(1)}, bf16[1,64,64]{2,1,0:T(8,128)(2,1)}, u32[]{:S(2)}) copy-start(bf16[1,64,64]{2,1,0:T(8,128)(2,1)} %param.9) | copy-start | bytes 24580
  2.4 1.0 copy-start.1
  3.5 1.7 copy-start.6
  70.8 27.6 %all-to-all-start.1 = ((bf16[8,32,1536]{2,0,1:T(8,128)(2,1)}), bf16[8,32,1536]{2,0,1:T(8,128)(2,1)}, u32[]{:S(2)}, u32[]{:S(2)}) async-start(bf16[8,32,1536]{2,0,1:T(8,128)(2,1)} %reshape.131), calls=%async_computation.1 | async-start | bytes 1572864 | tf_op jit(solution)/shard_map/all_to_all | solution.py:105
  85.5 18.8 %copy-start.7 = (s32[8]{0:T(128)S(1)}, s32[8]{0:T(128)}, u32[]{:S(2)}) copy-start(s32[8]{0:T(128)} %constant.136.clone) | copy-start | bytes 100
  85.5 26.0 %copy-start.5 = (s32[8]{0:T(128)S(1)}, s32[8]{0:T(128)}, u32[]{:S(2)}) copy-start(s32[8]{0:T(128)} %constant.137.clone) | copy-start | bytes 100
  98.4 25.8 %all-to-all-start = ((bf16[8,32,1536]{2,0,1:T(8,128)(2,1)}), bf16[8,32,1536]{2,0,1:T(8,128)(2,1)}, u32[]{:S(2)}, u32[]{:S(2)}) async-start(bf16[8,32,1536]{2,0,1:T(8,128)(2,1)} %reshape.130), calls=%async_computation | async-start | bytes 1572864 | tf_op jit(solution)/shard_map/all_to_all | solution.py:105
  121.5 20.8 %collective-permute-start.1 = (bf16[256,1536]{0,1:T(8,128)(2,1)}, bf16[256,1536]{0,1:T(8,128)(2,1)}, u32[]{:S(2)}, u32[]{:S(2)}) collective-permute-start(bf16[256,1536]{0,1:T(8,128)(2,1)} %reshape.104), channel_id=1, source_target_pairs={{0,8},{8,16},{16,24},{24,28},{28,20},{20,12},{12,4},{4,0},{1,9},{9... | collective-permute-start | bytes 2359304 | tf_op jit(solution)/shard_map/ppermute | solution.py:117
  123.5 22.6 %collective-permute-start.5 = (bf16[256,1536]{0,1:T(8,128)(2,1)}, bf16[256,1536]{0,1:T(8,128)(2,1)}, u32[]{:S(2)}, u32[]{:S(2)}) collective-permute-start(bf16[256,1536]{0,1:T(8,128)(2,1)} %reshape.104), channel_id=1, source_target_pairs={{0,4},{8,0},{16,8},{24,16},{28,24},{20,28},{12,20},{4,12},{1,5},{9... | collective-permute-start | bytes 2359304 | tf_op jit(solution)/shard_map/ppermute | solution.py:119
  132.0 27.0 %collective-permute-start = (bf16[256,1536]{0,1:T(8,128)(2,1)}, bf16[256,1536]{0,1:T(8,128)(2,1)S(1)}, u32[]{:S(2)}, u32[]{:S(2)}) collective-permute-start(bf16[256,1536]{0,1:T(8,128)(2,1)} %reshape.101), channel_id=1, source_target_pairs={{0,8},{8,16},{16,24},{24,28},{28,20},{20,12},{12,4},{4,0},{1,9},{9... | collective-permute-start | bytes 2359304 | tf_op jit(solution)/shard_map/ppermute | solution.py:117
  133.4 25.6 %collective-permute-start.3 = (bf16[256,1536]{0,1:T(8,128)(2,1)}, bf16[256,1536]{0,1:T(8,128)(2,1)S(1)}, u32[]{:S(2)}, u32[]{:S(2)}) collective-permute-start(bf16[256,1536]{0,1:T(8,128)(2,1)} %reshape.101), channel_id=1, source_target_pairs={{0,4},{8,0},{16,8},{24,16},{28,24},{20,28},{12,20},{4,12},{1,5},{9... | collective-permute-start | bytes 2359304 | tf_op jit(solution)/shard_map/ppermute | solution.py:119
  142.3 38.4 %collective-permute-start.4 = (bf16[256,1536]{0,1:T(8,128)(2,1)}, bf16[256,1536]{0,1:T(8,128)(2,1)}, u32[]{:S(2)}, u32[]{:S(2)}) collective-permute-start(bf16[256,1536]{0,1:T(8,128)(2,1)} %collective-permute-done.1), channel_id=1, source_target_pairs={{0,8},{8,16},{16,24},{24,28},{28,20},{20,12},{12,4},{4,0},{1,9},{9... | collective-permute-start | bytes 2359304 | tf_op jit(solution)/shard_map/ppermute | solution.py:117
  159.0 2.8 %copy-start.2 = (bf16[256,1536]{0,1:T(8,128)(2,1)}, bf16[256,1536]{0,1:T(8,128)(2,1)S(1)}, u32[]{:S(2)}) copy-start(bf16[256,1536]{0,1:T(8,128)(2,1)S(1)} %collective-permute-done.3) | copy-start | bytes 2359300
  161.8 15.2 %collective-permute-start.7 = (f32[2,256,256]{1,2,0:T(8,128)}, f32[2,256,256]{1,2,0:T(8,128)}, u32[]{:S(2)}, u32[]{:S(2)}) collective-permute-start(f32[2,256,256]{1,2,0:T(8,128)} %pad_maximum_fusion), channel_id=1, source_target_pairs={{0,4},{8,0},{16,8},{24,16},{28,24},{20,28},{12,20},{4,12},{1,5},{9... | collective-permute-start | bytes 1572872 | tf_op jit(solution)/shard_map/ppermute | solution.py:149
  163.8 27.0 %collective-permute-start.2 = (bf16[256,1536]{0,1:T(8,128)(2,1)S(1)}, bf16[256,1536]{0,1:T(8,128)(2,1)}, u32[]{:S(2)}, u32[]{:S(2)}) collective-permute-start(bf16[256,1536]{0,1:T(8,128)(2,1)S(1)} %collective-permute-done), channel_id=1, source_target_pairs={{0,8},{8,16},{16,24},{24,28},{28,20},{20,12},{12,4},{4,0},{1,9},{9... | collective-permute-start | bytes 2359304 | tf_op jit(solution)/shard_map/ppermute | solution.py:117
  167.6 29.4 %collective-permute-start.10 = (bf16[256,1536]{0,1:T(8,128)(2,1)}, bf16[256,1536]{0,1:T(8,128)(2,1)}, u32[]{:S(2)}, u32[]{:S(2)}) collective-permute-start(bf16[256,1536]{0,1:T(8,128)(2,1)} %collective-permute-done.5), channel_id=1, source_target_pairs={{0,4},{8,0},{16,8},{24,16},{28,24},{20,28},{12,20},{4,12},{1,5},{9... | collective-permute-start | bytes 2359304 | tf_op jit(solution)/shard_map/ppermute | solution.py:119
  169.7 42.5 %collective-permute-start.9 = (bf16[256,1536]{0,1:T(8,128)(2,1)}, bf16[256,1536]{0,1:T(8,128)(2,1)}, u32[]{:S(2)}, u32[]{:S(2)}) collective-permute-start(bf16[256,1536]{0,1:T(8,128)(2,1)} %copy-done.2), channel_id=1, source_target_pairs={{0,4},{8,0},{16,8},{24,16},{28,24},{20,28},{12,20},{4,12},{1,5},{9... | collective-permute-start | bytes 2359304 | tf_op jit(solution)/shard_map/ppermute | solution.py:119
  192.6 26.1 %collective-permute-start.6 = (f32[1,256,256]{1,2,0:T(8,128)S(1)}, f32[1,256,256]{1,2,0:T(8,128)S(1)}, u32[]{:S(2)}, u32[]{:S(2)}) collective-permute-start(f32[1,256,256]{1,2,0:T(8,128)S(1)} %bitcast.146), channel_id=1, source_target_pairs={{0,12},{8,4},{16,0},{24,8},{28,16},{20,24},{12,28},{4,20},{1,13},{... | collective-permute-start | bytes 786440 | tf_op jit(solution)/shard_map/ppermute | solution.py:149
  196.1 24.4 %copy-start.3 = (f32[256,256]{1,0:T(8,128)S(1)}, f32[256,256]{1,0:T(8,128)}, u32[]{:S(2)}) copy-start(f32[256,256]{1,0:T(8,128)} %copy.58) | copy-start | bytes 786436
  196.1 24.4 %collective-permute-start.8 = (f32[2,256,256]{2,1,0:T(8,128)}, f32[2,256,256]{2,1,0:T(8,128)S(1)}, u32[]{:S(2)}, u32[]{:S(2)}) collective-permute-start(f32[2,256,256]{2,1,0:T(8,128)} %pad_maximum_fusion.1), channel_id=1, source_target_pairs={{0,8},{8,16},{16,24},{24,28},{28,20},{20,12},{12,4},{4,0},{1,9},{9... | collective-permute-start | bytes 1572872 | tf_op jit(solution)/shard_map/ppermute | solution.py:149
  214.7 8.0 %collective-permute-start.11 = (f32[1,256,256]{2,1,0:T(8,128)}, f32[1,256,256]{2,1,0:T(8,128)}, u32[]{:S(2)}, u32[]{:S(2)}) collective-permute-start(f32[1,256,256]{2,1,0:T(8,128)} %fusion.20), channel_id=1, source_target_pairs={{0,16},{8,24},{16,28},{24,20},{28,12},{20,4},{12,0},{4,8},{1,17},{... | collective-permute-start | bytes 786440 | tf_op jit(solution)/shard_map/ppermute | solution.py:149
  218.6 0.7 copy-start.4
  223.7 2.9 %collective-permute-start.12 = (f32[2,512,256]{2,1,0:T(8,128)S(1)}, f32[2,512,256]{2,1,0:T(8,128)}, u32[]{:S(2)}, u32[]{:S(2)}) collective-permute-start(f32[2,512,256]{2,1,0:T(8,128)S(1)} %dynamic-slice_bitcast_fusion), channel_id=1, source_target_pairs={{0,1},{1,0},{2,3},{3,2},{4,5},{5,4},{6,7},{7,6},{8,9},{9,8},{10,11... | collective-permute-start | bytes 3145736 | tf_op jit(solution)/shard_map/ppermute | solution.py:59
  228.0 14.0 %collective-permute-start.13 = (f32[512,256]{1,0:T(8,128)S(1)}, f32[512,256]{1,0:T(8,128)S(1)}, u32[]{:S(2)}, u32[]{:S(2)}) collective-permute-start(f32[512,256]{1,0:T(8,128)S(1)} %dynamic-slice_bitcast_fusion.1), channel_id=1, source_target_pairs={{0,2},{1,3},{2,0},{3,1},{4,6},{5,7},{6,4},{7,5},{8,10},{9,11},{10,... | collective-permute-start | bytes 1572872 | tf_op jit(solution)/shard_map/ppermute | solution.py:59

commit v16 on v11

--- a/solution.py
+++ b/solution.py
@@ -92,31 +92,36 @@
         half = jnp.einsum("qkmtl,mklc->qmtc", tc, weight, preferred_element_type=jnp.float32)
         half = half.reshape(aux_dev, n_mu, NB, n_occ)
         half = jnp.where(row_live[None, :, :, None], half, 0.0).astype(jnp.bfloat16)
-        half = half.reshape(aux_dev, n_mu, NB * n_occ)
-        regrouped = lax.all_to_all(half, "grp", split_axis=1, concat_axis=0, tiled=True)
-        n_aux = regrouped.shape[0]
-        mu_dev = regrouped.shape[1]
-        mixed = jnp.dot(metric[0], regrouped.reshape(n_aux, -1), preferred_element_type=jnp.float32)
-        mixed = mixed.astype(jnp.bfloat16).reshape(n_aux, mu_dev, NB, n_occ)
-        orbital = jnp.transpose(mixed, (1, 2, 0, 3))
-        rows = mu_dev * NB
-        orbital = orbital.reshape(rows, n_aux * n_occ)
+        mu_dev = n_mu // n
+        n_split = 2 if mu_dev % 2 == 0 else 1
+        mu_c = mu_dev // n_split
+        half = half.reshape(aux_dev, n, mu_dev, NB * n_occ)
         me = lax.axis_index("grp")
         pos = jnp.asarray(pos_of)[me]
         ring_c = jnp.asarray(ring_arr)
+        radius = n // 4
+        helds = []
+        for h in range(n_split):
+            part = half[:, :, h * mu_c:(h + 1) * mu_c].reshape(aux_dev, n * mu_c, NB * n_occ)
+            regrouped = lax.all_to_all(part, "grp", split_axis=1, concat_axis=0, tiled=True)
+            n_aux = regrouped.shape[0]
+            mixed = jnp.dot(metric[0], regrouped.reshape(n_aux, -1), preferred_element_type=jnp.float32)
+            mixed = mixed.astype(jnp.bfloat16).reshape(n_aux, mu_c, NB, n_occ)
+            orbital = jnp.transpose(mixed, (1, 2, 0, 3)).reshape(mu_c * NB, n_aux * n_occ)
+            held = {0: orbital}
+            fwd = orbital
+            bwd = orbital
+            for k in range(1, radius + 1):
+                fwd = lax.ppermute(fwd, "grp", shifted(1))
+                held[-k] = fwd
+                bwd = lax.ppermute(bwd, "grp", shifted(-1))
+                held[k] = bwd
+            helds.append(held)
+        held = {off: jnp.concatenate([hd[off] for hd in helds], axis=0) for off in helds[0]}
+        rows = mu_dev * NB
 
         def start_of(off):
             return ring_c[(pos + off) % n] * rows
-
-        radius = n // 4
-        held = {0: orbital}
-        fwd = orbital
-        bwd = orbital
-        for k in range(1, radius + 1):
-            fwd = lax.ppermute(fwd, "grp", shifted(1))
-            held[-k] = fwd
-            bwd = lax.ppermute(bwd, "grp", shifted(-1))
-            held[k] = bwd
 
         def prod(xo, yo):
             return jnp.dot(held[xo], held[yo].T, preferred_element_type=jnp.float32)

time: 219 us -> 209 us (0.954)
  waiting for transfers between devices: 87 us -> 67.4 us
  local copies, waits for them, and re-layouts: 36.8 us -> 54.6 us
  blocking collectives: 44.1 us -> 27.3 us
  starting transfers between devices: 12.2 us -> 20.7 us
    ppermute x4, waiting for transfers between devices: 47.7 us -> 11.6 us  [body(): got = lax.ppermute(stack, 'grp', shifted(s))]
    all_to_all x1, blocking collectives: 44.1 us -> 27.3 us  [body(): lax.all_to_all(part, 'grp', split_axis=1, concat_axis=0, tiled=True)]
    ppermute x2 -> x4, waiting for transfers between devices: 0.01 us -> 12.4 us  [body(): bwd = lax.ppermute(bwd, 'grp', shifted(-1))]
    unnamed x15 -> x23, local copies, waits for them, and re-layouts: 8.08 us -> 14.1 us
    ppermute x2 -> x4, starting transfers between devices: 1.85 us -> 7.54 us  [body(): fwd = lax.ppermute(fwd, 'grp', shifted(1))]
    reshape x2 -> x4, local copies, waits for them, and re-layouts: 8.33 us -> 12.5 us  [the longest x2 7.01 us: body(): jnp.transpose(mixed, (1, 2, 0, 3)).reshape(mu_c * NB, n_aux * n_occ)]
    ppermute x2 -> x4, waiting for transfers between devices: 24.1 us -> 28.2 us  [body(): fwd = lax.ppermute(fwd, 'grp', shifted(1))]
    concatenate x0 -> x4, local copies, waits for them, and re-layouts: none -> 3.78 us  [body(): jnp.concatenate([hd[off] for hd in helds], axis=0)]
  transfers between devices with their start and end apart: 10 -> 15, of which waited for: 7 -> 11; matrix products, arithmetic and copies ran while one was open for 7% -> 21% of each run, Pallas kernels for 0% -> 0%
where the time goes in v16:
time: 209 us; the launch traced here: 206 us
  waiting for transfers between devices  67.4 us (32%)
  local copies, waits for them, and re-layouts  54.6 us (26%)
  blocking collectives  27.3 us (13%)
  starting transfers between devices  20.7 us (10%)
  matrix products  17.2 us (8%)
  between operations  12.1 us (6%)
  other arithmetic  6.92 us (3%)
    ppermute x4, waiting for transfers between devices, body(): fwd = lax.ppermute(fwd, 'grp', shifted(1))  28.2 us
    all_to_all x1, blocking collectives, body(): lax.all_to_all(part, 'grp', split_axis=1, concat_axis=0, tiled=True)  27.3 us
    ppermute x2, waiting for transfers between devices, scatter_sum(): got = lax.ppermute(send, 'rep', [(i, i ^ d) for i in range(n_rep)])  15.2 us
    unnamed x23, local copies, waits for them, and re-layouts  14.1 us
    ppermute x4, waiting for transfers between devices, body(): bwd = lax.ppermute(bwd, 'grp', shifted(-1))  12.4 us
    ppermute x4, waiting for transfers between devices, body(): got = lax.ppermute(stack, 'grp', shifted(s))  11.6 us
    transpose x2, local copies, waits for them, and re-layouts, body(): jnp.transpose(mixed, (1, 2, 0, 3)).reshape(mu_c * NB, n_aux * n_occ)  8.5 us
    dot_general x5, matrix products, prod(): return jnp.dot(held[xo], held[yo].T, preferred_element_type=jnp.float32)  8.43 us
  transfers between devices with their start and end apart: 15, of which 11 were waited for; matrix products, arithmetic and copies ran while one was open for 21% of the time, Pallas kernels for 0%

profile of v16, /device:TPU:0, one launch (start us, length us, event | category | flops | bytes accessed | tf_op | source)
XLA Modules:
  0.0 206.2 jit_solution(4243646130246210751)
XLA Ops:
  0.0 0.7 compare_select_fusion
  0.9 1.3 reshape.104
  2.4 0.7 iota_compare_fusion.4
  3.2 1.6 gather_fusion
  4.7 1.0 gather_fusion.1
  5.9 7.4 %copy.30 = bf16[192,8,32,128]{3,2,1,0:T(8,128)(2,1)S(1)} copy(bf16[192,8,32,128]{3,1,2,0:T(8,128)(2,1)} %bitcast.112) | data formatting | bytes 25165824
  13.4 1.7 broadcast_select_fusion
  15.1 7.2 %fusion.14 = bf16[8,32,32,96]{3,2,0,1:T(8,128)(2,1)} fusion(bf16[8,6,32,32,128]{4,3,2,1,0:T(8,128)(2,1)S(1)} %bitcast.113, bf16[32,6,64,48]{2,3,1,0:T(8,128)(2,1)} %broadcast_select_fusion), kind=kOutput, calls=%fused_computation.20 | convolution fusion | flops 1226833920 | bytes 15335424 | tf_op jit(solution)/shard_map/qkmtl,mklc->qmtc/dot_general | solution.py:92
  22.3 4.2 %reshape.106 = bf16[8,8,4,3072]{3,0,2,1:T(8,128)(2,1)S(1)} reshape(bf16[8,32,32,96]{3,2,0,1:T(8,128)(2,1)} %fusion.14) | data formatting | bytes 3145728 | tf_op jit(solution)/shard_map/reshape | solution.py:93
  26.8 0.7 broadcast_in_dim.47
  27.6 0.5 select_convert_fusion
  28.1 1.0 fusion.35
  29.1 27.3 %all_to_all.30 = bf16[8,16,3072]{2,0,1:T(8,128)(2,1)S(1)} all-to-all(bf16[8,16,3072]{2,0,1:T(8,128)(2,1)S(1)} %bitcast.120), channel_id=1, replica_groups=mesh['grp'=8,'rep'=4] {'grp'}, dimensions={1} | all-to-all | bytes 1572864 | tf_op jit(solution)/shard_map/all_to_all | solution.py:106
  56.4 3.6 %all-to-all-start.1 = ((bf16[8,16,3072]{2,0,1:T(8,128)(2,1)}), bf16[8,16,3072]{2,0,1:T(8,128)(2,1)S(1)}, u32[]{:S(2)}, u32[]{:S(2)}) async-start(bf16[8,16,3072]{2,0,1:T(8,128)(2,1)} %bitcast.15), calls=%async_computation.1 | async-start | bytes 1572864 | tf_op jit(solution)/shard_map/all_to_all | solution.py:106
  60.0 0.6 dynamic_slice.41
  67.2 0.7 fusion.36
  69.2 1.2 fusion.4
  70.4 3.3 %reshape.109 = bf16[64,2,64,48]{3,2,1,0:T(8,128)(2,1)S(1)} reshape(bf16[64,6144]{1,0:T(8,128)(2,1)} %fusion.4) | data formatting | bytes 1572864 | tf_op jit(solution)/shard_map/reshape | solution.py:109
  73.7 4.2 %copy.23 = bf16[2,64,64,48]{1,0,3,2:T(2,128)(2,1)} copy(bf16[2,64,64,48]{3,1,0,2:T(8,128)(2,1)S(1)} %bitcast.116) | data formatting | bytes 1572864 | tf_op jit(solution)/shard_map/transpose | solution.py:110
  77.9 3.9 %reshape.110 = bf16[128,3072]{0,1:T(8,128)(2,1)} reshape(bf16[2,64,64,48]{1,0,3,2:T(2,128)(2,1)} %copy.23) | data formatting | bytes 1572864 | tf_op jit(solution)/shard_map/reshape | solution.py:110
  81.8 2.0 collective-permute-start
  83.8 2.2 %constant_dynamic-update-slice_fusion.1 = bf16[256,3072]{0,1:T(8,128)(2,1)} fusion(bf16[128,3072]{0,1:T(8,128)(2,1)} %reshape.110), kind=kLoop, calls=%fused_computation.43 | loop fusion | bytes 1572864
  86.3 2.2 %reshape.113 = bf16[64,2,64,48]{3,2,1,0:T(8,128)(2,1)S(1)} reshape(bf16[64,6144]{1,0:T(8,128)(2,1)S(1)} %fusion.5) | data formatting | bytes 1572864 | tf_op jit(solution)/shard_map/reshape | solution.py:109
  88.5 4.2 %copy.24 = bf16[2,64,64,48]{1,0,3,2:T(2,128)(2,1)} copy(bf16[2,64,64,48]{3,1,0,2:T(8,128)(2,1)S(1)} %bitcast.117) | data formatting | bytes 1572864 | tf_op jit(solution)/shard_map/transpose | solution.py:110
  92.8 3.1 %reshape.114 = bf16[128,3072]{0,1:T(8,128)(2,1)S(1)} reshape(bf16[2,64,64,48]{1,0,3,2:T(2,128)(2,1)} %copy.24) | data formatting | bytes 1572864 | tf_op jit(solution)/shard_map/reshape | solution.py:110
  95.9 2.0 collective-permute-start.1
  98.0 1.0 constant_dynamic-update-slice_fusion
  99.1 2.5 %convolution_dynamic-update-slice_fusion = f32[2048,256]{1,0:T(8,128)S(1)} fusion(f32[2048,256]{1,0:T(8,128)S(1)} %broadcast_in_dim.45, s32[]{:T(128)S(6)} %select_n.132, bf16[256,3072]{0,1:T(8,128)(2,1)} %constant_dynamic-update-slice_fusion), kind=kOutput, calls=%fused_computation.25 | convolution fusion | flops 402653184 | bytes 3407876 | tf_op jit(solution)/shard_map/dot_general | solution.py:127
  101.6 1.0 collective-permute-done
  102.6 1.3 constant_dynamic-update-slice_fusion.3
  103.9 0.7 collective-permute-done.4
  104.6 1.3 constant_dynamic-update-slice_fusion.7
  105.9 11.7 %collective-permute-done.1 = bf16[128,3072]{0,1:T(8,128)(2,1)} collective-permute-done((bf16[128,3072]{0,1:T(8,128)(2,1)S(1)}, bf16[128,3072]{0,1:T(8,128)(2,1)}, u32[]{:S(2)}, u32[]{:S(2)}) %collective-permute-start.1) | collective-permute-done | bytes 786464 | tf_op jit(solution)/shard_map/ppermute | solution.py:115
  117.6 1.3 constant_dynamic-update-slice_fusion.2
  119.2 0.6 fusion.38
  119.9 2.0 constant_dynamic-update-slice_fusion.11
  121.9 1.8 collective-permute-start.2
  123.7 0.4 collective-permute-start.7
  124.1 1.7 collective-permute-start.3
  129.7 0.4 collective-permute-start.10
  130.0 1.7 collective-permute-start.9
  131.7 7.0 %collective-permute-done.7 = f32[2,256,256]{1,2,0:T(8,128)} collective-permute-done((f32[2,256,256]{1,2,0:T(8,128)S(1)}, f32[2,256,256]{1,2,0:T(8,128)}, u32[]{:S(2)}, u32[]{:S(2)}) %collective-permute-start.7) | collective-permute-done | bytes 524320 | tf_op jit(solution)/shard_map/ppermute | solution.py:145
  138.7 1.1 slice_bitcast_fusion.2
  140.1 2.7 %collective-permute-done.2 = bf16[128,3072]{0,1:T(8,128)(2,1)} collective-permute-done((bf16[128,3072]{0,1:T(8,128)(2,1)}, bf16[128,3072]{0,1:T(8,128)(2,1)}, u32[]{:S(2)}, u32[]{:S(2)}) %collective-permute-start.2) | collective-permute-done | bytes 786464 | tf_op jit(solution)/shard_map/ppermute | solution.py:115
  142.8 1.3 constant_dynamic-update-slice_fusion.5
  144.0 12.8 %collective-permute-done.3 = bf16[128,3072]{0,1:T(8,128)(2,1)} collective-permute-done((bf16[128,3072]{0,1:T(8,128)(2,1)}, bf16[128,3072]{0,1:T(8,128)(2,1)}, u32[]{:S(2)}, u32[]{:S(2)}) %collective-permute-start.3) | collective-permute-done | bytes 786464 | tf_op jit(solution)/shard_map/ppermute | solution.py:115
  156.8 1.3 constant_dynamic-update-slice_fusion.4
  158.2 0.6 fusion.37
  158.8 2.4 %collective-permute-start.6 = (f32[1,256,256]{1,2,0:T(8,128)S(1)}, f32[1,256,256]{1,2,0:T(8,128)S(1)}, u32[]{:S(2)}, u32[]{:S(2)}) collective-permute-start(f32[1,256,256]{1,2,0:T(8,128)S(1)} %bitcast.124), channel_id=1, source_target_pairs={{0,12},{8,4},{16,0},{24,8},{28,16},{20,24},{12,28},{4,20},{1,13},{... | collective-permute-start | bytes 786440 | tf_op jit(solution)/shard_map/ppermute | solution.py:145
  161.2 0.8 pad_maximum_fusion.1
  162.0 0.6 collective-permute-start.8
  162.6 11.7 %collective-permute-done.9 = bf16[128,3072]{0,1:T(8,128)(2,1)} collective-permute-done((bf16[128,3072]{0,1:T(8,128)(2,1)}, bf16[128,3072]{0,1:T(8,128)(2,1)}, u32[]{:S(2)}, u32[]{:S(2)}) %collective-permute-start.9) | collective-permute-done | bytes 786464 | tf_op jit(solution)/shard_map/ppermute | solution.py:117
  174.2 2.7 %fusion.23 = f32[1,256,256]{2,1,0:T(8,128)} fusion(bf16[256,3072]{0,1:T(8,128)(2,1)S(1)} %constant_dynamic-update-slice_fusion.4, bf16[128,3072]{0,1:T(8,128)(2,1)} %collective-permute-done.10, bf16[128,3072]{0,1:T(8,128)(2,1)} %collective-permute-done.9), kind=kOutput, calls=%fused_computation.26 | convolution fusion | flops 405798912 | bytes 3407872 | tf_op jit(solution)/shard_map/dot_general | solution.py:127
  176.9 2.4 %collective-permute-start.11 = (f32[1,256,256]{2,1,0:T(8,128)}, f32[1,256,256]{2,1,0:T(8,128)}, u32[]{:S(2)}, u32[]{:S(2)}) collective-permute-start(f32[1,256,256]{2,1,0:T(8,128)} %fusion.23), channel_id=1, source_target_pairs={{0,16},{8,24},{16,28},{24,20},{28,12},{20,4},{12,0},{4,8},{1,17},{... | collective-permute-start | bytes 786440 | tf_op jit(solution)/shard_map/ppermute | solution.py:145
  179.3 1.8 collective-permute-done.6
  181.2 0.7 copy-done.5
  181.9 1.1 copy.25
  183.2 2.8 %collective-permute-done.11 = f32[1,256,256]{2,1,0:T(8,128)} collective-permute-done((f32[1,256,256]{2,1,0:T(8,128)}, f32[1,256,256]{2,1,0:T(8,128)}, u32[]{:S(2)}, u32[]{:S(2)}) %collective-permute-start.11) | collective-permute-done | bytes 262176 | tf_op jit(solution)/shard_map/ppermute | solution.py:145
  186.0 1.0 bitcast_dynamic-update-slice_fusion
  187.1 2.7 %collective-permute-done.12 = f32[2,512,256]{2,1,0:T(8,128)} collective-permute-done((f32[2,512,256]{2,1,0:T(8,128)S(1)}, f32[2,512,256]{2,1,0:T(8,128)}, u32[]{:S(2)}, u32[]{:S(2)}) %collective-permute-start.12) | collective-permute-done | bytes 1048608 | tf_op jit(solution)/shard_map/ppermute | solution.py:59
  189.9 1.4 bitcast_add_fusion
  191.3 1.6 collective-permute-start.13
  192.9 12.4 %collective-permute-done.13 = f32[512,256]{1,0:T(8,128)S(1)} collective-permute-done((f32[512,256]{1,0:T(8,128)S(1)}, f32[512,256]{1,0:T(8,128)S(1)}, u32[]{:S(2)}, u32[]{:S(2)}) %collective-permute-start.13) | collective-permute-done | bytes 524320 | tf_op jit(solution)/shard_map/ppermute | solution.py:59
  205.3 0.9 bitcast_add_fusion.1
  (45 shorter events, 2.5 us)
Async XLA Ops:
  0.0 69.1 %copy-start = (bf16[1,64,64]{2,1,0:T(8,128)(2,1)S(1)}, bf16[1,64,64]{2,1,0:T(8,128)(2,1)}, u32[]{:S(2)}) copy-start(bf16[1,64,64]{2,1,0:T(8,128)(2,1)} %param.9) | copy-start | bytes 24580
  0.0 3.2 %copy-start.1 = (s32[32]{0:T(128)S(1)}, s32[32]{0:T(128)}, u32[]{:S(2)}) copy-start(s32[32]{0:T(128)} %param.13) | copy-start | bytes 388
  4.7 1.1 copy-start.7
  29.1 30.9 %copy-start.8 = (s32[8]{0:T(128)S(1)}, s32[8]{0:T(128)}, u32[]{:S(2)}) copy-start(s32[8]{0:T(128)} %constant.133.clone) | copy-start | bytes 100
  29.1 38.1 %copy-start.6 = (s32[8]{0:T(128)S(1)}, s32[8]{0:T(128)}, u32[]{:S(2)}) copy-start(s32[8]{0:T(128)} %constant.134.clone) | copy-start | bytes 100
  56.4 29.5 %all-to-all-start.1 = ((bf16[8,16,3072]{2,0,1:T(8,128)(2,1)}), bf16[8,16,3072]{2,0,1:T(8,128)(2,1)S(1)}, u32[]{:S(2)}, u32[]{:S(2)}) async-start(bf16[8,16,3072]{2,0,1:T(8,128)(2,1)} %bitcast.15), calls=%async_computation.1 | async-start | bytes 1572864 | tf_op jit(solution)/shard_map/all_to_all | solution.py:106
  81.8 20.8 %collective-permute-start = (bf16[128,3072]{0,1:T(8,128)(2,1)}, bf16[128,3072]{0,1:T(8,128)(2,1)}, u32[]{:S(2)}, u32[]{:S(2)}) collective-permute-start(bf16[128,3072]{0,1:T(8,128)(2,1)} %reshape.110), channel_id=1, source_target_pairs={{0,8},{8,16},{16,24},{24,28},{28,20},{20,12},{12,4},{4,0},{1,9},{9... | collective-permute-start | bytes 2359304 | tf_op jit(solution)/shard_map/ppermute | solution.py:115
  83.8 20.8 %collective-permute-start.4 = (bf16[128,3072]{0,1:T(8,128)(2,1)}, bf16[128,3072]{0,1:T(8,128)(2,1)}, u32[]{:S(2)}, u32[]{:S(2)}) collective-permute-start(bf16[128,3072]{0,1:T(8,128)(2,1)} %reshape.110), channel_id=1, source_target_pairs={{0,4},{8,0},{16,8},{24,16},{28,24},{20,28},{12,20},{4,12},{1,5},{9... | collective-permute-start | bytes 2359304 | tf_op jit(solution)/shard_map/ppermute | solution.py:117
  95.9 21.7 %collective-permute-start.1 = (bf16[128,3072]{0,1:T(8,128)(2,1)S(1)}, bf16[128,3072]{0,1:T(8,128)(2,1)}, u32[]{:S(2)}, u32[]{:S(2)}) collective-permute-start(bf16[128,3072]{0,1:T(8,128)(2,1)S(1)} %reshape.114), channel_id=1, source_target_pairs={{0,8},{8,16},{16,24},{24,28},{28,20},{20,12},{12,4},{4,0},{1,9},{9... | collective-permute-start | bytes 2359304 | tf_op jit(solution)/shard_map/ppermute | solution.py:115
  98.0 21.0 %collective-permute-start.5 = (bf16[128,3072]{0,1:T(8,128)(2,1)S(1)}, bf16[128,3072]{0,1:T(8,128)(2,1)S(1)}, u32[]{:S(2)}, u32[]{:S(2)}) collective-permute-start(bf16[128,3072]{0,1:T(8,128)(2,1)S(1)} %reshape.114), channel_id=1, source_target_pairs={{0,4},{8,0},{16,8},{24,16},{28,24},{20,28},{12,20},{4,12},{1,5},{9... | collective-permute-start | bytes 2359304 | tf_op jit(solution)/shard_map/ppermute | solution.py:117
  119.0 0.9 copy-start.2
  119.2 2.7 %copy-start.3 = (bf16[256,3072]{0,1:T(8,128)(2,1)}, bf16[256,3072]{0,1:T(8,128)(2,1)S(1)}, u32[]{:S(2)}) copy-start(bf16[256,3072]{0,1:T(8,128)(2,1)S(1)} %constant_dynamic-update-slice_fusion.6) | copy-start | bytes 4718596
  121.9 20.8 %collective-permute-start.2 = (bf16[128,3072]{0,1:T(8,128)(2,1)}, bf16[128,3072]{0,1:T(8,128)(2,1)}, u32[]{:S(2)}, u32[]{:S(2)}) collective-permute-start(bf16[128,3072]{0,1:T(8,128)(2,1)} %collective-permute-done), channel_id=1, source_target_pairs={{0,8},{8,16},{16,24},{24,28},{28,20},{20,12},{12,4},{4,0},{1,9},{9... | collective-permute-start | bytes 2359304 | tf_op jit(solution)/shard_map/ppermute | solution.py:115
  123.7 15.0 %collective-permute-start.7 = (f32[2,256,256]{1,2,0:T(8,128)S(1)}, f32[2,256,256]{1,2,0:T(8,128)}, u32[]{:S(2)}, u32[]{:S(2)}) collective-permute-start(f32[2,256,256]{1,2,0:T(8,128)S(1)} %pad_maximum_fusion), channel_id=1, source_target_pairs={{0,4},{8,0},{16,8},{24,16},{28,24},{20,28},{12,20},{4,12},{1,5},{9... | collective-permute-start | bytes 1572872 | tf_op jit(solution)/shard_map/ppermute | solution.py:145
  124.1 32.8 %collective-permute-start.3 = (bf16[128,3072]{0,1:T(8,128)(2,1)}, bf16[128,3072]{0,1:T(8,128)(2,1)}, u32[]{:S(2)}, u32[]{:S(2)}) collective-permute-start(bf16[128,3072]{0,1:T(8,128)(2,1)} %collective-permute-done.1), channel_id=1, source_target_pairs={{0,8},{8,16},{16,24},{24,28},{28,20},{20,12},{12,4},{4,0},{1,9},{9... | collective-permute-start | bytes 2359304 | tf_op jit(solution)/shard_map/ppermute | solution.py:115
  129.7 32.9 %collective-permute-start.10 = (bf16[128,3072]{0,1:T(8,128)(2,1)}, bf16[128,3072]{0,1:T(8,128)(2,1)}, u32[]{:S(2)}, u32[]{:S(2)}) collective-permute-start(bf16[128,3072]{0,1:T(8,128)(2,1)} %copy-done.2), channel_id=1, source_target_pairs={{0,4},{8,0},{16,8},{24,16},{28,24},{20,28},{12,20},{4,12},{1,5},{9... | collective-permute-start | bytes 2359304 | tf_op jit(solution)/shard_map/ppermute | solution.py:117
  130.0 44.2 %collective-permute-start.9 = (bf16[128,3072]{0,1:T(8,128)(2,1)}, bf16[128,3072]{0,1:T(8,128)(2,1)}, u32[]{:S(2)}, u32[]{:S(2)}) collective-permute-start(bf16[128,3072]{0,1:T(8,128)(2,1)} %collective-permute-done.4), channel_id=1, source_target_pairs={{0,4},{8,0},{16,8},{24,16},{28,24},{20,28},{12,20},{4,12},{1,5},{9... | collective-permute-start | bytes 2359304 | tf_op jit(solution)/shard_map/ppermute | solution.py:117
  140.1 18.1 %copy-start.4 = (bf16[256,3072]{0,1:T(8,128)(2,1)S(1)}, bf16[256,3072]{0,1:T(8,128)(2,1)}, u32[]{:S(2)}) copy-start(bf16[256,3072]{0,1:T(8,128)(2,1)} %copy-done.3) | copy-start | bytes 4718596
  158.8 22.4 %collective-permute-start.6 = (f32[1,256,256]{1,2,0:T(8,128)S(1)}, f32[1,256,256]{1,2,0:T(8,128)S(1)}, u32[]{:S(2)}, u32[]{:S(2)}) collective-permute-start(f32[1,256,256]{1,2,0:T(8,128)S(1)} %bitcast.124), channel_id=1, source_target_pairs={{0,12},{8,4},{16,0},{24,8},{28,16},{20,24},{12,28},{4,20},{1,13},{... | collective-permute-start | bytes 786440 | tf_op jit(solution)/shard_map/ppermute | solution.py:145
  162.0 21.1 %collective-permute-start.8 = (f32[2,256,256]{2,1,0:T(8,128)}, f32[2,256,256]{2,1,0:T(8,128)S(1)}, u32[]{:S(2)}, u32[]{:S(2)}) collective-permute-start(f32[2,256,256]{2,1,0:T(8,128)} %pad_maximum_fusion.1), channel_id=1, source_target_pairs={{0,8},{8,16},{16,24},{24,28},{28,20},{20,12},{12,4},{4,0},{1,9},{9... | collective-permute-start | bytes 1572872 | tf_op jit(solution)/shard_map/ppermute | solution.py:145
  176.9 9.0 %collective-permute-start.11 = (f32[1,256,256]{2,1,0:T(8,128)}, f32[1,256,256]{2,1,0:T(8,128)}, u32[]{:S(2)}, u32[]{:S(2)}) collective-permute-start(f32[1,256,256]{2,1,0:T(8,128)} %fusion.23), channel_id=1, source_target_pairs={{0,16},{8,24},{16,28},{24,20},{28,12},{20,4},{12,0},{4,8},{1,17},{... | collective-permute-start | bytes 786440 | tf_op jit(solution)/shard_map/ppermute | solution.py:145
  181.2 0.7 copy-start.5
  187.0 2.9 %collective-permute-start.12 = (f32[2,512,256]{2,1,0:T(8,128)S(1)}, f32[2,512,256]{2,1,0:T(8,128)}, u32[]{:S(2)}, u32[]{:S(2)}) collective-permute-start(f32[2,512,256]{2,1,0:T(8,128)S(1)} %dynamic-slice_bitcast_fusion), channel_id=1, source_target_pairs={{0,1},{1,0},{2,3},{3,2},{4,5},{5,4},{6,7},{7,6},{8,9},{9,8},{10,11... | collective-permute-start | bytes 3145736 | tf_op jit(solution)/shard_map/ppermute | solution.py:59
  191.3 14.0 %collective-permute-start.13 = (f32[512,256]{1,0:T(8,128)S(1)}, f32[512,256]{1,0:T(8,128)S(1)}, u32[]{:S(2)}, u32[]{:S(2)}) collective-permute-start(f32[512,256]{1,0:T(8,128)S(1)} %dynamic-slice_bitcast_fusion.1), channel_id=1, source_target_pairs={{0,2},{1,3},{2,0},{3,1},{4,6},{5,7},{6,4},{7,5},{8,10},{9,11},{10,... | collective-permute-start | bytes 1572872 | tf_op jit(solution)/shard_map/ppermute | solution.py:59

commit v17 on v16

--- a/solution.py
+++ b/solution.py
@@ -93,7 +93,7 @@
         half = half.reshape(aux_dev, n_mu, NB, n_occ)
         half = jnp.where(row_live[None, :, :, None], half, 0.0).astype(jnp.bfloat16)
         mu_dev = n_mu // n
-        n_split = 2 if mu_dev % 2 == 0 else 1
+        n_split = mu_dev
         mu_c = mu_dev // n_split
         half = half.reshape(aux_dev, n, mu_dev, NB * n_occ)
         me = lax.axis_index("grp")

time: 209 us -> 218 us (1.043)
  starting transfers between devices: 20.7 us -> 42.8 us
  blocking collectives: 27.3 us -> 19.3 us
  matrix products: 17.2 us -> 13.4 us
    ppermute x4 -> x8, waiting for transfers between devices: 12.4 us -> 34 us  [body(): bwd = lax.ppermute(bwd, 'grp', shifted(-1))]
    all_to_all x1 -> x3, starting transfers between devices: 3.59 us -> 15.4 us  [body(): lax.all_to_all(part, 'grp', split_axis=1, concat_axis=0, tiled=True)]
    ppermute x4 -> x8, waiting for transfers between devices: 28.2 us -> 16.6 us  [body(): fwd = lax.ppermute(fwd, 'grp', shifted(1))]
    all_to_all x1, blocking collectives: 27.3 us -> 19.3 us  [body(): lax.all_to_all(part, 'grp', split_axis=1, concat_axis=0, tiled=True)]
    ppermute x4, waiting for transfers between devices: 11.6 us -> 3.67 us  [body(): got = lax.ppermute(stack, 'grp', shifted(s))]
    ppermute x4 -> x8, starting transfers between devices: 2.16 us -> 8.72 us  [body(): bwd = lax.ppermute(bwd, 'grp', shifted(-1))]
    ppermute x4 -> x8, starting transfers between devices: 7.54 us -> 13 us  [body(): fwd = lax.ppermute(fwd, 'grp', shifted(1))]
    reshape x2 -> x4, local copies, waits for them, and re-layouts: 7.01 us -> 11.8 us  [body(): jnp.transpose(mixed, (1, 2, 0, 3)).reshape(mu_c * NB, n_aux * n_occ)]
  transfers between devices with their start and end apart: 15 -> 25, of which waited for: 11 -> 14; matrix products, arithmetic and copies ran while one was open for 21% -> 19% of each run, Pallas kernels for 0% -> 0%
where the time goes in v17:
time: 218 us; the launch traced here: 216 us
  waiting for transfers between devices  69.4 us (32%)
  local copies, waits for them, and re-layouts  52.6 us (24%)
  starting transfers between devices  42.8 us (20%)
  blocking collectives  19.3 us (9%)
  matrix products  13.4 us (6%)
  between operations  12 us (6%)
  other arithmetic  6.91 us (3%)
    ppermute x8, waiting for transfers between devices, body(): bwd = lax.ppermute(bwd, 'grp', shifted(-1))  34 us
    all_to_all x1, blocking collectives, body(): lax.all_to_all(part, 'grp', split_axis=1, concat_axis=0, tiled=True)  19.3 us
    ppermute x8, waiting for transfers between devices, body(): fwd = lax.ppermute(fwd, 'grp', shifted(1))  16.6 us
    all_to_all x3, starting transfers between devices, body(): lax.all_to_all(part, 'grp', split_axis=1, concat_axis=0, tiled=True)  15.4 us
    ppermute x2, waiting for transfers between devices, scatter_sum(): got = lax.ppermute(send, 'rep', [(i, i ^ d) for i in range(n_rep)])  15.2 us
    unnamed x31, local copies, waits for them, and re-layouts  14 us
    ppermute x8, starting transfers between devices, body(): fwd = lax.ppermute(fwd, 'grp', shifted(1))  13 us
    reshape x4, local copies, waits for them, and re-layouts, body(): jnp.transpose(mixed, (1, 2, 0, 3)).reshape(mu_c * NB, n_aux * n_occ)  11.8 us
  transfers between devices with their start and end apart: 25, of which 14 were waited for; matrix products, arithmetic and copies ran while one was open for 19% of the time, Pallas kernels for 0%

profile of v17, /device:TPU:0, one launch (start us, length us, event | category | flops | bytes accessed | tf_op | source)
XLA Modules:
  0.0 216.4 jit_solution(8209107721036517268)
XLA Ops:
  0.9 1.3 reshape.130
  3.2 1.6 gather_fusion
  4.7 1.0 gather_fusion.1
  5.9 7.4 %copy.34 = bf16[192,8,32,128]{3,2,1,0:T(8,128)(2,1)S(1)} copy(bf16[192,8,32,128]{3,1,2,0:T(8,128)(2,1)} %bitcast.148) | data formatting | bytes 25165824
  13.4 1.7 broadcast_select_fusion
  15.1 7.2 %fusion.16 = bf16[8,32,32,96]{3,2,0,1:T(8,128)(2,1)} fusion(bf16[8,6,32,32,128]{4,3,2,1,0:T(8,128)(2,1)S(1)} %bitcast.149, bf16[32,6,64,48]{2,3,1,0:T(8,128)(2,1)} %broadcast_select_fusion), kind=kOutput, calls=%fused_computation.24 | convolution fusion | flops 1226833920 | bytes 15335424 | tf_op jit(solution)/shard_map/qkmtl,mklc->qmtc/dot_general | solution.py:92
  22.3 4.2 %reshape.132 = bf16[8,8,4,3072]{3,0,2,1:T(8,128)(2,1)S(1)} reshape(bf16[8,32,32,96]{3,2,0,1:T(8,128)(2,1)} %fusion.16) | data formatting | bytes 3145728 | tf_op jit(solution)/shard_map/reshape | solution.py:93
  28.1 1.0 slice_bitcast_fusion
  29.2 19.3 %all_to_all.60 = bf16[8,8,3072]{2,0,1:T(8,128)(2,1)S(1)} all-to-all(bf16[8,8,3072]{2,0,1:T(8,128)(2,1)S(1)} %get-tuple-element.8), channel_id=1, replica_groups=mesh['grp'=8,'rep'=4] {'grp'}, dimensions={1} | all-to-all | bytes 786432 | tf_op jit(solution)/shard_map/all_to_all | solution.py:106
  48.4 3.5 %all-to-all-start.1 = ((bf16[8,8,3072]{2,0,1:T(8,128)(2,1)}), bf16[8,8,3072]{2,0,1:T(8,128)(2,1)S(1)}, u32[]{:S(2)}, u32[]{:S(2)}) async-start(bf16[8,8,3072]{2,0,1:T(8,128)(2,1)} %get-tuple-element.7), calls=%async_computation.1 | async-start | bytes 786432 | tf_op jit(solution)/shard_map/all_to_all | solution.py:106
  64.7 5.9 %all-to-all-start.2 = ((bf16[8,8,3072]{2,0,1:T(8,128)(2,1)}), bf16[8,8,3072]{2,0,1:T(8,128)(2,1)S(1)}, u32[]{:S(2)}, u32[]{:S(2)}) async-start(bf16[8,8,3072]{2,0,1:T(8,128)(2,1)} %get-tuple-element.6), calls=%async_computation.2 | async-start | bytes 786432 | tf_op jit(solution)/shard_map/all_to_all | solution.py:106
  70.9 1.1 reshape.135
  72.6 2.8 %reshape.136 = bf16[64,3072]{1,0:T(8,128)(2,1)} reshape(bf16[1,64,64,48]{3,2,1,0:T(8,128)(2,1)S(1)} %copy.25) | data formatting | bytes 786432 | tf_op jit(solution)/shard_map/reshape | solution.py:110
  75.4 2.0 collective-permute-start
  77.7 1.1 reshape.139
  79.5 2.8 %reshape.140 = bf16[64,3072]{1,0:T(8,128)(2,1)} reshape(bf16[1,64,64,48]{3,2,1,0:T(8,128)(2,1)S(1)} %copy.26) | data formatting | bytes 786432 | tf_op jit(solution)/shard_map/reshape | solution.py:110
  82.2 1.0 constant_dynamic-update-slice_fusion.3
  83.3 6.0 %all-to-all-start.3 = ((bf16[8,8,3072]{2,0,1:T(8,128)(2,1)}), bf16[8,8,3072]{2,0,1:T(8,128)(2,1)S(1)}, u32[]{:S(2)}, u32[]{:S(2)}) async-start(bf16[8,8,3072]{2,0,1:T(8,128)(2,1)} %get-tuple-element.5), calls=%async_computation.3 | async-start | bytes 786432 | tf_op jit(solution)/shard_map/all_to_all | solution.py:106
  89.3 1.0 fusion.13
  90.3 2.1 reshape.143
  92.4 1.7 copy.27
  94.0 3.4 %reshape.144 = bf16[64,3072]{1,0:T(8,128)(2,1)} reshape(bf16[1,64,64,48]{3,2,1,0:T(8,128)(2,1)} %copy.27) | data formatting | bytes 786432 | tf_op jit(solution)/shard_map/reshape | solution.py:110
  97.5 2.0 collective-permute-start.1
  99.5 1.5 collective-permute-start.2
  101.0 1.0 constant_dynamic-update-slice_fusion.1
  102.0 1.0 fusion.14
  103.0 2.1 reshape.147
  105.1 1.7 copy.28
  106.8 2.8 %reshape.148 = bf16[64,3072]{1,0:T(8,128)(2,1)S(1)} reshape(bf16[1,64,64,48]{3,2,1,0:T(8,128)(2,1)} %copy.28) | data formatting | bytes 786432 | tf_op jit(solution)/shard_map/reshape | solution.py:110
  109.6 1.7 collective-permute-start.3
  113.0 1.0 constant_dynamic-update-slice_fusion.7
  114.7 1.0 constant_dynamic-update-slice_fusion.6
  115.7 2.6 %collective-permute-done.2 = bf16[64,3072]{1,0:T(8,128)(2,1)} collective-permute-done((bf16[64,3072]{1,0:T(8,128)(2,1)}, bf16[64,3072]{1,0:T(8,128)(2,1)}, u32[]{:S(2)}, u32[]{:S(2)}) %collective-permute-start.2) | collective-permute-done | bytes 393248 | tf_op jit(solution)/shard_map/ppermute | solution.py:115
  118.3 2.0 collective-permute-start.11
  120.3 1.0 constant_dynamic-update-slice_fusion.5
  121.3 2.3 %collective-permute-done.3 = bf16[64,3072]{1,0:T(8,128)(2,1)S(1)} collective-permute-done((bf16[64,3072]{1,0:T(8,128)(2,1)S(1)}, bf16[64,3072]{1,0:T(8,128)(2,1)S(1)}, u32[]{:S(2)}, u32[]{:S(2)}) %collective-permute-start.3) | collective-permute-done | bytes 393248 | tf_op jit(solution)/shard_map/ppermute | solution.py:115
  124.3 1.4 collective-permute-start.4
  125.6 1.5 collective-permute-start.5
  127.1 1.0 constant_dynamic-update-slice_fusion.15
  128.2 4.3 %collective-permute-done.10 = bf16[64,3072]{1,0:T(8,128)(2,1)S(1)} collective-permute-done((bf16[64,3072]{1,0:T(8,128)(2,1)}, bf16[64,3072]{1,0:T(8,128)(2,1)S(1)}, u32[]{:S(2)}, u32[]{:S(2)}) %collective-permute-start.10) | collective-permute-done | bytes 393248 | tf_op jit(solution)/shard_map/ppermute | solution.py:117
  132.5 5.3 %collective-permute-done.11 = bf16[64,3072]{1,0:T(8,128)(2,1)S(1)} collective-permute-done((bf16[64,3072]{1,0:T(8,128)(2,1)S(1)}, bf16[64,3072]{1,0:T(8,128)(2,1)S(1)}, u32[]{:S(2)}, u32[]{:S(2)}) %collective-permute-start.11) | collective-permute-done | bytes 393248 | tf_op jit(solution)/shard_map/ppermute | solution.py:117
  139.2 1.4 collective-permute-start.6
  140.6 1.5 collective-permute-start.7
  142.7 2.3 %collective-permute-done.5 = bf16[64,3072]{1,0:T(8,128)(2,1)S(1)} collective-permute-done((bf16[64,3072]{1,0:T(8,128)(2,1)}, bf16[64,3072]{1,0:T(8,128)(2,1)S(1)}, u32[]{:S(2)}, u32[]{:S(2)}) %collective-permute-start.5) | collective-permute-done | bytes 393248 | tf_op jit(solution)/shard_map/ppermute | solution.py:115
  145.0 1.7 collective-permute-start.16
  146.8 6.7 %collective-permute-done.6 = bf16[64,3072]{1,0:T(8,128)(2,1)S(1)} collective-permute-done((bf16[64,3072]{1,0:T(8,128)(2,1)}, bf16[64,3072]{1,0:T(8,128)(2,1)S(1)}, u32[]{:S(2)}, u32[]{:S(2)}) %collective-permute-start.6) | collective-permute-done | bytes 393248 | tf_op jit(solution)/shard_map/ppermute | solution.py:115
  153.4 1.7 collective-permute-start.17
  155.2 2.7 %collective-permute-done.7 = bf16[64,3072]{1,0:T(8,128)(2,1)S(1)} collective-permute-done((bf16[64,3072]{1,0:T(8,128)(2,1)S(1)}, bf16[64,3072]{1,0:T(8,128)(2,1)S(1)}, u32[]{:S(2)}, u32[]{:S(2)}) %collective-permute-start.7) | collective-permute-done | bytes 393248 | tf_op jit(solution)/shard_map/ppermute | solution.py:115
  158.0 1.5 collective-permute-start.18
  160.9 1.0 collective-permute-done.15
  162.4 7.9 %collective-permute-done.16 = bf16[64,3072]{1,0:T(8,128)(2,1)S(1)} collective-permute-done((bf16[64,3072]{1,0:T(8,128)(2,1)S(1)}, bf16[64,3072]{1,0:T(8,128)(2,1)S(1)}, u32[]{:S(2)}, u32[]{:S(2)}) %collective-permute-start.16) | collective-permute-done | bytes 393248 | tf_op jit(solution)/shard_map/ppermute | solution.py:117
  170.3 1.5 collective-permute-start.14
  171.8 7.5 %collective-permute-done.17 = bf16[64,3072]{1,0:T(8,128)(2,1)S(1)} collective-permute-done((bf16[64,3072]{1,0:T(8,128)(2,1)S(1)}, bf16[64,3072]{1,0:T(8,128)(2,1)S(1)}, u32[]{:S(2)}, u32[]{:S(2)}) %collective-permute-start.17) | collective-permute-done | bytes 393248 | tf_op jit(solution)/shard_map/ppermute | solution.py:117
  179.3 8.0 %collective-permute-done.18 = bf16[64,3072]{1,0:T(8,128)(2,1)S(1)} collective-permute-done((bf16[64,3072]{1,0:T(8,128)(2,1)S(1)}, bf16[64,3072]{1,0:T(8,128)(2,1)S(1)}, u32[]{:S(2)}, u32[]{:S(2)}) %collective-permute-start.18) | collective-permute-done | bytes 393248 | tf_op jit(solution)/shard_map/ppermute | solution.py:117
  187.3 1.3 fusion.29
  188.6 1.3 collective-permute-start.19
  190.2 3.7 %collective-permute-done.12 = f32[1,256,256]{1,2,0:T(8,128)} collective-permute-done((f32[1,256,256]{1,2,0:T(8,128)S(1)}, f32[1,256,256]{1,2,0:T(8,128)}, u32[]{:S(2)}, u32[]{:S(2)}) %collective-permute-start.12) | collective-permute-done | bytes 262176 | tf_op jit(solution)/shard_map/ppermute | solution.py:145
  193.9 1.1 copy.29
  195.1 1.0 fusion.37
  196.1 1.0 fusion.36
  197.3 2.7 %collective-permute-done.20 = f32[2,512,256]{2,1,0:T(8,128)} collective-permute-done((f32[2,512,256]{2,1,0:T(8,128)S(1)}, f32[2,512,256]{2,1,0:T(8,128)}, u32[]{:S(2)}, u32[]{:S(2)}) %collective-permute-start.20) | collective-permute-done | bytes 1048608 | tf_op jit(solution)/shard_map/ppermute | solution.py:59
  200.1 1.4 bitcast_add_fusion
  201.5 1.6 collective-permute-start.21
  203.1 12.4 %collective-permute-done.21 = f32[512,256]{1,0:T(8,128)S(1)} collective-permute-done((f32[512,256]{1,0:T(8,128)S(1)}, f32[512,256]{1,0:T(8,128)S(1)}, u32[]{:S(2)}, u32[]{:S(2)}) %collective-permute-start.21) | collective-permute-done | bytes 524320 | tf_op jit(solution)/shard_map/ppermute | solution.py:59
  (81 shorter events, 15.4 us)
Async XLA Ops:
  0.0 70.6 %copy-start = (bf16[1,64,64]{2,1,0:T(8,128)(2,1)S(1)}, bf16[1,64,64]{2,1,0:T(8,128)(2,1)}, u32[]{:S(2)}) copy-start(bf16[1,64,64]{2,1,0:T(8,128)(2,1)} %param.9) | copy-start | bytes 24580
  0.0 3.2 %copy-start.1 = (s32[32]{0:T(128)S(1)}, s32[32]{0:T(128)}, u32[]{:S(2)}) copy-start(s32[32]{0:T(128)} %param.13) | copy-start | bytes 388
  4.7 1.1 copy-start.7
  29.2 22.7 %copy-start.8 = (s32[8]{0:T(128)S(1)}, s32[8]{0:T(128)}, u32[]{:S(2)}) copy-start(s32[8]{0:T(128)} %constant.133.clone) | copy-start | bytes 100
  29.2 29.9 %copy-start.6 = (s32[8]{0:T(128)S(1)}, s32[8]{0:T(128)}, u32[]{:S(2)}) copy-start(s32[8]{0:T(128)} %constant.134.clone) | copy-start | bytes 100
  48.4 16.3 %all-to-all-start.1 = ((bf16[8,8,3072]{2,0,1:T(8,128)(2,1)}), bf16[8,8,3072]{2,0,1:T(8,128)(2,1)S(1)}, u32[]{:S(2)}, u32[]{:S(2)}) async-start(bf16[8,8,3072]{2,0,1:T(8,128)(2,1)} %get-tuple-element.7), calls=%async_computation.1 | async-start | bytes 786432 | tf_op jit(solution)/shard_map/all_to_all | solution.py:106
  64.7 18.6 %all-to-all-start.2 = ((bf16[8,8,3072]{2,0,1:T(8,128)(2,1)}), bf16[8,8,3072]{2,0,1:T(8,128)(2,1)S(1)}, u32[]{:S(2)}, u32[]{:S(2)}) async-start(bf16[8,8,3072]{2,0,1:T(8,128)(2,1)} %get-tuple-element.6), calls=%async_computation.2 | async-start | bytes 786432 | tf_op jit(solution)/shard_map/all_to_all | solution.py:106
  75.4 36.7 %collective-permute-start = (bf16[64,3072]{1,0:T(8,128)(2,1)}, bf16[64,3072]{1,0:T(8,128)(2,1)}, u32[]{:S(2)}, u32[]{:S(2)}) collective-permute-start(bf16[64,3072]{1,0:T(8,128)(2,1)} %reshape.136), channel_id=1, source_target_pairs={{0,8},{8,16},{16,24},{24,28},{28,20},{20,12},{12,4},{4,0},{1,9},{9... | collective-permute-start | bytes 1179656 | tf_op jit(solution)/shard_map/ppermute | solution.py:115
  77.4 48.2 %collective-permute-start.8 = (bf16[64,3072]{1,0:T(8,128)(2,1)}, bf16[64,3072]{1,0:T(8,128)(2,1)}, u32[]{:S(2)}, u32[]{:S(2)}) collective-permute-start(bf16[64,3072]{1,0:T(8,128)(2,1)} %reshape.136), channel_id=1, source_target_pairs={{0,4},{8,0},{16,8},{24,16},{28,24},{20,28},{12,20},{4,12},{1,5},{9... | collective-permute-start | bytes 1179656 | tf_op jit(solution)/shard_map/ppermute | solution.py:117
  83.3 18.8 %all-to-all-start.3 = ((bf16[8,8,3072]{2,0,1:T(8,128)(2,1)}), bf16[8,8,3072]{2,0,1:T(8,128)(2,1)S(1)}, u32[]{:S(2)}, u32[]{:S(2)}) async-start(bf16[8,8,3072]{2,0,1:T(8,128)(2,1)} %get-tuple-element.5), calls=%async_computation.3 | async-start | bytes 786432 | tf_op jit(solution)/shard_map/all_to_all | solution.py:106
  94.0 6.9 %copy-start.4 = (bf16[64,3072]{1,0:T(8,128)(2,1)S(1)}, bf16[64,3072]{1,0:T(8,128)(2,1)}, u32[]{:S(2)}) copy-start(bf16[64,3072]{1,0:T(8,128)(2,1)} %reshape.140) | copy-start | bytes 1179652
  97.5 16.6 %collective-permute-start.1 = (bf16[64,3072]{1,0:T(8,128)(2,1)}, bf16[64,3072]{1,0:T(8,128)(2,1)}, u32[]{:S(2)}, u32[]{:S(2)}) collective-permute-start(bf16[64,3072]{1,0:T(8,128)(2,1)} %reshape.140), channel_id=1, source_target_pairs={{0,8},{8,16},{16,24},{24,28},{28,20},{20,12},{12,4},{4,0},{1,9},{9... | collective-permute-start | bytes 1179656 | tf_op jit(solution)/shard_map/ppermute | solution.py:115
  99.5 18.8 %collective-permute-start.2 = (bf16[64,3072]{1,0:T(8,128)(2,1)}, bf16[64,3072]{1,0:T(8,128)(2,1)}, u32[]{:S(2)}, u32[]{:S(2)}) collective-permute-start(bf16[64,3072]{1,0:T(8,128)(2,1)} %reshape.144), channel_id=1, source_target_pairs={{0,8},{8,16},{16,24},{24,28},{28,20},{20,12},{12,4},{4,0},{1,9},{9... | collective-permute-start | bytes 1179656 | tf_op jit(solution)/shard_map/ppermute | solution.py:115
  109.6 14.0 %collective-permute-start.3 = (bf16[64,3072]{1,0:T(8,128)(2,1)S(1)}, bf16[64,3072]{1,0:T(8,128)(2,1)S(1)}, u32[]{:S(2)}, u32[]{:S(2)}) collective-permute-start(bf16[64,3072]{1,0:T(8,128)(2,1)S(1)} %reshape.148), channel_id=1, source_target_pairs={{0,8},{8,16},{16,24},{24,28},{28,20},{20,12},{12,4},{4,0},{1,9},{9... | collective-permute-start | bytes 1179656 | tf_op jit(solution)/shard_map/ppermute | solution.py:115
  111.5 1.0 copy-start.5
  112.5 15.7 %collective-permute-start.9 = (bf16[64,3072]{1,0:T(8,128)(2,1)S(1)}, bf16[64,3072]{1,0:T(8,128)(2,1)S(1)}, u32[]{:S(2)}, u32[]{:S(2)}) collective-permute-start(bf16[64,3072]{1,0:T(8,128)(2,1)S(1)} %copy-done.5), channel_id=1, source_target_pairs={{0,4},{8,0},{16,8},{24,16},{28,24},{20,28},{12,20},{4,12},{1,5},{9... | collective-permute-start | bytes 1179656 | tf_op jit(solution)/shard_map/ppermute | solution.py:117
  114.1 18.4 %collective-permute-start.10 = (bf16[64,3072]{1,0:T(8,128)(2,1)}, bf16[64,3072]{1,0:T(8,128)(2,1)S(1)}, u32[]{:S(2)}, u32[]{:S(2)}) collective-permute-start(bf16[64,3072]{1,0:T(8,128)(2,1)} %reshape.144), channel_id=1, source_target_pairs={{0,4},{8,0},{16,8},{24,16},{28,24},{20,28},{12,20},{4,12},{1,5},{9... | collective-permute-start | bytes 1179656 | tf_op jit(solution)/shard_map/ppermute | solution.py:117
  118.3 19.6 %collective-permute-start.11 = (bf16[64,3072]{1,0:T(8,128)(2,1)S(1)}, bf16[64,3072]{1,0:T(8,128)(2,1)S(1)}, u32[]{:S(2)}, u32[]{:S(2)}) collective-permute-start(bf16[64,3072]{1,0:T(8,128)(2,1)S(1)} %reshape.148), channel_id=1, source_target_pairs={{0,4},{8,0},{16,8},{24,16},{28,24},{20,28},{12,20},{4,12},{1,5},{9... | collective-permute-start | bytes 1179656 | tf_op jit(solution)/shard_map/ppermute | solution.py:117
  124.3 13.6 %copy-start.2 = (f32[2048,256]{1,0:T(8,128)}, f32[2048,256]{1,0:T(8,128)S(1)}, u32[]{:S(2)}) copy-start(f32[2048,256]{1,0:T(8,128)S(1)} %get-tuple-element.19) | copy-start | bytes 6291460
  124.3 17.8 %collective-permute-start.4 = (bf16[64,3072]{1,0:T(8,128)(2,1)}, bf16[64,3072]{1,0:T(8,128)(2,1)S(1)}, u32[]{:S(2)}, u32[]{:S(2)}) collective-permute-start(bf16[64,3072]{1,0:T(8,128)(2,1)} %collective-permute-done), channel_id=1, source_target_pairs={{0,8},{8,16},{16,24},{24,28},{28,20},{20,12},{12,4},{4,0},{1,9},{9... | collective-permute-start | bytes 1179656 | tf_op jit(solution)/shard_map/ppermute | solution.py:115
  125.6 19.4 %collective-permute-start.5 = (bf16[64,3072]{1,0:T(8,128)(2,1)}, bf16[64,3072]{1,0:T(8,128)(2,1)S(1)}, u32[]{:S(2)}, u32[]{:S(2)}) collective-permute-start(bf16[64,3072]{1,0:T(8,128)(2,1)} %collective-permute-done.1), channel_id=1, source_target_pairs={{0,8},{8,16},{16,24},{24,28},{28,20},{20,12},{12,4},{4,0},{1,9},{9... | collective-permute-start | bytes 1179656 | tf_op jit(solution)/shard_map/ppermute | solution.py:115
  138.5 51.4 %collective-permute-start.13 = (f32[2,256,256]{1,2,0:T(8,128)S(1)}, f32[2,256,256]{1,2,0:T(8,128)S(1)}, u32[]{:S(2)}, u32[]{:S(2)}) collective-permute-start(f32[2,256,256]{1,2,0:T(8,128)S(1)} %pad_maximum_fusion), channel_id=1, source_target_pairs={{0,4},{8,0},{16,8},{24,16},{28,24},{20,28},{12,20},{4,12},{1,5},{9... | collective-permute-start | bytes 1572872 | tf_op jit(solution)/shard_map/ppermute | solution.py:145
  139.2 14.3 %collective-permute-start.6 = (bf16[64,3072]{1,0:T(8,128)(2,1)}, bf16[64,3072]{1,0:T(8,128)(2,1)S(1)}, u32[]{:S(2)}, u32[]{:S(2)}) collective-permute-start(bf16[64,3072]{1,0:T(8,128)(2,1)} %collective-permute-done.2), channel_id=1, source_target_pairs={{0,8},{8,16},{16,24},{24,28},{28,20},{20,12},{12,4},{4,0},{1,9},{9... | collective-permute-start | bytes 1179656 | tf_op jit(solution)/shard_map/ppermute | solution.py:115
  140.6 17.3 %collective-permute-start.7 = (bf16[64,3072]{1,0:T(8,128)(2,1)S(1)}, bf16[64,3072]{1,0:T(8,128)(2,1)S(1)}, u32[]{:S(2)}, u32[]{:S(2)}) collective-permute-start(bf16[64,3072]{1,0:T(8,128)(2,1)S(1)} %collective-permute-done.3), channel_id=1, source_target_pairs={{0,8},{8,16},{16,24},{24,28},{28,20},{20,12},{12,4},{4,0},{1,9},{9... | collective-permute-start | bytes 1179656 | tf_op jit(solution)/shard_map/ppermute | solution.py:115
  142.1 19.8 %collective-permute-start.15 = (bf16[64,3072]{1,0:T(8,128)(2,1)}, bf16[64,3072]{1,0:T(8,128)(2,1)S(1)}, u32[]{:S(2)}, u32[]{:S(2)}) collective-permute-start(bf16[64,3072]{1,0:T(8,128)(2,1)} %collective-permute-done.8), channel_id=1, source_target_pairs={{0,4},{8,0},{16,8},{24,16},{28,24},{20,28},{12,20},{4,12},{1,5},{9... | collective-permute-start | bytes 1179656 | tf_op jit(solution)/shard_map/ppermute | solution.py:117
  145.0 25.3 %collective-permute-start.16 = (bf16[64,3072]{1,0:T(8,128)(2,1)S(1)}, bf16[64,3072]{1,0:T(8,128)(2,1)S(1)}, u32[]{:S(2)}, u32[]{:S(2)}) collective-permute-start(bf16[64,3072]{1,0:T(8,128)(2,1)S(1)} %collective-permute-done.9), channel_id=1, source_target_pairs={{0,4},{8,0},{16,8},{24,16},{28,24},{20,28},{12,20},{4,12},{1,5},{9... | collective-permute-start | bytes 1179656 | tf_op jit(solution)/shard_map/ppermute | solution.py:117
  153.4 25.8 %collective-permute-start.17 = (bf16[64,3072]{1,0:T(8,128)(2,1)S(1)}, bf16[64,3072]{1,0:T(8,128)(2,1)S(1)}, u32[]{:S(2)}, u32[]{:S(2)}) collective-permute-start(bf16[64,3072]{1,0:T(8,128)(2,1)S(1)} %collective-permute-done.10), channel_id=1, source_target_pairs={{0,4},{8,0},{16,8},{24,16},{28,24},{20,28},{12,20},{4,12},{1,5},{9... | collective-permute-start | bytes 1179656 | tf_op jit(solution)/shard_map/ppermute | solution.py:117
  158.0 29.3 %collective-permute-start.18 = (bf16[64,3072]{1,0:T(8,128)(2,1)S(1)}, bf16[64,3072]{1,0:T(8,128)(2,1)S(1)}, u32[]{:S(2)}, u32[]{:S(2)}) collective-permute-start(bf16[64,3072]{1,0:T(8,128)(2,1)S(1)} %collective-permute-done.11), channel_id=1, source_target_pairs={{0,4},{8,0},{16,8},{24,16},{28,24},{20,28},{12,20},{4,12},{1,5},{9... | collective-permute-start | bytes 1179656 | tf_op jit(solution)/shard_map/ppermute | solution.py:117
  161.9 32.0 %collective-permute-start.12 = (f32[1,256,256]{1,2,0:T(8,128)S(1)}, f32[1,256,256]{1,2,0:T(8,128)}, u32[]{:S(2)}, u32[]{:S(2)}) collective-permute-start(f32[1,256,256]{1,2,0:T(8,128)S(1)} %bitcast.159), channel_id=1, source_target_pairs={{0,12},{8,4},{16,0},{24,8},{28,16},{20,24},{12,28},{4,20},{1,13},{... | collective-permute-start | bytes 786440 | tf_op jit(solution)/shard_map/ppermute | solution.py:145
  170.3 24.8 %collective-permute-start.14 = (f32[2,256,256]{2,1,0:T(8,128)}, f32[2,256,256]{2,1,0:T(8,128)}, u32[]{:S(2)}, u32[]{:S(2)}) collective-permute-start(f32[2,256,256]{2,1,0:T(8,128)} %pad_maximum_fusion.1), channel_id=1, source_target_pairs={{0,8},{8,16},{16,24},{24,28},{28,20},{20,12},{12,4},{4,0},{1,9},{9... | collective-permute-start | bytes 1572872 | tf_op jit(solution)/shard_map/ppermute | solution.py:145
  188.6 6.4 %copy-start.3 = (f32[2048,256]{1,0:T(8,128)S(1)}, f32[2048,256]{1,0:T(8,128)}, u32[]{:S(2)}) copy-start(f32[2048,256]{1,0:T(8,128)} %copy-done.2) | copy-start | bytes 6291460
  188.6 8.5 %collective-permute-start.19 = (f32[1,256,256]{2,1,0:T(8,128)}, f32[1,256,256]{2,1,0:T(8,128)S(1)}, u32[]{:S(2)}, u32[]{:S(2)}) collective-permute-start(f32[1,256,256]{2,1,0:T(8,128)} %fusion.29), channel_id=1, source_target_pairs={{0,16},{8,24},{16,28},{24,20},{28,12},{20,4},{12,0},{4,8},{1,17},{... | collective-permute-start | bytes 786440 | tf_op jit(solution)/shard_map/ppermute | solution.py:145
  197.2 2.9 %collective-permute-start.20 = (f32[2,512,256]{2,1,0:T(8,128)S(1)}, f32[2,512,256]{2,1,0:T(8,128)}, u32[]{:S(2)}, u32[]{:S(2)}) collective-permute-start(f32[2,512,256]{2,1,0:T(8,128)S(1)} %dynamic-slice_bitcast_fusion), channel_id=1, source_target_pairs={{0,1},{1,0},{2,3},{3,2},{4,5},{5,4},{6,7},{7,6},{8,9},{9,8},{10,11... | collective-permute-start | bytes 3145736 | tf_op jit(solution)/shard_map/ppermute | solution.py:59
  201.5 14.0 %collective-permute-start.21 = (f32[512,256]{1,0:T(8,128)S(1)}, f32[512,256]{1,0:T(8,128)S(1)}, u32[]{:S(2)}, u32[]{:S(2)}) collective-permute-start(f32[512,256]{1,0:T(8,128)S(1)} %dynamic-slice_bitcast_fusion.1), channel_id=1, source_target_pairs={{0,2},{1,3},{2,0},{3,1},{4,6},{5,7},{6,4},{7,5},{8,10},{9,11},{10,... | collective-permute-start | bytes 1572872 | tf_op jit(solution)/shard_map/ppermute | solution.py:59

commit v18 on v16

--- a/solution.py
+++ b/solution.py
@@ -89,20 +89,26 @@
         )
         tiles = NB // pair
         tc = jnp.swapaxes(three_center[0], 1, 2).reshape(aux_dev, knu, n_mu, tiles, pair * NB)
-        half = jnp.einsum("qkmtl,mklc->qmtc", tc, weight, preferred_element_type=jnp.float32)
-        half = half.reshape(aux_dev, n_mu, NB, n_occ)
-        half = jnp.where(row_live[None, :, :, None], half, 0.0).astype(jnp.bfloat16)
         mu_dev = n_mu // n
         n_split = 2 if mu_dev % 2 == 0 else 1
         mu_c = mu_dev // n_split
-        half = half.reshape(aux_dev, n, mu_dev, NB * n_occ)
         me = lax.axis_index("grp")
         pos = jnp.asarray(pos_of)[me]
         ring_c = jnp.asarray(ring_arr)
         radius = n // 4
+        tc6 = tc.reshape(aux_dev, knu, n, mu_dev, tiles, pair * NB)
+        w5 = weight.reshape((n, mu_dev) + weight.shape[1:])
+        live3 = row_live.reshape(n, mu_dev, NB)
         helds = []
         for h in range(n_split):
-            part = half[:, :, h * mu_c:(h + 1) * mu_c].reshape(aux_dev, n * mu_c, NB * n_occ)
+            sl = slice(h * mu_c, (h + 1) * mu_c)
+            tc_h = tc6[:, :, :, sl].reshape(aux_dev, knu, n * mu_c, tiles, pair * NB)
+            w_h = w5[:, sl].reshape((n * mu_c,) + weight.shape[1:])
+            live_h = live3[:, sl].reshape(n * mu_c, NB)
+            part = jnp.einsum("qkmtl,mklc->qmtc", tc_h, w_h, preferred_element_type=jnp.float32)
+            part = part.reshape(aux_dev, n * mu_c, NB, n_occ)
+            part = jnp.where(live_h[None, :, :, None], part, 0.0).astype(jnp.bfloat16)
+            part = part.reshape(aux_dev, n * mu_c, NB * n_occ)
             regrouped = lax.all_to_all(part, "grp", split_axis=1, concat_axis=0, tiled=True)
             n_aux = regrouped.shape[0]
             mixed = jnp.dot(metric[0], regrouped.reshape(n_aux, -1), preferred_element_type=jnp.float32)

time: 209 us -> 213 us (1.019)
  blocking collectives: 27.3 us -> 0 us
  local copies, waits for them, and re-layouts: 54.6 us -> 67.1 us
  waiting for transfers between devices: 67.4 us -> 76.1 us
  starting transfers between devices: 20.7 us -> 28.9 us
  other arithmetic: 6.92 us -> 10.1 us
    all_to_all x1 -> x0, blocking collectives: 27.3 us -> none  [body(): lax.all_to_all(part, 'grp', split_axis=1, concat_axis=0, tiled=True)]
    all_to_all x1 -> x2, waiting for transfers between devices: 0.01 us -> 10.6 us  [body(): lax.all_to_all(part, 'grp', split_axis=1, concat_axis=0, tiled=True)]
    all_to_all x1 -> x2, starting transfers between devices: 3.59 us -> 10.8 us  [body(): lax.all_to_all(part, 'grp', split_axis=1, concat_axis=0, tiled=True)]
    unnamed x23 -> x25, local copies, waits for them, and re-layouts: 14.1 us -> 20.7 us
    slice x1 -> x3, local copies, waits for them, and re-layouts: 1.03 us -> 5.65 us  [the longest x1 4.72 us: body(): tc_h = tc6[:, :, :, sl].reshape(aux_dev, knu, n * mu_c, tiles, pair * NB)]
    dot_general x1 -> x2, matrix products: 7.15 us -> 3.59 us  [body(): jnp.einsum('qkmtl,mklc->qmtc', tc_h, w_h, preferred_element_type=jnp.floa...]
    convert_element_type x1 -> x2, other arithmetic: 0.51 us -> 3.45 us  [body(): part = jnp.where(live_h[None, :, :, None], part, 0.0).astype(jnp.bfloat16)]
    concatenate x0 -> x1, other arithmetic: none -> 2.31 us  [body(): jnp.concatenate([jnp.concatenate([picked, blank], axis=-1), jnp.concatena...]
  transfers between devices with their start and end apart: 15 -> 16, of which waited for: 11 -> 10; matrix products, arithmetic and copies ran while one was open for 21% -> 26% of each run, Pallas kernels for 0% -> 0%
where the time goes in v18:
time: 213 us; the launch traced here: 210 us
  waiting for transfers between devices  76.1 us (36%)
  local copies, waits for them, and re-layouts  67.1 us (32%)
  starting transfers between devices  28.9 us (14%)
  matrix products  15.6 us (7%)
  between operations  12.1 us (6%)
  other arithmetic  10.1 us (5%)
    ppermute x4, waiting for transfers between devices, body(): fwd = lax.ppermute(fwd, 'grp', shifted(1))  27.8 us
    unnamed x25, local copies, waits for them, and re-layouts  20.7 us
    ppermute x2, waiting for transfers between devices, scatter_sum(): got = lax.ppermute(send, 'rep', [(i, i ^ d) for i in range(n_rep)])  15.2 us
    ppermute x4, waiting for transfers between devices, body(): got = lax.ppermute(stack, 'grp', shifted(s))  11.5 us
    ppermute x4, waiting for transfers between devices, body(): bwd = lax.ppermute(bwd, 'grp', shifted(-1))  11 us
    all_to_all x2, starting transfers between devices, body(): lax.all_to_all(part, 'grp', split_axis=1, concat_axis=0, tiled=True)  10.8 us
    all_to_all x2, waiting for transfers between devices, body(): lax.all_to_all(part, 'grp', split_axis=1, concat_axis=0, tiled=True)  10.6 us
    transpose x2, local copies, waits for them, and re-layouts, body(): jnp.transpose(mixed, (1, 2, 0, 3)).reshape(mu_c * NB, n_aux * n_occ)  8.47 us
  transfers between devices with their start and end apart: 16, of which 10 were waited for; matrix products, arithmetic and copies ran while one was open for 26% of the time, Pallas kernels for 0%

profile of v18, /device:TPU:0, one launch (start us, length us, event | category | flops | bytes accessed | tf_op | source)
XLA Modules:
  0.0 210.0 jit_solution(7565180972881715391)
XLA Ops:
  0.0 0.7 compare_select_fusion
  0.9 1.3 reshape.107
  2.4 0.7 lt.162
  3.2 1.6 gather_fusion
  4.7 1.0 gather_fusion.1
  6.3 2.3 %fusion.4 = bf16[32,6,128,96]{2,3,1,0:T(8,128)(2,1)S(1)} fusion(bf16[32,6,64,48]{2,3,1,0:T(8,128)(2,1)S(1)} %broadcast_select_fusion), kind=kLoop, calls=%fused_computation.10 | loop fusion | flops 18874368 | bytes 5898240 | tf_op jit(solution)/shard_map/concatenate | solution.py:87
  8.6 0.9 fusion.19
  9.6 7.4 %copy.38 = bf16[192,8,32,128]{3,2,1,0:T(8,128)(2,1)S(1)} copy(bf16[192,8,32,128]{3,1,2,0:T(8,128)(2,1)} %bitcast.133) | data formatting | bytes 25165824
  16.9 4.7 %fusion.18 = (bf16[8,6,8,2,32,128]{5,4,3,2,1,0:T(8,128)(2,1)}, bf16[8,6,8,2,32,128]{5,4,3,2,1,0:T(8,128)(2,1)S(1)}) fusion(bf16[8,6,8,4,32,128]{5,4,3,2,1,0:T(8,128)(2,1)S(1)} %bitcast.128), kind=kLoop, calls=%fused_computation.56 | loop fusion | bytes 25165824 | tf_op jit(solution)/shard_map/slice | solution.py:105
  21.7 1.9 copy.36
  23.6 1.8 convolution_bitcast_fusion.1
  25.4 2.3 %reshape.111 = bf16[8,16,3072]{2,0,1:T(8,128)(2,1)} reshape(bf16[8,16,32,96]{3,2,0,1:T(8,128)(2,1)S(1)} %convolution_bitcast_fusion.1) | data formatting | bytes 1572864 | tf_op jit(solution)/shard_map/reshape | solution.py:109
  28.3 2.3 %select_convert_fusion.1 = bf16[8,16,3072]{2,0,1:T(8,128)(2,1)} fusion(bf16[8,16,3072]{2,0,1:T(8,128)(2,1)} %reshape.111, pred[16,3072]{1,0:T(8,128)(4,1)S(1)} %broadcast_in_dim.61), kind=kLoop, calls=%fused_computation.19 | loop fusion | flops 393216 | bytes 1622016 | tf_op jit(solution)/shard_map/convert_element_type | solution.py:110
  30.6 7.3 %all-to-all-start = ((bf16[8,16,3072]{2,0,1:T(8,128)(2,1)}), bf16[8,16,3072]{2,0,1:T(8,128)(2,1)}, u32[]{:S(2)}, u32[]{:S(2)}) async-start(bf16[8,16,3072]{2,0,1:T(8,128)(2,1)} %select_convert_fusion.1), calls=%async_computation | async-start | bytes 1572864 | tf_op jit(solution)/shard_map/all_to_all | solution.py:112
  37.9 4.7 %copy.37 = bf16[8,6,8,2,32,128]{5,4,1,0,3,2:T(8,128)(2,1)S(1)} copy(bf16[8,6,8,2,32,128]{5,4,3,2,1,0:T(8,128)(2,1)} %get-tuple-element.5) | data formatting | bytes 12582912
  42.6 1.8 convolution_bitcast_fusion
  44.4 1.4 reshape.117
  46.4 1.2 select_convert_fusion
  47.6 10.6 %all-to-all-done = bf16[8,16,3072]{2,0,1:T(8,128)(2,1)} async-done(((bf16[8,16,3072]{2,0,1:T(8,128)(2,1)}), bf16[8,16,3072]{2,0,1:T(8,128)(2,1)}, u32[]{:S(2)}, u32[]{:S(2)}) %all-to-all-start) | async-done | bytes 786464 | tf_op jit(solution)/shard_map/all_to_all | solution.py:112
  58.2 3.6 %all-to-all-start.1 = ((bf16[8,16,3072]{2,0,1:T(8,128)(2,1)}), bf16[8,16,3072]{2,0,1:T(8,128)(2,1)S(1)}, u32[]{:S(2)}, u32[]{:S(2)}) async-start(bf16[8,16,3072]{2,0,1:T(8,128)(2,1)} %select_convert_fusion), calls=%async_computation.1 | async-start | bytes 1572864 | tf_op jit(solution)/shard_map/all_to_all | solution.py:112
  68.9 0.7 fusion.21
  70.9 2.4 %fusion.2 = bf16[64,6144]{1,0:T(8,128)(2,1)} fusion(bf16[64,6144]{1,0:T(8,128)(2,1)} %bitcast.13, bf16[1,64,64]{2,1,0:T(8,128)(2,1)S(1)} %copy-done), kind=kOutput, calls=%fused_computation.8 | convolution fusion | flops 50724864 | bytes 1581056 | tf_op jit(solution)/shard_map/dot_general | solution.py:114
  73.2 3.3 %reshape.113 = bf16[64,2,64,48]{3,2,1,0:T(8,128)(2,1)S(1)} reshape(bf16[64,6144]{1,0:T(8,128)(2,1)} %fusion.2) | data formatting | bytes 1572864 | tf_op jit(solution)/shard_map/reshape | solution.py:115
  76.5 4.2 %copy.26 = bf16[2,64,64,48]{1,0,3,2:T(2,128)(2,1)} copy(bf16[2,64,64,48]{3,1,0,2:T(8,128)(2,1)S(1)} %bitcast.138) | data formatting | bytes 1572864 | tf_op jit(solution)/shard_map/transpose | solution.py:116
  80.7 3.9 %reshape.114 = bf16[128,3072]{0,1:T(8,128)(2,1)} reshape(bf16[2,64,64,48]{1,0,3,2:T(2,128)(2,1)} %copy.26) | data formatting | bytes 1572864 | tf_op jit(solution)/shard_map/reshape | solution.py:116
  84.6 2.0 collective-permute-start
  86.6 2.2 %constant_dynamic-update-slice_fusion.1 = bf16[256,3072]{0,1:T(8,128)(2,1)} fusion(bf16[128,3072]{0,1:T(8,128)(2,1)} %reshape.114), kind=kLoop, calls=%fused_computation.38 | loop fusion | bytes 1572864
  88.8 1.3 fusion.3
  90.1 3.3 %reshape.119 = bf16[64,2,64,48]{3,2,1,0:T(8,128)(2,1)S(1)} reshape(bf16[64,6144]{1,0:T(8,128)(2,1)} %fusion.3) | data formatting | bytes 1572864 | tf_op jit(solution)/shard_map/reshape | solution.py:115
  93.3 4.2 %copy.28 = bf16[2,64,64,48]{1,0,3,2:T(2,128)(2,1)} copy(bf16[2,64,64,48]{3,1,0,2:T(8,128)(2,1)S(1)} %bitcast.139) | data formatting | bytes 1572864 | tf_op jit(solution)/shard_map/transpose | solution.py:116
  97.6 3.1 %reshape.120 = bf16[128,3072]{0,1:T(8,128)(2,1)S(1)} reshape(bf16[2,64,64,48]{1,0,3,2:T(2,128)(2,1)} %copy.28) | data formatting | bytes 1572864 | tf_op jit(solution)/shard_map/reshape | solution.py:116
  100.7 2.0 collective-permute-start.1
  103.0 1.0 constant_dynamic-update-slice_fusion
  104.1 2.5 %convolution_dynamic-update-slice_fusion = f32[2048,256]{1,0:T(8,128)S(1)} fusion(f32[2048,256]{1,0:T(8,128)S(1)} %broadcast_in_dim.58, s32[]{:T(128)S(6)} %select_n.137, bf16[256,3072]{0,1:T(8,128)(2,1)} %constant_dynamic-update-slice_fusion), kind=kOutput, calls=%fused_computation.20 | convolution fusion | flops 402653184 | bytes 3407876 | tf_op jit(solution)/shard_map/dot_general | solution.py:133
  106.7 1.3 constant_dynamic-update-slice_fusion.3
  108.0 1.3 constant_dynamic-update-slice_fusion.7
  109.2 11.7 %collective-permute-done.1 = bf16[128,3072]{0,1:T(8,128)(2,1)} collective-permute-done((bf16[128,3072]{0,1:T(8,128)(2,1)S(1)}, bf16[128,3072]{0,1:T(8,128)(2,1)}, u32[]{:S(2)}, u32[]{:S(2)}) %collective-permute-start.1) | collective-permute-done | bytes 786464 | tf_op jit(solution)/shard_map/ppermute | solution.py:121
  121.0 1.3 constant_dynamic-update-slice_fusion.2
  122.5 0.6 fusion.23
  123.2 2.0 constant_dynamic-update-slice_fusion.11
  125.3 1.8 collective-permute-start.2
  127.4 1.7 collective-permute-start.3
  133.3 1.7 collective-permute-start.9
  135.0 7.0 %collective-permute-done.7 = f32[2,256,256]{1,2,0:T(8,128)} collective-permute-done((f32[2,256,256]{1,2,0:T(8,128)S(1)}, f32[2,256,256]{1,2,0:T(8,128)}, u32[]{:S(2)}, u32[]{:S(2)}) %collective-permute-start.7) | collective-permute-done | bytes 524320 | tf_op jit(solution)/shard_map/ppermute | solution.py:151
  142.1 1.1 slice_bitcast_fusion.2
  143.4 2.7 %collective-permute-done.2 = bf16[128,3072]{0,1:T(8,128)(2,1)} collective-permute-done((bf16[128,3072]{0,1:T(8,128)(2,1)}, bf16[128,3072]{0,1:T(8,128)(2,1)}, u32[]{:S(2)}, u32[]{:S(2)}) %collective-permute-start.2) | collective-permute-done | bytes 786464 | tf_op jit(solution)/shard_map/ppermute | solution.py:121
  146.1 1.3 constant_dynamic-update-slice_fusion.5
  147.4 13.4 %collective-permute-done.3 = bf16[128,3072]{0,1:T(8,128)(2,1)} collective-permute-done((bf16[128,3072]{0,1:T(8,128)(2,1)}, bf16[128,3072]{0,1:T(8,128)(2,1)}, u32[]{:S(2)}, u32[]{:S(2)}) %collective-permute-start.3) | collective-permute-done | bytes 786464 | tf_op jit(solution)/shard_map/ppermute | solution.py:121
  160.7 1.3 constant_dynamic-update-slice_fusion.4
  162.7 2.5 %collective-permute-start.6 = (f32[1,256,256]{1,2,0:T(8,128)S(1)}, f32[1,256,256]{1,2,0:T(8,128)S(1)}, u32[]{:S(2)}, u32[]{:S(2)}) collective-permute-start(f32[1,256,256]{1,2,0:T(8,128)S(1)} %bitcast.144), channel_id=1, source_target_pairs={{0,12},{8,4},{16,0},{24,8},{28,16},{20,24},{12,28},{4,20},{1,13},{... | collective-permute-start | bytes 786440 | tf_op jit(solution)/shard_map/ppermute | solution.py:151
  165.2 0.8 pad_maximum_fusion.1
  166.6 11.0 %collective-permute-done.9 = bf16[128,3072]{0,1:T(8,128)(2,1)} collective-permute-done((bf16[128,3072]{0,1:T(8,128)(2,1)}, bf16[128,3072]{0,1:T(8,128)(2,1)}, u32[]{:S(2)}, u32[]{:S(2)}) %collective-permute-start.9) | collective-permute-done | bytes 786464 | tf_op jit(solution)/shard_map/ppermute | solution.py:123
  177.6 2.7 %fusion.9 = f32[1,256,256]{2,1,0:T(8,128)} fusion(bf16[256,3072]{0,1:T(8,128)(2,1)S(1)} %constant_dynamic-update-slice_fusion.4, bf16[128,3072]{0,1:T(8,128)(2,1)} %collective-permute-done.10, bf16[128,3072]{0,1:T(8,128)(2,1)} %collective-permute-done.9), kind=kOutput, calls=%fused_computation.21 | convolution fusion | flops 405798912 | bytes 3407872 | tf_op jit(solution)/shard_map/dot_general | solution.py:133
  180.2 3.0 %collective-permute-start.11 = (f32[1,256,256]{2,1,0:T(8,128)}, f32[1,256,256]{2,1,0:T(8,128)}, u32[]{:S(2)}, u32[]{:S(2)}) collective-permute-start(f32[1,256,256]{2,1,0:T(8,128)} %fusion.9), channel_id=1, source_target_pairs={{0,16},{8,24},{16,28},{24,20},{28,12},{20,4},{12,0},{4,8},{1,17},{... | collective-permute-start | bytes 786440 | tf_op jit(solution)/shard_map/ppermute | solution.py:151
  183.3 1.9 collective-permute-done.6
  185.2 0.7 copy-done.5
  185.9 1.1 copy.29
  187.1 2.6 %collective-permute-done.11 = f32[1,256,256]{2,1,0:T(8,128)} collective-permute-done((f32[1,256,256]{2,1,0:T(8,128)}, f32[1,256,256]{2,1,0:T(8,128)}, u32[]{:S(2)}, u32[]{:S(2)}) %collective-permute-start.11) | collective-permute-done | bytes 262176 | tf_op jit(solution)/shard_map/ppermute | solution.py:151
  189.7 1.0 bitcast_dynamic-update-slice_fusion
  190.9 2.7 %collective-permute-done.12 = f32[2,512,256]{2,1,0:T(8,128)} collective-permute-done((f32[2,512,256]{2,1,0:T(8,128)S(1)}, f32[2,512,256]{2,1,0:T(8,128)}, u32[]{:S(2)}, u32[]{:S(2)}) %collective-permute-start.12) | collective-permute-done | bytes 1048608 | tf_op jit(solution)/shard_map/ppermute | solution.py:59
  193.7 1.4 bitcast_add_fusion
  195.1 1.6 collective-permute-start.13
  196.6 12.4 %collective-permute-done.13 = f32[512,256]{1,0:T(8,128)S(1)} collective-permute-done((f32[512,256]{1,0:T(8,128)S(1)}, f32[512,256]{1,0:T(8,128)S(1)}, u32[]{:S(2)}, u32[]{:S(2)}) %collective-permute-start.13) | collective-permute-done | bytes 524320 | tf_op jit(solution)/shard_map/ppermute | solution.py:59
  209.1 0.9 bitcast_add_fusion.1
  (59 shorter events, 6.0 us)
Async XLA Ops:
  0.0 70.8 %copy-start = (bf16[1,64,64]{2,1,0:T(8,128)(2,1)S(1)}, bf16[1,64,64]{2,1,0:T(8,128)(2,1)}, u32[]{:S(2)}) copy-start(bf16[1,64,64]{2,1,0:T(8,128)(2,1)} %param.9) | copy-start | bytes 24580
  0.0 3.2 %copy-start.1 = (s32[32]{0:T(128)S(1)}, s32[32]{0:T(128)}, u32[]{:S(2)}) copy-start(s32[32]{0:T(128)} %param.13) | copy-start | bytes 388
  4.7 1.1 copy-start.7
  30.6 27.5 %all-to-all-start = ((bf16[8,16,3072]{2,0,1:T(8,128)(2,1)}), bf16[8,16,3072]{2,0,1:T(8,128)(2,1)}, u32[]{:S(2)}, u32[]{:S(2)}) async-start(bf16[8,16,3072]{2,0,1:T(8,128)(2,1)} %select_convert_fusion.1), calls=%async_computation | async-start | bytes 1572864 | tf_op jit(solution)/shard_map/all_to_all | solution.py:112
  45.8 15.9 %copy-start.8 = (s32[8]{0:T(128)S(1)}, s32[8]{0:T(128)}, u32[]{:S(2)}) copy-start(s32[8]{0:T(128)} %constant.133.clone) | copy-start | bytes 100
  45.8 23.1 %copy-start.6 = (s32[8]{0:T(128)S(1)}, s32[8]{0:T(128)}, u32[]{:S(2)}) copy-start(s32[8]{0:T(128)} %constant.134.clone) | copy-start | bytes 100
  58.2 30.6 %all-to-all-start.1 = ((bf16[8,16,3072]{2,0,1:T(8,128)(2,1)}), bf16[8,16,3072]{2,0,1:T(8,128)(2,1)S(1)}, u32[]{:S(2)}, u32[]{:S(2)}) async-start(bf16[8,16,3072]{2,0,1:T(8,128)(2,1)} %select_convert_fusion), calls=%async_computation.1 | async-start | bytes 1572864 | tf_op jit(solution)/shard_map/all_to_all | solution.py:112
  84.6 22.1 %collective-permute-start = (bf16[128,3072]{0,1:T(8,128)(2,1)}, bf16[128,3072]{0,1:T(8,128)(2,1)}, u32[]{:S(2)}, u32[]{:S(2)}) collective-permute-start(bf16[128,3072]{0,1:T(8,128)(2,1)} %reshape.114), channel_id=1, source_target_pairs={{0,8},{8,16},{16,24},{24,28},{28,20},{20,12},{12,4},{4,0},{1,9},{9... | collective-permute-start | bytes 2359304 | tf_op jit(solution)/shard_map/ppermute | solution.py:121
  86.6 21.3 %collective-permute-start.4 = (bf16[128,3072]{0,1:T(8,128)(2,1)}, bf16[128,3072]{0,1:T(8,128)(2,1)}, u32[]{:S(2)}, u32[]{:S(2)}) collective-permute-start(bf16[128,3072]{0,1:T(8,128)(2,1)} %reshape.114), channel_id=1, source_target_pairs={{0,4},{8,0},{16,8},{24,16},{28,24},{20,28},{12,20},{4,12},{1,5},{9... | collective-permute-start | bytes 2359304 | tf_op jit(solution)/shard_map/ppermute | solution.py:123
  100.7 20.3 %collective-permute-start.1 = (bf16[128,3072]{0,1:T(8,128)(2,1)S(1)}, bf16[128,3072]{0,1:T(8,128)(2,1)}, u32[]{:S(2)}, u32[]{:S(2)}) collective-permute-start(bf16[128,3072]{0,1:T(8,128)(2,1)S(1)} %reshape.120), channel_id=1, source_target_pairs={{0,8},{8,16},{16,24},{24,28},{28,20},{20,12},{12,4},{4,0},{1,9},{9... | collective-permute-start | bytes 2359304 | tf_op jit(solution)/shard_map/ppermute | solution.py:121
  102.8 19.6 %collective-permute-start.5 = (bf16[128,3072]{0,1:T(8,128)(2,1)S(1)}, bf16[128,3072]{0,1:T(8,128)(2,1)S(1)}, u32[]{:S(2)}, u32[]{:S(2)}) collective-permute-start(bf16[128,3072]{0,1:T(8,128)(2,1)S(1)} %reshape.120), channel_id=1, source_target_pairs={{0,4},{8,0},{16,8},{24,16},{28,24},{20,28},{12,20},{4,12},{1,5},{9... | collective-permute-start | bytes 2359304 | tf_op jit(solution)/shard_map/ppermute | solution.py:123
  122.3 0.9 copy-start.2
  122.5 2.7 %copy-start.3 = (bf16[256,3072]{0,1:T(8,128)(2,1)}, bf16[256,3072]{0,1:T(8,128)(2,1)S(1)}, u32[]{:S(2)}) copy-start(bf16[256,3072]{0,1:T(8,128)(2,1)S(1)} %constant_dynamic-update-slice_fusion.6) | copy-start | bytes 4718596
  125.3 20.9 %collective-permute-start.2 = (bf16[128,3072]{0,1:T(8,128)(2,1)}, bf16[128,3072]{0,1:T(8,128)(2,1)}, u32[]{:S(2)}, u32[]{:S(2)}) collective-permute-start(bf16[128,3072]{0,1:T(8,128)(2,1)} %collective-permute-done), channel_id=1, source_target_pairs={{0,8},{8,16},{16,24},{24,28},{28,20},{20,12},{12,4},{4,0},{1,9},{9... | collective-permute-start | bytes 2359304 | tf_op jit(solution)/shard_map/ppermute | solution.py:121
  127.1 15.0 %collective-permute-start.7 = (f32[2,256,256]{1,2,0:T(8,128)S(1)}, f32[2,256,256]{1,2,0:T(8,128)}, u32[]{:S(2)}, u32[]{:S(2)}) collective-permute-start(f32[2,256,256]{1,2,0:T(8,128)S(1)} %pad_maximum_fusion), channel_id=1, source_target_pairs={{0,4},{8,0},{16,8},{24,16},{28,24},{20,28},{12,20},{4,12},{1,5},{9... | collective-permute-start | bytes 1572872 | tf_op jit(solution)/shard_map/ppermute | solution.py:151
  127.4 33.3 %collective-permute-start.3 = (bf16[128,3072]{0,1:T(8,128)(2,1)}, bf16[128,3072]{0,1:T(8,128)(2,1)}, u32[]{:S(2)}, u32[]{:S(2)}) collective-permute-start(bf16[128,3072]{0,1:T(8,128)(2,1)} %collective-permute-done.1), channel_id=1, source_target_pairs={{0,8},{8,16},{16,24},{24,28},{28,20},{20,12},{12,4},{4,0},{1,9},{9... | collective-permute-start | bytes 2359304 | tf_op jit(solution)/shard_map/ppermute | solution.py:121
  133.0 33.6 %collective-permute-start.10 = (bf16[128,3072]{0,1:T(8,128)(2,1)}, bf16[128,3072]{0,1:T(8,128)(2,1)}, u32[]{:S(2)}, u32[]{:S(2)}) collective-permute-start(bf16[128,3072]{0,1:T(8,128)(2,1)} %copy-done.2), channel_id=1, source_target_pairs={{0,4},{8,0},{16,8},{24,16},{28,24},{20,28},{12,20},{4,12},{1,5},{9... | collective-permute-start | bytes 2359304 | tf_op jit(solution)/shard_map/ppermute | solution.py:123
  133.3 44.2 %collective-permute-start.9 = (bf16[128,3072]{0,1:T(8,128)(2,1)}, bf16[128,3072]{0,1:T(8,128)(2,1)}, u32[]{:S(2)}, u32[]{:S(2)}) collective-permute-start(bf16[128,3072]{0,1:T(8,128)(2,1)} %collective-permute-done.4), channel_id=1, source_target_pairs={{0,4},{8,0},{16,8},{24,16},{28,24},{20,28},{12,20},{4,12},{1,5},{9... | collective-permute-start | bytes 2359304 | tf_op jit(solution)/shard_map/ppermute | solution.py:123
  143.4 18.6 %copy-start.4 = (bf16[256,3072]{0,1:T(8,128)(2,1)S(1)}, bf16[256,3072]{0,1:T(8,128)(2,1)}, u32[]{:S(2)}) copy-start(bf16[256,3072]{0,1:T(8,128)(2,1)} %copy-done.3) | copy-start | bytes 4718596
  162.7 22.5 %collective-permute-start.6 = (f32[1,256,256]{1,2,0:T(8,128)S(1)}, f32[1,256,256]{1,2,0:T(8,128)S(1)}, u32[]{:S(2)}, u32[]{:S(2)}) collective-permute-start(f32[1,256,256]{1,2,0:T(8,128)S(1)} %bitcast.144), channel_id=1, source_target_pairs={{0,12},{8,4},{16,0},{24,8},{28,16},{20,24},{12,28},{4,20},{1,13},{... | collective-permute-start | bytes 786440 | tf_op jit(solution)/shard_map/ppermute | solution.py:151
  166.0 21.0 %collective-permute-start.8 = (f32[2,256,256]{2,1,0:T(8,128)}, f32[2,256,256]{2,1,0:T(8,128)S(1)}, u32[]{:S(2)}, u32[]{:S(2)}) collective-permute-start(f32[2,256,256]{2,1,0:T(8,128)} %pad_maximum_fusion.1), channel_id=1, source_target_pairs={{0,8},{8,16},{16,24},{24,28},{28,20},{20,12},{12,4},{4,0},{1,9},{9... | collective-permute-start | bytes 1572872 | tf_op jit(solution)/shard_map/ppermute | solution.py:151
  180.2 9.5 %collective-permute-start.11 = (f32[1,256,256]{2,1,0:T(8,128)}, f32[1,256,256]{2,1,0:T(8,128)}, u32[]{:S(2)}, u32[]{:S(2)}) collective-permute-start(f32[1,256,256]{2,1,0:T(8,128)} %fusion.9), channel_id=1, source_target_pairs={{0,16},{8,24},{16,28},{24,20},{28,12},{20,4},{12,0},{4,8},{1,17},{... | collective-permute-start | bytes 786440 | tf_op jit(solution)/shard_map/ppermute | solution.py:151
  185.2 0.7 copy-start.5
  190.8 2.9 %collective-permute-start.12 = (f32[2,512,256]{2,1,0:T(8,128)S(1)}, f32[2,512,256]{2,1,0:T(8,128)}, u32[]{:S(2)}, u32[]{:S(2)}) collective-permute-start(f32[2,512,256]{2,1,0:T(8,128)S(1)} %dynamic-slice_bitcast_fusion), channel_id=1, source_target_pairs={{0,1},{1,0},{2,3},{3,2},{4,5},{5,4},{6,7},{7,6},{8,9},{9,8},{10,11... | collective-permute-start | bytes 3145736 | tf_op jit(solution)/shard_map/ppermute | solution.py:59
  195.1 14.0 %collective-permute-start.13 = (f32[512,256]{1,0:T(8,128)S(1)}, f32[512,256]{1,0:T(8,128)S(1)}, u32[]{:S(2)}, u32[]{:S(2)}) collective-permute-start(f32[512,256]{1,0:T(8,128)S(1)} %dynamic-slice_bitcast_fusion.1), channel_id=1, source_target_pairs={{0,2},{1,3},{2,0},{3,1},{4,6},{5,7},{6,4},{7,5},{8,10},{9,11},{10,... | collective-permute-start | bytes 1572872 | tf_op jit(solution)/shard_map/ppermute | solution.py:59

commit v19 on v17

--- a/solution.py
+++ b/solution.py
@@ -93,16 +93,16 @@
         half = half.reshape(aux_dev, n_mu, NB, n_occ)
         half = jnp.where(row_live[None, :, :, None], half, 0.0).astype(jnp.bfloat16)
         mu_dev = n_mu // n
-        n_split = mu_dev
-        mu_c = mu_dev // n_split
+        bounds = [0, 1, mu_dev] if mu_dev > 1 else [0, mu_dev]
         half = half.reshape(aux_dev, n, mu_dev, NB * n_occ)
         me = lax.axis_index("grp")
         pos = jnp.asarray(pos_of)[me]
         ring_c = jnp.asarray(ring_arr)
         radius = n // 4
         helds = []
-        for h in range(n_split):
-            part = half[:, :, h * mu_c:(h + 1) * mu_c].reshape(aux_dev, n * mu_c, NB * n_occ)
+        for lo, hi in zip(bounds[:-1], bounds[1:]):
+            mu_c = hi - lo
+            part = half[:, :, lo:hi].reshape(aux_dev, n * mu_c, NB * n_occ)
             regrouped = lax.all_to_all(part, "grp", split_axis=1, concat_axis=0, tiled=True)
             n_aux = regrouped.shape[0]
             mixed = jnp.dot(metric[0], regrouped.reshape(n_aux, -1), preferred_element_type=jnp.float32)

time: 218 us -> 218 us (level)
  waiting for transfers between devices: 69.4 us -> 95.7 us
  blocking collectives: 19.3 us -> 0 us
  starting transfers between devices: 42.8 us -> 25.6 us
  local copies, waits for them, and re-layouts: 52.6 us -> 59.7 us
    all_to_all x3 -> x2, waiting for transfers between devices: 0.01 us -> 25 us  [body(): lax.all_to_all(part, 'grp', split_axis=1, concat_axis=0, tiled=True)]
    all_to_all x1 -> x0, blocking collectives: 19.3 us -> none  [body(): lax.all_to_all(part, 'grp', split_axis=1, concat_axis=0, tiled=True)]
    ppermute x8 -> x4, waiting for transfers between devices: 34 us -> 16.9 us  [body(): bwd = lax.ppermute(bwd, 'grp', shifted(-1))]
    ppermute x8 -> x4, waiting for transfers between devices: 16.6 us -> 27.6 us  [body(): fwd = lax.ppermute(fwd, 'grp', shifted(1))]
    ppermute x8 -> x4, starting transfers between devices: 13 us -> 2.33 us  [body(): fwd = lax.ppermute(fwd, 'grp', shifted(1))]
    ppermute x4, waiting for transfers between devices: 3.67 us -> 11.1 us  [body(): got = lax.ppermute(stack, 'grp', shifted(s))]
    ppermute x8 -> x4, starting transfers between devices: 8.72 us -> 3.17 us  [body(): bwd = lax.ppermute(bwd, 'grp', shifted(-1))]
    squeeze x4, local copies, waits for them, and re-layouts: 1.37 us -> 6.51 us  [body(): placed += [(off, got[i]) for i, (off, _) in enumerate(items)]]
  transfers between devices with their start and end apart: 25 -> 16, of which waited for: 14 -> 10; matrix products, arithmetic and copies ran while one was open for 19% -> 22% of each run, Pallas kernels for 0% -> 0%
where the time goes in v19:
time: 218 us; the launch traced here: 215 us
  waiting for transfers between devices  95.7 us (44%)
  local copies, waits for them, and re-layouts  59.7 us (27%)
  starting transfers between devices  25.6 us (12%)
  matrix products  14.4 us (7%)
  between operations  12.2 us (6%)
  other arithmetic  7.69 us (4%)
    ppermute x4, waiting for transfers between devices, body(): fwd = lax.ppermute(fwd, 'grp', shifted(1))  27.6 us
    all_to_all x2, waiting for transfers between devices, body(): lax.all_to_all(part, 'grp', split_axis=1, concat_axis=0, tiled=True)  25 us
    ppermute x4, waiting for transfers between devices, body(): bwd = lax.ppermute(bwd, 'grp', shifted(-1))  16.9 us
    ppermute x2, waiting for transfers between devices, scatter_sum(): got = lax.ppermute(send, 'rep', [(i, i ^ d) for i in range(n_rep)])  15.2 us
    unnamed x29, local copies, waits for them, and re-layouts  12.7 us
    ppermute x4, waiting for transfers between devices, body(): got = lax.ppermute(stack, 'grp', shifted(s))  11.1 us
    all_to_all x2, starting transfers between devices, body(): lax.all_to_all(part, 'grp', split_axis=1, concat_axis=0, tiled=True)  10.9 us
    reshape x2, local copies, waits for them, and re-layouts, body(): jnp.transpose(mixed, (1, 2, 0, 3)).reshape(mu_c * NB, n_aux * n_occ)  9.32 us
  transfers between devices with their start and end apart: 16, of which 10 were waited for; matrix products, arithmetic and copies ran while one was open for 22% of the time, Pallas kernels for 0%

profile of v19, /device:TPU:0, one launch (start us, length us, event | category | flops | bytes accessed | tf_op | source)
XLA Modules:
  0.0 215.2 jit_solution(9099526041827075821)
XLA Ops:
  0.0 0.7 compare_select_fusion
  0.9 1.3 reshape.104
  2.4 0.7 iota_compare_fusion.4
  3.2 1.6 gather_fusion
  4.7 1.0 gather_fusion.1
  5.9 7.4 %copy.30 = bf16[192,8,32,128]{3,2,1,0:T(8,128)(2,1)S(1)} copy(bf16[192,8,32,128]{3,1,2,0:T(8,128)(2,1)} %bitcast.114) | data formatting | bytes 25165824
  13.5 1.6 broadcast_select_fusion
  15.1 7.1 %fusion.14 = bf16[8,32,32,96]{3,2,0,1:T(8,128)(2,1)} fusion(bf16[8,6,32,32,128]{4,3,2,1,0:T(8,128)(2,1)S(1)} %bitcast.115, bf16[32,6,64,48]{2,3,1,0:T(8,128)(2,1)} %broadcast_select_fusion), kind=kOutput, calls=%fused_computation.20 | convolution fusion | flops 1226833920 | bytes 15335424 | tf_op jit(solution)/shard_map/qkmtl,mklc->qmtc/dot_general | solution.py:92
  22.2 4.2 %reshape.106 = bf16[8,8,4,3072]{3,0,2,1:T(8,128)(2,1)S(1)} reshape(bf16[8,32,32,96]{3,2,0,1:T(8,128)(2,1)} %fusion.14) | data formatting | bytes 3145728 | tf_op jit(solution)/shard_map/reshape | solution.py:93
  26.8 0.7 broadcast_in_dim.47
  28.0 0.8 slice_bitcast_fusion
  28.8 7.2 %all-to-all-start = ((bf16[8,8,3072]{2,0,1:T(8,128)(2,1)}), bf16[8,8,3072]{2,0,1:T(8,128)(2,1)S(1)}, u32[]{:S(2)}, u32[]{:S(2)}) async-start(bf16[8,8,3072]{2,0,1:T(8,128)(2,1)} %slice_bitcast_fusion), calls=%async_computation | async-start | bytes 786432 | tf_op jit(solution)/shard_map/all_to_all | solution.py:106
  36.0 1.1 slice.29
  37.2 10.6 %all-to-all-done = bf16[8,8,3072]{2,0,1:T(8,128)(2,1)S(1)} async-done(((bf16[8,8,3072]{2,0,1:T(8,128)(2,1)}), bf16[8,8,3072]{2,0,1:T(8,128)(2,1)S(1)}, u32[]{:S(2)}, u32[]{:S(2)}) %all-to-all-start) | async-done | bytes 393248 | tf_op jit(solution)/shard_map/all_to_all | solution.py:106
  47.7 3.6 %all-to-all-start.1 = ((bf16[8,24,3072]{2,0,1:T(8,128)(2,1)}), bf16[8,24,3072]{2,0,1:T(8,128)(2,1)S(1)}, u32[]{:S(2)}, u32[]{:S(2)}) async-start(bf16[8,24,3072]{2,0,1:T(8,128)(2,1)} %bitcast.15), calls=%async_computation.1 | async-start | bytes 2359296 | tf_op jit(solution)/shard_map/all_to_all | solution.py:106
  51.4 0.6 dynamic_slice.41
  58.6 0.7 fusion.36
  60.9 1.1 reshape.109
  62.0 0.7 copy.23
  62.7 2.0 reshape.110
  64.7 2.1 collective-permute-start
  67.0 14.4 %all-to-all-done.1 = bf16[8,24,3072]{2,0,1:T(8,128)(2,1)S(1)} async-done(((bf16[8,24,3072]{2,0,1:T(8,128)(2,1)}), bf16[8,24,3072]{2,0,1:T(8,128)(2,1)S(1)}, u32[]{:S(2)}, u32[]{:S(2)}) %all-to-all-start.1) | async-done | bytes 1179680 | tf_op jit(solution)/shard_map/all_to_all | solution.py:106
  81.4 1.5 fusion.2
  82.9 5.4 %reshape.113 = bf16[64,3,64,48]{3,2,1,0:T(8,128)(2,1)} reshape(bf16[64,9216]{1,0:T(8,128)(2,1)} %fusion.2) | data formatting | bytes 2359296 | tf_op jit(solution)/shard_map/reshape | solution.py:109
  88.4 5.6 %copy.24 = bf16[3,64,64,48]{3,2,1,0:T(8,128)(2,1)} copy(bf16[3,64,64,48]{3,1,0,2:T(8,128)(2,1)} %bitcast.116) | data formatting | bytes 2359296 | tf_op jit(solution)/shard_map/transpose | solution.py:110
  94.0 7.3 %reshape.114 = bf16[192,3072]{1,0:T(8,128)(2,1)} reshape(bf16[3,64,64,48]{3,2,1,0:T(8,128)(2,1)} %copy.24) | data formatting | bytes 2359296 | tf_op jit(solution)/shard_map/reshape | solution.py:110
  101.3 1.0 constant_dynamic-update-slice_fusion.3
  102.6 1.0 constant_dynamic-update-slice_fusion.7
  103.6 1.9 collective-permute-start.5
  105.5 1.4 constant_dynamic-update-slice_fusion
  107.0 0.6 convolution_dynamic-update-slice_fusion
  107.6 22.9 %collective-permute-done.1 = bf16[192,3072]{1,0:T(8,128)(2,1)} collective-permute-done((bf16[192,3072]{1,0:T(8,128)(2,1)}, bf16[192,3072]{1,0:T(8,128)(2,1)}, u32[]{:S(2)}, u32[]{:S(2)}) %collective-permute-start.1) | collective-permute-done | bytes 1179680 | tf_op jit(solution)/shard_map/ppermute | solution.py:115
  130.5 1.4 constant_dynamic-update-slice_fusion.2
  131.9 0.6 constant_dynamic-update-slice_fusion.11
  132.6 0.6 fusion.38
  133.2 0.6 copy-done.2
  134.2 0.8 pad_maximum_fusion
  135.0 2.0 collective-permute-start.7
  140.8 1.0 collective-permute-start.9
  141.9 1.0 constant_dynamic-update-slice_fusion.5
  142.9 7.3 %collective-permute-done.7 = f32[2,256,256]{1,2,0:T(8,128)} collective-permute-done((f32[2,256,256]{1,2,0:T(8,128)}, f32[2,256,256]{1,2,0:T(8,128)}, u32[]{:S(2)}, u32[]{:S(2)}) %collective-permute-start.7) | collective-permute-done | bytes 524320 | tf_op jit(solution)/shard_map/ppermute | solution.py:145
  150.2 1.9 slice_bitcast_fusion.3
  152.1 1.8 copy.26
  153.9 1.8 copy.27
  155.6 4.7 %collective-permute-done.3 = bf16[192,3072]{1,0:T(8,128)(2,1)} collective-permute-done((bf16[192,3072]{1,0:T(8,128)(2,1)}, bf16[192,3072]{1,0:T(8,128)(2,1)}, u32[]{:S(2)}, u32[]{:S(2)}) %collective-permute-start.3) | collective-permute-done | bytes 1179680 | tf_op jit(solution)/shard_map/ppermute | solution.py:115
  160.3 1.3 constant_dynamic-update-slice_fusion.4
  161.7 0.6 fusion.37
  162.3 0.5 copy-done.4
  162.8 0.9 collective-permute-start.6
  163.7 0.8 pad_maximum_fusion.1
  164.5 2.3 %collective-permute-start.8 = (f32[2,256,256]{2,1,0:T(8,128)}, f32[2,256,256]{2,1,0:T(8,128)S(1)}, u32[]{:S(2)}, u32[]{:S(2)}) collective-permute-start(f32[2,256,256]{2,1,0:T(8,128)} %pad_maximum_fusion.1), channel_id=1, source_target_pairs={{0,8},{8,16},{16,24},{24,28},{28,20},{20,12},{12,4},{4,0},{1,9},{9... | collective-permute-start | bytes 1572872 | tf_op jit(solution)/shard_map/ppermute | solution.py:145
  166.9 16.9 %collective-permute-done.10 = bf16[192,3072]{1,0:T(8,128)(2,1)} collective-permute-done((bf16[192,3072]{1,0:T(8,128)(2,1)}, bf16[192,3072]{1,0:T(8,128)(2,1)}, u32[]{:S(2)}, u32[]{:S(2)}) %collective-permute-start.10) | collective-permute-done | bytes 1179680 | tf_op jit(solution)/shard_map/ppermute | solution.py:117
  183.8 3.1 %fusion.23 = f32[1,256,256]{2,1,0:T(8,128)} fusion(bf16[256,3072]{1,0:T(8,128)(2,1)} %copy-done.4, bf16[192,3072]{1,0:T(8,128)(2,1)} %collective-permute-done.10, bf16[64,3072]{1,0:T(8,128)(2,1)} %collective-permute-done.9), kind=kOutput, calls=%fused_computation.26 | convolution fusion | flops 405798912 | bytes 3407872 | tf_op jit(solution)/shard_map/dot_general | solution.py:127
  186.9 2.3 %collective-permute-start.11 = (f32[1,256,256]{2,1,0:T(8,128)}, f32[1,256,256]{2,1,0:T(8,128)}, u32[]{:S(2)}, u32[]{:S(2)}) collective-permute-start(f32[1,256,256]{2,1,0:T(8,128)} %fusion.23), channel_id=1, source_target_pairs={{0,16},{8,24},{16,28},{24,20},{28,12},{20,4},{12,0},{4,8},{1,17},{... | collective-permute-start | bytes 786440 | tf_op jit(solution)/shard_map/ppermute | solution.py:145
  189.2 1.3 collective-permute-done.6
  190.5 0.7 copy-done.8
  191.2 1.1 copy.25
  192.5 2.5 %collective-permute-done.11 = f32[1,256,256]{2,1,0:T(8,128)} collective-permute-done((f32[1,256,256]{2,1,0:T(8,128)}, f32[1,256,256]{2,1,0:T(8,128)}, u32[]{:S(2)}, u32[]{:S(2)}) %collective-permute-start.11) | collective-permute-done | bytes 262176 | tf_op jit(solution)/shard_map/ppermute | solution.py:145
  195.0 1.0 bitcast_dynamic-update-slice_fusion
  196.2 2.7 %collective-permute-done.12 = f32[2,512,256]{2,1,0:T(8,128)} collective-permute-done((f32[2,512,256]{2,1,0:T(8,128)S(1)}, f32[2,512,256]{2,1,0:T(8,128)}, u32[]{:S(2)}, u32[]{:S(2)}) %collective-permute-start.12) | collective-permute-done | bytes 1048608 | tf_op jit(solution)/shard_map/ppermute | solution.py:59
  198.9 1.4 bitcast_add_fusion
  200.4 1.6 collective-permute-start.13
  201.9 12.5 %collective-permute-done.13 = f32[512,256]{1,0:T(8,128)S(1)} collective-permute-done((f32[512,256]{1,0:T(8,128)S(1)}, f32[512,256]{1,0:T(8,128)S(1)}, u32[]{:S(2)}, u32[]{:S(2)}) %collective-permute-start.13) | collective-permute-done | bytes 524320 | tf_op jit(solution)/shard_map/ppermute | solution.py:59
  214.4 0.9 bitcast_add_fusion.1
  (53 shorter events, 3.3 us)
Async XLA Ops:
  0.0 60.6 %copy-start = (bf16[1,64,64]{2,1,0:T(8,128)(2,1)S(1)}, bf16[1,64,64]{2,1,0:T(8,128)(2,1)}, u32[]{:S(2)}) copy-start(bf16[1,64,64]{2,1,0:T(8,128)(2,1)} %param.9) | copy-start | bytes 24580
  0.0 3.2 %copy-start.1 = (s32[32]{0:T(128)S(1)}, s32[32]{0:T(128)}, u32[]{:S(2)}) copy-start(s32[32]{0:T(128)} %param.13) | copy-start | bytes 388
  4.7 1.1 copy-start.10
  28.8 18.9 %all-to-all-start = ((bf16[8,8,3072]{2,0,1:T(8,128)(2,1)}), bf16[8,8,3072]{2,0,1:T(8,128)(2,1)S(1)}, u32[]{:S(2)}, u32[]{:S(2)}) async-start(bf16[8,8,3072]{2,0,1:T(8,128)(2,1)} %slice_bitcast_fusion), calls=%async_computation | async-start | bytes 786432 | tf_op jit(solution)/shard_map/all_to_all | solution.py:106
  37.2 14.2 %copy-start.11 = (s32[8]{0:T(128)S(1)}, s32[8]{0:T(128)}, u32[]{:S(2)}) copy-start(s32[8]{0:T(128)} %constant.133.clone) | copy-start | bytes 100
  37.2 21.4 %copy-start.9 = (s32[8]{0:T(128)S(1)}, s32[8]{0:T(128)}, u32[]{:S(2)}) copy-start(s32[8]{0:T(128)} %constant.134.clone) | copy-start | bytes 100
  47.7 33.7 %all-to-all-start.1 = ((bf16[8,24,3072]{2,0,1:T(8,128)(2,1)}), bf16[8,24,3072]{2,0,1:T(8,128)(2,1)S(1)}, u32[]{:S(2)}, u32[]{:S(2)}) async-start(bf16[8,24,3072]{2,0,1:T(8,128)(2,1)} %bitcast.15), calls=%async_computation.1 | async-start | bytes 2359296 | tf_op jit(solution)/shard_map/all_to_all | solution.py:106
  64.7 36.6 %collective-permute-start = (bf16[64,3072]{1,0:T(8,128)(2,1)S(1)}, bf16[64,3072]{1,0:T(8,128)(2,1)}, u32[]{:S(2)}, u32[]{:S(2)}) collective-permute-start(bf16[64,3072]{1,0:T(8,128)(2,1)S(1)} %reshape.110), channel_id=1, source_target_pairs={{0,8},{8,16},{16,24},{24,28},{28,20},{20,12},{12,4},{4,0},{1,9},{9... | collective-permute-start | bytes 1179656 | tf_op jit(solution)/shard_map/ppermute | solution.py:115
  66.8 35.8 %collective-permute-start.4 = (bf16[64,3072]{1,0:T(8,128)(2,1)S(1)}, bf16[64,3072]{1,0:T(8,128)(2,1)}, u32[]{:S(2)}, u32[]{:S(2)}) collective-permute-start(bf16[64,3072]{1,0:T(8,128)(2,1)S(1)} %reshape.110), channel_id=1, source_target_pairs={{0,4},{8,0},{16,8},{24,16},{28,24},{20,28},{12,20},{4,12},{1,5},{9... | collective-permute-start | bytes 1179656 | tf_op jit(solution)/shard_map/ppermute | solution.py:117
  101.3 29.2 %collective-permute-start.1 = (bf16[192,3072]{1,0:T(8,128)(2,1)}, bf16[192,3072]{1,0:T(8,128)(2,1)}, u32[]{:S(2)}, u32[]{:S(2)}) collective-permute-start(bf16[192,3072]{1,0:T(8,128)(2,1)} %reshape.114), channel_id=1, source_target_pairs={{0,8},{8,16},{16,24},{24,28},{28,20},{20,12},{12,4},{4,0},{1,9},{9... | collective-permute-start | bytes 3538952 | tf_op jit(solution)/shard_map/ppermute | solution.py:115
  102.3 39.6 %collective-permute-start.2 = (bf16[64,3072]{1,0:T(8,128)(2,1)}, bf16[64,3072]{1,0:T(8,128)(2,1)}, u32[]{:S(2)}, u32[]{:S(2)}) collective-permute-start(bf16[64,3072]{1,0:T(8,128)(2,1)} %collective-permute-done), channel_id=1, source_target_pairs={{0,8},{8,16},{16,24},{24,28},{28,20},{20,12},{12,4},{4,0},{1,9},{9... | collective-permute-start | bytes 1179656 | tf_op jit(solution)/shard_map/ppermute | solution.py:115
  103.6 28.9 %collective-permute-start.5 = (bf16[192,3072]{1,0:T(8,128)(2,1)}, bf16[192,3072]{1,0:T(8,128)(2,1)S(1)}, u32[]{:S(2)}, u32[]{:S(2)}) collective-permute-start(bf16[192,3072]{1,0:T(8,128)(2,1)} %reshape.114), channel_id=1, source_target_pairs={{0,4},{8,0},{16,8},{24,16},{28,24},{20,28},{12,20},{4,12},{1,5},{9... | collective-permute-start | bytes 3538952 | tf_op jit(solution)/shard_map/ppermute | solution.py:117
  130.5 29.8 %collective-permute-start.3 = (bf16[192,3072]{1,0:T(8,128)(2,1)}, bf16[192,3072]{1,0:T(8,128)(2,1)}, u32[]{:S(2)}, u32[]{:S(2)}) collective-permute-start(bf16[192,3072]{1,0:T(8,128)(2,1)} %collective-permute-done.1), channel_id=1, source_target_pairs={{0,8},{8,16},{16,24},{24,28},{28,20},{20,12},{12,4},{4,0},{1,9},{9... | collective-permute-start | bytes 3538952 | tf_op jit(solution)/shard_map/ppermute | solution.py:115
  132.5 1.4 copy-start.2
  132.5 1.7 copy-start.5
  135.0 15.2 %collective-permute-start.7 = (f32[2,256,256]{1,2,0:T(8,128)}, f32[2,256,256]{1,2,0:T(8,128)}, u32[]{:S(2)}, u32[]{:S(2)}) collective-permute-start(f32[2,256,256]{1,2,0:T(8,128)} %pad_maximum_fusion), channel_id=1, source_target_pairs={{0,4},{8,0},{16,8},{24,16},{28,24},{20,28},{12,20},{4,12},{1,5},{9... | collective-permute-start | bytes 1572872 | tf_op jit(solution)/shard_map/ppermute | solution.py:145
  140.8 26.0 %collective-permute-start.9 = (bf16[64,3072]{1,0:T(8,128)(2,1)}, bf16[64,3072]{1,0:T(8,128)(2,1)}, u32[]{:S(2)}, u32[]{:S(2)}) collective-permute-start(bf16[64,3072]{1,0:T(8,128)(2,1)} %collective-permute-done.4), channel_id=1, source_target_pairs={{0,4},{8,0},{16,8},{24,16},{28,24},{20,28},{12,20},{4,12},{1,5},{9... | collective-permute-start | bytes 1179656 | tf_op jit(solution)/shard_map/ppermute | solution.py:117
  141.8 42.0 %collective-permute-start.10 = (bf16[192,3072]{1,0:T(8,128)(2,1)}, bf16[192,3072]{1,0:T(8,128)(2,1)}, u32[]{:S(2)}, u32[]{:S(2)}) collective-permute-start(bf16[192,3072]{1,0:T(8,128)(2,1)} %copy-done.5), channel_id=1, source_target_pairs={{0,4},{8,0},{16,8},{24,16},{28,24},{20,28},{12,20},{4,12},{1,5},{9... | collective-permute-start | bytes 3538952 | tf_op jit(solution)/shard_map/ppermute | solution.py:117
  161.7 1.1 copy-start.4
  162.8 27.7 %collective-permute-start.6 = (f32[1,256,256]{1,2,0:T(8,128)S(1)}, f32[1,256,256]{1,2,0:T(8,128)S(1)}, u32[]{:S(2)}, u32[]{:S(2)}) collective-permute-start(f32[1,256,256]{1,2,0:T(8,128)S(1)} %bitcast.123), channel_id=1, source_target_pairs={{0,12},{8,4},{16,0},{24,8},{28,16},{20,24},{12,28},{4,20},{1,13},{... | collective-permute-start | bytes 786440 | tf_op jit(solution)/shard_map/ppermute | solution.py:145
  164.5 27.8 %copy-start.3 = (f32[2048,256]{1,0:T(8,128)S(1)}, f32[2048,256]{1,0:T(8,128)}, u32[]{:S(2)}) copy-start(f32[2048,256]{1,0:T(8,128)} %copy-done.2) | copy-start | bytes 6291460
  164.5 27.8 %copy-start.7 = (f32[256,256]{1,0:T(8,128)S(1)}, f32[256,256]{1,0:T(8,128)}, u32[]{:S(2)}) copy-start(f32[256,256]{1,0:T(8,128)} %copy.26) | copy-start | bytes 786436
  164.5 27.9 %collective-permute-start.8 = (f32[2,256,256]{2,1,0:T(8,128)}, f32[2,256,256]{2,1,0:T(8,128)S(1)}, u32[]{:S(2)}, u32[]{:S(2)}) collective-permute-start(f32[2,256,256]{2,1,0:T(8,128)} %pad_maximum_fusion.1), channel_id=1, source_target_pairs={{0,8},{8,16},{16,24},{24,28},{28,20},{20,12},{12,4},{4,0},{1,9},{9... | collective-permute-start | bytes 1572872 | tf_op jit(solution)/shard_map/ppermute | solution.py:145
  186.9 5.5 %copy-start.6 = (f32[256,256]{1,0:T(8,128)S(1)}, f32[256,256]{1,0:T(8,128)}, u32[]{:S(2)}) copy-start(f32[256,256]{1,0:T(8,128)} %copy.27) | copy-start | bytes 786436
  186.9 8.1 %collective-permute-start.11 = (f32[1,256,256]{2,1,0:T(8,128)}, f32[1,256,256]{2,1,0:T(8,128)}, u32[]{:S(2)}, u32[]{:S(2)}) collective-permute-start(f32[1,256,256]{2,1,0:T(8,128)} %fusion.23), channel_id=1, source_target_pairs={{0,16},{8,24},{16,28},{24,20},{28,12},{20,4},{12,0},{4,8},{1,17},{... | collective-permute-start | bytes 786440 | tf_op jit(solution)/shard_map/ppermute | solution.py:145
  190.5 0.7 copy-start.8
  196.1 2.9 %collective-permute-start.12 = (f32[2,512,256]{2,1,0:T(8,128)S(1)}, f32[2,512,256]{2,1,0:T(8,128)}, u32[]{:S(2)}, u32[]{:S(2)}) collective-permute-start(f32[2,512,256]{2,1,0:T(8,128)S(1)} %dynamic-slice_bitcast_fusion), channel_id=1, source_target_pairs={{0,1},{1,0},{2,3},{3,2},{4,5},{5,4},{6,7},{7,6},{8,9},{9,8},{10,11... | collective-permute-start | bytes 3145736 | tf_op jit(solution)/shard_map/ppermute | solution.py:59
  200.4 14.0 %collective-permute-start.13 = (f32[512,256]{1,0:T(8,128)S(1)}, f32[512,256]{1,0:T(8,128)S(1)}, u32[]{:S(2)}, u32[]{:S(2)}) collective-permute-start(f32[512,256]{1,0:T(8,128)S(1)} %dynamic-slice_bitcast_fusion.1), channel_id=1, source_target_pairs={{0,2},{1,3},{2,0},{3,1},{4,6},{5,7},{6,4},{7,5},{8,10},{9,11},{10,... | collective-permute-start | bytes 1572872 | tf_op jit(solution)/shard_map/ppermute | solution.py:59
